TPU v7x, 32 devices: a whole 2x2x4 slice. The times are simulated.
32 devices in a mesh: blk: 16 (over z, y, x), mp: 2 (over core).
Axes of the slice: x: 2, y: 2, z: 4, core: 2. Of those that a mesh axis runs over, the one named last changes fastest.
Arguments:
- queries: bfloat16 [6144, 2560], P('blk', 'mp'), may hold values from -11 to 11
- keys: bfloat16 [2048, 2560], P('blk', 'mp'), may hold values from -11 to 11
- values: bfloat16 [2048, 2560], P('blk', 'mp'), may hold values from -6 to 6
- out_weight: bfloat16 [2560, 5120], P('mp'), may hold values from -0.125 to 0.125
Outputs:
- mixed: bfloat16 [6144, 5120], P('blk', 'mp')
All inputs are finite; a program needn't handle non-finite values.
Results may differ from a plain program's by a relative error of at most 0.018.
Values may be sent and summed in bfloat16 or wider, within the bound.
No kernel may reach another device: no remote copies, remote signals or barrier semaphores. Data moves between devices by JAX's collectives and lax.ppermute only.
A program may use at most 64 MiB of HBM per device.

v0:
```python
import math

import jax
import jax.numpy as jnp
from jax import lax
from jax.sharding import PartitionSpec as P

HS = 128


def from_behind(value, axis, steps):
    count = lax.axis_size(axis)
    pairs = [(source, (source + steps) % count) for source in range(count)]
    return lax.ppermute(value, axis, pairs)


def fold_block(state, stacked_blocks, query_heads):
    running_max, running_sum, numerator = state
    head_count = query_heads.shape[1]
    key_heads = stacked_blocks[0].reshape(stacked_blocks.shape[1], head_count, HS)
    value_heads = stacked_blocks[1].reshape(stacked_blocks.shape[1], head_count, HS)
    scores = jnp.einsum("qhd,khd->qhk", query_heads, key_heads, preferred_element_type=jnp.float32)
    scores = scores * (1.0 / math.sqrt(HS))
    new_max = jnp.maximum(running_max, jnp.max(scores, axis=-1))
    rescale = jnp.exp(running_max - new_max)
    weights = jnp.exp(scores - new_max[:, :, None])
    new_sum = running_sum * rescale + jnp.sum(weights, axis=-1)
    product = jnp.einsum(
        "qhk,khd->qhd",
        weights.astype(jnp.bfloat16),
        value_heads,
        preferred_element_type=jnp.float32,
    )
    new_numerator = numerator * rescale[:, :, None] + product
    return (new_max, new_sum, new_numerator)


def on_device(queries, keys, values, out_weight):
    row_count = queries.shape[0]
    head_count = queries.shape[1] // HS
    query_heads = queries.reshape(row_count, head_count, HS)
    state = (
        jnp.full((row_count, head_count), -jnp.inf, jnp.float32),
        jnp.zeros((row_count, head_count), jnp.float32),
        jnp.zeros((row_count, head_count, HS), jnp.float32),
    )
    stacked_blocks = jnp.stack((keys, values))
    moving = from_behind(stacked_blocks, "blk", -2)
    state = fold_block(state, moving, query_heads)
    for repeat in range(4):
        moving = from_behind(moving, "blk", 1)
        state = fold_block(state, moving, query_heads)
    running_max, running_sum, numerator = state
    attended = (
        (numerator / running_sum[:, :, None])
        .reshape(row_count, head_count * HS)
        .astype(jnp.bfloat16)
    )
    window_partial_sum = jnp.dot(attended, out_weight, preferred_element_type=jnp.float32)
    summed = lax.psum_scatter(
        window_partial_sum.astype(jnp.bfloat16), "mp", scatter_dimension=1, tiled=True
    )
    return summed


def solution(mesh):
    placed = (P("blk", "mp"), P("blk", "mp"), P("blk", "mp"), P("mp", None))
    return jax.shard_map(
        on_device, mesh=mesh, in_specs=placed, out_specs=P("blk", "mp"), check_vma=False
    )
```

profile of v0, /device:TPU:1, one launch (start us, length us, event | category | flops | bytes accessed | tf_op | source)
XLA Modules:
  0.0 130.9 jit_solution(17651420629400904696)
XLA Ops:
  6.5 1.3 copy.20
  7.8 1.2 copy.21
  9.1 5.1 %collective-permute-start = (bf16[2,128,1280]{1,2,0:T(8,128)(2,1)S(1)}, bf16[2,128,1280]{1,2,0:T(8,128)(2,1)S(1)}, u32[]{:S(2)}, u32[]{:S(2)}) collective-permute-start(bf16[2,128,1280]{1,2,0:T(8,128)(2,1)S(1)} %pad_maximum_fusion), channel_id=1, source_target_pairs={{0,28},{2,30},{4,0},{6,2},{8,4},{10,6},{12,8},{14,10},{16,12},{18,... | collective-permute-start | bytes 1966088 | tf_op jit(solution)/shard_map/ppermute | solution.py:14
  14.2 0.6 copy.22
  14.9 12.8 %collective-permute-done = bf16[2,128,1280]{1,2,0:T(8,128)(2,1)S(1)} collective-permute-done((bf16[2,128,1280]{1,2,0:T(8,128)(2,1)S(1)}, bf16[2,128,1280]{1,2,0:T(8,128)(2,1)S(1)}, u32[]{:S(2)}, u32[]{:S(2)}) %collective-permute-start) | collective-permute-done | bytes 655392 | tf_op jit(solution)/shard_map/ppermute | solution.py:14
  27.7 1.3 collective-permute-start.1
  28.9 0.5 bitcast_reduce_fusion.4
  29.8 0.5 fusion.28
  30.2 16.9 %collective-permute-done.1 = bf16[2,128,1280]{1,2,0:T(8,128)(2,1)S(1)} collective-permute-done((bf16[2,128,1280]{1,2,0:T(8,128)(2,1)S(1)}, bf16[2,128,1280]{1,2,0:T(8,128)(2,1)S(1)}, u32[]{:S(2)}, u32[]{:S(2)}) %collective-permute-start.1) | collective-permute-done | bytes 655392 | tf_op jit(solution)/shard_map/ppermute | solution.py:14
  47.2 0.5 bitcast_reduce_fusion.3
  47.7 17.2 %collective-permute-done.2 = bf16[2,128,1280]{1,2,0:T(8,128)(2,1)S(1)} collective-permute-done((bf16[2,128,1280]{1,2,0:T(8,128)(2,1)S(1)}, bf16[2,128,1280]{1,2,0:T(8,128)(2,1)S(1)}, u32[]{:S(2)}, u32[]{:S(2)}) %collective-permute-start.2) | collective-permute-done | bytes 655392 | tf_op jit(solution)/shard_map/ppermute | solution.py:14
  65.0 0.5 bitcast_reduce_fusion.2
  65.5 16.4 %collective-permute-done.3 = bf16[2,128,1280]{1,2,0:T(8,128)(2,1)S(1)} collective-permute-done((bf16[2,128,1280]{1,2,0:T(8,128)(2,1)S(1)}, bf16[2,128,1280]{1,2,0:T(8,128)(2,1)S(1)}, u32[]{:S(2)}, u32[]{:S(2)}) %collective-permute-start.3) | collective-permute-done | bytes 655392 | tf_op jit(solution)/shard_map/ppermute | solution.py:14
  81.9 0.5 bitcast_reduce_fusion.1
  82.4 15.5 %collective-permute-done.4 = bf16[2,128,1280]{1,2,0:T(8,128)(2,1)S(1)} collective-permute-done((bf16[2,128,1280]{1,2,0:T(8,128)(2,1)S(1)}, bf16[2,128,1280]{1,2,0:T(8,128)(2,1)S(1)}, u32[]{:S(2)}, u32[]{:S(2)}) %collective-permute-start.4) | collective-permute-done | bytes 655392 | tf_op jit(solution)/shard_map/ppermute | solution.py:14
  98.0 0.5 bitcast_reduce_fusion
  98.5 0.5 fusion.24
  98.9 0.7 fusion.13
  100.6 0.7 fusion.17
  101.4 1.1 fusion.1
  102.6 0.8 slice-done.2
  103.4 1.1 slice-done.3
  104.5 7.0 %convolution_convert_fusion = bf16[384,5120]{1,0:T(8,128)(2,1)} fusion(bf16[384,1280]{0,1:T(8,128)(2,1)S(1)} %bitcast.130, bf16[1280,5120]{1,0:T(8,128)(2,1)S(1)} %bitcast.129), kind=kOutput, calls=%fused_computation | convolution fusion | flops 5035130880 | bytes 18022400 | tf_op jit(solution)/shard_map/dot_general | solution.py:59
  111.5 12.5 %reduce-scatter.2.cloned.1.call-done = bf16[384,2560]{1,0:T(8,128)(2,1)} async-done(((bf16[384,5120]{1,0:T(8,128)(2,1)}), bf16[384,2560]{1,0:T(8,128)(2,1)}) %reduce-scatter.2.cloned.1.call-update) | async-done | bytes 1966096 | tf_op jit(solution)/shard_map/reduce_scatter | solution.py:60
  (25 shorter events, 1.7 us)
Async XLA Ops:
  6.5 7.7 %copy-start = (bf16[384,1280]{1,0:T(8,128)(2,1)S(1)}, bf16[384,1280]{1,0:T(8,128)(2,1)}, u32[]{:S(2)}) copy-start(bf16[384,1280]{1,0:T(8,128)(2,1)} %param.4) | copy-start | bytes 2949124
  6.5 117.5 %reduce-scatter.2.cloned.1.call-start = ((), (), s32[]{:S(2)}) async-start(), calls=%async_computation.1 | async-start | bytes 5898240 | tf_op jit(solution)/shard_map/reduce_scatter | solution.py:60
  9.1 18.6 %collective-permute-start = (bf16[2,128,1280]{1,2,0:T(8,128)(2,1)S(1)}, bf16[2,128,1280]{1,2,0:T(8,128)(2,1)S(1)}, u32[]{:S(2)}, u32[]{:S(2)}) collective-permute-start(bf16[2,128,1280]{1,2,0:T(8,128)(2,1)S(1)} %pad_maximum_fusion), channel_id=1, source_target_pairs={{0,28},{2,30},{4,0},{6,2},{8,4},{10,6},{12,8},{14,10},{16,12},{18,... | collective-permute-start | bytes 1966088 | tf_op jit(solution)/shard_map/ppermute | solution.py:14
  27.7 19.5 %collective-permute-start.1 = (bf16[2,128,1280]{1,2,0:T(8,128)(2,1)S(1)}, bf16[2,128,1280]{1,2,0:T(8,128)(2,1)S(1)}, u32[]{:S(2)}, u32[]{:S(2)}) collective-permute-start(bf16[2,128,1280]{1,2,0:T(8,128)(2,1)S(1)} %collective-permute-done), channel_id=1, source_target_pairs={{0,2},{2,4},{4,6},{6,8},{8,10},{10,12},{12,14},{14,16},{16,18},{18... | collective-permute-start | bytes 1966088 | tf_op jit(solution)/shard_map/ppermute | solution.py:14
  47.1 17.8 %collective-permute-start.2 = (bf16[2,128,1280]{1,2,0:T(8,128)(2,1)S(1)}, bf16[2,128,1280]{1,2,0:T(8,128)(2,1)S(1)}, u32[]{:S(2)}, u32[]{:S(2)}) collective-permute-start(bf16[2,128,1280]{1,2,0:T(8,128)(2,1)S(1)} %collective-permute-done.1), channel_id=1, source_target_pairs={{0,2},{2,4},{4,6},{6,8},{8,10},{10,12},{12,14},{14,16},{16,18},{18... | collective-permute-start | bytes 1966088 | tf_op jit(solution)/shard_map/ppermute | solution.py:14
  64.9 16.9 %collective-permute-start.3 = (bf16[2,128,1280]{1,2,0:T(8,128)(2,1)S(1)}, bf16[2,128,1280]{1,2,0:T(8,128)(2,1)S(1)}, u32[]{:S(2)}, u32[]{:S(2)}) collective-permute-start(bf16[2,128,1280]{1,2,0:T(8,128)(2,1)S(1)} %collective-permute-done.2), channel_id=1, source_target_pairs={{0,2},{2,4},{4,6},{6,8},{8,10},{10,12},{12,14},{14,16},{16,18},{18... | collective-permute-start | bytes 1966088 | tf_op jit(solution)/shard_map/ppermute | solution.py:14
  81.8 16.1 %collective-permute-start.4 = (bf16[2,128,1280]{1,2,0:T(8,128)(2,1)S(1)}, bf16[2,128,1280]{1,2,0:T(8,128)(2,1)S(1)}, u32[]{:S(2)}, u32[]{:S(2)}) collective-permute-start(bf16[2,128,1280]{1,2,0:T(8,128)(2,1)S(1)} %collective-permute-done.3), channel_id=1, source_target_pairs={{0,2},{2,4},{4,6},{6,8},{8,10},{10,12},{12,14},{14,16},{16,18},{18... | collective-permute-start | bytes 1966088 | tf_op jit(solution)/shard_map/ppermute | solution.py:14
  98.9 3.6 %slice-start = ((s8[13107200]{0:T(1024)(128)(4,1)}), s8[524288]{0:T(1024)(128)(4,1)S(1)}, s32[]{:S(2)}) async-start(s8[13107200]{0:T(1024)(128)(4,1)} %bitcast.128), calls=%async_computation.2 | async-start | bytes 1048576
  99.7 2.9 %slice-start.1 = ((s8[13107200]{0:T(1024)(128)(4,1)}), s8[4194304]{0:T(1024)(128)(4,1)S(1)}, s32[]{:S(2)}) async-start(s8[13107200]{0:T(1024)(128)(4,1)} %bitcast.128), calls=%async_computation.3 | async-start | bytes 8388608
  100.6 2.8 %slice-start.2 = ((s8[13107200]{0:T(1024)(128)(4,1)}), s8[4194304]{0:T(1024)(128)(4,1)S(1)}, s32[]{:S(2)}) async-start(s8[13107200]{0:T(1024)(128)(4,1)} %bitcast.128), calls=%async_computation.4 | async-start | bytes 8388608
  101.4 3.1 %slice-start.3 = ((s8[13107200]{0:T(1024)(128)(4,1)}), s8[4194304]{0:T(1024)(128)(4,1)S(1)}, s32[]{:S(2)}) async-start(s8[13107200]{0:T(1024)(128)(4,1)} %bitcast.128), calls=%async_computation.5 | async-start | bytes 8388608
Sparse Core Ops, SparseCore 0:
  111.6 12.3 reduce-scatter.1
where the time goes:
time: 131 us
  waiting for transfers between devices  91.3 us (70%)
  between operations  13.6 us (10%)
  matrix products  12.3 us (9%)
  starting transfers between devices  6.42 us (5%)
  local copies, waits for them, and re-layouts  5.28 us (4%)
  other arithmetic  1.91 us (1%)
    ppermute x5, waiting for transfers between devices, from_behind(): return lax.ppermute(value, axis, pairs)  78.8 us
    reduce_scatter x1, waiting for transfers between devices, on_device(): lax.psum_scatter(window_partial_sum.astype(jnp.bfloat16), 'mp', scatter_d...  12.5 us
    dot_general x1, matrix products, on_device(): jnp.dot(attended, out_weight, preferred_element_type=jnp.float32)  7 us
    ppermute x5, starting transfers between devices, from_behind(): return lax.ppermute(value, axis, pairs)  6.42 us
    unnamed x13, local copies, waits for them, and re-layouts  5.06 us
    dot_general x5, matrix products, fold_block(): jnp.einsum('qhk,khd->qhd', weights.astype(jnp.bfloat16), value_heads, pre...  2.96 us
  transfers between devices with their start and end apart: 6, of which 6 were waited for; matrix products, arithmetic and copies ran while one was open for 3% of the time, Pallas kernels for 0%

commit v1 on v0

--- a/solution.py
+++ b/solution.py
@@ -45,10 +45,9 @@
         jnp.zeros((row_count, head_count, HS), jnp.float32),
     )
     stacked_blocks = jnp.stack((keys, values))
-    moving = from_behind(stacked_blocks, "blk", -2)
-    state = fold_block(state, moving, query_heads)
-    for repeat in range(4):
-        moving = from_behind(moving, "blk", 1)
+    arrivals = [from_behind(stacked_blocks, "blk", steps) for steps in (1, -1, 2, -2)]
+    state = fold_block(state, stacked_blocks, query_heads)
+    for moving in arrivals:
         state = fold_block(state, moving, query_heads)
     running_max, running_sum, numerator = state
     attended = (

time: 131 us -> 95.4 us (0.73)
  waiting for transfers between devices: 91.3 us -> 47.7 us
  starting transfers between devices: 6.42 us -> 10.2 us
  local copies, waits for them, and re-layouts: 5.28 us -> 8.47 us
    ppermute x5 -> x4, waiting for transfers between devices: 78.8 us -> 33.7 us  [from_behind(): return lax.ppermute(value, axis, pairs)]
    ppermute x5 -> x4, starting transfers between devices: 6.42 us -> 10.2 us  [from_behind(): return lax.ppermute(value, axis, pairs)]
    slice x4 -> x3, local copies, waits for them, and re-layouts: 0.17 us -> 2.28 us  [fold_block(): stacked_blocks[1].reshape(stacked_blocks.shape[1], head_count, HS)]
    reduce_scatter x1, waiting for transfers between devices: 12.5 us -> 14 us  [on_device(): lax.psum_scatter(window_partial_sum.astype(jnp.bfloat16), 'mp', scatter_d...]
  transfers between devices with their start and end apart: 6 -> 5, of which waited for: 6 -> 2; matrix products, arithmetic and copies ran while one was open for 3% -> 7% of each run, Pallas kernels for 0% -> 0%
where the time goes in v1:
time: 95.4 us; the launch traced here: 95 us
  waiting for transfers between devices  47.7 us (50%)
  between operations  13.6 us (14%)
  matrix products  12.3 us (13%)
  starting transfers between devices  10.2 us (11%)
  local copies, waits for them, and re-layouts  8.47 us (9%)
  other arithmetic  2.74 us (3%)
    ppermute x4, waiting for transfers between devices, from_behind(): return lax.ppermute(value, axis, pairs)  33.7 us
    reduce_scatter x1, waiting for transfers between devices, on_device(): lax.psum_scatter(window_partial_sum.astype(jnp.bfloat16), 'mp', scatter_d...  14 us
    ppermute x4, starting transfers between devices, from_behind(): return lax.ppermute(value, axis, pairs)  10.2 us
    dot_general x1, matrix products, on_device(): jnp.dot(attended, out_weight, preferred_element_type=jnp.float32)  7 us
    unnamed x13, local copies, waits for them, and re-layouts  5.07 us
    dot_general x5, matrix products, fold_block(): jnp.einsum('qhk,khd->qhd', weights.astype(jnp.bfloat16), value_heads, pre...  2.95 us
    dot_general x5, matrix products, fold_block(): jnp.einsum('qhd,khd->qhk', query_heads, key_heads, preferred_element_type...  2.38 us
    slice x3, local copies, waits for them, and re-layouts, fold_block(): stacked_blocks[1].reshape(stacked_blocks.shape[1], head_count, HS)  2.28 us
  transfers between devices with their start and end apart: 5, of which 2 were waited for; matrix products, arithmetic and copies ran while one was open for 7% of the time, Pallas kernels for 0%

profile of v1, /device:TPU:1, one launch (start us, length us, event | category | flops | bytes accessed | tf_op | source)
XLA Modules:
  0.0 95.0 jit_solution(12660141940636852528)
XLA Ops:
  6.5 1.3 %copy.21 = bf16[128,1280]{0,1:T(8,128)(2,1)S(1)} copy(bf16[128,1280]{1,0:T(8,128)(2,1)} %param.5) | data formatting | bytes 655360 | tf_op args[1]
  7.8 1.2 %copy.25 = bf16[128,1280]{0,1:T(8,128)(2,1)S(1)} copy(bf16[128,1280]{1,0:T(8,128)(2,1)} %param.6) | data formatting | bytes 655360 | tf_op args[2]
  9.0 0.9 pad_maximum_fusion
  9.9 5.1 %collective-permute-start.3 = (bf16[2,128,1280]{1,2,0:T(8,128)(2,1)}, bf16[2,128,1280]{1,2,0:T(8,128)(2,1)S(1)}, u32[]{:S(2)}, u32[]{:S(2)}) collective-permute-start(bf16[2,128,1280]{1,2,0:T(8,128)(2,1)} %pad_maximum_fusion), channel_id=1, source_target_pairs={{0,28},{2,30},{4,0},{6,2},{8,4},{10,6},{12,8},{14,10},{16,12},{18,... | collective-permute-start | bytes 1966088 | tf_op jit(solution)/shard_map/ppermute | solution.py:14
  15.0 5.1 %collective-permute-start.1 = (bf16[2,128,1280]{1,2,0:T(8,128)(2,1)}, bf16[2,128,1280]{1,2,0:T(8,128)(2,1)}, u32[]{:S(2)}, u32[]{:S(2)}) collective-permute-start(bf16[2,128,1280]{1,2,0:T(8,128)(2,1)} %pad_maximum_fusion), channel_id=1, source_target_pairs={{0,30},{2,0},{4,2},{6,4},{8,6},{10,8},{12,10},{14,12},{16,14},{18,... | collective-permute-start | bytes 1966088 | tf_op jit(solution)/shard_map/ppermute | solution.py:14
  20.1 0.6 copy.22
  20.7 0.5 bitcast_reduce_fusion.4
  22.0 33.7 %collective-permute-done.2 = bf16[2,128,1280]{1,2,0:T(8,128)(2,1)} collective-permute-done((bf16[2,128,1280]{1,2,0:T(8,128)(2,1)}, bf16[2,128,1280]{1,2,0:T(8,128)(2,1)}, u32[]{:S(2)}, u32[]{:S(2)}) %collective-permute-start.2) | collective-permute-done | bytes 655392 | tf_op jit(solution)/shard_map/ppermute | solution.py:14
  55.7 1.1 %fusion.49 = (bf16[1,128,1280]{1,2,0:T(8,128)(2,1)S(1)}, bf16[1,128,1280]{1,2,0:T(8,128)(2,1)S(1)}) fusion(bf16[2,128,1280]{1,2,0:T(8,128)(2,1)} %collective-permute-done.2), kind=kLoop, calls=%fused_computation.67 | loop fusion | bytes 1310720 | tf_op jit(solution)/shard_map/slice | solution.py:20
  56.8 1.1 %fusion.48 = (bf16[1,128,1280]{1,2,0:T(8,128)(2,1)S(1)}, bf16[1,128,1280]{1,2,0:T(8,128)(2,1)S(1)}) fusion(bf16[2,128,1280]{1,2,0:T(8,128)(2,1)} %collective-permute-done.1), kind=kLoop, calls=%fused_computation.66 | loop fusion | bytes 1310720 | tf_op jit(solution)/shard_map/slice | solution.py:21
  58.0 1.1 %fusion.47 = (bf16[1,128,1280]{1,2,0:T(8,128)(2,1)S(1)}, bf16[1,128,1280]{1,2,0:T(8,128)(2,1)S(1)}) fusion(bf16[2,128,1280]{1,2,0:T(8,128)(2,1)} %collective-permute-done), kind=kLoop, calls=%fused_computation.65 | loop fusion | bytes 1310720 | tf_op jit(solution)/shard_map/slice | solution.py:21
  59.1 0.5 bitcast_reduce_fusion.3
  59.6 0.5 bitcast_reduce_fusion.2
  60.1 0.5 bitcast_reduce_fusion.1
  60.6 0.5 bitcast_reduce_fusion
  61.1 0.5 fusion.24
  61.6 0.7 fusion.13
  62.8 0.5 fusion.22
  63.3 0.7 fusion.17
  64.1 1.1 %fusion.1 = bf16[384,10,128]{0,2,1:T(8,128)(2,1)S(1)} fusion(f32[10,128,384]{2,1,0:T(8,128)S(1)} %fusion.22, f32[10,128,384]{2,1,0:T(8,128)S(1)} %fusion.24, f32[10,128,384]{2,1,0:T(8,128)S(1)} %fusion.26, f32[10,384,128]{1,2,0:T(8,128)S(1)} %fusion.28, bf16[128,10,128]{0,2,1:T(8,128)(2,1)S(1)} %bitcast.127, f32[10,128,384]{2,1,0:T(8,128)S(1)} %get-tuple-element.24, ...), kind=kOutput, calls=%fused_computation.3 | convolution fusion | flops 132710400 | bytes 11248640 | tf_op jit(solution)/shard_map/qhk,khd->qhd/dot_general | solution.py:28
  65.2 0.8 slice-done.2
  66.0 1.1 %slice-done.3 = s8[4194304]{0:T(1024)(128)(4,1)S(1)} async-done(((s8[13107200]{0:T(1024)(128)(4,1)}), s8[4194304]{0:T(1024)(128)(4,1)S(1)}, s32[]{:S(2)}) %slice-start.3) | async-done | bytes 4194328
  67.1 7.0 %convolution_convert_fusion = bf16[384,5120]{1,0:T(8,128)(2,1)} fusion(bf16[384,1280]{0,1:T(8,128)(2,1)S(1)} %bitcast.130, bf16[1280,5120]{1,0:T(8,128)(2,1)S(1)} %bitcast.129), kind=kOutput, calls=%fused_computation | convolution fusion | flops 5035130880 | bytes 18022400 | tf_op jit(solution)/shard_map/dot_general | solution.py:58
  74.2 14.0 %reduce-scatter.2.cloned.1.call-done = bf16[384,2560]{1,0:T(8,128)(2,1)} async-done(((bf16[384,5120]{1,0:T(8,128)(2,1)}), bf16[384,2560]{1,0:T(8,128)(2,1)}) %reduce-scatter.2.cloned.1.call-update) | async-done | bytes 1966096 | tf_op jit(solution)/shard_map/reduce_scatter | solution.py:59
  (22 shorter events, 1.4 us)
Async XLA Ops:
  6.5 13.6 %copy-start = (bf16[384,1280]{1,0:T(8,128)(2,1)S(1)}, bf16[384,1280]{1,0:T(8,128)(2,1)}, u32[]{:S(2)}) copy-start(bf16[384,1280]{1,0:T(8,128)(2,1)} %param.4) | copy-start | bytes 2949124
  6.5 81.6 %reduce-scatter.2.cloned.1.call-start = ((), (), s32[]{:S(2)}) async-start(), calls=%async_computation.1 | async-start | bytes 5898240 | tf_op jit(solution)/shard_map/reduce_scatter | solution.py:59
  9.9 50.6 %collective-permute-start.3 = (bf16[2,128,1280]{1,2,0:T(8,128)(2,1)}, bf16[2,128,1280]{1,2,0:T(8,128)(2,1)S(1)}, u32[]{:S(2)}, u32[]{:S(2)}) collective-permute-start(bf16[2,128,1280]{1,2,0:T(8,128)(2,1)} %pad_maximum_fusion), channel_id=1, source_target_pairs={{0,28},{2,30},{4,0},{6,2},{8,4},{10,6},{12,8},{14,10},{16,12},{18,... | collective-permute-start | bytes 1966088 | tf_op jit(solution)/shard_map/ppermute | solution.py:14
  15.0 40.7 %collective-permute-start.2 = (bf16[2,128,1280]{1,2,0:T(8,128)(2,1)}, bf16[2,128,1280]{1,2,0:T(8,128)(2,1)}, u32[]{:S(2)}, u32[]{:S(2)}) collective-permute-start(bf16[2,128,1280]{1,2,0:T(8,128)(2,1)} %pad_maximum_fusion), channel_id=1, source_target_pairs={{0,4},{2,6},{4,8},{6,10},{8,12},{10,14},{12,16},{14,18},{16,20},{1... | collective-permute-start | bytes 1966088 | tf_op jit(solution)/shard_map/ppermute | solution.py:14
  15.0 41.8 %collective-permute-start.1 = (bf16[2,128,1280]{1,2,0:T(8,128)(2,1)}, bf16[2,128,1280]{1,2,0:T(8,128)(2,1)}, u32[]{:S(2)}, u32[]{:S(2)}) collective-permute-start(bf16[2,128,1280]{1,2,0:T(8,128)(2,1)} %pad_maximum_fusion), channel_id=1, source_target_pairs={{0,30},{2,0},{4,2},{6,4},{8,6},{10,8},{12,10},{14,12},{16,14},{18,... | collective-permute-start | bytes 1966088 | tf_op jit(solution)/shard_map/ppermute | solution.py:14
  20.1 37.9 %collective-permute-start = (bf16[2,128,1280]{1,2,0:T(8,128)(2,1)}, bf16[2,128,1280]{1,2,0:T(8,128)(2,1)}, u32[]{:S(2)}, u32[]{:S(2)}) collective-permute-start(bf16[2,128,1280]{1,2,0:T(8,128)(2,1)} %pad_maximum_fusion), channel_id=1, source_target_pairs={{0,2},{2,4},{4,6},{6,8},{8,10},{10,12},{12,14},{14,16},{16,18},{18... | collective-permute-start | bytes 1966088 | tf_op jit(solution)/shard_map/ppermute | solution.py:14
  61.6 3.6 %slice-start = ((s8[13107200]{0:T(1024)(128)(4,1)}), s8[524288]{0:T(1024)(128)(4,1)S(1)}, s32[]{:S(2)}) async-start(s8[13107200]{0:T(1024)(128)(4,1)} %bitcast.128), calls=%async_computation.2 | async-start | bytes 1048576
  62.3 2.9 %slice-start.1 = ((s8[13107200]{0:T(1024)(128)(4,1)}), s8[4194304]{0:T(1024)(128)(4,1)S(1)}, s32[]{:S(2)}) async-start(s8[13107200]{0:T(1024)(128)(4,1)} %bitcast.128), calls=%async_computation.3 | async-start | bytes 8388608
  63.3 2.8 %slice-start.2 = ((s8[13107200]{0:T(1024)(128)(4,1)}), s8[4194304]{0:T(1024)(128)(4,1)S(1)}, s32[]{:S(2)}) async-start(s8[13107200]{0:T(1024)(128)(4,1)} %bitcast.128), calls=%async_computation.4 | async-start | bytes 8388608
  64.0 3.1 %slice-start.3 = ((s8[13107200]{0:T(1024)(128)(4,1)}), s8[4194304]{0:T(1024)(128)(4,1)S(1)}, s32[]{:S(2)}) async-start(s8[13107200]{0:T(1024)(128)(4,1)} %bitcast.128), calls=%async_computation.5 | async-start | bytes 8388608
Sparse Core Ops, SparseCore 0:
  74.3 13.8 reduce-scatter.1

commit v2 on v1

--- a/solution.py
+++ b/solution.py
@@ -55,11 +55,24 @@
         .reshape(row_count, head_count * HS)
         .astype(jnp.bfloat16)
     )
-    window_partial_sum = jnp.dot(attended, out_weight, preferred_element_type=jnp.float32)
-    summed = lax.psum_scatter(
-        window_partial_sum.astype(jnp.bfloat16), "mp", scatter_dimension=1, tiled=True
-    )
-    return summed
+    groups = lax.axis_size("mp")
+    me = lax.axis_index("mp")
+    width = out_weight.shape[1] // groups
+    weight_cols = out_weight.reshape(out_weight.shape[0], groups, width)
+
+    def partial_for(owner):
+        cols = lax.dynamic_index_in_dim(weight_cols, owner, 1, keepdims=False)
+        return jnp.dot(attended, cols, preferred_element_type=jnp.float32).astype(jnp.bfloat16)
+
+    received = []
+    for offset in range(1, groups):
+        sent = partial_for((me + offset) % groups)
+        pairs = [(source, (source + offset) % groups) for source in range(groups)]
+        received.append(lax.ppermute(sent, "mp", pairs))
+    summed = lax.optimization_barrier(partial_for(me)).astype(jnp.float32)
+    for part in received:
+        summed = summed + part.astype(jnp.float32)
+    return summed.astype(jnp.bfloat16)
 
 
 def solution(mesh):

time: 95.4 us -> 74.4 us (0.78)
  waiting for transfers between devices: 47.7 us -> 15 us
  local copies, waits for them, and re-layouts: 8.47 us -> 26.6 us
  between operations: 13.6 us -> 0.24 us
  matrix products: 12.3 us -> 15.9 us
  other arithmetic: 2.74 us -> 4.53 us
    ppermute x4, waiting for transfers between devices: 33.7 us -> 15 us  [from_behind(): return lax.ppermute(value, axis, pairs)]
    unnamed x13 -> x16, local copies, waits for them, and re-layouts: 5.07 us -> 22.1 us
    reduce_scatter x1 -> x0, waiting for transfers between devices: 14 us -> none  [on_device(): lax.psum_scatter(window_partial_sum.astype(jnp.bfloat16), 'mp', scatter_d...]
    dot_general x1 -> x2, matrix products: 7 us -> 9.61 us  [partial_for(): jnp.dot(attended, cols, preferred_element_type=jnp.float32)]
    convert_element_type x0 -> x1, other arithmetic: none -> 1.74 us  [on_device(): return summed.astype(jnp.bfloat16)]
    slice x3, local copies, waits for them, and re-layouts: 2.28 us -> 3.35 us  [fold_block(): stacked_blocks[1].reshape(stacked_blocks.shape[1], head_count, HS)]
    dot_general x5, matrix products: 2.38 us -> 3.33 us  [fold_block(): jnp.einsum('qhd,khd->qhk', query_heads, key_heads, preferred_element_type...]
  transfers between devices with their start and end apart: 5 -> 5, of which waited for: 2 -> 1; matrix products, arithmetic and copies ran while one was open for 7% -> 42% of each run, Pallas kernels for 0% -> 0%
where the time goes in v2:
time: 74.4 us; the launch traced here: 73.1 us
  local copies, waits for them, and re-layouts  26.6 us (36%)
  matrix products  15.9 us (21%)
  waiting for transfers between devices  15 us (20%)
  starting transfers between devices  10.7 us (14%)
  other arithmetic  4.53 us (6%)
    unnamed x16, local copies, waits for them, and re-layouts  22.1 us
    ppermute x4, waiting for transfers between devices, from_behind(): return lax.ppermute(value, axis, pairs)  15 us
    ppermute x4, starting transfers between devices, from_behind(): return lax.ppermute(value, axis, pairs)  10.2 us
    dot_general x2, matrix products, partial_for(): jnp.dot(attended, cols, preferred_element_type=jnp.float32)  9.61 us
    slice x3, local copies, waits for them, and re-layouts, fold_block(): stacked_blocks[1].reshape(stacked_blocks.shape[1], head_count, HS)  3.35 us
    dot_general x5, matrix products, fold_block(): jnp.einsum('qhd,khd->qhk', query_heads, key_heads, preferred_element_type...  3.33 us
    dot_general x5, matrix products, fold_block(): jnp.einsum('qhk,khd->qhd', weights.astype(jnp.bfloat16), value_heads, pre...  2.98 us
    reduce_sum x3, other arithmetic, fold_block(): new_sum = running_sum * rescale + jnp.sum(weights, axis=-1)  1.82 us
  transfers between devices with their start and end apart: 5, of which 1 were waited for; matrix products, arithmetic and copies ran while one was open for 42% of the time, Pallas kernels for 0%

profile of v2, /device:TPU:1, one launch (start us, length us, event | category | flops | bytes accessed | tf_op | source)
XLA Modules:
  0.0 73.1 jit_solution(8225225643295931406)
XLA Ops:
  0.0 1.3 %copy.41 = bf16[128,1280]{0,1:T(8,128)(2,1)S(1)} copy(bf16[128,1280]{1,0:T(8,128)(2,1)} %param.5) | data formatting | bytes 655360 | tf_op args[1]
  1.3 1.3 %copy.45 = bf16[128,1280]{0,1:T(8,128)(2,1)S(1)} copy(bf16[128,1280]{1,0:T(8,128)(2,1)} %param.6) | data formatting | bytes 655360 | tf_op args[2]
  2.6 0.9 %pad_maximum_fusion = bf16[2,128,1280]{1,2,0:T(8,128)(2,1)} fusion(bf16[1,128,1280]{1,2,0:T(8,128)(2,1)S(1)} %bitcast.133, bf16[1,128,1280]{1,2,0:T(8,128)(2,1)S(1)} %bitcast.135), kind=kLoop, calls=%fused_computation.59 | loop fusion | flops 327680 | bytes 1310720 | tf_op jit(solution)/shard_map/stack | solution.py:47
  3.5 5.1 %collective-permute-start.3 = (bf16[2,128,1280]{1,2,0:T(8,128)(2,1)}, bf16[2,128,1280]{1,2,0:T(8,128)(2,1)}, u32[]{:S(2)}, u32[]{:S(2)}) collective-permute-start(bf16[2,128,1280]{1,2,0:T(8,128)(2,1)} %pad_maximum_fusion), channel_id=1, source_target_pairs={{0,28},{2,30},{4,0},{6,2},{8,4},{10,6},{12,8},{14,10},{16,12},{18,... | collective-permute-start | bytes 1966088 | tf_op jit(solution)/shard_map/ppermute | solution.py:14
  8.6 5.1 %collective-permute-start.1 = (bf16[2,128,1280]{1,2,0:T(8,128)(2,1)}, bf16[2,128,1280]{1,2,0:T(8,128)(2,1)}, u32[]{:S(2)}, u32[]{:S(2)}) collective-permute-start(bf16[2,128,1280]{1,2,0:T(8,128)(2,1)} %pad_maximum_fusion), channel_id=1, source_target_pairs={{0,30},{2,0},{4,2},{6,4},{8,6},{10,8},{12,10},{14,12},{16,14},{18,... | collective-permute-start | bytes 1966088 | tf_op jit(solution)/shard_map/ppermute | solution.py:14
  13.7 0.6 copy.42
  14.3 1.4 %bitcast_reduce_fusion.4 = (f32[384,10]{0,1:T(8,128)S(1)}, f32[10,128,384]{2,1,0:T(8,128)S(1)}) fusion(bf16[128,10,128]{0,2,1:T(8,128)(2,1)} %bitcast.136, bf16[384,10,128]{0,2,1:T(8,128)(2,1)S(1)} %bitcast.124), kind=kOutput, calls=%fused_computation.33 | convolution fusion | flops 126808320 | bytes 3292160 | tf_op jit(solution)/shard_map/qhd,khd->qhk/dot_general | solution.py:22
  15.8 17.6 %copy.61 = bf16[1280,5120]{0,1:T(8,128)(2,1)} copy(bf16[1280,5120]{1,0:T(8,128)(2,1)} %param.7) | data formatting | bytes 26214400 | tf_op args[3]
  34.3 15.0 %collective-permute-done.2 = bf16[2,128,1280]{1,2,0:T(8,128)(2,1)} collective-permute-done((bf16[2,128,1280]{1,2,0:T(8,128)(2,1)}, bf16[2,128,1280]{1,2,0:T(8,128)(2,1)}, u32[]{:S(2)}, u32[]{:S(2)}) %collective-permute-start.2) | collective-permute-done | bytes 655392 | tf_op jit(solution)/shard_map/ppermute | solution.py:14
  49.3 1.1 %fusion.63 = (bf16[1,128,1280]{1,2,0:T(8,128)(2,1)S(1)}, bf16[1,128,1280]{1,2,0:T(8,128)(2,1)S(1)}) fusion(bf16[2,128,1280]{1,2,0:T(8,128)(2,1)} %collective-permute-done.2), kind=kLoop, calls=%fused_computation.77 | loop fusion | bytes 1310720 | tf_op jit(solution)/shard_map/slice | solution.py:20
  50.4 1.1 %fusion.62 = (bf16[1,128,1280]{1,2,0:T(8,128)(2,1)S(1)}, bf16[1,128,1280]{1,2,0:T(8,128)(2,1)S(1)}) fusion(bf16[2,128,1280]{1,2,0:T(8,128)(2,1)} %collective-permute-done.1), kind=kLoop, calls=%fused_computation.76 | loop fusion | bytes 1310720 | tf_op jit(solution)/shard_map/slice | solution.py:21
  51.6 1.1 %fusion.61 = (bf16[1,128,1280]{1,2,0:T(8,128)(2,1)S(1)}, bf16[1,128,1280]{1,2,0:T(8,128)(2,1)S(1)}) fusion(bf16[2,128,1280]{1,2,0:T(8,128)(2,1)} %collective-permute-done), kind=kLoop, calls=%fused_computation.75 | loop fusion | bytes 1310720 | tf_op jit(solution)/shard_map/slice | solution.py:21
  53.2 0.5 bitcast_reduce_fusion.2
  53.6 0.5 bitcast_reduce_fusion.1
  54.1 1.1 %fusion.60 = (bf16[1,128,1280]{1,2,0:T(8,128)(2,1)S(1)}, bf16[1,128,1280]{1,2,0:T(8,128)(2,1)S(1)}) fusion(bf16[2,128,1280]{1,2,0:T(8,128)(2,1)} %collective-permute-done.3), kind=kLoop, calls=%fused_computation.74 | loop fusion | bytes 1310720 | tf_op jit(solution)/shard_map/slice | solution.py:21
  55.7 0.5 fusion.36
  56.2 0.7 %fusion.25 = (f32[384,10]{0,1:T(8,128)S(1)}, f32[384,10]{0,1:T(8,128)S(1)}) fusion(f32[10,128,384]{2,1,0:T(8,128)S(1)} %get-tuple-element.32, f32[384,10]{0,1:T(8,128)S(1)} %get-tuple-element.13, f32[384,10]{0,1:T(8,128)S(1)} %get-tuple-element.12, f32[10,128,384]{2,1,0:T(8,128)S(1)} %get-tuple-element.28), kind=kLoop, calls=%fused_computation.37 | loop fusion | flops 2941440 | bytes 3993600 | tf_op jit(solution)/shard_map/reduce_sum | solution.py:27
  57.9 0.7 %fusion.29 = (f32[384,10]{0,1:T(8,128)S(1)}, f32[384,10]{0,1:T(8,128)S(1)}) fusion(f32[10,128,384]{2,1,0:T(8,128)S(1)} %get-tuple-element.26, f32[384,10]{0,1:T(8,128)S(1)} %get-tuple-element.11, f32[384,10]{0,1:T(8,128)S(1)} %get-tuple-element.10, f32[10,128,384]{2,1,0:T(8,128)S(1)} %get-tuple-element.24), kind=kLoop, calls=%fused_computation.41 | loop fusion | flops 2941440 | bytes 3993600 | tf_op jit(solution)/shard_map/reduce_sum | solution.py:27
  58.7 1.1 %fusion.13 = bf16[384,10,128]{0,2,1:T(8,128)(2,1)S(1)} fusion(f32[10,128,384]{2,1,0:T(8,128)S(1)} %fusion.34, f32[10,128,384]{2,1,0:T(8,128)S(1)} %fusion.36, f32[10,128,384]{2,1,0:T(8,128)S(1)} %fusion.38, f32[10,384,128]{1,2,0:T(8,128)S(1)} %fusion.40, bf16[128,10,128]{0,2,1:T(8,128)(2,1)S(1)} %bitcast.144, f32[10,128,384]{2,1,0:T(8,128)S(1)} %get-tuple-element.24, ...), kind=kOutput, calls=%fused_computation.11 | convolution fusion | flops 132710400 | bytes 11248640 | tf_op jit(solution)/shard_map/qhk,khd->qhd/dot_general | solution.py:28
  59.9 1.2 %slice-done.2 = s8[4194304]{0:T(1024)(128)(4,1)S(1)} async-done(((s8[13107200]{0:T(1024)(128)(4,1)}), s8[4194304]{0:T(1024)(128)(4,1)S(1)}, s32[]{:S(2)}) %slice-start.2) | async-done | bytes 4194328
  61.1 4.0 %fusion.9 = bf16[384,2560]{1,0:T(8,128)(2,1)} fusion(bf16[384,1280]{0,1:T(8,128)(2,1)S(1)} %bitcast.145, bf16[1280,2,2560]{0,2,1:T(8,128)(2,1)S(1)} %bitcast.132, s32[]{:T(128)S(6)} %select_n.16), kind=kOutput, calls=%fused_computation.7 | convolution fusion | flops 2517565440 | bytes 9502724 | tf_op jit(solution)/shard_map/dot_general | solution.py:65
  65.1 0.5 collective-permute-start.4
  65.7 5.6 %fusion.6 = bf16[384,2560]{1,0:T(8,128)(2,1)S(1)} fusion(bf16[384,1280]{0,1:T(8,128)(2,1)S(1)} %bitcast.146, bf16[1280,2,2560]{0,2,1:T(8,128)(2,1)} %bitcast.129, s32[]{:T(128)S(6)} %select_n.14), kind=kOutput, calls=%fused_computation.6 | convolution fusion | flops 2517565440 | bytes 9502724 | tf_op jit(solution)/shard_map/dot_general | solution.py:65
  71.3 1.7 %add_convert_fusion = bf16[384,2560]{1,0:T(8,128)(2,1)} fusion(bf16[384,2560]{1,0:T(8,128)(2,1)S(1)} %collective-permute-done.4, bf16[384,2560]{1,0:T(8,128)(2,1)S(1)} %fusion.6), kind=kLoop, calls=%fused_computation.8 | loop fusion | flops 3932160 | bytes 5898240 | tf_op jit(solution)/shard_map/convert_element_type | solution.py:75
  (26 shorter events, 2.9 us)
Async XLA Ops:
  0.0 13.7 %copy-start.1 = (bf16[384,1280]{1,0:T(8,128)(2,1)S(1)}, bf16[384,1280]{1,0:T(8,128)(2,1)}, u32[]{:S(2)}) copy-start(bf16[384,1280]{1,0:T(8,128)(2,1)} %param.4) | copy-start | bytes 2949124
  1.3 13.1 %copy-start = (bf16[128,1280]{0,1:T(8,128)(2,1)}, bf16[128,1280]{0,1:T(8,128)(2,1)S(1)}, u32[]{:S(2)}) copy-start(bf16[128,1280]{0,1:T(8,128)(2,1)S(1)} %copy.41) | copy-start | bytes 983044
  3.5 50.6 %collective-permute-start.3 = (bf16[2,128,1280]{1,2,0:T(8,128)(2,1)}, bf16[2,128,1280]{1,2,0:T(8,128)(2,1)}, u32[]{:S(2)}, u32[]{:S(2)}) collective-permute-start(bf16[2,128,1280]{1,2,0:T(8,128)(2,1)} %pad_maximum_fusion), channel_id=1, source_target_pairs={{0,28},{2,30},{4,0},{6,2},{8,4},{10,6},{12,8},{14,10},{16,12},{18,... | collective-permute-start | bytes 1966088 | tf_op jit(solution)/shard_map/ppermute | solution.py:14
  8.6 40.7 %collective-permute-start.2 = (bf16[2,128,1280]{1,2,0:T(8,128)(2,1)}, bf16[2,128,1280]{1,2,0:T(8,128)(2,1)}, u32[]{:S(2)}, u32[]{:S(2)}) collective-permute-start(bf16[2,128,1280]{1,2,0:T(8,128)(2,1)} %pad_maximum_fusion), channel_id=1, source_target_pairs={{0,4},{2,6},{4,8},{6,10},{8,12},{10,14},{12,16},{14,18},{16,20},{1... | collective-permute-start | bytes 1966088 | tf_op jit(solution)/shard_map/ppermute | solution.py:14
  8.6 41.8 %collective-permute-start.1 = (bf16[2,128,1280]{1,2,0:T(8,128)(2,1)}, bf16[2,128,1280]{1,2,0:T(8,128)(2,1)}, u32[]{:S(2)}, u32[]{:S(2)}) collective-permute-start(bf16[2,128,1280]{1,2,0:T(8,128)(2,1)} %pad_maximum_fusion), channel_id=1, source_target_pairs={{0,30},{2,0},{4,2},{6,4},{8,6},{10,8},{12,10},{14,12},{16,14},{18,... | collective-permute-start | bytes 1966088 | tf_op jit(solution)/shard_map/ppermute | solution.py:14
  13.7 37.9 %collective-permute-start = (bf16[2,128,1280]{1,2,0:T(8,128)(2,1)}, bf16[2,128,1280]{1,2,0:T(8,128)(2,1)}, u32[]{:S(2)}, u32[]{:S(2)}) collective-permute-start(bf16[2,128,1280]{1,2,0:T(8,128)(2,1)} %pad_maximum_fusion), channel_id=1, source_target_pairs={{0,2},{2,4},{4,6},{6,8},{8,10},{10,12},{12,14},{14,16},{16,18},{18... | collective-permute-start | bytes 1966088 | tf_op jit(solution)/shard_map/ppermute | solution.py:14
  56.2 3.6 %slice-start = ((s8[13107200]{0:T(1024)(128)(4,1)}), s8[4194304]{0:T(1024)(128)(4,1)S(1)}, s32[]{:S(2)}) async-start(s8[13107200]{0:T(1024)(128)(4,1)} %bitcast.130), calls=%async_computation | async-start | bytes 8388608
  57.0 2.9 %slice-start.1 = ((s8[13107200]{0:T(1024)(128)(4,1)}), s8[4194304]{0:T(1024)(128)(4,1)S(1)}, s32[]{:S(2)}) async-start(s8[13107200]{0:T(1024)(128)(4,1)} %bitcast.130), calls=%async_computation.1 | async-start | bytes 8388608
  57.9 3.1 %slice-start.2 = ((s8[13107200]{0:T(1024)(128)(4,1)}), s8[4194304]{0:T(1024)(128)(4,1)S(1)}, s32[]{:S(2)}) async-start(s8[13107200]{0:T(1024)(128)(4,1)} %bitcast.130), calls=%async_computation.2 | async-start | bytes 8388608
  58.7 2.4 %slice-start.3 = ((s8[13107200]{0:T(1024)(128)(4,1)}), s8[524288]{0:T(1024)(128)(4,1)S(1)}, s32[]{:S(2)}) async-start(s8[13107200]{0:T(1024)(128)(4,1)} %bitcast.130), calls=%async_computation.3 | async-start | bytes 1048576
  65.1 6.2 %collective-permute-start.4 = (bf16[384,2560]{1,0:T(8,128)(2,1)}, bf16[384,2560]{1,0:T(8,128)(2,1)S(1)}, u32[]{:S(2)}, u32[]{:S(2)}) collective-permute-start(bf16[384,2560]{1,0:T(8,128)(2,1)} %fusion.9), channel_id=1, source_target_pairs={{0,1},{1,0},{2,3},{3,2},{4,5},{5,4},{6,7},{7,6},{8,9},{9,8},{10,11... | collective-permute-start | bytes 5898248 | tf_op jit(solution)/shard_map/ppermute | solution.py:71

commit v3 on v2

--- a/solution.py
+++ b/solution.py
@@ -8,17 +8,37 @@
 HS = 128
 
 
-def from_behind(value, axis, steps):
-    count = lax.axis_size(axis)
-    pairs = [(source, (source + steps) % count) for source in range(count)]
-    return lax.ppermute(value, axis, pairs)
+def swap_within_four(value, bit):
+    count = lax.axis_size("blk")
+    return lax.ppermute(value, "blk", [(source, source ^ bit) for source in range(count)])
 
 
-def fold_block(state, stacked_blocks, query_heads):
+def shift_groups(value):
+    count = lax.axis_size("blk")
+    groups = count // 4
+    pairs = []
+    for source in range(count):
+        group, position = divmod(source, 4)
+        step = 1 if position < 2 else -1
+        pairs.append((source, ((group + step) % groups) * 4 + position))
+    return lax.ppermute(value, "blk", pairs)
+
+
+def relay_blocks(own):
+    position = lax.axis_index("blk") % 4
+    from_x = swap_within_four(own, 1)
+    from_y = swap_within_four(own, 2)
+    from_z = shift_groups(from_y)
+    forward = jnp.where((position == 0) | (position == 3), from_y, from_z)
+    from_last = swap_within_four(forward, 1)
+    return [from_x, from_y, from_z, from_last]
+
+
+def fold_block(state, key_rows, value_rows, query_heads):
     running_max, running_sum, numerator = state
     head_count = query_heads.shape[1]
-    key_heads = stacked_blocks[0].reshape(stacked_blocks.shape[1], head_count, HS)
-    value_heads = stacked_blocks[1].reshape(stacked_blocks.shape[1], head_count, HS)
+    key_heads = key_rows.reshape(key_rows.shape[0], head_count, HS)
+    value_heads = value_rows.reshape(value_rows.shape[0], head_count, HS)
     scores = jnp.einsum("qhd,khd->qhk", query_heads, key_heads, preferred_element_type=jnp.float32)
     scores = scores * (1.0 / math.sqrt(HS))
     new_max = jnp.maximum(running_max, jnp.max(scores, axis=-1))
@@ -44,11 +64,11 @@
         jnp.zeros((row_count, head_count), jnp.float32),
         jnp.zeros((row_count, head_count, HS), jnp.float32),
     )
-    stacked_blocks = jnp.stack((keys, values))
-    arrivals = [from_behind(stacked_blocks, "blk", steps) for steps in (1, -1, 2, -2)]
-    state = fold_block(state, stacked_blocks, query_heads)
-    for moving in arrivals:
-        state = fold_block(state, moving, query_heads)
+    key_arrivals = relay_blocks(keys)
+    value_arrivals = relay_blocks(values)
+    state = fold_block(state, keys, values, query_heads)
+    for key_rows, value_rows in zip(key_arrivals, value_arrivals):
+        state = fold_block(state, key_rows, value_rows, query_heads)
     running_max, running_sum, numerator = state
     attended = (
         (numerator / running_sum[:, :, None])
@@ -58,10 +78,9 @@
     groups = lax.axis_size("mp")
     me = lax.axis_index("mp")
     width = out_weight.shape[1] // groups
-    weight_cols = out_weight.reshape(out_weight.shape[0], groups, width)
 
     def partial_for(owner):
-        cols = lax.dynamic_index_in_dim(weight_cols, owner, 1, keepdims=False)
+        cols = lax.dynamic_slice_in_dim(out_weight, owner * width, width, axis=1)
         return jnp.dot(attended, cols, preferred_element_type=jnp.float32).astype(jnp.bfloat16)
 
     received = []

time: 74.4 us -> 58.6 us (0.79)
  local copies, waits for them, and re-layouts: 26.6 us -> 7.98 us
  matrix products: 15.9 us -> 21.5 us
  waiting for transfers between devices: 15 us -> 12.4 us
    unnamed x16 -> x19, local copies, waits for them, and re-layouts: 22.1 us -> 6.1 us
    slice x4 -> x0, local copies, waits for them, and re-layouts: 4.47 us -> none  [the longest x3 3.35 us: fold_block(): stacked_blocks[1].reshape(stacked_blocks.shape[1], head_count, HS)]
    dot_general x5, matrix products: 3.33 us -> 6.28 us  [fold_block(): jnp.einsum('qhd,khd->qhk', query_heads, key_heads, preferred_element_type...]
    ppermute x4 -> x8, waiting for transfers between devices: 15 us -> 12.4 us  [the longest x6 8.13 us: swap_within_four(): lax.ppermute(value, 'blk', [(source, source ^ bit) for source in range(co...]
    dot_general x5, matrix products: 2.98 us -> 5.31 us  [fold_block(): jnp.einsum('qhk,khd->qhd', weights.astype(jnp.bfloat16), value_heads, pre...]
    ppermute x0 -> x1, local copies, waits for them, and re-layouts: none -> 1.89 us  [swap_within_four(): lax.ppermute(value, 'blk', [(source, source ^ bit) for source in range(co...]
    ppermute x1, starting transfers between devices: 0.55 us -> 2.14 us  [on_device(): received.append(lax.ppermute(sent, 'mp', pairs))]
    ppermute x4 -> x8, starting transfers between devices: 10.2 us -> 8.95 us  [the longest x6 6.08 us: swap_within_four(): lax.ppermute(value, 'blk', [(source, source ^ bit) for source in range(co...]
  transfers between devices with their start and end apart: 5 -> 9, of which waited for: 1 -> 3; matrix products, arithmetic and copies ran while one was open for 42% -> 39% of each run, Pallas kernels for 0% -> 0%
where the time goes in v3:
time: 58.6 us; the launch traced here: 57.9 us
  matrix products  21.5 us (37%)
  waiting for transfers between devices  12.4 us (21%)
  starting transfers between devices  11.1 us (19%)
  local copies, waits for them, and re-layouts  7.98 us (14%)
  other arithmetic  4.66 us (8%)
    dot_general x2, matrix products, partial_for(): jnp.dot(attended, cols, preferred_element_type=jnp.float32)  9.86 us
    ppermute x6, waiting for transfers between devices, swap_within_four(): lax.ppermute(value, 'blk', [(source, source ^ bit) for source in range(co...  8.13 us
    dot_general x5, matrix products, fold_block(): jnp.einsum('qhd,khd->qhk', query_heads, key_heads, preferred_element_type...  6.28 us
    unnamed x19, local copies, waits for them, and re-layouts  6.1 us
    ppermute x6, starting transfers between devices, swap_within_four(): lax.ppermute(value, 'blk', [(source, source ^ bit) for source in range(co...  6.08 us
    dot_general x5, matrix products, fold_block(): jnp.einsum('qhk,khd->qhd', weights.astype(jnp.bfloat16), value_heads, pre...  5.31 us
    ppermute x2, waiting for transfers between devices, shift_groups(): return lax.ppermute(value, 'blk', pairs)  4.32 us
    ppermute x2, starting transfers between devices, shift_groups(): return lax.ppermute(value, 'blk', pairs)  2.87 us
  transfers between devices with their start and end apart: 9, of which 3 were waited for; matrix products, arithmetic and copies ran while one was open for 39% of the time, Pallas kernels for 0%

profile of v3, /device:TPU:1, one launch (start us, length us, event | category | flops | bytes accessed | tf_op | source)
XLA Modules:
  0.0 57.9 jit_solution(5452018186443563546)
XLA Ops:
  0.0 2.0 %copy.21 = bf16[128,1280]{0,1:T(8,128)(2,1)} copy(bf16[128,1280]{1,0:T(8,128)(2,1)} %param.5) | data formatting | bytes 655360 | tf_op args[1]
  2.0 2.1 %collective-permute-start.2 = (bf16[128,1280]{0,1:T(8,128)(2,1)}, bf16[128,1280]{0,1:T(8,128)(2,1)}, u32[]{:S(2)}, u32[]{:S(2)}) collective-permute-start(bf16[128,1280]{0,1:T(8,128)(2,1)} %copy.21), channel_id=1, source_target_pairs={{0,4},{2,6},{4,0},{6,2},{8,12},{10,14},{12,8},{14,10},{16,20},{18,... | collective-permute-start | bytes 983048 | tf_op jit(solution)/shard_map/ppermute | solution.py:13
  4.0 1.2 %collective-permute-start = (bf16[128,1280]{0,1:T(8,128)(2,1)}, bf16[128,1280]{0,1:T(8,128)(2,1)}, u32[]{:S(2)}, u32[]{:S(2)}) collective-permute-start(bf16[128,1280]{0,1:T(8,128)(2,1)} %copy.21), channel_id=1, source_target_pairs={{0,2},{2,0},{4,6},{6,4},{8,10},{10,8},{12,14},{14,12},{16,18},{18,... | collective-permute-start | bytes 983048 | tf_op jit(solution)/shard_map/ppermute | solution.py:13
  5.5 1.9 %copy.25 = bf16[128,1280]{0,1:T(8,128)(2,1)} copy(bf16[128,1280]{1,0:T(8,128)(2,1)} %param.6) | data formatting | bytes 655360 | tf_op args[2]
  8.0 1.4 %bitcast_reduce_fusion.4 = (f32[384,10]{0,1:T(8,128)S(1)}, f32[10,128,384]{2,1,0:T(8,128)S(1)}) fusion(bf16[128,10,128]{0,2,1:T(8,128)(2,1)} %bitcast, bf16[384,10,128]{0,2,1:T(8,128)(2,1)S(1)} %bitcast.109), kind=kOutput, calls=%fused_computation.31 | convolution fusion | flops 126808320 | bytes 3292160 | tf_op jit(solution)/shard_map/qhd,khd->qhk/dot_general | solution.py:42
  9.5 2.7 %fusion.38 = f32[10,384,128]{1,2,0:T(8,128)} fusion(bf16[128,10,128]{0,2,1:T(8,128)(2,1)} %bitcast.3, f32[10,128,384]{2,1,0:T(8,128)S(1)} %get-tuple-element.22, f32[384,10]{0,1:T(8,128)S(1)} %get-tuple-element.21), kind=kOutput, calls=%fused_computation.46 | convolution fusion | flops 127303680 | bytes 4275200 | tf_op jit(solution)/shard_map/qhk,khd->qhd/dot_general | solution.py:48
  12.6 1.6 %collective-permute-start.4 = (bf16[128,1280]{0,1:T(8,128)(2,1)}, bf16[128,1280]{0,1:T(8,128)(2,1)}, u32[]{:S(2)}, u32[]{:S(2)}) collective-permute-start(bf16[128,1280]{0,1:T(8,128)(2,1)} %collective-permute-done.2), channel_id=1, source_target_pairs={{0,8},{2,10},{4,28},{6,30},{8,16},{10,18},{12,4},{14,6},{16,24},{1... | collective-permute-start | bytes 983048 | tf_op jit(solution)/shard_map/ppermute | solution.py:24
  14.2 1.5 %bitcast_reduce_fusion.2 = (f32[384,10]{0,1:T(8,128)S(1)}, f32[10,128,384]{2,1,0:T(8,128)S(1)}) fusion(bf16[128,10,128]{0,2,1:T(8,128)(2,1)} %bitcast.9, bf16[384,10,128]{0,2,1:T(8,128)(2,1)S(1)} %bitcast.110), kind=kOutput, calls=%fused_computation.21 | convolution fusion | flops 126808320 | bytes 3292160 | tf_op jit(solution)/shard_map/qhd,khd->qhk/dot_general | solution.py:42
  15.6 4.0 %collective-permute-done.1 = bf16[128,1280]{1,0:T(8,128)(2,1)} collective-permute-done((bf16[128,1280]{1,0:T(8,128)(2,1)}, bf16[128,1280]{1,0:T(8,128)(2,1)}, u32[]{:S(2)}, u32[]{:S(2)}) %collective-permute-start.1) | collective-permute-done | bytes 327712 | tf_op jit(solution)/shard_map/ppermute | solution.py:13
  19.7 1.9 %copy.30 = bf16[128,1280]{0,1:T(8,128)(2,1)} copy(bf16[128,1280]{1,0:T(8,128)(2,1)} %collective-permute-done.1) | data formatting | bytes 655360 | tf_op jit(solution)/shard_map/ppermute | solution.py:13
  21.6 1.3 %collective-permute-start.5 = (bf16[128,1280]{0,1:T(8,128)(2,1)S(1)}, bf16[128,1280]{0,1:T(8,128)(2,1)S(1)}, u32[]{:S(2)}, u32[]{:S(2)}) collective-permute-start(bf16[128,1280]{0,1:T(8,128)(2,1)S(1)} %collective-permute-done.3), channel_id=1, source_target_pairs={{0,8},{2,10},{4,28},{6,30},{8,16},{10,18},{12,4},{14,6},{16,24},{1... | collective-permute-start | bytes 983048 | tf_op jit(solution)/shard_map/ppermute | solution.py:24
  22.9 1.4 %bitcast_reduce_fusion.3 = (f32[384,10]{0,1:T(8,128)S(1)}, f32[10,128,384]{2,1,0:T(8,128)S(1)}) fusion(bf16[128,10,128]{0,2,1:T(8,128)(2,1)} %bitcast.5, bf16[384,10,128]{0,2,1:T(8,128)(2,1)S(1)} %bitcast.111), kind=kOutput, calls=%fused_computation.26 | convolution fusion | flops 126808320 | bytes 3292160 | tf_op jit(solution)/shard_map/qhd,khd->qhk/dot_general | solution.py:42
  24.3 1.0 %broadcast_select_fusion.1 = bf16[128,1280]{0,1:T(8,128)(2,1)S(1)} fusion(bf16[128,1280]{0,1:T(8,128)(2,1)} %collective-permute-done.2, bf16[128,1280]{0,1:T(8,128)(2,1)} %collective-permute-done.4, pred[]{:T(512)S(6)} %or.4), kind=kLoop, calls=%fused_computation.58 | loop fusion | flops 163840 | bytes 983041 | tf_op jit(solution)/shard_map/jit(_where)/select_n | solution.py:32
  25.4 1.3 %collective-permute-start.6 = (bf16[128,1280]{0,1:T(8,128)(2,1)S(1)}, bf16[128,1280]{0,1:T(8,128)(2,1)S(1)}, u32[]{:S(2)}, u32[]{:S(2)}) collective-permute-start(bf16[128,1280]{0,1:T(8,128)(2,1)S(1)} %broadcast_select_fusion.1), channel_id=1, source_target_pairs={{0,2},{2,0},{4,6},{6,4},{8,10},{10,8},{12,14},{14,12},{16,18},{18,... | collective-permute-start | bytes 983048 | tf_op jit(solution)/shard_map/ppermute | solution.py:13
  26.6 4.3 %collective-permute-done.5 = bf16[128,1280]{0,1:T(8,128)(2,1)S(1)} collective-permute-done((bf16[128,1280]{0,1:T(8,128)(2,1)S(1)}, bf16[128,1280]{0,1:T(8,128)(2,1)S(1)}, u32[]{:S(2)}, u32[]{:S(2)}) %collective-permute-start.5) | collective-permute-done | bytes 327712 | tf_op jit(solution)/shard_map/ppermute | solution.py:24
  31.0 1.3 %collective-permute-start.7 = (bf16[128,1280]{0,1:T(8,128)(2,1)S(1)}, bf16[128,1280]{0,1:T(8,128)(2,1)S(1)}, u32[]{:S(2)}, u32[]{:S(2)}) collective-permute-start(bf16[128,1280]{0,1:T(8,128)(2,1)S(1)} %broadcast_select_fusion), channel_id=1, source_target_pairs={{0,2},{2,0},{4,6},{6,4},{8,10},{10,8},{12,14},{14,12},{16,18},{18,... | collective-permute-start | bytes 983048 | tf_op jit(solution)/shard_map/ppermute | solution.py:13
  32.3 1.4 %bitcast_reduce_fusion.1 = (f32[384,10]{0,1:T(8,128)S(1)}, f32[10,128,384]{2,1,0:T(8,128)S(1)}) fusion(bf16[128,10,128]{0,2,1:T(8,128)(2,1)} %bitcast.13, bf16[384,10,128]{0,2,1:T(8,128)(2,1)S(1)} %bitcast.112), kind=kOutput, calls=%fused_computation.16 | convolution fusion | flops 126808320 | bytes 3292160 | tf_op jit(solution)/shard_map/qhd,khd->qhk/dot_general | solution.py:42
  36.4 4.1 %collective-permute-done.7 = bf16[128,1280]{0,1:T(8,128)(2,1)S(1)} collective-permute-done((bf16[128,1280]{0,1:T(8,128)(2,1)S(1)}, bf16[128,1280]{0,1:T(8,128)(2,1)S(1)}, u32[]{:S(2)}, u32[]{:S(2)}) %collective-permute-start.7) | collective-permute-done | bytes 327712 | tf_op jit(solution)/shard_map/ppermute | solution.py:13
  41.8 0.7 %copy-done = f32[10,384,128]{1,2,0:T(8,128)S(1)} copy-done((f32[10,384,128]{1,2,0:T(8,128)S(1)}, f32[10,384,128]{1,2,0:T(8,128)}, u32[]{:S(2)}) %copy-start) | copy-done | bytes 1966104
  42.5 1.2 %fusion.11 = bf16[384,10,128]{0,2,1:T(8,128)(2,1)S(1)} fusion(f32[10,128,384]{2,1,0:T(8,128)S(1)} %fusion.31, f32[10,384,128]{1,2,0:T(8,128)S(1)} %fusion.34, f32[10,384,128]{1,2,0:T(8,128)S(1)} %fusion.36, f32[10,384,128]{1,2,0:T(8,128)S(1)} %copy-done, bf16[128,10,128]{0,2,1:T(8,128)(2,1)S(1)} %bitcast.117, f32[10,128,384]{2,1,0:T(8,128)S(1)} %get-tuple-element.18, ...), kind=kOutput, calls=%fused_computation.9 | convolution fusion | flops 132710400 | bytes 11248640 | tf_op jit(solution)/shard_map/qhk,khd->qhd/dot_general | solution.py:48
  44.1 3.9 %fusion.7 = bf16[384,2560]{1,0:T(8,128)(2,1)} fusion(bf16[384,1280]{0,1:T(8,128)(2,1)S(1)} %bitcast.121, bf16[1280,5120]{1,0:T(8,128)(2,1)S(1)} %bitcast.120, s32[]{:T(128)S(6)} %select_n.37), kind=kOutput, calls=%fused_computation.5 | convolution fusion | flops 2517565440 | bytes 9502724 | tf_op jit(solution)/shard_map/dot_general | solution.py:84
  48.1 2.1 %collective-permute-start.8 = (bf16[384,2560]{1,0:T(8,128)(2,1)}, bf16[384,2560]{1,0:T(8,128)(2,1)S(1)}, u32[]{:S(2)}, u32[]{:S(2)}) collective-permute-start(bf16[384,2560]{1,0:T(8,128)(2,1)} %fusion.7), channel_id=1, source_target_pairs={{0,1},{1,0},{2,3},{3,2},{4,5},{5,4},{6,7},{7,6},{8,9},{9,8},{10,11... | collective-permute-start | bytes 5898248 | tf_op jit(solution)/shard_map/ppermute | solution.py:90
  50.2 5.9 %fusion.4 = bf16[384,2560]{1,0:T(8,128)(2,1)S(1)} fusion(bf16[384,1280]{0,1:T(8,128)(2,1)} %bitcast.122, bf16[1280,5120]{1,0:T(8,128)(2,1)} %param.7, s32[]{:T(128)S(6)} %select_n.35), kind=kOutput, calls=%fused_computation.4 | convolution fusion | flops 2517565440 | bytes 9502724 | tf_op jit(solution)/shard_map/dot_general | solution.py:84
  56.1 1.7 %add_convert_fusion = bf16[384,2560]{1,0:T(8,128)(2,1)} fusion(bf16[384,2560]{1,0:T(8,128)(2,1)S(1)} %collective-permute-done.8, bf16[384,2560]{1,0:T(8,128)(2,1)S(1)} %fusion.4), kind=kLoop, calls=%fused_computation.6 | loop fusion | flops 3932160 | bytes 5898240 | tf_op jit(solution)/shard_map/convert_element_type | solution.py:94
  (35 shorter events, 5.6 us)
Async XLA Ops:
  0.0 7.4 %copy-start.2 = (bf16[384,1280]{1,0:T(8,128)(2,1)S(1)}, bf16[384,1280]{1,0:T(8,128)(2,1)}, u32[]{:S(2)}) copy-start(bf16[384,1280]{1,0:T(8,128)(2,1)} %param.4) | copy-start | bytes 2949124
  2.0 10.6 %collective-permute-start.2 = (bf16[128,1280]{0,1:T(8,128)(2,1)}, bf16[128,1280]{0,1:T(8,128)(2,1)}, u32[]{:S(2)}, u32[]{:S(2)}) collective-permute-start(bf16[128,1280]{0,1:T(8,128)(2,1)} %copy.21), channel_id=1, source_target_pairs={{0,4},{2,6},{4,0},{6,2},{8,12},{10,14},{12,8},{14,10},{16,20},{18,... | collective-permute-start | bytes 983048 | tf_op jit(solution)/shard_map/ppermute | solution.py:13
  4.0 18.8 %collective-permute-start = (bf16[128,1280]{0,1:T(8,128)(2,1)}, bf16[128,1280]{0,1:T(8,128)(2,1)}, u32[]{:S(2)}, u32[]{:S(2)}) collective-permute-start(bf16[128,1280]{0,1:T(8,128)(2,1)} %copy.21), channel_id=1, source_target_pairs={{0,2},{2,0},{4,6},{6,4},{8,10},{10,8},{12,14},{14,12},{16,18},{18,... | collective-permute-start | bytes 983048 | tf_op jit(solution)/shard_map/ppermute | solution.py:13
  5.2 14.4 %collective-permute-start.1 = (bf16[128,1280]{1,0:T(8,128)(2,1)}, bf16[128,1280]{1,0:T(8,128)(2,1)}, u32[]{:S(2)}, u32[]{:S(2)}) collective-permute-start(bf16[128,1280]{1,0:T(8,128)(2,1)} %param.6), channel_id=1, source_target_pairs={{0,2},{2,0},{4,6},{6,4},{8,10},{10,8},{12,14},{14,12},{16,18},{18,... | collective-permute-start | bytes 983048 | tf_op jit(solution)/shard_map/ppermute | solution.py:13
  7.4 14.2 %collective-permute-start.3 = (bf16[128,1280]{0,1:T(8,128)(2,1)}, bf16[128,1280]{0,1:T(8,128)(2,1)S(1)}, u32[]{:S(2)}, u32[]{:S(2)}) collective-permute-start(bf16[128,1280]{0,1:T(8,128)(2,1)} %copy.25), channel_id=1, source_target_pairs={{0,4},{2,6},{4,0},{6,2},{8,12},{10,14},{12,8},{14,10},{16,20},{18,... | collective-permute-start | bytes 983048 | tf_op jit(solution)/shard_map/ppermute | solution.py:13
  12.6 11.7 %collective-permute-start.4 = (bf16[128,1280]{0,1:T(8,128)(2,1)}, bf16[128,1280]{0,1:T(8,128)(2,1)}, u32[]{:S(2)}, u32[]{:S(2)}) collective-permute-start(bf16[128,1280]{0,1:T(8,128)(2,1)} %collective-permute-done.2), channel_id=1, source_target_pairs={{0,8},{2,10},{4,28},{6,30},{8,16},{10,18},{12,4},{14,6},{16,24},{1... | collective-permute-start | bytes 983048 | tf_op jit(solution)/shard_map/ppermute | solution.py:24
  21.6 9.4 %collective-permute-start.5 = (bf16[128,1280]{0,1:T(8,128)(2,1)S(1)}, bf16[128,1280]{0,1:T(8,128)(2,1)S(1)}, u32[]{:S(2)}, u32[]{:S(2)}) collective-permute-start(bf16[128,1280]{0,1:T(8,128)(2,1)S(1)} %collective-permute-done.3), channel_id=1, source_target_pairs={{0,8},{2,10},{4,28},{6,30},{8,16},{10,18},{12,4},{14,6},{16,24},{1... | collective-permute-start | bytes 983048 | tf_op jit(solution)/shard_map/ppermute | solution.py:24
  25.4 8.4 %collective-permute-start.6 = (bf16[128,1280]{0,1:T(8,128)(2,1)S(1)}, bf16[128,1280]{0,1:T(8,128)(2,1)S(1)}, u32[]{:S(2)}, u32[]{:S(2)}) collective-permute-start(bf16[128,1280]{0,1:T(8,128)(2,1)S(1)} %broadcast_select_fusion.1), channel_id=1, source_target_pairs={{0,2},{2,0},{4,6},{6,4},{8,10},{10,8},{12,14},{14,12},{16,18},{18,... | collective-permute-start | bytes 983048 | tf_op jit(solution)/shard_map/ppermute | solution.py:13
  31.0 9.5 %collective-permute-start.7 = (bf16[128,1280]{0,1:T(8,128)(2,1)S(1)}, bf16[128,1280]{0,1:T(8,128)(2,1)S(1)}, u32[]{:S(2)}, u32[]{:S(2)}) collective-permute-start(bf16[128,1280]{0,1:T(8,128)(2,1)S(1)} %broadcast_select_fusion), channel_id=1, source_target_pairs={{0,2},{2,0},{4,6},{6,4},{8,10},{10,8},{12,14},{14,12},{16,18},{18,... | collective-permute-start | bytes 983048 | tf_op jit(solution)/shard_map/ppermute | solution.py:13
  33.7 1.0 %copy-start.1 = (bf16[128,1280]{0,1:T(8,128)(2,1)S(1)}, bf16[128,1280]{0,1:T(8,128)(2,1)}, u32[]{:S(2)}) copy-start(bf16[128,1280]{0,1:T(8,128)(2,1)} %copy.30) | copy-start | bytes 983044
  34.7 9.0 %slice-start = ((s8[13107200]{0:T(1024)(128)(4,1)}), s8[4194304]{0:T(1024)(128)(4,1)S(1)}, s32[]{:S(2)}) async-start(s8[13107200]{0:T(1024)(128)(4,1)} %bitcast.119), calls=%async_computation | async-start | bytes 8388608
  35.9 7.8 %slice-start.1 = ((s8[13107200]{0:T(1024)(128)(4,1)}), s8[4194304]{0:T(1024)(128)(4,1)S(1)}, s32[]{:S(2)}) async-start(s8[13107200]{0:T(1024)(128)(4,1)} %bitcast.119), calls=%async_computation.1 | async-start | bytes 8388608
  41.0 1.5 %copy-start = (f32[10,384,128]{1,2,0:T(8,128)S(1)}, f32[10,384,128]{1,2,0:T(8,128)}, u32[]{:S(2)}) copy-start(f32[10,384,128]{1,2,0:T(8,128)} %fusion.38) | copy-start | bytes 5898244
  41.0 2.8 %slice-start.2 = ((s8[13107200]{0:T(1024)(128)(4,1)}), s8[4194304]{0:T(1024)(128)(4,1)S(1)}, s32[]{:S(2)}) async-start(s8[13107200]{0:T(1024)(128)(4,1)} %bitcast.119), calls=%async_computation.2 | async-start | bytes 8388608
  42.5 1.6 %slice-start.3 = ((s8[13107200]{0:T(1024)(128)(4,1)}), s8[524288]{0:T(1024)(128)(4,1)S(1)}, s32[]{:S(2)}) async-start(s8[13107200]{0:T(1024)(128)(4,1)} %bitcast.119), calls=%async_computation.3 | async-start | bytes 1048576
  43.7 4.3 %copy-start.3 = (bf16[384,10,128]{0,2,1:T(8,128)(2,1)}, bf16[384,10,128]{0,2,1:T(8,128)(2,1)S(1)}, u32[]{:S(2)}) copy-start(bf16[384,10,128]{0,2,1:T(8,128)(2,1)S(1)} %fusion.11) | copy-start | bytes 2949124
  48.1 8.1 %collective-permute-start.8 = (bf16[384,2560]{1,0:T(8,128)(2,1)}, bf16[384,2560]{1,0:T(8,128)(2,1)S(1)}, u32[]{:S(2)}, u32[]{:S(2)}) collective-permute-start(bf16[384,2560]{1,0:T(8,128)(2,1)} %fusion.7), channel_id=1, source_target_pairs={{0,1},{1,0},{2,3},{3,2},{4,5},{5,4},{6,7},{7,6},{8,9},{9,8},{10,11... | collective-permute-start | bytes 5898248 | tf_op jit(solution)/shard_map/ppermute | solution.py:90

commit v4 on v3

--- a/solution.py
+++ b/solution.py
@@ -55,40 +55,59 @@
     return (new_max, new_sum, new_numerator)
 
 
-def on_device(queries, keys, values, out_weight):
+def attend_chunk(queries, keys, values, low, high, hold=None):
     row_count = queries.shape[0]
-    head_count = queries.shape[1] // HS
-    query_heads = queries.reshape(row_count, head_count, HS)
+    cols = slice(low * HS, high * HS)
+    count = high - low
+    query_heads = queries[:, cols].reshape(row_count, count, HS)
+    own = jnp.stack((keys[:, cols], values[:, cols]))
     state = (
-        jnp.full((row_count, head_count), -jnp.inf, jnp.float32),
-        jnp.zeros((row_count, head_count), jnp.float32),
-        jnp.zeros((row_count, head_count, HS), jnp.float32),
+        jnp.full((row_count, count), -jnp.inf, jnp.float32),
+        jnp.zeros((row_count, count), jnp.float32),
+        jnp.zeros((row_count, count, HS), jnp.float32),
     )
-    key_arrivals = relay_blocks(keys)
-    value_arrivals = relay_blocks(values)
-    state = fold_block(state, keys, values, query_heads)
-    for key_rows, value_rows in zip(key_arrivals, value_arrivals):
-        state = fold_block(state, key_rows, value_rows, query_heads)
+    state = fold_block(state, own[0], own[1], query_heads)
+    arrivals = relay_blocks(own)
+    for moving in arrivals[:-1]:
+        state = fold_block(state, moving[0], moving[1], query_heads)
+    last = arrivals[-1]
+    if hold is not None:
+        last, state, hold = lax.optimization_barrier((last, state, hold))
+    state = fold_block(state, last[0], last[1], query_heads)
     running_max, running_sum, numerator = state
     attended = (
         (numerator / running_sum[:, :, None])
-        .reshape(row_count, head_count * HS)
+        .reshape(row_count, count * HS)
         .astype(jnp.bfloat16)
     )
+    return attended, hold
+
+
+def project_chunk(attended, weight_rows, owners, width):
+    parts = []
+    for owner in owners:
+        block = lax.dynamic_slice_in_dim(weight_rows, owner * width, width, axis=1)
+        parts.append(jnp.dot(attended, block, preferred_element_type=jnp.float32))
+    return parts
+
+
+def on_device(queries, keys, values, out_weight):
+    head_count = queries.shape[1] // HS
+    first = (head_count + 1) // 2
     groups = lax.axis_size("mp")
     me = lax.axis_index("mp")
     width = out_weight.shape[1] // groups
-
-    def partial_for(owner):
-        cols = lax.dynamic_slice_in_dim(out_weight, owner * width, width, axis=1)
-        return jnp.dot(attended, cols, preferred_element_type=jnp.float32).astype(jnp.bfloat16)
-
+    owners = [(me + offset) % groups for offset in range(groups)]
+    attended, _ = attend_chunk(queries, keys, values, 0, first)
+    early = project_chunk(attended, out_weight[: first * HS], owners, width)
+    attended, early = attend_chunk(queries, keys, values, first, head_count, hold=early)
+    late = project_chunk(attended, out_weight[first * HS:], owners, width)
+    totals = [a + b for a, b in zip(early, late)]
     received = []
     for offset in range(1, groups):
-        sent = partial_for((me + offset) % groups)
         pairs = [(source, (source + offset) % groups) for source in range(groups)]
-        received.append(lax.ppermute(sent, "mp", pairs))
-    summed = lax.optimization_barrier(partial_for(me)).astype(jnp.float32)
+        received.append(lax.ppermute(totals[offset].astype(jnp.bfloat16), "mp", pairs))
+    summed = lax.optimization_barrier(totals[0].astype(jnp.bfloat16)).astype(jnp.float32)
     for part in received:
         summed = summed + part.astype(jnp.float32)
     return summed.astype(jnp.bfloat16)

time: 58.6 us -> 68.4 us (1.17)
  local copies, waits for them, and re-layouts: 7.98 us -> 18.9 us
  waiting for transfers between devices: 12.4 us -> 9.25 us
  other arithmetic: 4.66 us -> 7.47 us
    slice x0 -> x12, local copies, waits for them, and re-layouts: none -> 15.8 us  [the longest x1 10.4 us: on_device(): late = project_chunk(attended, out_weight[first * HS:], owners, width)]
    ppermute x6, waiting for transfers between devices: 8.13 us -> 0.02 us  [swap_within_four(): lax.ppermute(value, 'blk', [(source, source ^ bit) for source in range(co...]
    ppermute x2, waiting for transfers between devices: 4.32 us -> 8.22 us  [shift_groups(): return lax.ppermute(value, 'blk', pairs)]
    unnamed x19 -> x20, local copies, waits for them, and re-layouts: 6.1 us -> 2.78 us
    dot_general x2 -> x4, matrix products: 9.86 us -> 13 us  [project_chunk(): parts.append(jnp.dot(attended, block, preferred_element_type=jnp.float32))]
    dot_general x5 -> x10, matrix products: 6.28 us -> 3.37 us  [fold_block(): jnp.einsum('qhd,khd->qhk', query_heads, key_heads, preferred_element_type...]
    ppermute x1 -> x0, local copies, waits for them, and re-layouts: 1.89 us -> none  [swap_within_four(): lax.ppermute(value, 'blk', [(source, source ^ bit) for source in range(co...]
    convert_element_type x0 -> x2, other arithmetic: none -> 1.62 us  [the longest x1 0.81 us: on_device(): totals[offset].astype(jnp.bfloat16)]
  transfers between devices with their start and end apart: 9 -> 9, of which waited for: 3 -> 3; matrix products, arithmetic and copies ran while one was open for 39% -> 51% of each run, Pallas kernels for 0% -> 0%
where the time goes in v4:
time: 68.4 us; the launch traced here: 67.8 us
  matrix products  21.2 us (31%)
  local copies, waits for them, and re-layouts  18.9 us (28%)
  starting transfers between devices  10.5 us (15%)
  waiting for transfers between devices  9.25 us (14%)
  other arithmetic  7.47 us (11%)
    dot_general x4, matrix products, project_chunk(): parts.append(jnp.dot(attended, block, preferred_element_type=jnp.float32))  13 us
    slice x1, local copies, waits for them, and re-layouts, on_device(): late = project_chunk(attended, out_weight[first * HS:], owners, width)  10.4 us
    ppermute x2, waiting for transfers between devices, shift_groups(): return lax.ppermute(value, 'blk', pairs)  8.22 us
    dot_general x10, matrix products, fold_block(): jnp.einsum('qhk,khd->qhd', weights.astype(jnp.bfloat16), value_heads, pre...  4.86 us
    ppermute x6, starting transfers between devices, swap_within_four(): lax.ppermute(value, 'blk', [(source, source ^ bit) for source in range(co...  4.68 us
    dot_general x10, matrix products, fold_block(): jnp.einsum('qhd,khd->qhk', query_heads, key_heads, preferred_element_type...  3.37 us
    slice x6, local copies, waits for them, and re-layouts, attend_chunk(): state = fold_block(state, moving[0], moving[1], query_heads)  3.12 us
    ppermute x1, starting transfers between devices, on_device(): lax.ppermute(totals[offset].astype(jnp.bfloat16), 'mp', pairs)  2.94 us
  transfers between devices with their start and end apart: 9, of which 3 were waited for; matrix products, arithmetic and copies ran while one was open for 51% of the time, Pallas kernels for 0%

profile of v4, /device:TPU:1, one launch (start us, length us, event | category | flops | bytes accessed | tf_op | source)
XLA Modules:
  0.0 67.8 jit_solution(3309285395517188474)
XLA Ops:
  0.0 1.1 %fusion.91 = (bf16[128,640]{1,0:T(8,128)(2,1)S(1)}, bf16[128,640]{1,0:T(8,128)(2,1)S(1)}) fusion(bf16[128,1280]{1,0:T(8,128)(2,1)} %param.5), kind=kLoop, calls=%fused_computation.130 | loop fusion | bytes 655360 | tf_op jit(solution)/shard_map/slice | solution.py:63
  1.3 1.0 %fusion.92 = (bf16[128,640]{1,0:T(8,128)(2,1)S(1)}, bf16[128,640]{1,0:T(8,128)(2,1)S(1)}) fusion(bf16[128,1280]{1,0:T(8,128)(2,1)} %param.6), kind=kLoop, calls=%fused_computation.131 | loop fusion | bytes 655360 | tf_op jit(solution)/shard_map/slice | solution.py:63
  3.2 2.1 %collective-permute-start.5 = (bf16[2,128,640]{1,2,0:T(8,128)(2,1)}, bf16[2,128,640]{1,2,0:T(8,128)(2,1)}, u32[]{:S(2)}, u32[]{:S(2)}) collective-permute-start(bf16[2,128,640]{1,2,0:T(8,128)(2,1)} %pad_maximum_fusion.1), channel_id=1, source_target_pairs={{0,4},{2,6},{4,0},{6,2},{8,12},{10,14},{12,8},{14,10},{16,20},{18,... | collective-permute-start | bytes 983048 | tf_op jit(solution)/shard_map/ppermute | solution.py:13
  5.3 1.2 %collective-permute-start.4 = (bf16[2,128,640]{1,2,0:T(8,128)(2,1)}, bf16[2,128,640]{1,2,0:T(8,128)(2,1)}, u32[]{:S(2)}, u32[]{:S(2)}) collective-permute-start(bf16[2,128,640]{1,2,0:T(8,128)(2,1)} %pad_maximum_fusion.1), channel_id=1, source_target_pairs={{0,2},{2,0},{4,6},{6,4},{8,10},{10,8},{12,14},{14,12},{16,18},{18,... | collective-permute-start | bytes 983048 | tf_op jit(solution)/shard_map/ppermute | solution.py:13
  8.2 10.4 %fusion.84 = (bf16[640,5120]{1,0:T(8,128)(2,1)}, bf16[640,5120]{1,0:T(8,128)(2,1)}) fusion(bf16[1280,5120]{1,0:T(8,128)(2,1)} %param.7), kind=kLoop, calls=%fused_computation.123 | loop fusion | bytes 26214400 | tf_op jit(solution)/shard_map/slice | solution.py:104
  19.8 1.6 %collective-permute-start.6 = (bf16[2,128,640]{1,2,0:T(8,128)(2,1)}, bf16[2,128,640]{1,2,0:T(8,128)(2,1)S(1)}, u32[]{:S(2)}, u32[]{:S(2)}) collective-permute-start(bf16[2,128,640]{1,2,0:T(8,128)(2,1)} %collective-permute-done.5), channel_id=1, source_target_pairs={{0,8},{2,10},{4,28},{6,30},{8,16},{10,18},{12,4},{14,6},{16,24},{1... | collective-permute-start | bytes 983048 | tf_op jit(solution)/shard_map/ppermute | solution.py:24
  21.4 1.0 %fusion.89 = (bf16[1,128,640]{1,2,0:T(8,128)(2,1)S(1)}, bf16[1,128,640]{1,2,0:T(8,128)(2,1)S(1)}) fusion(bf16[2,128,640]{1,2,0:T(8,128)(2,1)} %collective-permute-done.5), kind=kLoop, calls=%fused_computation.128 | loop fusion | bytes 655360 | tf_op jit(solution)/shard_map/slice | solution.py:72
  22.8 1.0 %fusion.90 = (bf16[1,128,640]{1,2,0:T(8,128)(2,1)S(1)}, bf16[1,128,640]{1,2,0:T(8,128)(2,1)S(1)}) fusion(bf16[2,128,640]{1,2,0:T(8,128)(2,1)} %collective-permute-done.4), kind=kLoop, calls=%fused_computation.129 | loop fusion | bytes 655360 | tf_op jit(solution)/shard_map/slice | solution.py:72
  24.1 1.3 %collective-permute-start.1 = (bf16[2,128,640]{1,2,0:T(8,128)(2,1)S(1)}, bf16[2,128,640]{1,2,0:T(8,128)(2,1)S(1)}, u32[]{:S(2)}, u32[]{:S(2)}) collective-permute-start(bf16[2,128,640]{1,2,0:T(8,128)(2,1)S(1)} %collective-permute-done), channel_id=1, source_target_pairs={{0,8},{2,10},{4,28},{6,30},{8,16},{10,18},{12,4},{14,6},{16,24},{1... | collective-permute-start | bytes 983048 | tf_op jit(solution)/shard_map/ppermute | solution.py:24
  25.9 1.0 %fusion.95 = (bf16[1,128,640]{1,2,0:T(8,128)(2,1)S(1)}, bf16[1,128,640]{1,2,0:T(8,128)(2,1)S(1)}) fusion(bf16[2,128,640]{1,2,0:T(8,128)(2,1)} %collective-permute-done.3), kind=kLoop, calls=%fused_computation.134 | loop fusion | bytes 655360 | tf_op jit(solution)/shard_map/slice | solution.py:72
  27.2 2.7 %collective-permute-done.6 = bf16[2,128,640]{1,2,0:T(8,128)(2,1)S(1)} collective-permute-done((bf16[2,128,640]{1,2,0:T(8,128)(2,1)}, bf16[2,128,640]{1,2,0:T(8,128)(2,1)S(1)}, u32[]{:S(2)}, u32[]{:S(2)}) %collective-permute-start.6) | collective-permute-done | bytes 327712 | tf_op jit(solution)/shard_map/ppermute | solution.py:24
  29.9 1.0 %broadcast_select_fusion = bf16[2,128,640]{1,2,0:T(8,128)(2,1)S(1)} fusion(bf16[2,128,640]{1,2,0:T(8,128)(2,1)} %collective-permute-done.5, bf16[2,128,640]{1,2,0:T(8,128)(2,1)S(1)} %collective-permute-done.6, pred[]{:T(512)S(6)} %or.4), kind=kLoop, calls=%fused_computation.102 | loop fusion | flops 163840 | bytes 983041 | tf_op jit(solution)/shard_map/jit(_where)/select_n | solution.py:32
  31.4 5.5 %collective-permute-done.1 = bf16[2,128,640]{1,2,0:T(8,128)(2,1)S(1)} collective-permute-done((bf16[2,128,640]{1,2,0:T(8,128)(2,1)S(1)}, bf16[2,128,640]{1,2,0:T(8,128)(2,1)S(1)}, u32[]{:S(2)}, u32[]{:S(2)}) %collective-permute-start.1) | collective-permute-done | bytes 327712 | tf_op jit(solution)/shard_map/ppermute | solution.py:24
  37.4 1.1 %collective-permute-start.2 = (bf16[2,128,640]{1,2,0:T(8,128)(2,1)S(1)}, bf16[2,128,640]{1,2,0:T(8,128)(2,1)S(1)}, u32[]{:S(2)}, u32[]{:S(2)}) collective-permute-start(bf16[2,128,640]{1,2,0:T(8,128)(2,1)S(1)} %broadcast_select_fusion.1), channel_id=1, source_target_pairs={{0,2},{2,0},{4,6},{6,4},{8,10},{10,8},{12,14},{14,12},{16,18},{18,... | collective-permute-start | bytes 983048 | tf_op jit(solution)/shard_map/ppermute | solution.py:13
  39.0 1.2 %fusion.24 = f32[384,5,128]{2,0,1:T(8,128)S(1)} fusion(bf16[128,5,128]{0,2,1:T(8,128)(2,1)S(1)} %bitcast.161, f32[384,5,128]{0,2,1:T(8,128)S(1)} %get-tuple-element.66, f32[384,5]{0,1:T(8,128)S(1)} %get-tuple-element.29, f32[384,5]{0,1:T(8,128)S(1)} %get-tuple-element.60, f32[384,5]{0,1:T(8,128)S(1)} %get-tuple-element.65), kind=kOutput, calls=%fused_computation.47 | convolution fusion | flops 63897600 | bytes 2152960 | tf_op jit(solution)/shard_map/qhk,khd->qhd/dot_general | solution.py:48
  44.9 0.9 %slice-done.3 = s8[2359296]{0:T(1024)(128)(4,1)S(1)} async-done(((s8[6553600]{0:T(1024)(128)(4,1)}), s8[2359296]{0:T(1024)(128)(4,1)S(1)}, s32[]{:S(2)}) %slice-start.3) | async-done | bytes 2359320
  45.8 3.7 %fusion.4 = f32[384,2560]{1,0:T(8,128)} fusion(bf16[384,640]{0,1:T(8,128)(2,1)S(1)} %bitcast.156, bf16[640,5120]{1,0:T(8,128)(2,1)S(1)} %bitcast.143, s32[]{:T(128)S(6)} %select_n.44), kind=kOutput, calls=%fused_computation.7 | convolution fusion | flops 1258291200 | bytes 7700484 | tf_op jit(solution)/shard_map/dot_general | solution.py:90
  49.5 3.7 %fusion.6 = f32[384,2560]{1,0:T(8,128)} fusion(bf16[384,640]{0,1:T(8,128)(2,1)S(1)} %bitcast.157, bf16[640,5120]{1,0:T(8,128)(2,1)S(1)} %bitcast.143, s32[]{:T(128)S(6)} %select_n.42), kind=kOutput, calls=%fused_computation.9 | convolution fusion | flops 1258291200 | bytes 7700484 | tf_op jit(solution)/shard_map/dot_general | solution.py:90
  54.9 3.8 %fusion = f32[384,2560]{1,0:T(8,128)S(1)} fusion(bf16[384,640]{0,1:T(8,128)(2,1)S(1)} %bitcast.154, bf16[640,5120]{1,0:T(8,128)(2,1)} %get-tuple-element.35, s32[]{:T(128)S(6)} %select_n.44), kind=kOutput, calls=%fused_computation.3 | convolution fusion | flops 1258291200 | bytes 7700484 | tf_op jit(solution)/shard_map/dot_general | solution.py:90
  58.7 0.8 %add_convert_fusion.1 = bf16[384,2560]{1,0:T(8,128)(2,1)S(1)} fusion(f32[384,2560]{1,0:T(8,128)S(1)} %copy-done.1, f32[384,2560]{1,0:T(8,128)S(1)} %fusion), kind=kLoop, calls=%fused_computation.1 | loop fusion | flops 1966080 | bytes 9830400 | tf_op jit(solution)/shard_map/convert_element_type | solution.py:109
  59.5 2.9 %collective-permute-start.8 = (bf16[384,2560]{1,0:T(8,128)(2,1)S(1)}, bf16[384,2560]{1,0:T(8,128)(2,1)S(1)}, u32[]{:S(2)}, u32[]{:S(2)}) collective-permute-start(bf16[384,2560]{1,0:T(8,128)(2,1)S(1)} %add_convert_fusion.1), channel_id=1, source_target_pairs={{0,1},{1,0},{2,3},{3,2},{4,5},{5,4},{6,7},{7,6},{8,9},{9,8},{10,11... | collective-permute-start | bytes 5898248 | tf_op jit(solution)/shard_map/ppermute | solution.py:109
  62.5 1.7 %fusion.2 = f32[384,2560]{1,0:T(8,128)S(1)} fusion(bf16[384,640]{0,1:T(8,128)(2,1)S(1)} %bitcast.155, bf16[640,5120]{1,0:T(8,128)(2,1)S(1)} %bitcast.141, s32[]{:T(128)S(6)} %select_n.42), kind=kOutput, calls=%fused_computation.5 | convolution fusion | flops 1258291200 | bytes 7700484 | tf_op jit(solution)/shard_map/dot_general | solution.py:90
  65.0 1.0 %collective-permute-done.8 = bf16[384,2560]{1,0:T(8,128)(2,1)S(1)} collective-permute-done((bf16[384,2560]{1,0:T(8,128)(2,1)S(1)}, bf16[384,2560]{1,0:T(8,128)(2,1)S(1)}, u32[]{:S(2)}, u32[]{:S(2)}) %collective-permute-start.8) | collective-permute-done | bytes 1966112 | tf_op jit(solution)/shard_map/ppermute | solution.py:109
  66.1 1.7 %add_convert_fusion = bf16[384,2560]{1,0:T(8,128)(2,1)} fusion(bf16[384,2560]{1,0:T(8,128)(2,1)S(1)} %collective-permute-done.8, bf16[384,2560]{1,0:T(8,128)(2,1)S(1)} %add_convert_fusion.2), kind=kLoop, calls=%fused_computation | loop fusion | flops 3932160 | bytes 5898240 | tf_op jit(solution)/shard_map/convert_element_type | solution.py:113
  (72 shorter events, 13.7 us)
Async XLA Ops:
  0.0 7.9 %copy-start.2 = (bf16[384,1280]{1,0:T(8,128)(2,1)S(1)}, bf16[384,1280]{1,0:T(8,128)(2,1)}, u32[]{:S(2)}) copy-start(bf16[384,1280]{1,0:T(8,128)(2,1)} %param.4) | copy-start | bytes 2949124
  3.2 16.6 %collective-permute-start.5 = (bf16[2,128,640]{1,2,0:T(8,128)(2,1)}, bf16[2,128,640]{1,2,0:T(8,128)(2,1)}, u32[]{:S(2)}, u32[]{:S(2)}) collective-permute-start(bf16[2,128,640]{1,2,0:T(8,128)(2,1)} %pad_maximum_fusion.1), channel_id=1, source_target_pairs={{0,4},{2,6},{4,0},{6,2},{8,12},{10,14},{12,8},{14,10},{16,20},{18,... | collective-permute-start | bytes 983048 | tf_op jit(solution)/shard_map/ppermute | solution.py:13
  5.3 17.5 %collective-permute-start.4 = (bf16[2,128,640]{1,2,0:T(8,128)(2,1)}, bf16[2,128,640]{1,2,0:T(8,128)(2,1)}, u32[]{:S(2)}, u32[]{:S(2)}) collective-permute-start(bf16[2,128,640]{1,2,0:T(8,128)(2,1)} %pad_maximum_fusion.1), channel_id=1, source_target_pairs={{0,2},{2,0},{4,6},{6,4},{8,10},{10,8},{12,14},{14,12},{16,18},{18,... | collective-permute-start | bytes 983048 | tf_op jit(solution)/shard_map/ppermute | solution.py:13
  7.6 16.5 %collective-permute-start = (bf16[2,128,640]{1,2,0:T(8,128)(2,1)}, bf16[2,128,640]{1,2,0:T(8,128)(2,1)S(1)}, u32[]{:S(2)}, u32[]{:S(2)}) collective-permute-start(bf16[2,128,640]{1,2,0:T(8,128)(2,1)} %pad_maximum_fusion), channel_id=1, source_target_pairs={{0,4},{2,6},{4,0},{6,2},{8,12},{10,14},{12,8},{14,10},{16,20},{18,... | collective-permute-start | bytes 983048 | tf_op jit(solution)/shard_map/ppermute | solution.py:13
  7.8 18.0 %collective-permute-start.3 = (bf16[2,128,640]{1,2,0:T(8,128)(2,1)}, bf16[2,128,640]{1,2,0:T(8,128)(2,1)}, u32[]{:S(2)}, u32[]{:S(2)}) collective-permute-start(bf16[2,128,640]{1,2,0:T(8,128)(2,1)} %pad_maximum_fusion), channel_id=1, source_target_pairs={{0,2},{2,0},{4,6},{6,4},{8,10},{10,8},{12,14},{14,12},{16,18},{18,... | collective-permute-start | bytes 983048 | tf_op jit(solution)/shard_map/ppermute | solution.py:13
  19.8 10.1 %collective-permute-start.6 = (bf16[2,128,640]{1,2,0:T(8,128)(2,1)}, bf16[2,128,640]{1,2,0:T(8,128)(2,1)S(1)}, u32[]{:S(2)}, u32[]{:S(2)}) collective-permute-start(bf16[2,128,640]{1,2,0:T(8,128)(2,1)} %collective-permute-done.5), channel_id=1, source_target_pairs={{0,8},{2,10},{4,28},{6,30},{8,16},{10,18},{12,4},{14,6},{16,24},{1... | collective-permute-start | bytes 983048 | tf_op jit(solution)/shard_map/ppermute | solution.py:24
  24.1 12.8 %collective-permute-start.1 = (bf16[2,128,640]{1,2,0:T(8,128)(2,1)S(1)}, bf16[2,128,640]{1,2,0:T(8,128)(2,1)S(1)}, u32[]{:S(2)}, u32[]{:S(2)}) collective-permute-start(bf16[2,128,640]{1,2,0:T(8,128)(2,1)S(1)} %collective-permute-done), channel_id=1, source_target_pairs={{0,8},{2,10},{4,28},{6,30},{8,16},{10,18},{12,4},{14,6},{16,24},{1... | collective-permute-start | bytes 983048 | tf_op jit(solution)/shard_map/ppermute | solution.py:24
  30.9 10.7 %collective-permute-start.7 = (bf16[2,128,640]{1,2,0:T(8,128)(2,1)S(1)}, bf16[2,128,640]{1,2,0:T(8,128)(2,1)S(1)}, u32[]{:S(2)}, u32[]{:S(2)}) collective-permute-start(bf16[2,128,640]{1,2,0:T(8,128)(2,1)S(1)} %broadcast_select_fusion), channel_id=1, source_target_pairs={{0,2},{2,0},{4,6},{6,4},{8,10},{10,8},{12,14},{14,12},{16,18},{18,... | collective-permute-start | bytes 983048 | tf_op jit(solution)/shard_map/ppermute | solution.py:13
  37.4 15.9 %collective-permute-start.2 = (bf16[2,128,640]{1,2,0:T(8,128)(2,1)S(1)}, bf16[2,128,640]{1,2,0:T(8,128)(2,1)S(1)}, u32[]{:S(2)}, u32[]{:S(2)}) collective-permute-start(bf16[2,128,640]{1,2,0:T(8,128)(2,1)S(1)} %broadcast_select_fusion.1), channel_id=1, source_target_pairs={{0,2},{2,0},{4,6},{6,4},{8,10},{10,8},{12,14},{14,12},{16,18},{18,... | collective-permute-start | bytes 983048 | tf_op jit(solution)/shard_map/ppermute | solution.py:13
  42.7 2.2 %slice-start.2 = ((s8[6553600]{0:T(1024)(128)(4,1)}), s8[4194304]{0:T(1024)(128)(4,1)S(1)}, s32[]{:S(2)}) async-start(s8[6553600]{0:T(1024)(128)(4,1)} %bitcast.142), calls=%async_computation.2 | async-start | bytes 8388608
  43.3 2.5 %slice-start.3 = ((s8[6553600]{0:T(1024)(128)(4,1)}), s8[2359296]{0:T(1024)(128)(4,1)S(1)}, s32[]{:S(2)}) async-start(s8[6553600]{0:T(1024)(128)(4,1)} %bitcast.142), calls=%async_computation.3 | async-start | bytes 4718592
  54.8 3.8 %copy-start.1 = (f32[384,2560]{1,0:T(8,128)S(1)}, f32[384,2560]{1,0:T(8,128)}, u32[]{:S(2)}) copy-start(f32[384,2560]{1,0:T(8,128)} %fusion.4) | copy-start | bytes 11796484
  54.9 7.6 %slice-start = ((s8[6553600]{0:T(1024)(128)(4,1)}), s8[4194304]{0:T(1024)(128)(4,1)S(1)}, s32[]{:S(2)}) async-start(s8[6553600]{0:T(1024)(128)(4,1)} %bitcast.140), calls=%async_computation | async-start | bytes 8388608
  58.7 3.8 %slice-start.1 = ((s8[6553600]{0:T(1024)(128)(4,1)}), s8[2359296]{0:T(1024)(128)(4,1)S(1)}, s32[]{:S(2)}) async-start(s8[6553600]{0:T(1024)(128)(4,1)} %bitcast.140), calls=%async_computation.1 | async-start | bytes 4718592
  59.5 4.7 %copy-start = (f32[384,2560]{1,0:T(8,128)S(1)}, f32[384,2560]{1,0:T(8,128)}, u32[]{:S(2)}) copy-start(f32[384,2560]{1,0:T(8,128)} %fusion.6) | copy-start | bytes 11796484
  59.5 6.5 %collective-permute-start.8 = (bf16[384,2560]{1,0:T(8,128)(2,1)S(1)}, bf16[384,2560]{1,0:T(8,128)(2,1)S(1)}, u32[]{:S(2)}, u32[]{:S(2)}) collective-permute-start(bf16[384,2560]{1,0:T(8,128)(2,1)S(1)} %add_convert_fusion.1), channel_id=1, source_target_pairs={{0,1},{1,0},{2,3},{3,2},{4,5},{5,4},{6,7},{7,6},{8,9},{9,8},{10,11... | collective-permute-start | bytes 5898248 | tf_op jit(solution)/shard_map/ppermute | solution.py:109

commit v5 on v3

--- a/solution.py
+++ b/solution.py
@@ -24,14 +24,13 @@
     return lax.ppermute(value, "blk", pairs)
 
 
-def relay_blocks(own):
+def relay_stages(own):
     position = lax.axis_index("blk") % 4
     from_x = swap_within_four(own, 1)
     from_y = swap_within_four(own, 2)
     from_z = shift_groups(from_y)
     forward = jnp.where((position == 0) | (position == 3), from_y, from_z)
-    from_last = swap_within_four(forward, 1)
-    return [from_x, from_y, from_z, from_last]
+    return [from_x, from_y, from_z], forward
 
 
 def fold_block(state, key_rows, value_rows, query_heads):
@@ -64,10 +63,16 @@
         jnp.zeros((row_count, head_count), jnp.float32),
         jnp.zeros((row_count, head_count, HS), jnp.float32),
     )
-    key_arrivals = relay_blocks(keys)
-    value_arrivals = relay_blocks(values)
-    state = fold_block(state, keys, values, query_heads)
-    for key_rows, value_rows in zip(key_arrivals, value_arrivals):
+    key_early, key_forward = relay_stages(keys)
+    value_early, value_forward = relay_stages(values)
+    key_last = swap_within_four(key_forward, 1)
+    value_last = swap_within_four(value_forward, 1)
+    _, *held = lax.optimization_barrier(
+        (value_forward, keys, values, *key_early, *value_early)
+    )
+    key_blocks = [held[0]] + held[2:5] + [key_last]
+    value_blocks = [held[1]] + held[5:8] + [value_last]
+    for key_rows, value_rows in zip(key_blocks, value_blocks):
         state = fold_block(state, key_rows, value_rows, query_heads)
     running_max, running_sum, numerator = state
     attended = (

time: 58.6 us -> 64.8 us (1.11)
  the two profiles are of different devices: /device:TPU:1 before, /device:TPU:5 now
where the time goes in v5:
time: 64.8 us; the launch traced here: 64.5 us
  waiting for transfers between devices  18.5 us (29%)
  matrix products  18.5 us (29%)
  starting transfers between devices  15.8 us (24%)
  local copies, waits for them, and re-layouts  6.35 us (10%)
  other arithmetic  5.18 us (8%)
    ppermute x6, waiting for transfers between devices, swap_within_four(): lax.ppermute(value, 'blk', [(source, source ^ bit) for source in range(co...  15.1 us
    dot_general x2, matrix products, partial_for(): jnp.dot(attended, cols, preferred_element_type=jnp.float32)  9.57 us
    ppermute x2, starting transfers between devices, shift_groups(): return lax.ppermute(value, 'blk', pairs)  6.64 us
    unnamed x19, local copies, waits for them, and re-layouts  5.93 us
    ppermute x6, starting transfers between devices, swap_within_four(): lax.ppermute(value, 'blk', [(source, source ^ bit) for source in range(co...  5.35 us
    dot_general x5, matrix products, fold_block(): jnp.einsum('qhk,khd->qhd', weights.astype(jnp.bfloat16), value_heads, pre...  4.58 us
    dot_general x5, matrix products, fold_block(): jnp.einsum('qhd,khd->qhk', query_heads, key_heads, preferred_element_type...  4.31 us
    ppermute x1, starting transfers between devices, on_device(): received.append(lax.ppermute(sent, 'mp', pairs))  3.77 us
  transfers between devices with their start and end apart: 9, of which 4 were waited for; matrix products, arithmetic and copies ran while one was open for 28% of the time, Pallas kernels for 0%

profile of v5, /device:TPU:5, one launch (start us, length us, event | category | flops | bytes accessed | tf_op | source)
XLA Modules:
  0.0 64.5 jit_solution(2698395348613423125)
XLA Ops:
  0.0 1.9 %copy.24 = bf16[128,1280]{0,1:T(8,128)(2,1)} copy(bf16[128,1280]{1,0:T(8,128)(2,1)} %param.6) | data formatting | bytes 655360 | tf_op args[2]
  1.9 1.9 %copy.25 = bf16[128,1280]{0,1:T(8,128)(2,1)} copy(bf16[128,1280]{1,0:T(8,128)(2,1)} %param.5) | data formatting | bytes 655360 | tf_op args[1]
  3.7 1.5 %collective-permute-start.3 = (bf16[128,1280]{0,1:T(8,128)(2,1)}, bf16[128,1280]{0,1:T(8,128)(2,1)S(1)}, u32[]{:S(2)}, u32[]{:S(2)}) collective-permute-start(bf16[128,1280]{0,1:T(8,128)(2,1)} %copy.25), channel_id=1, source_target_pairs={{0,4},{2,6},{4,0},{6,2},{8,12},{10,14},{12,8},{14,10},{16,20},{18,... | collective-permute-start | bytes 983048 | tf_op jit(solution)/shard_map/ppermute | solution.py:13
  5.2 5.5 %collective-permute-done = bf16[128,1280]{0,1:T(8,128)(2,1)S(1)} collective-permute-done((bf16[128,1280]{0,1:T(8,128)(2,1)}, bf16[128,1280]{0,1:T(8,128)(2,1)S(1)}, u32[]{:S(2)}, u32[]{:S(2)}) %collective-permute-start) | collective-permute-done | bytes 327712 | tf_op jit(solution)/shard_map/ppermute | solution.py:13
  10.7 3.3 %collective-permute-start.1 = (bf16[128,1280]{0,1:T(8,128)(2,1)S(1)}, bf16[128,1280]{0,1:T(8,128)(2,1)S(1)}, u32[]{:S(2)}, u32[]{:S(2)}) collective-permute-start(bf16[128,1280]{0,1:T(8,128)(2,1)S(1)} %collective-permute-done), channel_id=1, source_target_pairs={{0,8},{2,10},{4,28},{6,30},{8,16},{10,18},{12,4},{14,6},{16,24},{1... | collective-permute-start | bytes 983048 | tf_op jit(solution)/shard_map/ppermute | solution.py:24
  14.0 1.2 %collective-permute-start.5 = (bf16[128,1280]{0,1:T(8,128)(2,1)}, bf16[128,1280]{0,1:T(8,128)(2,1)S(1)}, u32[]{:S(2)}, u32[]{:S(2)}) collective-permute-start(bf16[128,1280]{0,1:T(8,128)(2,1)} %copy.24), channel_id=1, source_target_pairs={{0,2},{2,0},{4,6},{6,4},{8,10},{10,8},{12,14},{14,12},{16,18},{18,... | collective-permute-start | bytes 983048 | tf_op jit(solution)/shard_map/ppermute | solution.py:13
  15.5 1.6 %copy.29 = bf16[384,1280]{0,1:T(8,128)(2,1)S(1)} copy(bf16[384,1280]{1,0:T(8,128)(2,1)} %param.4) | data formatting | bytes 1966080 | tf_op args[0]
  17.7 3.3 %collective-permute-start.4 = (bf16[128,1280]{0,1:T(8,128)(2,1)S(1)}, bf16[128,1280]{0,1:T(8,128)(2,1)S(1)}, u32[]{:S(2)}, u32[]{:S(2)}) collective-permute-start(bf16[128,1280]{0,1:T(8,128)(2,1)S(1)} %collective-permute-done.3), channel_id=1, source_target_pairs={{0,8},{2,10},{4,28},{6,30},{8,16},{10,18},{12,4},{14,6},{16,24},{1... | collective-permute-start | bytes 983048 | tf_op jit(solution)/shard_map/ppermute | solution.py:24
  21.0 0.8 %broadcast_select_fusion.1 = bf16[128,1280]{0,1:T(8,128)(2,1)} fusion(bf16[128,1280]{0,1:T(8,128)(2,1)S(1)} %collective-permute-done, bf16[128,1280]{0,1:T(8,128)(2,1)S(1)} %collective-permute-done.1, pred[]{:T(512)S(6)} %or.4), kind=kLoop, calls=%fused_computation.58 | loop fusion | flops 163840 | bytes 983041 | tf_op jit(solution)/shard_map/jit(_where)/select_n | solution.py:32
  21.9 1.2 %collective-permute-start.7 = (bf16[128,1280]{0,1:T(8,128)(2,1)}, bf16[128,1280]{0,1:T(8,128)(2,1)}, u32[]{:S(2)}, u32[]{:S(2)}) collective-permute-start(bf16[128,1280]{0,1:T(8,128)(2,1)} %broadcast_select_fusion.1), channel_id=1, source_target_pairs={{0,2},{2,0},{4,6},{6,4},{8,10},{10,8},{12,14},{14,12},{16,18},{18,... | collective-permute-start | bytes 983048 | tf_op jit(solution)/shard_map/ppermute | solution.py:13
  23.1 3.5 %collective-permute-done.4 = bf16[128,1280]{0,1:T(8,128)(2,1)S(1)} collective-permute-done((bf16[128,1280]{0,1:T(8,128)(2,1)S(1)}, bf16[128,1280]{0,1:T(8,128)(2,1)S(1)}, u32[]{:S(2)}, u32[]{:S(2)}) %collective-permute-start.4) | collective-permute-done | bytes 327712 | tf_op jit(solution)/shard_map/ppermute | solution.py:24
  26.6 0.7 %broadcast_select_fusion = bf16[128,1280]{0,1:T(8,128)(2,1)} fusion(bf16[128,1280]{0,1:T(8,128)(2,1)S(1)} %collective-permute-done.3, bf16[128,1280]{0,1:T(8,128)(2,1)S(1)} %collective-permute-done.4, pred[]{:T(512)S(6)} %or.4), kind=kLoop, calls=%fused_computation.57 | loop fusion | flops 163840 | bytes 983041 | tf_op jit(solution)/shard_map/jit(_where)/select_n | solution.py:32
  27.3 1.2 %collective-permute-start.6 = (bf16[128,1280]{0,1:T(8,128)(2,1)}, bf16[128,1280]{0,1:T(8,128)(2,1)}, u32[]{:S(2)}, u32[]{:S(2)}) collective-permute-start(bf16[128,1280]{0,1:T(8,128)(2,1)} %broadcast_select_fusion), channel_id=1, source_target_pairs={{0,2},{2,0},{4,6},{6,4},{8,10},{10,8},{12,14},{14,12},{16,18},{18,... | collective-permute-start | bytes 983048 | tf_op jit(solution)/shard_map/ppermute | solution.py:13
  29.0 1.4 %bitcast_reduce_fusion.3 = (f32[384,10]{0,1:T(8,128)S(1)}, f32[10,128,384]{2,1,0:T(8,128)S(1)}) fusion(bf16[128,10,128]{0,2,1:T(8,128)(2,1)} %bitcast.5, bf16[384,10,128]{0,2,1:T(8,128)(2,1)S(1)} %bitcast.109), kind=kOutput, calls=%fused_computation.26 | convolution fusion | flops 126808320 | bytes 3292160 | tf_op jit(solution)/shard_map/qhd,khd->qhk/dot_general | solution.py:41
  32.7 9.0 %collective-permute-done.6 = bf16[128,1280]{0,1:T(8,128)(2,1)} collective-permute-done((bf16[128,1280]{0,1:T(8,128)(2,1)}, bf16[128,1280]{0,1:T(8,128)(2,1)}, u32[]{:S(2)}, u32[]{:S(2)}) %collective-permute-start.6) | collective-permute-done | bytes 327712 | tf_op jit(solution)/shard_map/ppermute | solution.py:13
  41.7 1.4 %bitcast_reduce_fusion = (f32[384,10]{0,1:T(8,128)S(1)}, f32[10,128,384]{2,1,0:T(8,128)S(1)}) fusion(bf16[128,10,128]{0,2,1:T(8,128)(2,1)} %bitcast.17, bf16[384,10,128]{0,2,1:T(8,128)(2,1)S(1)} %bitcast.113), kind=kOutput, calls=%fused_computation.11 | convolution fusion | flops 126808320 | bytes 3292160 | tf_op jit(solution)/shard_map/qhd,khd->qhk/dot_general | solution.py:41
  43.7 0.7 %fusion.23 = (f32[384,10]{0,1:T(8,128)S(1)}, f32[384,10]{0,1:T(8,128)S(1)}) fusion(f32[10,128,384]{2,1,0:T(8,128)S(1)} %get-tuple-element.40, f32[384,10]{0,1:T(8,128)S(1)} %get-tuple-element.29, f32[384,10]{0,1:T(8,128)S(1)} %get-tuple-element.28, f32[10,128,384]{2,1,0:T(8,128)S(1)} %get-tuple-element.36), kind=kLoop, calls=%fused_computation.35 | loop fusion | flops 2941440 | bytes 3993600 | tf_op jit(solution)/shard_map/reduce_sum | solution.py:46
  44.9 2.0 %fusion.31 = f32[10,128,384]{2,1,0:T(8,128)S(1)} fusion(bf16[128,10,128]{0,2,1:T(8,128)(2,1)} %bitcast.19, f32[10,128,384]{2,1,0:T(8,128)S(1)} %get-tuple-element.32, f32[384,10]{0,1:T(8,128)S(1)} %get-tuple-element.26), kind=kOutput, calls=%fused_computation.43 | convolution fusion | flops 127303680 | bytes 4275200 | tf_op jit(solution)/shard_map/qhk,khd->qhd/dot_general | solution.py:47
  46.9 0.7 %fusion.27 = (f32[384,10]{0,1:T(8,128)S(1)}, f32[384,10]{0,1:T(8,128)S(1)}) fusion(f32[10,128,384]{2,1,0:T(8,128)S(1)} %get-tuple-element.34, f32[384,10]{0,1:T(8,128)S(1)} %get-tuple-element.27, f32[384,10]{0,1:T(8,128)S(1)} %get-tuple-element.26, f32[10,128,384]{2,1,0:T(8,128)S(1)} %get-tuple-element.32), kind=kLoop, calls=%fused_computation.39 | loop fusion | flops 2941440 | bytes 3993600 | tf_op jit(solution)/shard_map/reduce_sum | solution.py:46
  47.9 1.1 %fusion.11 = bf16[384,10,128]{0,2,1:T(8,128)(2,1)S(1)} fusion(f32[10,128,384]{2,1,0:T(8,128)S(1)} %fusion.31, f32[10,128,384]{2,1,0:T(8,128)S(1)} %fusion.34, f32[10,128,384]{2,1,0:T(8,128)S(1)} %fusion.36, f32[10,128,384]{2,1,0:T(8,128)S(1)} %fusion.38, bf16[128,10,128]{0,2,1:T(8,128)(2,1)S(1)} %bitcast.120, f32[10,128,384]{2,1,0:T(8,128)S(1)} %get-tuple-element.34, ...), kind=kOutput, calls=%fused_computation.9 | convolution fusion | flops 132710400 | bytes 11248640 | tf_op jit(solution)/shard_map/qhk,khd->qhd/dot_general | solution.py:47
  49.4 4.0 %fusion.7 = bf16[384,2560]{1,0:T(8,128)(2,1)} fusion(bf16[384,1280]{0,1:T(8,128)(2,1)S(1)} %bitcast.123, bf16[1280,5120]{1,0:T(8,128)(2,1)S(1)} %bitcast.122, s32[]{:T(128)S(6)} %select_n.37), kind=kOutput, calls=%fused_computation.5 | convolution fusion | flops 2517565440 | bytes 9502724 | tf_op jit(solution)/shard_map/dot_general | solution.py:89
  53.4 3.8 %collective-permute-start.8 = (bf16[384,2560]{1,0:T(8,128)(2,1)}, bf16[384,2560]{1,0:T(8,128)(2,1)S(1)}, u32[]{:S(2)}, u32[]{:S(2)}) collective-permute-start(bf16[384,2560]{1,0:T(8,128)(2,1)} %fusion.7), channel_id=1, source_target_pairs={{0,1},{1,0},{2,3},{3,2},{4,5},{5,4},{6,7},{7,6},{8,9},{9,8},{10,11... | collective-permute-start | bytes 5898248 | tf_op jit(solution)/shard_map/ppermute | solution.py:95
  57.2 5.6 %fusion.4 = bf16[384,2560]{1,0:T(8,128)(2,1)S(1)} fusion(bf16[384,1280]{0,1:T(8,128)(2,1)S(1)} %bitcast.124, bf16[1280,5120]{1,0:T(8,128)(2,1)} %param.7, s32[]{:T(128)S(6)} %select_n.35), kind=kOutput, calls=%fused_computation.4 | convolution fusion | flops 2517565440 | bytes 9502724 | tf_op jit(solution)/shard_map/dot_general | solution.py:89
  62.8 1.7 %add_convert_fusion = bf16[384,2560]{1,0:T(8,128)(2,1)} fusion(bf16[384,2560]{1,0:T(8,128)(2,1)S(1)} %collective-permute-done.8, bf16[384,2560]{1,0:T(8,128)(2,1)S(1)} %fusion.4), kind=kLoop, calls=%fused_computation.6 | loop fusion | flops 3932160 | bytes 5898240 | tf_op jit(solution)/shard_map/convert_element_type | solution.py:99
  (36 shorter events, 5.0 us)
Async XLA Ops:
  1.9 8.8 %collective-permute-start = (bf16[128,1280]{0,1:T(8,128)(2,1)}, bf16[128,1280]{0,1:T(8,128)(2,1)S(1)}, u32[]{:S(2)}, u32[]{:S(2)}) collective-permute-start(bf16[128,1280]{0,1:T(8,128)(2,1)} %copy.24), channel_id=1, source_target_pairs={{0,4},{2,6},{4,0},{6,2},{8,12},{10,14},{12,8},{14,10},{16,20},{18,... | collective-permute-start | bytes 983048 | tf_op jit(solution)/shard_map/ppermute | solution.py:13
  3.7 13.9 %collective-permute-start.3 = (bf16[128,1280]{0,1:T(8,128)(2,1)}, bf16[128,1280]{0,1:T(8,128)(2,1)S(1)}, u32[]{:S(2)}, u32[]{:S(2)}) collective-permute-start(bf16[128,1280]{0,1:T(8,128)(2,1)} %copy.25), channel_id=1, source_target_pairs={{0,4},{2,6},{4,0},{6,2},{8,12},{10,14},{12,8},{14,10},{16,20},{18,... | collective-permute-start | bytes 983048 | tf_op jit(solution)/shard_map/ppermute | solution.py:13
  10.7 10.3 %collective-permute-start.1 = (bf16[128,1280]{0,1:T(8,128)(2,1)S(1)}, bf16[128,1280]{0,1:T(8,128)(2,1)S(1)}, u32[]{:S(2)}, u32[]{:S(2)}) collective-permute-start(bf16[128,1280]{0,1:T(8,128)(2,1)S(1)} %collective-permute-done), channel_id=1, source_target_pairs={{0,8},{2,10},{4,28},{6,30},{8,16},{10,18},{12,4},{14,6},{16,24},{1... | collective-permute-start | bytes 983048 | tf_op jit(solution)/shard_map/ppermute | solution.py:24
  14.0 14.5 %collective-permute-start.5 = (bf16[128,1280]{0,1:T(8,128)(2,1)}, bf16[128,1280]{0,1:T(8,128)(2,1)S(1)}, u32[]{:S(2)}, u32[]{:S(2)}) collective-permute-start(bf16[128,1280]{0,1:T(8,128)(2,1)} %copy.24), channel_id=1, source_target_pairs={{0,2},{2,0},{4,6},{6,4},{8,10},{10,8},{12,14},{14,12},{16,18},{18,... | collective-permute-start | bytes 983048 | tf_op jit(solution)/shard_map/ppermute | solution.py:13
  15.2 13.3 %collective-permute-start.2 = (bf16[128,1280]{0,1:T(8,128)(2,1)}, bf16[128,1280]{0,1:T(8,128)(2,1)}, u32[]{:S(2)}, u32[]{:S(2)}) collective-permute-start(bf16[128,1280]{0,1:T(8,128)(2,1)} %copy.25), channel_id=1, source_target_pairs={{0,2},{2,0},{4,6},{6,4},{8,10},{10,8},{12,14},{14,12},{16,18},{18,... | collective-permute-start | bytes 983048 | tf_op jit(solution)/shard_map/ppermute | solution.py:13
  15.5 13.1 %copy-start = (bf16[128,1280]{1,0:T(8,128)(2,1)S(1)}, bf16[128,1280]{1,0:T(8,128)(2,1)}, u32[]{:S(2)}) copy-start(bf16[128,1280]{1,0:T(8,128)(2,1)} %param.5) | copy-start | bytes 983044
  15.5 13.3 %copy-start.1 = (bf16[128,1280]{1,0:T(8,128)(2,1)S(1)}, bf16[128,1280]{1,0:T(8,128)(2,1)}, u32[]{:S(2)}) copy-start(bf16[128,1280]{1,0:T(8,128)(2,1)} %param.6) | copy-start | bytes 983044
  17.7 8.9 %collective-permute-start.4 = (bf16[128,1280]{0,1:T(8,128)(2,1)S(1)}, bf16[128,1280]{0,1:T(8,128)(2,1)S(1)}, u32[]{:S(2)}, u32[]{:S(2)}) collective-permute-start(bf16[128,1280]{0,1:T(8,128)(2,1)S(1)} %collective-permute-done.3), channel_id=1, source_target_pairs={{0,8},{2,10},{4,28},{6,30},{8,16},{10,18},{12,4},{14,6},{16,24},{1... | collective-permute-start | bytes 983048 | tf_op jit(solution)/shard_map/ppermute | solution.py:24
  21.0 7.5 %copy-start.2 = (bf16[128,1280]{0,1:T(8,128)(2,1)}, bf16[128,1280]{0,1:T(8,128)(2,1)S(1)}, u32[]{:S(2)}) copy-start(bf16[128,1280]{0,1:T(8,128)(2,1)S(1)} %collective-permute-done.1) | copy-start | bytes 983044
  21.9 23.0 %collective-permute-start.7 = (bf16[128,1280]{0,1:T(8,128)(2,1)}, bf16[128,1280]{0,1:T(8,128)(2,1)}, u32[]{:S(2)}, u32[]{:S(2)}) collective-permute-start(bf16[128,1280]{0,1:T(8,128)(2,1)} %broadcast_select_fusion.1), channel_id=1, source_target_pairs={{0,2},{2,0},{4,6},{6,4},{8,10},{10,8},{12,14},{14,12},{16,18},{18,... | collective-permute-start | bytes 983048 | tf_op jit(solution)/shard_map/ppermute | solution.py:13
  27.3 14.4 %collective-permute-start.6 = (bf16[128,1280]{0,1:T(8,128)(2,1)}, bf16[128,1280]{0,1:T(8,128)(2,1)}, u32[]{:S(2)}, u32[]{:S(2)}) collective-permute-start(bf16[128,1280]{0,1:T(8,128)(2,1)} %broadcast_select_fusion), channel_id=1, source_target_pairs={{0,2},{2,0},{4,6},{6,4},{8,10},{10,8},{12,14},{14,12},{16,18},{18,... | collective-permute-start | bytes 983048 | tf_op jit(solution)/shard_map/ppermute | solution.py:13
  43.7 5.4 %slice-start = ((s8[13107200]{0:T(1024)(128)(4,1)}), s8[4194304]{0:T(1024)(128)(4,1)S(1)}, s32[]{:S(2)}) async-start(s8[13107200]{0:T(1024)(128)(4,1)} %bitcast.121), calls=%async_computation | async-start | bytes 8388608
  44.4 4.7 %slice-start.1 = ((s8[13107200]{0:T(1024)(128)(4,1)}), s8[4194304]{0:T(1024)(128)(4,1)S(1)}, s32[]{:S(2)}) async-start(s8[13107200]{0:T(1024)(128)(4,1)} %bitcast.121), calls=%async_computation.1 | async-start | bytes 8388608
  46.9 1.0 %copy-start.3 = (bf16[128,1280]{0,1:T(8,128)(2,1)S(1)}, bf16[128,1280]{0,1:T(8,128)(2,1)}, u32[]{:S(2)}) copy-start(bf16[128,1280]{0,1:T(8,128)(2,1)} %copy-done.2) | copy-start | bytes 983044
  46.9 2.4 %slice-start.2 = ((s8[13107200]{0:T(1024)(128)(4,1)}), s8[4194304]{0:T(1024)(128)(4,1)S(1)}, s32[]{:S(2)}) async-start(s8[13107200]{0:T(1024)(128)(4,1)} %bitcast.121), calls=%async_computation.2 | async-start | bytes 8388608
  47.9 1.5 %slice-start.3 = ((s8[13107200]{0:T(1024)(128)(4,1)}), s8[524288]{0:T(1024)(128)(4,1)S(1)}, s32[]{:S(2)}) async-start(s8[13107200]{0:T(1024)(128)(4,1)} %bitcast.121), calls=%async_computation.3 | async-start | bytes 1048576
  53.4 9.4 %collective-permute-start.8 = (bf16[384,2560]{1,0:T(8,128)(2,1)}, bf16[384,2560]{1,0:T(8,128)(2,1)S(1)}, u32[]{:S(2)}, u32[]{:S(2)}) collective-permute-start(bf16[384,2560]{1,0:T(8,128)(2,1)} %fusion.7), channel_id=1, source_target_pairs={{0,1},{1,0},{2,3},{3,2},{4,5},{5,4},{6,7},{7,6},{8,9},{9,8},{10,11... | collective-permute-start | bytes 5898248 | tf_op jit(solution)/shard_map/ppermute | solution.py:95

commit v6 on v3

--- a/solution.py
+++ b/solution.py
@@ -24,14 +24,19 @@
     return lax.ppermute(value, "blk", pairs)
 
 
-def relay_blocks(own):
+def relay_pair(keys, values):
     position = lax.axis_index("blk") % 4
-    from_x = swap_within_four(own, 1)
-    from_y = swap_within_four(own, 2)
-    from_z = shift_groups(from_y)
-    forward = jnp.where((position == 0) | (position == 3), from_y, from_z)
-    from_last = swap_within_four(forward, 1)
-    return [from_x, from_y, from_z, from_last]
+    key_x = swap_within_four(keys, 1)
+    value_x = swap_within_four(values, 1)
+    key_y = swap_within_four(keys, 2)
+    values, _ = lax.optimization_barrier((values, key_y))
+    value_y = swap_within_four(values, 2)
+    key_z = shift_groups(key_y)
+    value_z = shift_groups(value_y)
+    keep = (position == 0) | (position == 3)
+    key_last = swap_within_four(jnp.where(keep, key_y, key_z), 1)
+    value_last = swap_within_four(jnp.where(keep, value_y, value_z), 1)
+    return [(key_x, value_x), (key_y, value_y), (key_z, value_z), (key_last, value_last)]
 
 
 def fold_block(state, key_rows, value_rows, query_heads):
@@ -64,10 +69,9 @@
         jnp.zeros((row_count, head_count), jnp.float32),
         jnp.zeros((row_count, head_count, HS), jnp.float32),
     )
-    key_arrivals = relay_blocks(keys)
-    value_arrivals = relay_blocks(values)
+    arrivals = relay_pair(keys, values)
     state = fold_block(state, keys, values, query_heads)
-    for key_rows, value_rows in zip(key_arrivals, value_arrivals):
+    for key_rows, value_rows in arrivals:
         state = fold_block(state, key_rows, value_rows, query_heads)
     running_max, running_sum, numerator = state
     attended = (

time: 58.6 us -> 65.7 us (1.12)
  matrix products: 21.5 us -> 25.4 us
  starting transfers between devices: 11.1 us -> 14.4 us
  other arithmetic: 4.66 us -> 5.36 us
    ppermute x6, waiting for transfers between devices: 8.13 us -> 4.37 us  [swap_within_four(): lax.ppermute(value, 'blk', [(source, source ^ bit) for source in range(co...]
    ppermute x2, waiting for transfers between devices: 4.32 us -> 7.85 us  [shift_groups(): return lax.ppermute(value, 'blk', pairs)]
    dot_general x2, matrix products: 9.86 us -> 12.5 us  [partial_for(): jnp.dot(attended, cols, preferred_element_type=jnp.float32)]
    ppermute x1, starting transfers between devices: 2.14 us -> 4.62 us  [on_device(): received.append(lax.ppermute(sent, 'mp', pairs))]
    ppermute x6, starting transfers between devices: 6.08 us -> 8.54 us  [swap_within_four(): lax.ppermute(value, 'blk', [(source, source ^ bit) for source in range(co...]
    dot_general x5, matrix products: 6.28 us -> 8.63 us  [fold_block(): jnp.einsum('qhd,khd->qhk', query_heads, key_heads, preferred_element_type...]
    ppermute x2, starting transfers between devices: 2.87 us -> 1.24 us  [shift_groups(): return lax.ppermute(value, 'blk', pairs)]
    unnamed x19 -> x13, local copies, waits for them, and re-layouts: 6.1 us -> 4.91 us
  transfers between devices with their start and end apart: 9 -> 9, of which waited for: 3 -> 5; matrix products, arithmetic and copies ran while one was open for 39% -> 39% of each run, Pallas kernels for 0% -> 0%
where the time goes in v6:
time: 65.7 us; the launch traced here: 65.2 us
  matrix products  25.4 us (39%)
  starting transfers between devices  14.4 us (22%)
  waiting for transfers between devices  12.2 us (19%)
  local copies, waits for them, and re-layouts  7.69 us (12%)
  other arithmetic  5.36 us (8%)
    dot_general x2, matrix products, partial_for(): jnp.dot(attended, cols, preferred_element_type=jnp.float32)  12.5 us
    dot_general x5, matrix products, fold_block(): jnp.einsum('qhd,khd->qhk', query_heads, key_heads, preferred_element_type...  8.63 us
    ppermute x6, starting transfers between devices, swap_within_four(): lax.ppermute(value, 'blk', [(source, source ^ bit) for source in range(co...  8.54 us
    ppermute x2, waiting for transfers between devices, shift_groups(): return lax.ppermute(value, 'blk', pairs)  7.85 us
    unnamed x13, local copies, waits for them, and re-layouts  4.91 us
    ppermute x1, starting transfers between devices, on_device(): received.append(lax.ppermute(sent, 'mp', pairs))  4.62 us
    ppermute x6, waiting for transfers between devices, swap_within_four(): lax.ppermute(value, 'blk', [(source, source ^ bit) for source in range(co...  4.37 us
    dot_general x5, matrix products, fold_block(): jnp.einsum('qhk,khd->qhd', weights.astype(jnp.bfloat16), value_heads, pre...  4.25 us
  transfers between devices with their start and end apart: 9, of which 5 were waited for; matrix products, arithmetic and copies ran while one was open for 39% of the time, Pallas kernels for 0%

profile of v6, /device:TPU:1, one launch (start us, length us, event | category | flops | bytes accessed | tf_op | source)
XLA Modules:
  0.0 65.2 jit_solution(10242687756374345785)
XLA Ops:
  0.0 2.0 %copy.21 = bf16[128,1280]{0,1:T(8,128)(2,1)} copy(bf16[128,1280]{1,0:T(8,128)(2,1)} %param.5) | data formatting | bytes 655360 | tf_op args[1]
  2.0 2.1 %collective-permute-start.2 = (bf16[128,1280]{0,1:T(8,128)(2,1)}, bf16[128,1280]{0,1:T(8,128)(2,1)}, u32[]{:S(2)}, u32[]{:S(2)}) collective-permute-start(bf16[128,1280]{0,1:T(8,128)(2,1)} %copy.21), channel_id=1, source_target_pairs={{0,4},{2,6},{4,0},{6,2},{8,12},{10,14},{12,8},{14,10},{16,20},{18,... | collective-permute-start | bytes 983048 | tf_op jit(solution)/shard_map/ppermute | solution.py:13
  4.0 1.2 %collective-permute-start = (bf16[128,1280]{0,1:T(8,128)(2,1)}, bf16[128,1280]{0,1:T(8,128)(2,1)}, u32[]{:S(2)}, u32[]{:S(2)}) collective-permute-start(bf16[128,1280]{0,1:T(8,128)(2,1)} %copy.21), channel_id=1, source_target_pairs={{0,2},{2,0},{4,6},{6,4},{8,10},{10,8},{12,14},{14,12},{16,18},{18,... | collective-permute-start | bytes 983048 | tf_op jit(solution)/shard_map/ppermute | solution.py:13
  5.5 1.2 %copy.25 = bf16[128,1280]{0,1:T(8,128)(2,1)S(1)} copy(bf16[128,1280]{1,0:T(8,128)(2,1)} %param.6) | data formatting | bytes 655360 | tf_op args[2]
  7.4 1.4 %bitcast_reduce_fusion.4 = (f32[384,10]{0,1:T(8,128)S(1)}, f32[10,128,384]{2,1,0:T(8,128)S(1)}) fusion(bf16[128,10,128]{0,2,1:T(8,128)(2,1)} %bitcast, bf16[384,10,128]{0,2,1:T(8,128)(2,1)S(1)} %bitcast.109), kind=kOutput, calls=%fused_computation.31 | convolution fusion | flops 126808320 | bytes 3292160 | tf_op jit(solution)/shard_map/qhd,khd->qhk/dot_general | solution.py:47
  8.8 1.7 %fusion.38 = f32[10,384,128]{1,2,0:T(8,128)} fusion(bf16[128,10,128]{0,2,1:T(8,128)(2,1)S(1)} %bitcast.116, f32[10,128,384]{2,1,0:T(8,128)S(1)} %get-tuple-element.24, f32[384,10]{0,1:T(8,128)S(1)} %get-tuple-element.23), kind=kOutput, calls=%fused_computation.46 | convolution fusion | flops 127303680 | bytes 4275200 | tf_op jit(solution)/shard_map/qhk,khd->qhd/dot_general | solution.py:53
  10.6 1.2 %collective-permute-done.2 = bf16[128,1280]{0,1:T(8,128)(2,1)} collective-permute-done((bf16[128,1280]{0,1:T(8,128)(2,1)}, bf16[128,1280]{0,1:T(8,128)(2,1)}, u32[]{:S(2)}, u32[]{:S(2)}) %collective-permute-start.2) | collective-permute-done | bytes 327712 | tf_op jit(solution)/shard_map/ppermute | solution.py:13
  11.7 1.2 %collective-permute-start.4 = (bf16[128,1280]{0,1:T(8,128)(2,1)}, bf16[128,1280]{0,1:T(8,128)(2,1)}, u32[]{:S(2)}, u32[]{:S(2)}) collective-permute-start(bf16[128,1280]{0,1:T(8,128)(2,1)} %collective-permute-done.2), channel_id=1, source_target_pairs={{0,8},{2,10},{4,28},{6,30},{8,16},{10,18},{12,4},{14,6},{16,24},{1... | collective-permute-start | bytes 983048 | tf_op jit(solution)/shard_map/ppermute | solution.py:24
  14.3 3.3 %collective-permute-start.3 = (bf16[128,1280]{0,1:T(8,128)(2,1)}, bf16[128,1280]{0,1:T(8,128)(2,1)S(1)}, u32[]{:S(2)}, u32[]{:S(2)}) collective-permute-start(bf16[128,1280]{0,1:T(8,128)(2,1)} %copy.35), channel_id=1, source_target_pairs={{0,4},{2,6},{4,0},{6,2},{8,12},{10,14},{12,8},{14,10},{16,20},{18,... | collective-permute-start | bytes 983048 | tf_op jit(solution)/shard_map/ppermute | solution.py:13
  17.5 1.4 %bitcast_reduce_fusion.2 = (f32[384,10]{0,1:T(8,128)S(1)}, f32[10,128,384]{2,1,0:T(8,128)S(1)}) fusion(bf16[128,10,128]{0,2,1:T(8,128)(2,1)} %bitcast.9, bf16[384,10,128]{0,2,1:T(8,128)(2,1)S(1)} %bitcast.110), kind=kOutput, calls=%fused_computation.21 | convolution fusion | flops 126808320 | bytes 3292160 | tf_op jit(solution)/shard_map/qhd,khd->qhk/dot_general | solution.py:47
  19.0 2.9 %collective-permute-done.4 = bf16[128,1280]{0,1:T(8,128)(2,1)} collective-permute-done((bf16[128,1280]{0,1:T(8,128)(2,1)}, bf16[128,1280]{0,1:T(8,128)(2,1)}, u32[]{:S(2)}, u32[]{:S(2)}) %collective-permute-start.4) | collective-permute-done | bytes 327712 | tf_op jit(solution)/shard_map/ppermute | solution.py:24
  21.9 1.7 %broadcast_select_fusion.1 = bf16[128,1280]{0,1:T(8,128)(2,1)} fusion(bf16[128,1280]{0,1:T(8,128)(2,1)} %collective-permute-done.2, bf16[128,1280]{0,1:T(8,128)(2,1)} %collective-permute-done.4, pred[]{:T(512)S(6)} %or.3), kind=kLoop, calls=%fused_computation.58 | loop fusion | flops 163840 | bytes 983041 | tf_op jit(solution)/shard_map/jit(_where)/select_n | solution.py:37
  24.6 2.7 %bitcast_reduce_fusion.3 = (f32[384,10]{0,1:T(8,128)S(1)}, f32[10,128,384]{2,1,0:T(8,128)}) fusion(bf16[128,10,128]{0,2,1:T(8,128)(2,1)} %bitcast.5, bf16[384,10,128]{0,2,1:T(8,128)(2,1)S(1)} %bitcast.111), kind=kOutput, calls=%fused_computation.26 | convolution fusion | flops 126808320 | bytes 3292160 | tf_op jit(solution)/shard_map/qhd,khd->qhk/dot_general | solution.py:47
  27.3 1.9 %copy.30 = bf16[128,1280]{0,1:T(8,128)(2,1)} copy(bf16[128,1280]{1,0:T(8,128)(2,1)} %collective-permute-done.1) | data formatting | bytes 655360 | tf_op jit(solution)/shard_map/ppermute | solution.py:13
  29.2 1.4 %bitcast_reduce_fusion.1 = (f32[384,10]{0,1:T(8,128)S(1)}, f32[10,128,384]{2,1,0:T(8,128)S(1)}) fusion(bf16[128,10,128]{0,2,1:T(8,128)(2,1)} %bitcast.13, bf16[384,10,128]{0,2,1:T(8,128)(2,1)S(1)} %bitcast.112), kind=kOutput, calls=%fused_computation.16 | convolution fusion | flops 126808320 | bytes 3292160 | tf_op jit(solution)/shard_map/qhd,khd->qhk/dot_general | solution.py:47
  31.1 1.6 %bitcast_reduce_fusion = (f32[384,10]{0,1:T(8,128)S(1)}, f32[10,128,384]{2,1,0:T(8,128)S(1)}) fusion(bf16[128,10,128]{0,2,1:T(8,128)(2,1)} %bitcast.17, bf16[384,10,128]{0,2,1:T(8,128)(2,1)S(1)} %bitcast.113), kind=kOutput, calls=%fused_computation.11 | convolution fusion | flops 126808320 | bytes 3292160 | tf_op jit(solution)/shard_map/qhd,khd->qhk/dot_general | solution.py:47
  32.7 5.0 %collective-permute-done.5 = bf16[128,1280]{0,1:T(8,128)(2,1)S(1)} collective-permute-done((bf16[128,1280]{0,1:T(8,128)(2,1)S(1)}, bf16[128,1280]{0,1:T(8,128)(2,1)S(1)}, u32[]{:S(2)}, u32[]{:S(2)}) %collective-permute-start.5) | collective-permute-done | bytes 327712 | tf_op jit(solution)/shard_map/ppermute | solution.py:24
  40.9 2.8 %collective-permute-done.7 = bf16[128,1280]{0,1:T(8,128)(2,1)S(1)} collective-permute-done((bf16[128,1280]{0,1:T(8,128)(2,1)S(1)}, bf16[128,1280]{0,1:T(8,128)(2,1)S(1)}, u32[]{:S(2)}, u32[]{:S(2)}) %collective-permute-start.7) | collective-permute-done | bytes 327712 | tf_op jit(solution)/shard_map/ppermute | solution.py:13
  44.2 1.1 %copy-done.1 = f32[10,384,128]{1,2,0:T(8,128)S(1)} copy-done((f32[10,384,128]{1,2,0:T(8,128)S(1)}, f32[10,384,128]{1,2,0:T(8,128)}, u32[]{:S(2)}) %copy-start.1) | copy-done | bytes 1966104
  45.2 1.1 %fusion.11 = bf16[384,10,128]{0,2,1:T(8,128)(2,1)S(1)} fusion(f32[10,128,384]{2,1,0:T(8,128)S(1)} %fusion.31, f32[10,128,384]{2,1,0:T(8,128)S(1)} %fusion.34, f32[10,384,128]{1,2,0:T(8,128)S(1)} %fusion.36, f32[10,384,128]{1,2,0:T(8,128)S(1)} %copy-done.1, bf16[128,10,128]{0,2,1:T(8,128)(2,1)S(1)} %bitcast.118, f32[10,128,384]{2,1,0:T(8,128)S(1)} %get-tuple-element.20, ...), kind=kOutput, calls=%fused_computation.9 | convolution fusion | flops 132710400 | bytes 11248640 | tf_op jit(solution)/shard_map/qhk,khd->qhd/dot_general | solution.py:53
  46.4 6.9 %fusion.7 = bf16[384,2560]{1,0:T(8,128)(2,1)} fusion(bf16[384,1280]{0,1:T(8,128)(2,1)S(1)} %bitcast.119, bf16[1280,5120]{1,0:T(8,128)(2,1)} %param.7, s32[]{:T(128)S(6)} %select_n.35), kind=kOutput, calls=%fused_computation.5 | convolution fusion | flops 2517565440 | bytes 9502724 | tf_op jit(solution)/shard_map/dot_general | solution.py:88
  53.3 4.6 %collective-permute-start.8 = (bf16[384,2560]{1,0:T(8,128)(2,1)}, bf16[384,2560]{1,0:T(8,128)(2,1)S(1)}, u32[]{:S(2)}, u32[]{:S(2)}) collective-permute-start(bf16[384,2560]{1,0:T(8,128)(2,1)} %fusion.7), channel_id=1, source_target_pairs={{0,1},{1,0},{2,3},{3,2},{4,5},{5,4},{6,7},{7,6},{8,9},{9,8},{10,11... | collective-permute-start | bytes 5898248 | tf_op jit(solution)/shard_map/ppermute | solution.py:94
  57.9 5.6 %fusion.4 = bf16[384,2560]{1,0:T(8,128)(2,1)S(1)} fusion(bf16[384,1280]{0,1:T(8,128)(2,1)S(1)} %bitcast.120, bf16[1280,5120]{1,0:T(8,128)(2,1)} %param.7, s32[]{:T(128)S(6)} %select_n.33), kind=kOutput, calls=%fused_computation.4 | convolution fusion | flops 2517565440 | bytes 9502724 | tf_op jit(solution)/shard_map/dot_general | solution.py:88
  63.5 1.7 %add_convert_fusion = bf16[384,2560]{1,0:T(8,128)(2,1)} fusion(bf16[384,2560]{1,0:T(8,128)(2,1)S(1)} %collective-permute-done.8, bf16[384,2560]{1,0:T(8,128)(2,1)S(1)} %fusion.4), kind=kLoop, calls=%fused_computation.6 | loop fusion | flops 3932160 | bytes 5898240 | tf_op jit(solution)/shard_map/convert_element_type | solution.py:98
  (29 shorter events, 7.3 us)
Async XLA Ops:
  0.0 6.7 %copy-start.4 = (bf16[384,1280]{1,0:T(8,128)(2,1)S(1)}, bf16[384,1280]{1,0:T(8,128)(2,1)}, u32[]{:S(2)}) copy-start(bf16[384,1280]{1,0:T(8,128)(2,1)} %param.4) | copy-start | bytes 2949124
  2.0 9.8 %collective-permute-start.2 = (bf16[128,1280]{0,1:T(8,128)(2,1)}, bf16[128,1280]{0,1:T(8,128)(2,1)}, u32[]{:S(2)}, u32[]{:S(2)}) collective-permute-start(bf16[128,1280]{0,1:T(8,128)(2,1)} %copy.21), channel_id=1, source_target_pairs={{0,4},{2,6},{4,0},{6,2},{8,12},{10,14},{12,8},{14,10},{16,20},{18,... | collective-permute-start | bytes 983048 | tf_op jit(solution)/shard_map/ppermute | solution.py:13
  4.0 20.6 %collective-permute-start = (bf16[128,1280]{0,1:T(8,128)(2,1)}, bf16[128,1280]{0,1:T(8,128)(2,1)}, u32[]{:S(2)}, u32[]{:S(2)}) collective-permute-start(bf16[128,1280]{0,1:T(8,128)(2,1)} %copy.21), channel_id=1, source_target_pairs={{0,2},{2,0},{4,6},{6,4},{8,10},{10,8},{12,14},{14,12},{16,18},{18,... | collective-permute-start | bytes 983048 | tf_op jit(solution)/shard_map/ppermute | solution.py:13
  5.2 22.1 %collective-permute-start.1 = (bf16[128,1280]{1,0:T(8,128)(2,1)}, bf16[128,1280]{1,0:T(8,128)(2,1)}, u32[]{:S(2)}, u32[]{:S(2)}) collective-permute-start(bf16[128,1280]{1,0:T(8,128)(2,1)} %param.6), channel_id=1, source_target_pairs={{0,2},{2,0},{4,6},{6,4},{8,10},{10,8},{12,14},{14,12},{16,18},{18,... | collective-permute-start | bytes 983048 | tf_op jit(solution)/shard_map/ppermute | solution.py:13
  10.6 2.8 %copy-start.3 = (bf16[128,1280]{1,0:T(8,128)(2,1)S(1)}, bf16[128,1280]{1,0:T(8,128)(2,1)}, u32[]{:S(2)}) copy-start(bf16[128,1280]{1,0:T(8,128)(2,1)} %param.6) | copy-start | bytes 983044
  11.7 10.1 %collective-permute-start.4 = (bf16[128,1280]{0,1:T(8,128)(2,1)}, bf16[128,1280]{0,1:T(8,128)(2,1)}, u32[]{:S(2)}, u32[]{:S(2)}) collective-permute-start(bf16[128,1280]{0,1:T(8,128)(2,1)} %collective-permute-done.2), channel_id=1, source_target_pairs={{0,8},{2,10},{4,28},{6,30},{8,16},{10,18},{12,4},{14,6},{16,24},{1... | collective-permute-start | bytes 983048 | tf_op jit(solution)/shard_map/ppermute | solution.py:24
  14.3 14.9 %collective-permute-start.3 = (bf16[128,1280]{0,1:T(8,128)(2,1)}, bf16[128,1280]{0,1:T(8,128)(2,1)S(1)}, u32[]{:S(2)}, u32[]{:S(2)}) collective-permute-start(bf16[128,1280]{0,1:T(8,128)(2,1)} %copy.35), channel_id=1, source_target_pairs={{0,4},{2,6},{4,0},{6,2},{8,12},{10,14},{12,8},{14,10},{16,20},{18,... | collective-permute-start | bytes 983048 | tf_op jit(solution)/shard_map/ppermute | solution.py:13
  23.6 7.5 %collective-permute-start.6 = (bf16[128,1280]{0,1:T(8,128)(2,1)}, bf16[128,1280]{0,1:T(8,128)(2,1)}, u32[]{:S(2)}, u32[]{:S(2)}) collective-permute-start(bf16[128,1280]{0,1:T(8,128)(2,1)} %broadcast_select_fusion.1), channel_id=1, source_target_pairs={{0,2},{2,0},{4,6},{6,4},{8,10},{10,8},{12,14},{14,12},{16,18},{18,... | collective-permute-start | bytes 983048 | tf_op jit(solution)/shard_map/ppermute | solution.py:13
  29.2 8.5 %collective-permute-start.5 = (bf16[128,1280]{0,1:T(8,128)(2,1)S(1)}, bf16[128,1280]{0,1:T(8,128)(2,1)S(1)}, u32[]{:S(2)}, u32[]{:S(2)}) collective-permute-start(bf16[128,1280]{0,1:T(8,128)(2,1)S(1)} %collective-permute-done.3), channel_id=1, source_target_pairs={{0,8},{2,10},{4,28},{6,30},{8,16},{10,18},{12,4},{14,6},{16,24},{1... | collective-permute-start | bytes 983048 | tf_op jit(solution)/shard_map/ppermute | solution.py:24
  31.1 7.4 %copy-start = (f32[10,128,384]{2,1,0:T(8,128)S(1)}, f32[10,128,384]{2,1,0:T(8,128)}, u32[]{:S(2)}) copy-start(f32[10,128,384]{2,1,0:T(8,128)} %get-tuple-element.26) | copy-start | bytes 5898244
  31.1 7.4 %copy-start.2 = (bf16[128,1280]{0,1:T(8,128)(2,1)S(1)}, bf16[128,1280]{0,1:T(8,128)(2,1)}, u32[]{:S(2)}) copy-start(bf16[128,1280]{0,1:T(8,128)(2,1)} %copy.30) | copy-start | bytes 983044
  37.7 6.0 %collective-permute-start.7 = (bf16[128,1280]{0,1:T(8,128)(2,1)S(1)}, bf16[128,1280]{0,1:T(8,128)(2,1)S(1)}, u32[]{:S(2)}, u32[]{:S(2)}) collective-permute-start(bf16[128,1280]{0,1:T(8,128)(2,1)S(1)} %broadcast_select_fusion), channel_id=1, source_target_pairs={{0,2},{2,0},{4,6},{6,4},{8,10},{10,8},{12,14},{14,12},{16,18},{18,... | collective-permute-start | bytes 983048 | tf_op jit(solution)/shard_map/ppermute | solution.py:13
  43.7 1.5 %copy-start.1 = (f32[10,384,128]{1,2,0:T(8,128)S(1)}, f32[10,384,128]{1,2,0:T(8,128)}, u32[]{:S(2)}) copy-start(f32[10,384,128]{1,2,0:T(8,128)} %fusion.38) | copy-start | bytes 5898244
  53.3 10.2 %collective-permute-start.8 = (bf16[384,2560]{1,0:T(8,128)(2,1)}, bf16[384,2560]{1,0:T(8,128)(2,1)S(1)}, u32[]{:S(2)}, u32[]{:S(2)}) collective-permute-start(bf16[384,2560]{1,0:T(8,128)(2,1)} %fusion.7), channel_id=1, source_target_pairs={{0,1},{1,0},{2,3},{3,2},{4,5},{5,4},{6,7},{7,6},{8,9},{9,8},{10,11... | collective-permute-start | bytes 5898248 | tf_op jit(solution)/shard_map/ppermute | solution.py:94

commit v7 on v3

v7 whole, which is shorter than its diff:
```python
import math

import jax
import jax.numpy as jnp
from jax import lax
from jax.experimental import pallas as pl
from jax.experimental.pallas import tpu as pltpu
from jax.sharding import PartitionSpec as P

HS = 128


def swap_within_four(value, bit):
    count = lax.axis_size("blk")
    return lax.ppermute(value, "blk", [(source, source ^ bit) for source in range(count)])


def shift_groups(value):
    count = lax.axis_size("blk")
    groups = count // 4
    pairs = []
    for source in range(count):
        group, position = divmod(source, 4)
        step = 1 if position < 2 else -1
        pairs.append((source, ((group + step) % groups) * 4 + position))
    return lax.ppermute(value, "blk", pairs)


def relay_blocks(own):
    position = lax.axis_index("blk") % 4
    from_x = swap_within_four(own, 1)
    from_y = swap_within_four(own, 2)
    from_z = shift_groups(from_y)
    forward = jnp.where((position == 0) | (position == 3), from_y, from_z)
    from_last = swap_within_four(forward, 1)
    return [from_x, from_y, from_z, from_last]


def window_kernel(*refs):
    blocks = (len(refs) - 2) // 2
    q_ref = refs[0]
    key_refs = refs[1:1 + blocks]
    value_refs = refs[1 + blocks:1 + 2 * blocks]
    out_ref = refs[-1]
    head_count = q_ref.shape[1] // HS
    scale = 1.0 / math.sqrt(HS)
    for head in range(head_count):
        cols = pl.ds(head * HS, HS)
        query = q_ref[:, cols]
        scores = [
            lax.dot_general(query, k[:, cols], (((1,), (1,)), ((), ())),
                            preferred_element_type=jnp.float32) * scale
            for k in key_refs
        ]
        row_max = scores[0].max(axis=1, keepdims=True)
        for s in scores[1:]:
            row_max = jnp.maximum(row_max, s.max(axis=1, keepdims=True))
        total = None
        numerator = None
        for s, v in zip(scores, value_refs):
            weights = jnp.exp(s - row_max)
            part_sum = weights.sum(axis=1, keepdims=True)
            total = part_sum if total is None else total + part_sum
            product = jnp.dot(weights.astype(jnp.bfloat16), v[:, cols],
                              preferred_element_type=jnp.float32)
            numerator = product if numerator is None else numerator + product
        out_ref[:, cols] = (numerator / total).astype(out_ref.dtype)


def attend_window(queries, key_blocks, value_blocks):
    rows, width = queries.shape
    blocks = len(key_blocks)
    kv = key_blocks[0].shape[0]
    flops = 4 * rows * kv * blocks * width
    return pl.pallas_call(
        window_kernel,
        out_shape=jax.ShapeDtypeStruct((rows, width), jnp.bfloat16),
        in_specs=[pl.BlockSpec(memory_space=pltpu.VMEM)] * (1 + 2 * blocks),
        out_specs=pl.BlockSpec(memory_space=pltpu.VMEM),
        cost_estimate=pl.CostEstimate(
            flops=flops,
            transcendentals=rows * kv * blocks * (width // HS),
            bytes_accessed=2 * (2 * rows * width + 2 * blocks * kv * width),
        ),
    )(queries, *key_blocks, *value_blocks)


def on_device(queries, keys, values, out_weight):
    key_blocks = [keys] + relay_blocks(keys)
    value_blocks = [values] + relay_blocks(values)
    attended = attend_window(queries, key_blocks, value_blocks)
    groups = lax.axis_size("mp")
    me = lax.axis_index("mp")
    width = out_weight.shape[1] // groups

    def partial_for(owner):
        cols = lax.dynamic_slice_in_dim(out_weight, owner * width, width, axis=1)
        return jnp.dot(attended, cols, preferred_element_type=jnp.float32).astype(jnp.bfloat16)

    received = []
    for offset in range(1, groups):
        sent = partial_for((me + offset) % groups)
        pairs = [(source, (source + offset) % groups) for source in range(groups)]
        received.append(lax.ppermute(sent, "mp", pairs))
    summed = lax.optimization_barrier(partial_for(me)).astype(jnp.float32)
    for part in received:
        summed = summed + part.astype(jnp.float32)
    return summed.astype(jnp.bfloat16)


def solution(mesh):
    placed = (P("blk", "mp"), P("blk", "mp"), P("blk", "mp"), P("mp", None))
    return jax.shard_map(
        on_device, mesh=mesh, in_specs=placed, out_specs=P("blk", "mp"), check_vma=False
    )
```

time: 58.6 us -> 68.6 us (1.17)
  waiting for transfers between devices: 12.4 us -> 30.3 us
  Pallas kernels: 0 us -> 9.57 us
  matrix products: 21.5 us -> 12.8 us
  local copies, waits for them, and re-layouts: 7.98 us -> 0.75 us
  other arithmetic: 4.66 us -> 1.81 us
  starting transfers between devices: 11.1 us -> 11.9 us
    ppermute x6, waiting for transfers between devices: 8.13 us -> 22.8 us  [swap_within_four(): lax.ppermute(value, 'blk', [(source, source ^ bit) for source in range(co...]
    dot_general x10 -> x0, matrix products: 11.6 us -> none  [the longest x5 6.28 us: fold_block(): jnp.einsum('qhd,khd->qhk', query_heads, key_heads, preferred_element_type...]
    pallas_call x0 -> x1, Pallas kernels: none -> 9.57 us  [attend_window(): pl.pallas_call(window_kernel, out_shape=jax.ShapeDtypeStruct((rows, width...]
    unnamed x19 -> x18, local copies, waits for them, and re-layouts: 6.1 us -> 0.75 us
    ppermute x2, waiting for transfers between devices: 4.32 us -> 7.48 us  [shift_groups(): return lax.ppermute(value, 'blk', pairs)]
    dot_general x2, matrix products: 9.86 us -> 12.8 us  [partial_for(): jnp.dot(attended, cols, preferred_element_type=jnp.float32)]
    ppermute x1 -> x0, local copies, waits for them, and re-layouts: 1.89 us -> none  [swap_within_four(): lax.ppermute(value, 'blk', [(source, source ^ bit) for source in range(co...]
    reduce_sum x3 -> x0, other arithmetic: 1.8 us -> none  [fold_block(): new_sum = running_sum * rescale + jnp.sum(weights, axis=-1)]
  transfers between devices with their start and end apart: 9 -> 9, of which waited for: 3 -> 6; matrix products, arithmetic and copies ran while one was open for 39% -> 8% of each run, Pallas kernels for 0% -> 0%
where the time goes in v7:
time: 68.6 us; the launch traced here: 67.2 us
  waiting for transfers between devices  30.3 us (44%)
  matrix products  12.8 us (19%)
  starting transfers between devices  11.9 us (17%)
  Pallas kernels  9.57 us (14%)
  other arithmetic  1.81 us (3%)
  local copies, waits for them, and re-layouts  0.75 us (1%)
    ppermute x6, waiting for transfers between devices, swap_within_four(): lax.ppermute(value, 'blk', [(source, source ^ bit) for source in range(co...  22.8 us
    dot_general x2, matrix products, partial_for(): jnp.dot(attended, cols, preferred_element_type=jnp.float32)  12.8 us
    pallas_call x1, Pallas kernels, attend_window(): pl.pallas_call(window_kernel, out_shape=jax.ShapeDtypeStruct((rows, width...  9.57 us
    ppermute x2, waiting for transfers between devices, shift_groups(): return lax.ppermute(value, 'blk', pairs)  7.48 us
    ppermute x6, starting transfers between devices, swap_within_four(): lax.ppermute(value, 'blk', [(source, source ^ bit) for source in range(co...  5.66 us
    ppermute x1, starting transfers between devices, on_device(): received.append(lax.ppermute(sent, 'mp', pairs))  3.8 us
    ppermute x2, starting transfers between devices, shift_groups(): return lax.ppermute(value, 'blk', pairs)  2.48 us
    convert_element_type x1, other arithmetic, on_device(): return summed.astype(jnp.bfloat16)  1.74 us
  transfers between devices with their start and end apart: 9, of which 6 were waited for; matrix products, arithmetic and copies ran while one was open for 8% of the time, Pallas kernels for 0%

profile of v7, /device:TPU:1, one launch (start us, length us, event | category | flops | bytes accessed | tf_op | source)
XLA Modules:
  0.0 67.2 jit_solution(15164934199892010886)
XLA Ops:
  0.0 2.1 %collective-permute-start.5 = (bf16[128,1280]{1,0:T(8,128)(2,1)}, bf16[128,1280]{1,0:T(8,128)(2,1)S(1)}, u32[]{:S(2)}, u32[]{:S(2)}) collective-permute-start(bf16[128,1280]{1,0:T(8,128)(2,1)} %refs_6_.1), channel_id=1, source_target_pairs={{0,4},{2,6},{4,0},{6,2},{8,12},{10,14},{12,8},{14,10},{16,20},{18,... | collective-permute-start | bytes 983048 | tf_op jit(solution)/shard_map/ppermute | solution.py:15
  2.1 0.0 collective-permute-start.1
  2.1 7.6 %collective-permute-done.5.refs_8_ = bf16[128,1280]{1,0:T(8,128)(2,1)S(1)} collective-permute-done((bf16[128,1280]{1,0:T(8,128)(2,1)}, bf16[128,1280]{1,0:T(8,128)(2,1)S(1)}, u32[]{:S(2)}, u32[]{:S(2)}) %collective-permute-start.5) | collective-permute-done | bytes 327712 | tf_op jit(solution)/shard_map/ppermute | solution.py:15
  9.7 1.2 %collective-permute-start.6 = (bf16[128,1280]{1,0:T(8,128)(2,1)S(1)}, bf16[128,1280]{1,0:T(8,128)(2,1)S(1)}, u32[]{:S(2)}, u32[]{:S(2)}) collective-permute-start(bf16[128,1280]{1,0:T(8,128)(2,1)S(1)} %collective-permute-done.5.refs_8_), channel_id=1, source_target_pairs={{0,8},{2,10},{4,28},{6,30},{8,16},{10,18},{12,4},{14,6},{16,24},{1... | collective-permute-start | bytes 983048 | tf_op jit(solution)/shard_map/ppermute | solution.py:26
  10.9 1.2 %collective-permute-start = (bf16[128,1280]{1,0:T(8,128)(2,1)}, bf16[128,1280]{1,0:T(8,128)(2,1)S(1)}, u32[]{:S(2)}, u32[]{:S(2)}) collective-permute-start(bf16[128,1280]{1,0:T(8,128)(2,1)} %refs_1_.1), channel_id=1, source_target_pairs={{0,2},{2,0},{4,6},{6,4},{8,10},{10,8},{12,14},{14,12},{16,18},{18,... | collective-permute-start | bytes 983048 | tf_op jit(solution)/shard_map/ppermute | solution.py:15
  12.1 0.3 collective-permute-start.4
  12.4 4.3 %collective-permute-done.1.refs_3_ = bf16[128,1280]{1,0:T(8,128)(2,1)S(1)} collective-permute-done((bf16[128,1280]{1,0:T(8,128)(2,1)}, bf16[128,1280]{1,0:T(8,128)(2,1)S(1)}, u32[]{:S(2)}, u32[]{:S(2)}) %collective-permute-start.1) | collective-permute-done | bytes 327712 | tf_op jit(solution)/shard_map/ppermute | solution.py:15
  16.7 1.2 %collective-permute-start.2 = (bf16[128,1280]{1,0:T(8,128)(2,1)S(1)}, bf16[128,1280]{1,0:T(8,128)(2,1)S(1)}, u32[]{:S(2)}, u32[]{:S(2)}) collective-permute-start(bf16[128,1280]{1,0:T(8,128)(2,1)S(1)} %collective-permute-done.1.refs_3_), channel_id=1, source_target_pairs={{0,8},{2,10},{4,28},{6,30},{8,16},{10,18},{12,4},{14,6},{16,24},{1... | collective-permute-start | bytes 983048 | tf_op jit(solution)/shard_map/ppermute | solution.py:26
  17.9 0.4 collective-permute-done.6.refs_9_
  18.4 1.1 %collective-permute-start.7 = (bf16[128,1280]{1,0:T(8,128)(2,1)S(1)}, bf16[128,1280]{1,0:T(8,128)(2,1)S(1)}, u32[]{:S(2)}, u32[]{:S(2)}) collective-permute-start(bf16[128,1280]{1,0:T(8,128)(2,1)S(1)} %broadcast_select_fusion), channel_id=1, source_target_pairs={{0,2},{2,0},{4,6},{6,4},{8,10},{10,8},{12,14},{14,12},{16,18},{18,... | collective-permute-start | bytes 983048 | tf_op jit(solution)/shard_map/ppermute | solution.py:15
  19.5 7.1 %collective-permute-done.2.refs_4_ = bf16[128,1280]{1,0:T(8,128)(2,1)S(1)} collective-permute-done((bf16[128,1280]{1,0:T(8,128)(2,1)S(1)}, bf16[128,1280]{1,0:T(8,128)(2,1)S(1)}, u32[]{:S(2)}, u32[]{:S(2)}) %collective-permute-start.2) | collective-permute-done | bytes 327712 | tf_op jit(solution)/shard_map/ppermute | solution.py:26
  26.6 1.1 %collective-permute-start.3 = (bf16[128,1280]{1,0:T(8,128)(2,1)S(1)}, bf16[128,1280]{1,0:T(8,128)(2,1)S(1)}, u32[]{:S(2)}, u32[]{:S(2)}) collective-permute-start(bf16[128,1280]{1,0:T(8,128)(2,1)S(1)} %broadcast_select_fusion.1), channel_id=1, source_target_pairs={{0,2},{2,0},{4,6},{6,4},{8,10},{10,8},{12,14},{14,12},{16,18},{18,... | collective-permute-start | bytes 983048 | tf_op jit(solution)/shard_map/ppermute | solution.py:15
  27.6 0.0 collective-permute-done.refs_2_
  27.6 0.0 collective-permute-done.4.refs_7_
  27.6 3.9 %collective-permute-done.7.refs_10_ = bf16[128,1280]{1,0:T(8,128)(2,1)S(1)} collective-permute-done((bf16[128,1280]{1,0:T(8,128)(2,1)S(1)}, bf16[128,1280]{1,0:T(8,128)(2,1)S(1)}, u32[]{:S(2)}, u32[]{:S(2)}) %collective-permute-start.7) | collective-permute-done | bytes 327712 | tf_op jit(solution)/shard_map/ppermute | solution.py:15
  31.5 7.0 %collective-permute-done.3.refs_5_ = bf16[128,1280]{1,0:T(8,128)(2,1)S(1)} collective-permute-done((bf16[128,1280]{1,0:T(8,128)(2,1)S(1)}, bf16[128,1280]{1,0:T(8,128)(2,1)S(1)}, u32[]{:S(2)}, u32[]{:S(2)}) %collective-permute-start.3) | collective-permute-done | bytes 327712 | tf_op jit(solution)/shard_map/ppermute | solution.py:15
  38.5 0.0 copy-done.2
  38.6 0.7 %copy-done.8 = bf16[128,1280]{1,0:T(8,128)(2,1)} copy-done((bf16[128,1280]{1,0:T(8,128)(2,1)}, bf16[128,1280]{1,0:T(8,128)(2,1)S(1)}, u32[]{:S(2)}) %copy-start.8) | copy-done | bytes 327704
  39.3 9.6 %shard_map.46 = bf16[384,1280]{1,0:T(8,128)(2,1)} custom-call(bf16[384,1280]{1,0:T(8,128)(2,1)} %refs_0_.1, bf16[128,1280]{1,0:T(8,128)(2,1)} %refs_1_.1, bf16[128,1280]{1,0:T(8,128)(2,1)} %copy-done.5, bf16[128,1280]{1,0:T(8,128)(2,1)} %copy-done.1, bf16[128,1280]{1,0:T(8,128)(2,1)} %copy-done.3, bf16[128,1280]{1,0:T(8,128)(2,1)} %copy-done.8, ...), custom_call_target="tpu_custom_call" | custom-call | flops 1258291200 | bytes 5242880 | tf_op jit(solution)/shard_map/pallas_call | solution.py:75
  48.9 7.2 %fusion.7 = bf16[384,2560]{1,0:T(8,128)(2,1)} fusion(bf16[384,1280]{1,0:T(8,128)(2,1)} %shard_map.46, bf16[1280,5120]{1,0:T(8,128)(2,1)} %param.7, s32[]{:T(128)S(6)} %select_n.37), kind=kOutput, calls=%fused_computation.5 | convolution fusion | flops 2517565440 | bytes 9502724 | tf_op jit(solution)/shard_map/dot_general | solution.py:98
  56.1 3.8 %collective-permute-start.8 = (bf16[384,2560]{1,0:T(8,128)(2,1)}, bf16[384,2560]{1,0:T(8,128)(2,1)S(1)}, u32[]{:S(2)}, u32[]{:S(2)}) collective-permute-start(bf16[384,2560]{1,0:T(8,128)(2,1)} %fusion.7), channel_id=1, source_target_pairs={{0,1},{1,0},{2,3},{3,2},{4,5},{5,4},{6,7},{7,6},{8,9},{9,8},{10,11... | collective-permute-start | bytes 5898248 | tf_op jit(solution)/shard_map/ppermute | solution.py:104
  59.9 5.6 %fusion.4 = bf16[384,2560]{1,0:T(8,128)(2,1)S(1)} fusion(bf16[384,1280]{1,0:T(8,128)(2,1)S(1)} %copy-done.4, bf16[1280,5120]{1,0:T(8,128)(2,1)} %param.7, s32[]{:T(128)S(6)} %select_n.35), kind=kOutput, calls=%fused_computation.4 | convolution fusion | flops 2517565440 | bytes 9502724 | tf_op jit(solution)/shard_map/dot_general | solution.py:98
  65.5 0.0 collective-permute-done.8
  65.5 1.7 %add_convert_fusion = bf16[384,2560]{1,0:T(8,128)(2,1)} fusion(bf16[384,2560]{1,0:T(8,128)(2,1)S(1)} %collective-permute-done.8, bf16[384,2560]{1,0:T(8,128)(2,1)S(1)} %fusion.4), kind=kLoop, calls=%fused_computation.6 | loop fusion | flops 3932160 | bytes 5898240 | tf_op jit(solution)/shard_map/convert_element_type | solution.py:108
  (18 shorter events, 0.1 us)
Async XLA Ops:
  0.0 9.7 %collective-permute-start.5 = (bf16[128,1280]{1,0:T(8,128)(2,1)}, bf16[128,1280]{1,0:T(8,128)(2,1)S(1)}, u32[]{:S(2)}, u32[]{:S(2)}) collective-permute-start(bf16[128,1280]{1,0:T(8,128)(2,1)} %refs_6_.1), channel_id=1, source_target_pairs={{0,4},{2,6},{4,0},{6,2},{8,12},{10,14},{12,8},{14,10},{16,20},{18,... | collective-permute-start | bytes 983048 | tf_op jit(solution)/shard_map/ppermute | solution.py:15
  2.1 14.6 %collective-permute-start.1 = (bf16[128,1280]{1,0:T(8,128)(2,1)}, bf16[128,1280]{1,0:T(8,128)(2,1)S(1)}, u32[]{:S(2)}, u32[]{:S(2)}) collective-permute-start(bf16[128,1280]{1,0:T(8,128)(2,1)} %refs_1_.1), channel_id=1, source_target_pairs={{0,4},{2,6},{4,0},{6,2},{8,12},{10,14},{12,8},{14,10},{16,20},{18,... | collective-permute-start | bytes 983048 | tf_op jit(solution)/shard_map/ppermute | solution.py:15
  9.7 28.9 %copy-start = (bf16[128,1280]{1,0:T(8,128)(2,1)}, bf16[128,1280]{1,0:T(8,128)(2,1)S(1)}, u32[]{:S(2)}) copy-start(bf16[128,1280]{1,0:T(8,128)(2,1)S(1)} %collective-permute-done.5.refs_8_) | copy-start | bytes 983044
  9.7 8.7 %collective-permute-start.6 = (bf16[128,1280]{1,0:T(8,128)(2,1)S(1)}, bf16[128,1280]{1,0:T(8,128)(2,1)S(1)}, u32[]{:S(2)}, u32[]{:S(2)}) collective-permute-start(bf16[128,1280]{1,0:T(8,128)(2,1)S(1)} %collective-permute-done.5.refs_8_), channel_id=1, source_target_pairs={{0,8},{2,10},{4,28},{6,30},{8,16},{10,18},{12,4},{14,6},{16,24},{1... | collective-permute-start | bytes 983048 | tf_op jit(solution)/shard_map/ppermute | solution.py:26
  10.9 16.7 %collective-permute-start = (bf16[128,1280]{1,0:T(8,128)(2,1)}, bf16[128,1280]{1,0:T(8,128)(2,1)S(1)}, u32[]{:S(2)}, u32[]{:S(2)}) collective-permute-start(bf16[128,1280]{1,0:T(8,128)(2,1)} %refs_1_.1), channel_id=1, source_target_pairs={{0,2},{2,0},{4,6},{6,4},{8,10},{10,8},{12,14},{14,12},{16,18},{18,... | collective-permute-start | bytes 983048 | tf_op jit(solution)/shard_map/ppermute | solution.py:15
  12.1 15.5 %collective-permute-start.4 = (bf16[128,1280]{1,0:T(8,128)(2,1)}, bf16[128,1280]{1,0:T(8,128)(2,1)S(1)}, u32[]{:S(2)}, u32[]{:S(2)}) collective-permute-start(bf16[128,1280]{1,0:T(8,128)(2,1)} %refs_6_.1), channel_id=1, source_target_pairs={{0,2},{2,0},{4,6},{6,4},{8,10},{10,8},{12,14},{14,12},{16,18},{18,... | collective-permute-start | bytes 983048 | tf_op jit(solution)/shard_map/ppermute | solution.py:15
  16.7 21.8 %copy-start.1 = (bf16[128,1280]{1,0:T(8,128)(2,1)}, bf16[128,1280]{1,0:T(8,128)(2,1)S(1)}, u32[]{:S(2)}) copy-start(bf16[128,1280]{1,0:T(8,128)(2,1)S(1)} %collective-permute-done.1.refs_3_) | copy-start | bytes 983044
  16.7 9.8 %collective-permute-start.2 = (bf16[128,1280]{1,0:T(8,128)(2,1)S(1)}, bf16[128,1280]{1,0:T(8,128)(2,1)S(1)}, u32[]{:S(2)}, u32[]{:S(2)}) collective-permute-start(bf16[128,1280]{1,0:T(8,128)(2,1)S(1)} %collective-permute-done.1.refs_3_), channel_id=1, source_target_pairs={{0,8},{2,10},{4,28},{6,30},{8,16},{10,18},{12,4},{14,6},{16,24},{1... | collective-permute-start | bytes 983048 | tf_op jit(solution)/shard_map/ppermute | solution.py:26
  18.4 20.2 %copy-start.2 = (bf16[128,1280]{1,0:T(8,128)(2,1)}, bf16[128,1280]{1,0:T(8,128)(2,1)S(1)}, u32[]{:S(2)}) copy-start(bf16[128,1280]{1,0:T(8,128)(2,1)S(1)} %collective-permute-done.6.refs_9_) | copy-start | bytes 983044
  18.4 13.1 %collective-permute-start.7 = (bf16[128,1280]{1,0:T(8,128)(2,1)S(1)}, bf16[128,1280]{1,0:T(8,128)(2,1)S(1)}, u32[]{:S(2)}, u32[]{:S(2)}) collective-permute-start(bf16[128,1280]{1,0:T(8,128)(2,1)S(1)} %broadcast_select_fusion), channel_id=1, source_target_pairs={{0,2},{2,0},{4,6},{6,4},{8,10},{10,8},{12,14},{14,12},{16,18},{18,... | collective-permute-start | bytes 983048 | tf_op jit(solution)/shard_map/ppermute | solution.py:15
  26.5 12.0 %copy-start.3 = (bf16[128,1280]{1,0:T(8,128)(2,1)}, bf16[128,1280]{1,0:T(8,128)(2,1)S(1)}, u32[]{:S(2)}) copy-start(bf16[128,1280]{1,0:T(8,128)(2,1)S(1)} %collective-permute-done.2.refs_4_) | copy-start | bytes 983044
  26.6 12.0 %collective-permute-start.3 = (bf16[128,1280]{1,0:T(8,128)(2,1)S(1)}, bf16[128,1280]{1,0:T(8,128)(2,1)S(1)}, u32[]{:S(2)}, u32[]{:S(2)}) collective-permute-start(bf16[128,1280]{1,0:T(8,128)(2,1)S(1)} %broadcast_select_fusion.1), channel_id=1, source_target_pairs={{0,2},{2,0},{4,6},{6,4},{8,10},{10,8},{12,14},{14,12},{16,18},{18,... | collective-permute-start | bytes 983048 | tf_op jit(solution)/shard_map/ppermute | solution.py:15
  27.6 10.9 %copy-start.5 = (bf16[128,1280]{1,0:T(8,128)(2,1)}, bf16[128,1280]{1,0:T(8,128)(2,1)S(1)}, u32[]{:S(2)}) copy-start(bf16[128,1280]{1,0:T(8,128)(2,1)S(1)} %collective-permute-done.refs_2_) | copy-start | bytes 983044
  27.6 10.9 %copy-start.6 = (bf16[128,1280]{1,0:T(8,128)(2,1)}, bf16[128,1280]{1,0:T(8,128)(2,1)S(1)}, u32[]{:S(2)}) copy-start(bf16[128,1280]{1,0:T(8,128)(2,1)S(1)} %collective-permute-done.4.refs_7_) | copy-start | bytes 983044
  31.5 7.1 %copy-start.7 = (bf16[128,1280]{1,0:T(8,128)(2,1)}, bf16[128,1280]{1,0:T(8,128)(2,1)S(1)}, u32[]{:S(2)}) copy-start(bf16[128,1280]{1,0:T(8,128)(2,1)S(1)} %collective-permute-done.7.refs_10_) | copy-start | bytes 983044
  38.6 0.7 %copy-start.8 = (bf16[128,1280]{1,0:T(8,128)(2,1)}, bf16[128,1280]{1,0:T(8,128)(2,1)S(1)}, u32[]{:S(2)}) copy-start(bf16[128,1280]{1,0:T(8,128)(2,1)S(1)} %collective-permute-done.3.refs_5_) | copy-start | bytes 983044
  48.9 11.0 %copy-start.4 = (bf16[384,1280]{1,0:T(8,128)(2,1)S(1)}, bf16[384,1280]{1,0:T(8,128)(2,1)}, u32[]{:S(2)}) copy-start(bf16[384,1280]{1,0:T(8,128)(2,1)} %shard_map.46) | copy-start | bytes 2949124
  56.1 9.4 %collective-permute-start.8 = (bf16[384,2560]{1,0:T(8,128)(2,1)}, bf16[384,2560]{1,0:T(8,128)(2,1)S(1)}, u32[]{:S(2)}, u32[]{:S(2)}) collective-permute-start(bf16[384,2560]{1,0:T(8,128)(2,1)} %fusion.7), channel_id=1, source_target_pairs={{0,1},{1,0},{2,3},{3,2},{4,5},{5,4},{6,7},{7,6},{8,9},{9,8},{10,11... | collective-permute-start | bytes 5898248 | tf_op jit(solution)/shard_map/ppermute | solution.py:104

commit v8 on v3

--- a/solution.py
+++ b/solution.py
@@ -79,18 +79,18 @@
     me = lax.axis_index("mp")
     width = out_weight.shape[1] // groups
 
-    def partial_for(owner):
-        cols = lax.dynamic_slice_in_dim(out_weight, owner * width, width, axis=1)
-        return jnp.dot(attended, cols, preferred_element_type=jnp.float32).astype(jnp.bfloat16)
+    def columns_of(weight, owner):
+        return lax.dynamic_slice_in_dim(weight, owner * width, width, axis=1)
 
-    received = []
+    def project(rows, weight_cols):
+        return jnp.dot(rows, weight_cols, preferred_element_type=jnp.float32).astype(jnp.bfloat16)
+
+    summed = lax.optimization_barrier(project(attended, columns_of(out_weight, me))).astype(jnp.float32)
     for offset in range(1, groups):
-        sent = partial_for((me + offset) % groups)
         pairs = [(source, (source + offset) % groups) for source in range(groups)]
-        received.append(lax.ppermute(sent, "mp", pairs))
-    summed = lax.optimization_barrier(partial_for(me)).astype(jnp.float32)
-    for part in received:
-        summed = summed + part.astype(jnp.float32)
+        weight_cols = lax.ppermute(columns_of(out_weight, (me + offset) % groups), "mp", pairs)
+        rows = lax.ppermute(attended, "mp", pairs)
+        summed = summed + project(rows, weight_cols).astype(jnp.float32)
     return summed.astype(jnp.bfloat16)
 
 

time: 58.6 us -> 67.3 us (1.15)
  local copies, waits for them, and re-layouts: 7.98 us -> 13.2 us
  matrix products: 21.5 us -> 24 us
  other arithmetic: 4.66 us -> 2.9 us
  starting transfers between devices: 11.1 us -> 12.6 us
  waiting for transfers between devices: 12.4 us -> 13.8 us
    dynamic_slice x0 -> x1, local copies, waits for them, and re-layouts: none -> 6.1 us  [columns_of(): return lax.dynamic_slice_in_dim(weight, owner * width, width, axis=1)]
    ppermute x2, waiting for transfers between devices: 4.32 us -> 9.06 us  [shift_groups(): return lax.ppermute(value, 'blk', pairs)]
    ppermute x6, waiting for transfers between devices: 8.13 us -> 4.77 us  [swap_within_four(): lax.ppermute(value, 'blk', [(source, source ^ bit) for source in range(co...]
    dot_general x2, matrix products: 9.86 us -> 12.5 us  [project(): jnp.dot(rows, weight_cols, preferred_element_type=jnp.float32)]
    convert_element_type x1 -> x0, other arithmetic: 1.74 us -> none  [on_device(): return summed.astype(jnp.bfloat16)]
    dot_general x5, matrix products: 6.28 us -> 5.27 us  [fold_block(): jnp.einsum('qhd,khd->qhk', query_heads, key_heads, preferred_element_type...]
    dot_general x5, matrix products: 5.31 us -> 6.2 us  [fold_block(): jnp.einsum('qhk,khd->qhd', weights.astype(jnp.bfloat16), value_heads, pre...]
    unnamed x19 -> x9, local copies, waits for them, and re-layouts: 6.1 us -> 5.28 us
  transfers between devices with their start and end apart: 9 -> 10, of which waited for: 3 -> 3; matrix products, arithmetic and copies ran while one was open for 39% -> 46% of each run, Pallas kernels for 0% -> 0%
where the time goes in v8:
time: 67.3 us; the launch traced here: 66.7 us
  matrix products  24 us (36%)
  waiting for transfers between devices  13.8 us (21%)
  local copies, waits for them, and re-layouts  13.2 us (20%)
  starting transfers between devices  12.6 us (19%)
  other arithmetic  2.9 us (4%)
    dot_general x2, matrix products, project(): jnp.dot(rows, weight_cols, preferred_element_type=jnp.float32)  12.5 us
    ppermute x2, waiting for transfers between devices, shift_groups(): return lax.ppermute(value, 'blk', pairs)  9.06 us
    ppermute x6, starting transfers between devices, swap_within_four(): lax.ppermute(value, 'blk', [(source, source ^ bit) for source in range(co...  6.76 us
    dot_general x5, matrix products, fold_block(): jnp.einsum('qhk,khd->qhd', weights.astype(jnp.bfloat16), value_heads, pre...  6.2 us
    dynamic_slice x1, local copies, waits for them, and re-layouts, columns_of(): return lax.dynamic_slice_in_dim(weight, owner * width, width, axis=1)  6.1 us
    unnamed x9, local copies, waits for them, and re-layouts  5.28 us
    dot_general x5, matrix products, fold_block(): jnp.einsum('qhd,khd->qhk', query_heads, key_heads, preferred_element_type...  5.27 us
    ppermute x6, waiting for transfers between devices, swap_within_four(): lax.ppermute(value, 'blk', [(source, source ^ bit) for source in range(co...  4.77 us
  transfers between devices with their start and end apart: 10, of which 3 were waited for; matrix products, arithmetic and copies ran while one was open for 46% of the time, Pallas kernels for 0%

profile of v8, /device:TPU:1, one launch (start us, length us, event | category | flops | bytes accessed | tf_op | source)
XLA Modules:
  0.0 66.7 jit_solution(16278578023552814118)
XLA Ops:
  0.0 1.2 %copy.21 = bf16[128,1280]{0,1:T(8,128)(2,1)S(1)} copy(bf16[128,1280]{1,0:T(8,128)(2,1)} %param.5) | data formatting | bytes 655360 | tf_op args[1]
  1.2 2.1 %collective-permute-start.2 = (bf16[128,1280]{0,1:T(8,128)(2,1)S(1)}, bf16[128,1280]{0,1:T(8,128)(2,1)}, u32[]{:S(2)}, u32[]{:S(2)}) collective-permute-start(bf16[128,1280]{0,1:T(8,128)(2,1)S(1)} %copy.21), channel_id=1, source_target_pairs={{0,4},{2,6},{4,0},{6,2},{8,12},{10,14},{12,8},{14,10},{16,20},{18,... | collective-permute-start | bytes 983048 | tf_op jit(solution)/shard_map/ppermute | solution.py:13
  3.3 1.2 %collective-permute-start = (bf16[128,1280]{0,1:T(8,128)(2,1)S(1)}, bf16[128,1280]{0,1:T(8,128)(2,1)}, u32[]{:S(2)}, u32[]{:S(2)}) collective-permute-start(bf16[128,1280]{0,1:T(8,128)(2,1)S(1)} %copy.21), channel_id=1, source_target_pairs={{0,2},{2,0},{4,6},{6,4},{8,10},{10,8},{12,14},{14,12},{16,18},{18,... | collective-permute-start | bytes 983048 | tf_op jit(solution)/shard_map/ppermute | solution.py:13
  4.8 1.9 %copy.25 = bf16[128,1280]{0,1:T(8,128)(2,1)} copy(bf16[128,1280]{1,0:T(8,128)(2,1)} %param.6) | data formatting | bytes 655360 | tf_op args[2]
  6.7 6.1 %constant_dynamic-slice_fusion = bf16[1280,2560]{1,0:T(8,128)(2,1)} fusion(bf16[1280,5120]{1,0:T(8,128)(2,1)} %param.7, s32[]{:T(128)S(6)} %select_n.37), kind=kLoop, calls=%fused_computation.65 | loop fusion | bytes 13107204 | tf_op jit(solution)/shard_map/dynamic_slice | solution.py:83
  12.8 1.5 %collective-permute-start.9 = (bf16[1280,2560]{1,0:T(8,128)(2,1)}, bf16[1280,2560]{1,0:T(8,128)(2,1)}, u32[]{:S(2)}, u32[]{:S(2)}) collective-permute-start(bf16[1280,2560]{1,0:T(8,128)(2,1)} %constant_dynamic-slice_fusion), channel_id=1, source_target_pairs={{0,1},{1,0},{2,3},{3,2},{4,5},{5,4},{6,7},{7,6},{8,9},{9,8},{10,11... | collective-permute-start | bytes 19660808 | tf_op jit(solution)/shard_map/ppermute | solution.py:91
  15.5 2.7 %fusion.36 = f32[10,384,128]{1,2,0:T(8,128)} fusion(bf16[128,10,128]{0,2,1:T(8,128)(2,1)} %bitcast.3, f32[10,128,384]{2,1,0:T(8,128)S(1)} %get-tuple-element.22, f32[384,10]{0,1:T(8,128)S(1)} %get-tuple-element.21), kind=kOutput, calls=%fused_computation.46 | convolution fusion | flops 127303680 | bytes 4275200 | tf_op jit(solution)/shard_map/qhk,khd->qhd/dot_general | solution.py:48
  18.6 1.8 %collective-permute-start.4 = (bf16[128,1280]{0,1:T(8,128)(2,1)}, bf16[128,1280]{0,1:T(8,128)(2,1)}, u32[]{:S(2)}, u32[]{:S(2)}) collective-permute-start(bf16[128,1280]{0,1:T(8,128)(2,1)} %collective-permute-done.2), channel_id=1, source_target_pairs={{0,8},{2,10},{4,28},{6,30},{8,16},{10,18},{12,4},{14,6},{16,24},{1... | collective-permute-start | bytes 983048 | tf_op jit(solution)/shard_map/ppermute | solution.py:24
  20.4 1.4 %bitcast_reduce_fusion.3 = (f32[384,10]{0,1:T(8,128)S(1)}, f32[10,128,384]{2,1,0:T(8,128)S(1)}) fusion(bf16[128,10,128]{0,2,1:T(8,128)(2,1)} %bitcast.5, bf16[384,10,128]{0,2,1:T(8,128)(2,1)S(1)} %bitcast.111), kind=kOutput, calls=%fused_computation.26 | convolution fusion | flops 126808320 | bytes 3292160 | tf_op jit(solution)/shard_map/qhd,khd->qhk/dot_general | solution.py:42
  21.8 1.5 %collective-permute-start.5 = (bf16[128,1280]{0,1:T(8,128)(2,1)S(1)}, bf16[128,1280]{0,1:T(8,128)(2,1)}, u32[]{:S(2)}, u32[]{:S(2)}) collective-permute-start(bf16[128,1280]{0,1:T(8,128)(2,1)S(1)} %collective-permute-done.3), channel_id=1, source_target_pairs={{0,8},{2,10},{4,28},{6,30},{8,16},{10,18},{12,4},{14,6},{16,24},{1... | collective-permute-start | bytes 983048 | tf_op jit(solution)/shard_map/ppermute | solution.py:24
  23.4 1.9 %copy.30 = bf16[128,1280]{0,1:T(8,128)(2,1)} copy(bf16[128,1280]{1,0:T(8,128)(2,1)} %collective-permute-done.1) | data formatting | bytes 655360 | tf_op jit(solution)/shard_map/ppermute | solution.py:13
  25.2 1.4 %bitcast_reduce_fusion.2 = (f32[384,10]{0,1:T(8,128)S(1)}, f32[10,128,384]{2,1,0:T(8,128)S(1)}) fusion(bf16[128,10,128]{0,2,1:T(8,128)(2,1)} %bitcast.9, bf16[384,10,128]{0,2,1:T(8,128)(2,1)S(1)} %bitcast.112), kind=kOutput, calls=%fused_computation.21 | convolution fusion | flops 126808320 | bytes 3292160 | tf_op jit(solution)/shard_map/qhd,khd->qhk/dot_general | solution.py:42
  26.7 4.1 %collective-permute-done.4 = bf16[128,1280]{0,1:T(8,128)(2,1)} collective-permute-done((bf16[128,1280]{0,1:T(8,128)(2,1)}, bf16[128,1280]{0,1:T(8,128)(2,1)}, u32[]{:S(2)}, u32[]{:S(2)}) %collective-permute-start.4) | collective-permute-done | bytes 327712 | tf_op jit(solution)/shard_map/ppermute | solution.py:24
  30.8 1.0 %broadcast_select_fusion.1 = bf16[128,1280]{0,1:T(8,128)(2,1)S(1)} fusion(bf16[128,1280]{0,1:T(8,128)(2,1)} %collective-permute-done.2, bf16[128,1280]{0,1:T(8,128)(2,1)} %collective-permute-done.4, pred[]{:T(512)S(6)} %or.4), kind=kLoop, calls=%fused_computation.58 | loop fusion | flops 163840 | bytes 983041 | tf_op jit(solution)/shard_map/jit(_where)/select_n | solution.py:32
  31.8 1.1 %collective-permute-start.6 = (bf16[128,1280]{0,1:T(8,128)(2,1)S(1)}, bf16[128,1280]{0,1:T(8,128)(2,1)S(1)}, u32[]{:S(2)}, u32[]{:S(2)}) collective-permute-start(bf16[128,1280]{0,1:T(8,128)(2,1)S(1)} %broadcast_select_fusion.1), channel_id=1, source_target_pairs={{0,2},{2,0},{4,6},{6,4},{8,10},{10,8},{12,14},{14,12},{16,18},{18,... | collective-permute-start | bytes 983048 | tf_op jit(solution)/shard_map/ppermute | solution.py:13
  32.9 4.9 %collective-permute-done.5 = bf16[128,1280]{0,1:T(8,128)(2,1)} collective-permute-done((bf16[128,1280]{0,1:T(8,128)(2,1)S(1)}, bf16[128,1280]{0,1:T(8,128)(2,1)}, u32[]{:S(2)}, u32[]{:S(2)}) %collective-permute-start.5) | collective-permute-done | bytes 327712 | tf_op jit(solution)/shard_map/ppermute | solution.py:24
  37.8 2.0 %collective-permute-start.7 = (bf16[128,1280]{0,1:T(8,128)(2,1)S(1)}, bf16[128,1280]{0,1:T(8,128)(2,1)S(1)}, u32[]{:S(2)}, u32[]{:S(2)}) collective-permute-start(bf16[128,1280]{0,1:T(8,128)(2,1)S(1)} %broadcast_select_fusion), channel_id=1, source_target_pairs={{0,2},{2,0},{4,6},{6,4},{8,10},{10,8},{12,14},{14,12},{16,18},{18,... | collective-permute-start | bytes 983048 | tf_op jit(solution)/shard_map/ppermute | solution.py:13
  39.9 1.4 %bitcast_reduce_fusion.1 = (f32[384,10]{0,1:T(8,128)S(1)}, f32[10,128,384]{2,1,0:T(8,128)S(1)}) fusion(bf16[128,10,128]{0,2,1:T(8,128)(2,1)} %bitcast.13, bf16[384,10,128]{0,2,1:T(8,128)(2,1)S(1)} %bitcast.113), kind=kOutput, calls=%fused_computation.16 | convolution fusion | flops 126808320 | bytes 3292160 | tf_op jit(solution)/shard_map/qhd,khd->qhk/dot_general | solution.py:42
  43.3 4.8 %collective-permute-done.7 = bf16[128,1280]{0,1:T(8,128)(2,1)S(1)} collective-permute-done((bf16[128,1280]{0,1:T(8,128)(2,1)S(1)}, bf16[128,1280]{0,1:T(8,128)(2,1)S(1)}, u32[]{:S(2)}, u32[]{:S(2)}) %collective-permute-start.7) | collective-permute-done | bytes 327712 | tf_op jit(solution)/shard_map/ppermute | solution.py:13
  50.0 1.1 %copy-done = f32[10,384,128]{1,2,0:T(8,128)S(1)} copy-done((f32[10,384,128]{1,2,0:T(8,128)S(1)}, f32[10,384,128]{1,2,0:T(8,128)}, u32[]{:S(2)}) %copy-start) | copy-done | bytes 1966104
  51.1 2.1 %fusion.9 = bf16[384,10,128]{0,2,1:T(8,128)(2,1)S(1)} fusion(f32[10,128,384]{2,1,0:T(8,128)S(1)} %fusion.29, f32[10,384,128]{1,2,0:T(8,128)S(1)} %fusion.32, f32[10,384,128]{1,2,0:T(8,128)S(1)} %fusion.34, f32[10,384,128]{1,2,0:T(8,128)S(1)} %copy-done, bf16[128,10,128]{0,2,1:T(8,128)(2,1)} %bitcast.15, f32[10,128,384]{2,1,0:T(8,128)S(1)} %get-tuple-element.18, ...), kind=kOutput, calls=%fused_computation.9 | convolution fusion | flops 132710400 | bytes 11248640 | tf_op jit(solution)/shard_map/qhk,khd->qhd/dot_general | solution.py:48
  53.2 1.0 %collective-permute-start.8 = (bf16[384,1280]{0,1:T(8,128)(2,1)S(1)}, bf16[384,1280]{0,1:T(8,128)(2,1)S(1)}, u32[]{:S(2)}, u32[]{:S(2)}) collective-permute-start(bf16[384,1280]{0,1:T(8,128)(2,1)S(1)} %bitcast.120), channel_id=1, source_target_pairs={{0,1},{1,0},{2,3},{3,2},{4,5},{5,4},{6,7},{7,6},{8,9},{9,8},{10,11... | collective-permute-start | bytes 2949128 | tf_op jit(solution)/shard_map/ppermute | solution.py:92
  54.2 5.6 %fusion.2 = bf16[384,2560]{1,0:T(8,128)(2,1)S(1)} fusion(bf16[384,1280]{0,1:T(8,128)(2,1)S(1)} %bitcast.121, bf16[1280,5120]{1,0:T(8,128)(2,1)} %param.7, s32[]{:T(128)S(6)} %select_n.35), kind=kOutput, calls=%fused_computation.2 | convolution fusion | flops 2517565440 | bytes 9502724 | tf_op jit(solution)/shard_map/dot_general | solution.py:86
  59.8 6.9 %fusion.7 = bf16[384,2560]{1,0:T(8,128)(2,1)} fusion(bf16[384,1280]{0,1:T(8,128)(2,1)S(1)} %collective-permute-done.8, bf16[1280,2560]{1,0:T(8,128)(2,1)} %collective-permute-done.9, bf16[384,2560]{1,0:T(8,128)(2,1)S(1)} %fusion.2), kind=kOutput, calls=%fused_computation.6 | convolution fusion | flops 2521497600 | bytes 11468800 | tf_op jit(solution)/shard_map/dot_general | solution.py:86
  (26 shorter events, 5.7 us)
Async XLA Ops:
  1.2 17.4 %collective-permute-start.2 = (bf16[128,1280]{0,1:T(8,128)(2,1)S(1)}, bf16[128,1280]{0,1:T(8,128)(2,1)}, u32[]{:S(2)}, u32[]{:S(2)}) collective-permute-start(bf16[128,1280]{0,1:T(8,128)(2,1)S(1)} %copy.21), channel_id=1, source_target_pairs={{0,4},{2,6},{4,0},{6,2},{8,12},{10,14},{12,8},{14,10},{16,20},{18,... | collective-permute-start | bytes 983048 | tf_op jit(solution)/shard_map/ppermute | solution.py:13
  3.3 17.1 %collective-permute-start = (bf16[128,1280]{0,1:T(8,128)(2,1)S(1)}, bf16[128,1280]{0,1:T(8,128)(2,1)}, u32[]{:S(2)}, u32[]{:S(2)}) collective-permute-start(bf16[128,1280]{0,1:T(8,128)(2,1)S(1)} %copy.21), channel_id=1, source_target_pairs={{0,2},{2,0},{4,6},{6,4},{8,10},{10,8},{12,14},{14,12},{16,18},{18,... | collective-permute-start | bytes 983048 | tf_op jit(solution)/shard_map/ppermute | solution.py:13
  4.5 18.8 %collective-permute-start.1 = (bf16[128,1280]{1,0:T(8,128)(2,1)}, bf16[128,1280]{1,0:T(8,128)(2,1)}, u32[]{:S(2)}, u32[]{:S(2)}) collective-permute-start(bf16[128,1280]{1,0:T(8,128)(2,1)} %param.6), channel_id=1, source_target_pairs={{0,2},{2,0},{4,6},{6,4},{8,10},{10,8},{12,14},{14,12},{16,18},{18,... | collective-permute-start | bytes 983048 | tf_op jit(solution)/shard_map/ppermute | solution.py:13
  6.7 15.2 %collective-permute-start.3 = (bf16[128,1280]{0,1:T(8,128)(2,1)}, bf16[128,1280]{0,1:T(8,128)(2,1)S(1)}, u32[]{:S(2)}, u32[]{:S(2)}) collective-permute-start(bf16[128,1280]{0,1:T(8,128)(2,1)} %copy.25), channel_id=1, source_target_pairs={{0,4},{2,6},{4,0},{6,2},{8,12},{10,14},{12,8},{14,10},{16,20},{18,... | collective-permute-start | bytes 983048 | tf_op jit(solution)/shard_map/ppermute | solution.py:13
  6.7 7.6 %copy-start.2 = (bf16[384,1280]{1,0:T(8,128)(2,1)S(1)}, bf16[384,1280]{1,0:T(8,128)(2,1)}, u32[]{:S(2)}) copy-start(bf16[384,1280]{1,0:T(8,128)(2,1)} %param.4) | copy-start | bytes 2949124
  12.8 46.9 %collective-permute-start.9 = (bf16[1280,2560]{1,0:T(8,128)(2,1)}, bf16[1280,2560]{1,0:T(8,128)(2,1)}, u32[]{:S(2)}, u32[]{:S(2)}) collective-permute-start(bf16[1280,2560]{1,0:T(8,128)(2,1)} %constant_dynamic-slice_fusion), channel_id=1, source_target_pairs={{0,1},{1,0},{2,3},{3,2},{4,5},{5,4},{6,7},{7,6},{8,9},{9,8},{10,11... | collective-permute-start | bytes 19660808 | tf_op jit(solution)/shard_map/ppermute | solution.py:91
  18.6 12.2 %collective-permute-start.4 = (bf16[128,1280]{0,1:T(8,128)(2,1)}, bf16[128,1280]{0,1:T(8,128)(2,1)}, u32[]{:S(2)}, u32[]{:S(2)}) collective-permute-start(bf16[128,1280]{0,1:T(8,128)(2,1)} %collective-permute-done.2), channel_id=1, source_target_pairs={{0,8},{2,10},{4,28},{6,30},{8,16},{10,18},{12,4},{14,6},{16,24},{1... | collective-permute-start | bytes 983048 | tf_op jit(solution)/shard_map/ppermute | solution.py:24
  21.8 16.0 %collective-permute-start.5 = (bf16[128,1280]{0,1:T(8,128)(2,1)S(1)}, bf16[128,1280]{0,1:T(8,128)(2,1)}, u32[]{:S(2)}, u32[]{:S(2)}) collective-permute-start(bf16[128,1280]{0,1:T(8,128)(2,1)S(1)} %collective-permute-done.3), channel_id=1, source_target_pairs={{0,8},{2,10},{4,28},{6,30},{8,16},{10,18},{12,4},{14,6},{16,24},{1... | collective-permute-start | bytes 983048 | tf_op jit(solution)/shard_map/ppermute | solution.py:24
  31.8 9.5 %collective-permute-start.6 = (bf16[128,1280]{0,1:T(8,128)(2,1)S(1)}, bf16[128,1280]{0,1:T(8,128)(2,1)S(1)}, u32[]{:S(2)}, u32[]{:S(2)}) collective-permute-start(bf16[128,1280]{0,1:T(8,128)(2,1)S(1)} %broadcast_select_fusion.1), channel_id=1, source_target_pairs={{0,2},{2,0},{4,6},{6,4},{8,10},{10,8},{12,14},{14,12},{16,18},{18,... | collective-permute-start | bytes 983048 | tf_op jit(solution)/shard_map/ppermute | solution.py:13
  37.8 10.3 %collective-permute-start.7 = (bf16[128,1280]{0,1:T(8,128)(2,1)S(1)}, bf16[128,1280]{0,1:T(8,128)(2,1)S(1)}, u32[]{:S(2)}, u32[]{:S(2)}) collective-permute-start(bf16[128,1280]{0,1:T(8,128)(2,1)S(1)} %broadcast_select_fusion), channel_id=1, source_target_pairs={{0,2},{2,0},{4,6},{6,4},{8,10},{10,8},{12,14},{14,12},{16,18},{18,... | collective-permute-start | bytes 983048 | tf_op jit(solution)/shard_map/ppermute | solution.py:13
  48.6 1.0 %copy-start.1 = (bf16[128,1280]{0,1:T(8,128)(2,1)S(1)}, bf16[128,1280]{0,1:T(8,128)(2,1)}, u32[]{:S(2)}) copy-start(bf16[128,1280]{0,1:T(8,128)(2,1)} %copy.30) | copy-start | bytes 983044
  49.5 1.5 %copy-start = (f32[10,384,128]{1,2,0:T(8,128)S(1)}, f32[10,384,128]{1,2,0:T(8,128)}, u32[]{:S(2)}) copy-start(f32[10,384,128]{1,2,0:T(8,128)} %fusion.36) | copy-start | bytes 5898244
  53.2 6.6 %collective-permute-start.8 = (bf16[384,1280]{0,1:T(8,128)(2,1)S(1)}, bf16[384,1280]{0,1:T(8,128)(2,1)S(1)}, u32[]{:S(2)}, u32[]{:S(2)}) collective-permute-start(bf16[384,1280]{0,1:T(8,128)(2,1)S(1)} %bitcast.120), channel_id=1, source_target_pairs={{0,1},{1,0},{2,3},{3,2},{4,5},{5,4},{6,7},{7,6},{8,9},{9,8},{10,11... | collective-permute-start | bytes 2949128 | tf_op jit(solution)/shard_map/ppermute | solution.py:92

commit v9 on v3

--- a/solution.py
+++ b/solution.py
@@ -3,6 +3,7 @@
 import jax
 import jax.numpy as jnp
 from jax import lax
+from jax.experimental.layout import Layout, with_layout_constraint
 from jax.sharding import PartitionSpec as P
 
 HS = 128
@@ -64,6 +65,8 @@
         jnp.zeros((row_count, head_count), jnp.float32),
         jnp.zeros((row_count, head_count, HS), jnp.float32),
     )
+    keys = with_layout_constraint(keys, Layout(major_to_minor=(1, 0)))
+    values = with_layout_constraint(values, Layout(major_to_minor=(1, 0)))
     key_arrivals = relay_blocks(keys)
     value_arrivals = relay_blocks(values)
     state = fold_block(state, keys, values, query_heads)

time: 58.6 us -> 55.6 us (0.949)
  the two profiles are of different devices: /device:TPU:1 before, /device:TPU:7 now
where the time goes in v9:
time: 55.6 us; the launch traced here: 55.1 us
  matrix products  19.8 us (36%)
  waiting for transfers between devices  12.9 us (23%)
  starting transfers between devices  12.5 us (22%)
  local copies, waits for them, and re-layouts  4.98 us (9%)
  other arithmetic  4.65 us (8%)
    dot_general x2, matrix products, partial_for(): jnp.dot(attended, cols, preferred_element_type=jnp.float32)  9.54 us
    ppermute x6, waiting for transfers between devices, swap_within_four(): lax.ppermute(value, 'blk', [(source, source ^ bit) for source in range(co...  9.44 us
    ppermute x2, starting transfers between devices, shift_groups(): return lax.ppermute(value, 'blk', pairs)  6.64 us
    dot_general x5, matrix products, fold_block(): jnp.einsum('qhd,khd->qhk', query_heads, key_heads, preferred_element_type...  5.31 us
    dot_general x5, matrix products, fold_block(): jnp.einsum('qhk,khd->qhd', weights.astype(jnp.bfloat16), value_heads, pre...  5 us
    unnamed x13, local copies, waits for them, and re-layouts  4.98 us
    ppermute x2, waiting for transfers between devices, shift_groups(): return lax.ppermute(value, 'blk', pairs)  3.5 us
    ppermute x6, starting transfers between devices, swap_within_four(): lax.ppermute(value, 'blk', [(source, source ^ bit) for source in range(co...  3.32 us
  transfers between devices with their start and end apart: 9, of which 5 were waited for; matrix products, arithmetic and copies ran while one was open for 34% of the time, Pallas kernels for 0%

profile of v9, /device:TPU:7, one launch (start us, length us, event | category | flops | bytes accessed | tf_op | source)
XLA Modules:
  0.0 55.1 jit_solution(14510397328018025953)
XLA Ops:
  0.0 2.0 %copy.21 = bf16[128,1280]{0,1:T(8,128)(2,1)} copy(bf16[128,1280]{1,0:T(8,128)(2,1)} %param.5) | data formatting | bytes 655360 | tf_op args[1]
  2.2 1.9 %copy.24 = bf16[128,1280]{0,1:T(8,128)(2,1)} copy(bf16[128,1280]{1,0:T(8,128)(2,1)} %param.6) | data formatting | bytes 655360 | tf_op args[2]
  4.1 1.4 %collective-permute-start.1 = (bf16[128,1280]{0,1:T(8,128)(2,1)}, bf16[128,1280]{0,1:T(8,128)(2,1)}, u32[]{:S(2)}, u32[]{:S(2)}) collective-permute-start(bf16[128,1280]{0,1:T(8,128)(2,1)} %copy.24), channel_id=1, source_target_pairs={{0,2},{2,0},{4,6},{6,4},{8,10},{10,8},{12,14},{14,12},{16,18},{18,... | collective-permute-start | bytes 983048 | tf_op jit(solution)/shard_map/ppermute | solution.py:14
  5.5 1.2 %collective-permute-start.3 = (bf16[128,1280]{0,1:T(8,128)(2,1)}, bf16[128,1280]{0,1:T(8,128)(2,1)S(1)}, u32[]{:S(2)}, u32[]{:S(2)}) collective-permute-start(bf16[128,1280]{0,1:T(8,128)(2,1)} %copy.24), channel_id=1, source_target_pairs={{0,4},{2,6},{4,0},{6,2},{8,12},{10,14},{12,8},{14,10},{16,20},{18,... | collective-permute-start | bytes 983048 | tf_op jit(solution)/shard_map/ppermute | solution.py:14
  6.8 0.6 %copy.22 = bf16[384,1280]{0,1:T(8,128)(2,1)S(1)} copy(bf16[384,1280]{1,0:T(8,128)(2,1)S(1)} %copy-done) | data formatting | bytes 1966080 | tf_op args[0]
  7.4 1.4 %bitcast_reduce_fusion.4 = (f32[384,10]{0,1:T(8,128)S(1)}, f32[10,128,384]{2,1,0:T(8,128)S(1)}) fusion(bf16[128,10,128]{0,2,1:T(8,128)(2,1)} %bitcast, bf16[384,10,128]{0,2,1:T(8,128)(2,1)S(1)} %bitcast.109), kind=kOutput, calls=%fused_computation.31 | convolution fusion | flops 126808320 | bytes 3292160 | tf_op jit(solution)/shard_map/qhd,khd->qhk/dot_general | solution.py:43
  8.9 1.4 %fusion.38 = f32[10,384,128]{1,2,0:T(8,128)S(1)} fusion(bf16[128,10,128]{0,2,1:T(8,128)(2,1)} %bitcast.3, f32[10,128,384]{2,1,0:T(8,128)S(1)} %get-tuple-element.22, f32[384,10]{0,1:T(8,128)S(1)} %get-tuple-element.21), kind=kOutput, calls=%fused_computation.46 | convolution fusion | flops 127303680 | bytes 4275200 | tf_op jit(solution)/shard_map/qhk,khd->qhd/dot_general | solution.py:49
  10.9 3.3 %collective-permute-start.4 = (bf16[128,1280]{0,1:T(8,128)(2,1)}, bf16[128,1280]{0,1:T(8,128)(2,1)S(1)}, u32[]{:S(2)}, u32[]{:S(2)}) collective-permute-start(bf16[128,1280]{0,1:T(8,128)(2,1)} %collective-permute-done.2), channel_id=1, source_target_pairs={{0,8},{2,10},{4,28},{6,30},{8,16},{10,18},{12,4},{14,6},{16,24},{1... | collective-permute-start | bytes 983048 | tf_op jit(solution)/shard_map/ppermute | solution.py:25
  14.2 1.5 %bitcast_reduce_fusion.2 = (f32[384,10]{0,1:T(8,128)S(1)}, f32[10,128,384]{2,1,0:T(8,128)S(1)}) fusion(bf16[128,10,128]{0,2,1:T(8,128)(2,1)} %bitcast.9, bf16[384,10,128]{0,2,1:T(8,128)(2,1)S(1)} %bitcast.110), kind=kOutput, calls=%fused_computation.21 | convolution fusion | flops 126808320 | bytes 3292160 | tf_op jit(solution)/shard_map/qhd,khd->qhk/dot_general | solution.py:43
  15.7 2.2 %collective-permute-done.3 = bf16[128,1280]{0,1:T(8,128)(2,1)S(1)} collective-permute-done((bf16[128,1280]{0,1:T(8,128)(2,1)}, bf16[128,1280]{0,1:T(8,128)(2,1)S(1)}, u32[]{:S(2)}, u32[]{:S(2)}) %collective-permute-start.3) | collective-permute-done | bytes 327712 | tf_op jit(solution)/shard_map/ppermute | solution.py:14
  17.9 3.3 %collective-permute-start.5 = (bf16[128,1280]{0,1:T(8,128)(2,1)S(1)}, bf16[128,1280]{0,1:T(8,128)(2,1)S(1)}, u32[]{:S(2)}, u32[]{:S(2)}) collective-permute-start(bf16[128,1280]{0,1:T(8,128)(2,1)S(1)} %collective-permute-done.3), channel_id=1, source_target_pairs={{0,8},{2,10},{4,28},{6,30},{8,16},{10,18},{12,4},{14,6},{16,24},{1... | collective-permute-start | bytes 983048 | tf_op jit(solution)/shard_map/ppermute | solution.py:25
  21.2 1.4 %bitcast_reduce_fusion.3 = (f32[384,10]{0,1:T(8,128)S(1)}, f32[10,128,384]{2,1,0:T(8,128)S(1)}) fusion(bf16[128,10,128]{0,2,1:T(8,128)(2,1)} %bitcast.5, bf16[384,10,128]{0,2,1:T(8,128)(2,1)S(1)} %bitcast.111), kind=kOutput, calls=%fused_computation.26 | convolution fusion | flops 126808320 | bytes 3292160 | tf_op jit(solution)/shard_map/qhd,khd->qhk/dot_general | solution.py:43
  22.7 1.0 %broadcast_select_fusion.1 = bf16[128,1280]{0,1:T(8,128)(2,1)S(1)} fusion(bf16[128,1280]{0,1:T(8,128)(2,1)} %collective-permute-done.2, bf16[128,1280]{0,1:T(8,128)(2,1)S(1)} %collective-permute-done.4, pred[]{:T(512)S(6)} %or.4), kind=kLoop, calls=%fused_computation.58 | loop fusion | flops 163840 | bytes 983041 | tf_op jit(solution)/shard_map/jit(_where)/select_n | solution.py:33
  23.8 3.5 %collective-permute-done.5 = bf16[128,1280]{0,1:T(8,128)(2,1)S(1)} collective-permute-done((bf16[128,1280]{0,1:T(8,128)(2,1)S(1)}, bf16[128,1280]{0,1:T(8,128)(2,1)S(1)}, u32[]{:S(2)}, u32[]{:S(2)}) %collective-permute-start.5) | collective-permute-done | bytes 327712 | tf_op jit(solution)/shard_map/ppermute | solution.py:25
  28.1 3.2 %collective-permute-done.6 = bf16[128,1280]{0,1:T(8,128)(2,1)S(1)} collective-permute-done((bf16[128,1280]{0,1:T(8,128)(2,1)S(1)}, bf16[128,1280]{0,1:T(8,128)(2,1)S(1)}, u32[]{:S(2)}, u32[]{:S(2)}) %collective-permute-start.6) | collective-permute-done | bytes 327712 | tf_op jit(solution)/shard_map/ppermute | solution.py:14
  31.8 1.4 %fusion.36 = f32[10,384,128]{1,2,0:T(8,128)S(1)} fusion(bf16[128,10,128]{0,2,1:T(8,128)(2,1)} %bitcast.7, f32[10,128,384]{2,1,0:T(8,128)S(1)} %get-tuple-element.24, f32[384,10]{0,1:T(8,128)S(1)} %get-tuple-element.13), kind=kOutput, calls=%fused_computation.45 | convolution fusion | flops 127303680 | bytes 4275200 | tf_op jit(solution)/shard_map/qhk,khd->qhd/dot_general | solution.py:49
  33.3 0.7 %fusion.23 = (f32[384,10]{0,1:T(8,128)S(1)}, f32[384,10]{0,1:T(8,128)S(1)}) fusion(f32[10,128,384]{2,1,0:T(8,128)S(1)} %get-tuple-element.24, f32[384,10]{0,1:T(8,128)S(1)} %get-tuple-element.13, f32[384,10]{0,1:T(8,128)S(1)} %get-tuple-element.12, f32[10,128,384]{2,1,0:T(8,128)S(1)} %get-tuple-element.20), kind=kLoop, calls=%fused_computation.35 | loop fusion | flops 2941440 | bytes 3993600 | tf_op jit(solution)/shard_map/reduce_sum | solution.py:48
  34.5 3.8 %collective-permute-done.7 = bf16[128,1280]{0,1:T(8,128)(2,1)S(1)} collective-permute-done((bf16[128,1280]{0,1:T(8,128)(2,1)S(1)}, bf16[128,1280]{0,1:T(8,128)(2,1)S(1)}, u32[]{:S(2)}, u32[]{:S(2)}) %collective-permute-start.7) | collective-permute-done | bytes 327712 | tf_op jit(solution)/shard_map/ppermute | solution.py:14
  38.9 0.7 %fusion.27 = (f32[384,10]{0,1:T(8,128)S(1)}, f32[384,10]{0,1:T(8,128)S(1)}) fusion(f32[10,128,384]{2,1,0:T(8,128)S(1)} %get-tuple-element.18, f32[384,10]{0,1:T(8,128)S(1)} %get-tuple-element.11, f32[384,10]{0,1:T(8,128)S(1)} %get-tuple-element.10, f32[10,128,384]{2,1,0:T(8,128)S(1)} %get-tuple-element.16), kind=kLoop, calls=%fused_computation.39 | loop fusion | flops 2941440 | bytes 3993600 | tf_op jit(solution)/shard_map/reduce_sum | solution.py:48
  39.6 1.2 %fusion.11 = bf16[384,10,128]{0,2,1:T(8,128)(2,1)S(1)} fusion(f32[10,128,384]{2,1,0:T(8,128)S(1)} %fusion.31, f32[10,384,128]{1,2,0:T(8,128)S(1)} %fusion.34, f32[10,384,128]{1,2,0:T(8,128)S(1)} %fusion.36, f32[10,384,128]{1,2,0:T(8,128)S(1)} %fusion.38, bf16[128,10,128]{0,2,1:T(8,128)(2,1)S(1)} %bitcast.117, f32[10,128,384]{2,1,0:T(8,128)S(1)} %get-tuple-element.18, ...), kind=kOutput, calls=%fused_computation.9 | convolution fusion | flops 132710400 | bytes 11248640 | tf_op jit(solution)/shard_map/qhk,khd->qhd/dot_general | solution.py:49
  41.3 3.9 %fusion.7 = bf16[384,2560]{1,0:T(8,128)(2,1)} fusion(bf16[384,1280]{0,1:T(8,128)(2,1)S(1)} %bitcast.121, bf16[1280,5120]{1,0:T(8,128)(2,1)S(1)} %bitcast.120, s32[]{:T(128)S(6)} %select_n.37), kind=kOutput, calls=%fused_computation.5 | convolution fusion | flops 2517565440 | bytes 9502724 | tf_op jit(solution)/shard_map/dot_general | solution.py:87
  45.3 2.5 %collective-permute-start.8 = (bf16[384,2560]{1,0:T(8,128)(2,1)}, bf16[384,2560]{1,0:T(8,128)(2,1)S(1)}, u32[]{:S(2)}, u32[]{:S(2)}) collective-permute-start(bf16[384,2560]{1,0:T(8,128)(2,1)} %fusion.7), channel_id=1, source_target_pairs={{0,1},{1,0},{2,3},{3,2},{4,5},{5,4},{6,7},{7,6},{8,9},{9,8},{10,11... | collective-permute-start | bytes 5898248 | tf_op jit(solution)/shard_map/ppermute | solution.py:93
  47.8 5.6 %fusion.4 = bf16[384,2560]{1,0:T(8,128)(2,1)S(1)} fusion(bf16[384,1280]{0,1:T(8,128)(2,1)S(1)} %bitcast.122, bf16[1280,5120]{1,0:T(8,128)(2,1)} %param.7, s32[]{:T(128)S(6)} %select_n.35), kind=kOutput, calls=%fused_computation.4 | convolution fusion | flops 2517565440 | bytes 9502724 | tf_op jit(solution)/shard_map/dot_general | solution.py:87
  53.4 1.7 %add_convert_fusion = bf16[384,2560]{1,0:T(8,128)(2,1)} fusion(bf16[384,2560]{1,0:T(8,128)(2,1)S(1)} %collective-permute-done.8, bf16[384,2560]{1,0:T(8,128)(2,1)S(1)} %fusion.4), kind=kLoop, calls=%fused_computation.6 | loop fusion | flops 3932160 | bytes 5898240 | tf_op jit(solution)/shard_map/convert_element_type | solution.py:97
  (28 shorter events, 3.7 us)
Async XLA Ops:
  0.0 6.8 %copy-start = (bf16[384,1280]{1,0:T(8,128)(2,1)S(1)}, bf16[384,1280]{1,0:T(8,128)(2,1)}, u32[]{:S(2)}) copy-start(bf16[384,1280]{1,0:T(8,128)(2,1)} %param.4) | copy-start | bytes 2949124
  2.0 8.9 %collective-permute-start.2 = (bf16[128,1280]{0,1:T(8,128)(2,1)}, bf16[128,1280]{0,1:T(8,128)(2,1)}, u32[]{:S(2)}, u32[]{:S(2)}) collective-permute-start(bf16[128,1280]{0,1:T(8,128)(2,1)} %copy.21), channel_id=1, source_target_pairs={{0,4},{2,6},{4,0},{6,2},{8,12},{10,14},{12,8},{14,10},{16,20},{18,... | collective-permute-start | bytes 983048 | tf_op jit(solution)/shard_map/ppermute | solution.py:14
  2.2 19.0 %collective-permute-start = (bf16[128,1280]{0,1:T(8,128)(2,1)}, bf16[128,1280]{0,1:T(8,128)(2,1)}, u32[]{:S(2)}, u32[]{:S(2)}) collective-permute-start(bf16[128,1280]{0,1:T(8,128)(2,1)} %copy.21), channel_id=1, source_target_pairs={{0,2},{2,0},{4,6},{6,4},{8,10},{10,8},{12,14},{14,12},{16,18},{18,... | collective-permute-start | bytes 983048 | tf_op jit(solution)/shard_map/ppermute | solution.py:14
  4.1 27.8 %collective-permute-start.1 = (bf16[128,1280]{0,1:T(8,128)(2,1)}, bf16[128,1280]{0,1:T(8,128)(2,1)}, u32[]{:S(2)}, u32[]{:S(2)}) collective-permute-start(bf16[128,1280]{0,1:T(8,128)(2,1)} %copy.24), channel_id=1, source_target_pairs={{0,2},{2,0},{4,6},{6,4},{8,10},{10,8},{12,14},{14,12},{16,18},{18,... | collective-permute-start | bytes 983048 | tf_op jit(solution)/shard_map/ppermute | solution.py:14
  5.5 12.4 %collective-permute-start.3 = (bf16[128,1280]{0,1:T(8,128)(2,1)}, bf16[128,1280]{0,1:T(8,128)(2,1)S(1)}, u32[]{:S(2)}, u32[]{:S(2)}) collective-permute-start(bf16[128,1280]{0,1:T(8,128)(2,1)} %copy.24), channel_id=1, source_target_pairs={{0,4},{2,6},{4,0},{6,2},{8,12},{10,14},{12,8},{14,10},{16,20},{18,... | collective-permute-start | bytes 983048 | tf_op jit(solution)/shard_map/ppermute | solution.py:14
  10.9 11.8 %collective-permute-start.4 = (bf16[128,1280]{0,1:T(8,128)(2,1)}, bf16[128,1280]{0,1:T(8,128)(2,1)S(1)}, u32[]{:S(2)}, u32[]{:S(2)}) collective-permute-start(bf16[128,1280]{0,1:T(8,128)(2,1)} %collective-permute-done.2), channel_id=1, source_target_pairs={{0,8},{2,10},{4,28},{6,30},{8,16},{10,18},{12,4},{14,6},{16,24},{1... | collective-permute-start | bytes 983048 | tf_op jit(solution)/shard_map/ppermute | solution.py:25
  17.9 9.4 %collective-permute-start.5 = (bf16[128,1280]{0,1:T(8,128)(2,1)S(1)}, bf16[128,1280]{0,1:T(8,128)(2,1)S(1)}, u32[]{:S(2)}, u32[]{:S(2)}) collective-permute-start(bf16[128,1280]{0,1:T(8,128)(2,1)S(1)} %collective-permute-done.3), channel_id=1, source_target_pairs={{0,8},{2,10},{4,28},{6,30},{8,16},{10,18},{12,4},{14,6},{16,24},{1... | collective-permute-start | bytes 983048 | tf_op jit(solution)/shard_map/ppermute | solution.py:25
  23.7 7.6 %collective-permute-start.6 = (bf16[128,1280]{0,1:T(8,128)(2,1)S(1)}, bf16[128,1280]{0,1:T(8,128)(2,1)S(1)}, u32[]{:S(2)}, u32[]{:S(2)}) collective-permute-start(bf16[128,1280]{0,1:T(8,128)(2,1)S(1)} %broadcast_select_fusion.1), channel_id=1, source_target_pairs={{0,2},{2,0},{4,6},{6,4},{8,10},{10,8},{12,14},{14,12},{16,18},{18,... | collective-permute-start | bytes 983048 | tf_op jit(solution)/shard_map/ppermute | solution.py:14
  27.3 11.0 %collective-permute-start.7 = (bf16[128,1280]{0,1:T(8,128)(2,1)S(1)}, bf16[128,1280]{0,1:T(8,128)(2,1)S(1)}, u32[]{:S(2)}, u32[]{:S(2)}) collective-permute-start(bf16[128,1280]{0,1:T(8,128)(2,1)S(1)} %broadcast_select_fusion), channel_id=1, source_target_pairs={{0,2},{2,0},{4,6},{6,4},{8,10},{10,8},{12,14},{14,12},{16,18},{18,... | collective-permute-start | bytes 983048 | tf_op jit(solution)/shard_map/ppermute | solution.py:14
  33.3 7.5 %slice-start = ((s8[13107200]{0:T(1024)(128)(4,1)}), s8[4194304]{0:T(1024)(128)(4,1)S(1)}, s32[]{:S(2)}) async-start(s8[13107200]{0:T(1024)(128)(4,1)} %bitcast.119), calls=%async_computation | async-start | bytes 8388608
  34.0 6.8 %slice-start.1 = ((s8[13107200]{0:T(1024)(128)(4,1)}), s8[4194304]{0:T(1024)(128)(4,1)S(1)}, s32[]{:S(2)}) async-start(s8[13107200]{0:T(1024)(128)(4,1)} %bitcast.119), calls=%async_computation.1 | async-start | bytes 8388608
  38.8 2.2 %slice-start.2 = ((s8[13107200]{0:T(1024)(128)(4,1)}), s8[4194304]{0:T(1024)(128)(4,1)S(1)}, s32[]{:S(2)}) async-start(s8[13107200]{0:T(1024)(128)(4,1)} %bitcast.119), calls=%async_computation.2 | async-start | bytes 8388608
  39.6 1.7 %slice-start.3 = ((s8[13107200]{0:T(1024)(128)(4,1)}), s8[524288]{0:T(1024)(128)(4,1)S(1)}, s32[]{:S(2)}) async-start(s8[13107200]{0:T(1024)(128)(4,1)} %bitcast.119), calls=%async_computation.3 | async-start | bytes 1048576
  45.3 8.1 %collective-permute-start.8 = (bf16[384,2560]{1,0:T(8,128)(2,1)}, bf16[384,2560]{1,0:T(8,128)(2,1)S(1)}, u32[]{:S(2)}, u32[]{:S(2)}) collective-permute-start(bf16[384,2560]{1,0:T(8,128)(2,1)} %fusion.7), channel_id=1, source_target_pairs={{0,1},{1,0},{2,3},{3,2},{4,5},{5,4},{6,7},{7,6},{8,9},{9,8},{10,11... | collective-permute-start | bytes 5898248 | tf_op jit(solution)/shard_map/ppermute | solution.py:93

commit v10 on v9

--- a/solution.py
+++ b/solution.py
@@ -25,14 +25,13 @@
     return lax.ppermute(value, "blk", pairs)
 
 
-def relay_blocks(own):
+def relay_chain(own):
     position = lax.axis_index("blk") % 4
-    from_x = swap_within_four(own, 1)
     from_y = swap_within_four(own, 2)
     from_z = shift_groups(from_y)
     forward = jnp.where((position == 0) | (position == 3), from_y, from_z)
     from_last = swap_within_four(forward, 1)
-    return [from_x, from_y, from_z, from_last]
+    return [from_y, from_z, from_last]
 
 
 def fold_block(state, key_rows, value_rows, query_heads):
@@ -67,8 +66,9 @@
     )
     keys = with_layout_constraint(keys, Layout(major_to_minor=(1, 0)))
     values = with_layout_constraint(values, Layout(major_to_minor=(1, 0)))
-    key_arrivals = relay_blocks(keys)
-    value_arrivals = relay_blocks(values)
+    from_x = swap_within_four(jnp.stack((keys, values)), 1)
+    key_arrivals = [from_x[0]] + relay_chain(keys)
+    value_arrivals = [from_x[1]] + relay_chain(values)
     state = fold_block(state, keys, values, query_heads)
     for key_rows, value_rows in zip(key_arrivals, value_arrivals):
         state = fold_block(state, key_rows, value_rows, query_heads)

time: 55.6 us -> 53.8 us (0.968)
  the two profiles are of different devices: /device:TPU:7 before, /device:TPU:1 now
where the time goes in v10:
time: 53.8 us; the launch traced here: 53.5 us
  matrix products  16.2 us (30%)
  waiting for transfers between devices  15.9 us (30%)
  starting transfers between devices  11.3 us (21%)
  local copies, waits for them, and re-layouts  5.41 us (10%)
  other arithmetic  4.57 us (8%)
    ppermute x5, waiting for transfers between devices, swap_within_four(): lax.ppermute(value, 'blk', [(source, source ^ bit) for source in range(co...  10.3 us
    dot_general x2, matrix products, partial_for(): jnp.dot(attended, cols, preferred_element_type=jnp.float32)  9.54 us
    ppermute x5, starting transfers between devices, swap_within_four(): lax.ppermute(value, 'blk', [(source, source ^ bit) for source in range(co...  5.92 us
    ppermute x2, waiting for transfers between devices, shift_groups(): return lax.ppermute(value, 'blk', pairs)  5.59 us
    unnamed x15, local copies, waits for them, and re-layouts  4.29 us
    dot_general x5, matrix products, fold_block(): jnp.einsum('qhk,khd->qhd', weights.astype(jnp.bfloat16), value_heads, pre...  4.28 us
    ppermute x1, starting transfers between devices, on_device(): received.append(lax.ppermute(sent, 'mp', pairs))  2.89 us
    ppermute x2, starting transfers between devices, shift_groups(): return lax.ppermute(value, 'blk', pairs)  2.48 us
  transfers between devices with their start and end apart: 8, of which 6 were waited for; matrix products, arithmetic and copies ran while one was open for 29% of the time, Pallas kernels for 0%

profile of v10, /device:TPU:1, one launch (start us, length us, event | category | flops | bytes accessed | tf_op | source)
XLA Modules:
  0.0 53.5 jit_solution(15304011000336968452)
XLA Ops:
  0.0 1.3 %copy.21 = bf16[128,1280]{0,1:T(8,128)(2,1)S(1)} copy(bf16[128,1280]{1,0:T(8,128)(2,1)} %param.5) | data formatting | bytes 655360 | tf_op args[1]
  1.3 2.1 %collective-permute-start.1 = (bf16[128,1280]{0,1:T(8,128)(2,1)S(1)}, bf16[128,1280]{0,1:T(8,128)(2,1)S(1)}, u32[]{:S(2)}, u32[]{:S(2)}) collective-permute-start(bf16[128,1280]{0,1:T(8,128)(2,1)S(1)} %copy.21), channel_id=1, source_target_pairs={{0,4},{2,6},{4,0},{6,2},{8,12},{10,14},{12,8},{14,10},{16,20},{18,... | collective-permute-start | bytes 983048 | tf_op jit(solution)/shard_map/ppermute | solution.py:14
  3.4 1.2 %copy.24 = bf16[128,1280]{0,1:T(8,128)(2,1)S(1)} copy(bf16[128,1280]{1,0:T(8,128)(2,1)} %param.6) | data formatting | bytes 655360 | tf_op args[2]
  4.7 0.9 %pad_maximum_fusion = bf16[2,128,1280]{1,2,0:T(8,128)(2,1)} fusion(bf16[1,128,1280]{1,2,0:T(8,128)(2,1)S(1)} %bitcast.116, bf16[1,128,1280]{1,2,0:T(8,128)(2,1)S(1)} %bitcast.118), kind=kLoop, calls=%fused_computation.57 | loop fusion | flops 327680 | bytes 1310720 | tf_op jit(solution)/shard_map/stack | solution.py:69
  5.5 1.4 %collective-permute-start = (bf16[2,128,1280]{1,2,0:T(8,128)(2,1)}, bf16[2,128,1280]{1,2,0:T(8,128)(2,1)}, u32[]{:S(2)}, u32[]{:S(2)}) collective-permute-start(bf16[2,128,1280]{1,2,0:T(8,128)(2,1)} %pad_maximum_fusion), channel_id=1, source_target_pairs={{0,2},{2,0},{4,6},{6,4},{8,10},{10,8},{12,14},{14,12},{16,18},{18,... | collective-permute-start | bytes 1966088 | tf_op jit(solution)/shard_map/ppermute | solution.py:14
  7.0 0.6 %copy.22 = bf16[384,1280]{0,1:T(8,128)(2,1)S(1)} copy(bf16[384,1280]{1,0:T(8,128)(2,1)S(1)} %copy-done.1) | data formatting | bytes 1966080 | tf_op args[0]
  8.1 1.7 %fusion.38 = f32[10,384,128]{1,2,0:T(8,128)} fusion(bf16[128,10,128]{0,2,1:T(8,128)(2,1)S(1)} %bitcast.117, f32[10,128,384]{2,1,0:T(8,128)S(1)} %get-tuple-element.24, f32[384,10]{0,1:T(8,128)S(1)} %get-tuple-element.23), kind=kOutput, calls=%fused_computation.46 | convolution fusion | flops 127303680 | bytes 4275200 | tf_op jit(solution)/shard_map/qhk,khd->qhd/dot_general | solution.py:48
  9.8 1.1 %collective-permute-done.1 = bf16[128,1280]{0,1:T(8,128)(2,1)S(1)} collective-permute-done((bf16[128,1280]{0,1:T(8,128)(2,1)S(1)}, bf16[128,1280]{0,1:T(8,128)(2,1)S(1)}, u32[]{:S(2)}, u32[]{:S(2)}) %collective-permute-start.1) | collective-permute-done | bytes 327712 | tf_op jit(solution)/shard_map/ppermute | solution.py:14
  10.9 1.2 %collective-permute-start.3 = (bf16[128,1280]{0,1:T(8,128)(2,1)S(1)}, bf16[128,1280]{0,1:T(8,128)(2,1)S(1)}, u32[]{:S(2)}, u32[]{:S(2)}) collective-permute-start(bf16[128,1280]{0,1:T(8,128)(2,1)S(1)} %collective-permute-done.1), channel_id=1, source_target_pairs={{0,8},{2,10},{4,28},{6,30},{8,16},{10,18},{12,4},{14,6},{16,24},{1... | collective-permute-start | bytes 983048 | tf_op jit(solution)/shard_map/ppermute | solution.py:25
  12.5 5.4 %collective-permute-done.2 = bf16[128,1280]{0,1:T(8,128)(2,1)S(1)} collective-permute-done((bf16[128,1280]{0,1:T(8,128)(2,1)S(1)}, bf16[128,1280]{0,1:T(8,128)(2,1)S(1)}, u32[]{:S(2)}, u32[]{:S(2)}) %collective-permute-start.2) | collective-permute-done | bytes 327712 | tf_op jit(solution)/shard_map/ppermute | solution.py:14
  17.9 1.2 %collective-permute-start.4 = (bf16[128,1280]{0,1:T(8,128)(2,1)S(1)}, bf16[128,1280]{0,1:T(8,128)(2,1)S(1)}, u32[]{:S(2)}, u32[]{:S(2)}) collective-permute-start(bf16[128,1280]{0,1:T(8,128)(2,1)S(1)} %collective-permute-done.2), channel_id=1, source_target_pairs={{0,8},{2,10},{4,28},{6,30},{8,16},{10,18},{12,4},{14,6},{16,24},{1... | collective-permute-start | bytes 983048 | tf_op jit(solution)/shard_map/ppermute | solution.py:25
  19.7 1.2 %collective-permute-start.5 = (bf16[128,1280]{0,1:T(8,128)(2,1)S(1)}, bf16[128,1280]{0,1:T(8,128)(2,1)S(1)}, u32[]{:S(2)}, u32[]{:S(2)}) collective-permute-start(bf16[128,1280]{0,1:T(8,128)(2,1)S(1)} %broadcast_select_fusion.1), channel_id=1, source_target_pairs={{0,2},{2,0},{4,6},{6,4},{8,10},{10,8},{12,14},{14,12},{16,18},{18,... | collective-permute-start | bytes 983048 | tf_op jit(solution)/shard_map/ppermute | solution.py:14
  21.2 1.1 %fusion.58 = (bf16[1,128,1280]{1,2,0:T(8,128)(2,1)S(1)}, bf16[1,128,1280]{1,2,0:T(8,128)(2,1)S(1)}) fusion(bf16[2,128,1280]{1,2,0:T(8,128)(2,1)} %collective-permute-done), kind=kLoop, calls=%fused_computation.74 | loop fusion | bytes 1310720 | tf_op jit(solution)/shard_map/slice | solution.py:71
  22.3 5.5 %collective-permute-done.4 = bf16[128,1280]{0,1:T(8,128)(2,1)S(1)} collective-permute-done((bf16[128,1280]{0,1:T(8,128)(2,1)S(1)}, bf16[128,1280]{0,1:T(8,128)(2,1)S(1)}, u32[]{:S(2)}, u32[]{:S(2)}) %collective-permute-start.4) | collective-permute-done | bytes 327712 | tf_op jit(solution)/shard_map/ppermute | solution.py:25
  28.4 1.1 %collective-permute-start.6 = (bf16[128,1280]{0,1:T(8,128)(2,1)S(1)}, bf16[128,1280]{0,1:T(8,128)(2,1)S(1)}, u32[]{:S(2)}, u32[]{:S(2)}) collective-permute-start(bf16[128,1280]{0,1:T(8,128)(2,1)S(1)} %broadcast_select_fusion), channel_id=1, source_target_pairs={{0,2},{2,0},{4,6},{6,4},{8,10},{10,8},{12,14},{14,12},{16,18},{18,... | collective-permute-start | bytes 983048 | tf_op jit(solution)/shard_map/ppermute | solution.py:14
  30.9 0.7 %fusion.23 = (f32[384,10]{0,1:T(8,128)S(1)}, f32[384,10]{0,1:T(8,128)S(1)}) fusion(f32[10,128,384]{2,1,0:T(8,128)S(1)} %get-tuple-element.26, f32[384,10]{0,1:T(8,128)S(1)} %get-tuple-element.13, f32[384,10]{0,1:T(8,128)S(1)} %get-tuple-element.12, f32[10,128,384]{2,1,0:T(8,128)S(1)} %get-tuple-element.22), kind=kLoop, calls=%fused_computation.35 | loop fusion | flops 2941440 | bytes 3993600 | tf_op jit(solution)/shard_map/reduce_sum | solution.py:47
  32.1 3.6 %collective-permute-done.6 = bf16[128,1280]{0,1:T(8,128)(2,1)S(1)} collective-permute-done((bf16[128,1280]{0,1:T(8,128)(2,1)S(1)}, bf16[128,1280]{0,1:T(8,128)(2,1)S(1)}, u32[]{:S(2)}, u32[]{:S(2)}) %collective-permute-start.6) | collective-permute-done | bytes 327712 | tf_op jit(solution)/shard_map/ppermute | solution.py:14
  36.2 0.7 %fusion.27 = (f32[384,10]{0,1:T(8,128)S(1)}, f32[384,10]{0,1:T(8,128)S(1)}) fusion(f32[10,128,384]{2,1,0:T(8,128)S(1)} %get-tuple-element.20, f32[384,10]{0,1:T(8,128)S(1)} %get-tuple-element.11, f32[384,10]{0,1:T(8,128)S(1)} %get-tuple-element.10, f32[10,128,384]{2,1,0:T(8,128)S(1)} %get-tuple-element.18), kind=kLoop, calls=%fused_computation.39 | loop fusion | flops 2941440 | bytes 3993600 | tf_op jit(solution)/shard_map/reduce_sum | solution.py:47
  37.0 0.7 %copy-done = f32[10,384,128]{1,2,0:T(8,128)S(1)} copy-done((f32[10,384,128]{1,2,0:T(8,128)S(1)}, f32[10,384,128]{1,2,0:T(8,128)}, u32[]{:S(2)}) %copy-start) | copy-done | bytes 1966104
  37.7 1.1 %fusion.11 = bf16[384,10,128]{0,2,1:T(8,128)(2,1)S(1)} fusion(f32[10,128,384]{2,1,0:T(8,128)S(1)} %fusion.31, f32[10,384,128]{1,2,0:T(8,128)S(1)} %fusion.34, f32[10,128,384]{2,1,0:T(8,128)S(1)} %fusion.36, f32[10,384,128]{1,2,0:T(8,128)S(1)} %copy-done, bf16[128,10,128]{0,2,1:T(8,128)(2,1)S(1)} %bitcast.126, f32[10,128,384]{2,1,0:T(8,128)S(1)} %get-tuple-element.20, ...), kind=kOutput, calls=%fused_computation.9 | convolution fusion | flops 132710400 | bytes 11248640 | tf_op jit(solution)/shard_map/qhk,khd->qhd/dot_general | solution.py:48
  39.3 3.9 %fusion.7 = bf16[384,2560]{1,0:T(8,128)(2,1)} fusion(bf16[384,1280]{0,1:T(8,128)(2,1)S(1)} %bitcast.130, bf16[1280,5120]{1,0:T(8,128)(2,1)S(1)} %bitcast.129, s32[]{:T(128)S(6)} %select_n.37), kind=kOutput, calls=%fused_computation.5 | convolution fusion | flops 2517565440 | bytes 9502724 | tf_op jit(solution)/shard_map/dot_general | solution.py:87
  43.3 2.9 %collective-permute-start.7 = (bf16[384,2560]{1,0:T(8,128)(2,1)}, bf16[384,2560]{1,0:T(8,128)(2,1)S(1)}, u32[]{:S(2)}, u32[]{:S(2)}) collective-permute-start(bf16[384,2560]{1,0:T(8,128)(2,1)} %fusion.7), channel_id=1, source_target_pairs={{0,1},{1,0},{2,3},{3,2},{4,5},{5,4},{6,7},{7,6},{8,9},{9,8},{10,11... | collective-permute-start | bytes 5898248 | tf_op jit(solution)/shard_map/ppermute | solution.py:93
  46.2 5.6 %fusion.4 = bf16[384,2560]{1,0:T(8,128)(2,1)S(1)} fusion(bf16[384,1280]{0,1:T(8,128)(2,1)S(1)} %bitcast.131, bf16[1280,5120]{1,0:T(8,128)(2,1)} %param.7, s32[]{:T(128)S(6)} %select_n.35), kind=kOutput, calls=%fused_computation.4 | convolution fusion | flops 2517565440 | bytes 9502724 | tf_op jit(solution)/shard_map/dot_general | solution.py:87
  51.8 1.7 %add_convert_fusion = bf16[384,2560]{1,0:T(8,128)(2,1)} fusion(bf16[384,2560]{1,0:T(8,128)(2,1)S(1)} %collective-permute-done.7, bf16[384,2560]{1,0:T(8,128)(2,1)S(1)} %fusion.4), kind=kLoop, calls=%fused_computation.6 | loop fusion | flops 3932160 | bytes 5898240 | tf_op jit(solution)/shard_map/convert_element_type | solution.py:97
  (30 shorter events, 5.1 us)
Async XLA Ops:
  0.0 7.0 %copy-start.1 = (bf16[384,1280]{1,0:T(8,128)(2,1)S(1)}, bf16[384,1280]{1,0:T(8,128)(2,1)}, u32[]{:S(2)}) copy-start(bf16[384,1280]{1,0:T(8,128)(2,1)} %param.4) | copy-start | bytes 2949124
  1.3 9.6 %collective-permute-start.1 = (bf16[128,1280]{0,1:T(8,128)(2,1)S(1)}, bf16[128,1280]{0,1:T(8,128)(2,1)S(1)}, u32[]{:S(2)}, u32[]{:S(2)}) collective-permute-start(bf16[128,1280]{0,1:T(8,128)(2,1)S(1)} %copy.21), channel_id=1, source_target_pairs={{0,4},{2,6},{4,0},{6,2},{8,12},{10,14},{12,8},{14,10},{16,20},{18,... | collective-permute-start | bytes 983048 | tf_op jit(solution)/shard_map/ppermute | solution.py:14
  4.6 13.4 %collective-permute-start.2 = (bf16[128,1280]{0,1:T(8,128)(2,1)S(1)}, bf16[128,1280]{0,1:T(8,128)(2,1)S(1)}, u32[]{:S(2)}, u32[]{:S(2)}) collective-permute-start(bf16[128,1280]{0,1:T(8,128)(2,1)S(1)} %copy.24), channel_id=1, source_target_pairs={{0,4},{2,6},{4,0},{6,2},{8,12},{10,14},{12,8},{14,10},{16,20},{18,... | collective-permute-start | bytes 983048 | tf_op jit(solution)/shard_map/ppermute | solution.py:14
  5.5 15.7 %collective-permute-start = (bf16[2,128,1280]{1,2,0:T(8,128)(2,1)}, bf16[2,128,1280]{1,2,0:T(8,128)(2,1)}, u32[]{:S(2)}, u32[]{:S(2)}) collective-permute-start(bf16[2,128,1280]{1,2,0:T(8,128)(2,1)} %pad_maximum_fusion), channel_id=1, source_target_pairs={{0,2},{2,0},{4,6},{6,4},{8,10},{10,8},{12,14},{14,12},{16,18},{18,... | collective-permute-start | bytes 1966088 | tf_op jit(solution)/shard_map/ppermute | solution.py:14
  10.9 8.8 %collective-permute-start.3 = (bf16[128,1280]{0,1:T(8,128)(2,1)S(1)}, bf16[128,1280]{0,1:T(8,128)(2,1)S(1)}, u32[]{:S(2)}, u32[]{:S(2)}) collective-permute-start(bf16[128,1280]{0,1:T(8,128)(2,1)S(1)} %collective-permute-done.1), channel_id=1, source_target_pairs={{0,8},{2,10},{4,28},{6,30},{8,16},{10,18},{12,4},{14,6},{16,24},{1... | collective-permute-start | bytes 983048 | tf_op jit(solution)/shard_map/ppermute | solution.py:25
  17.9 9.9 %collective-permute-start.4 = (bf16[128,1280]{0,1:T(8,128)(2,1)S(1)}, bf16[128,1280]{0,1:T(8,128)(2,1)S(1)}, u32[]{:S(2)}, u32[]{:S(2)}) collective-permute-start(bf16[128,1280]{0,1:T(8,128)(2,1)S(1)} %collective-permute-done.2), channel_id=1, source_target_pairs={{0,8},{2,10},{4,28},{6,30},{8,16},{10,18},{12,4},{14,6},{16,24},{1... | collective-permute-start | bytes 983048 | tf_op jit(solution)/shard_map/ppermute | solution.py:25
  19.7 10.2 %collective-permute-start.5 = (bf16[128,1280]{0,1:T(8,128)(2,1)S(1)}, bf16[128,1280]{0,1:T(8,128)(2,1)S(1)}, u32[]{:S(2)}, u32[]{:S(2)}) collective-permute-start(bf16[128,1280]{0,1:T(8,128)(2,1)S(1)} %broadcast_select_fusion.1), channel_id=1, source_target_pairs={{0,2},{2,0},{4,6},{6,4},{8,10},{10,8},{12,14},{14,12},{16,18},{18,... | collective-permute-start | bytes 983048 | tf_op jit(solution)/shard_map/ppermute | solution.py:14
  28.4 7.3 %collective-permute-start.6 = (bf16[128,1280]{0,1:T(8,128)(2,1)S(1)}, bf16[128,1280]{0,1:T(8,128)(2,1)S(1)}, u32[]{:S(2)}, u32[]{:S(2)}) collective-permute-start(bf16[128,1280]{0,1:T(8,128)(2,1)S(1)} %broadcast_select_fusion), channel_id=1, source_target_pairs={{0,2},{2,0},{4,6},{6,4},{8,10},{10,8},{12,14},{14,12},{16,18},{18,... | collective-permute-start | bytes 983048 | tf_op jit(solution)/shard_map/ppermute | solution.py:14
  30.4 8.5 %slice-start = ((s8[13107200]{0:T(1024)(128)(4,1)}), s8[4194304]{0:T(1024)(128)(4,1)S(1)}, s32[]{:S(2)}) async-start(s8[13107200]{0:T(1024)(128)(4,1)} %bitcast.128), calls=%async_computation | async-start | bytes 8388608
  31.7 7.2 %slice-start.1 = ((s8[13107200]{0:T(1024)(128)(4,1)}), s8[4194304]{0:T(1024)(128)(4,1)S(1)}, s32[]{:S(2)}) async-start(s8[13107200]{0:T(1024)(128)(4,1)} %bitcast.128), calls=%async_computation.1 | async-start | bytes 8388608
  36.2 1.5 %copy-start = (f32[10,384,128]{1,2,0:T(8,128)S(1)}, f32[10,384,128]{1,2,0:T(8,128)}, u32[]{:S(2)}) copy-start(f32[10,384,128]{1,2,0:T(8,128)} %fusion.38) | copy-start | bytes 5898244
  36.2 2.8 %slice-start.2 = ((s8[13107200]{0:T(1024)(128)(4,1)}), s8[4194304]{0:T(1024)(128)(4,1)S(1)}, s32[]{:S(2)}) async-start(s8[13107200]{0:T(1024)(128)(4,1)} %bitcast.128), calls=%async_computation.2 | async-start | bytes 8388608
  37.7 1.6 %slice-start.3 = ((s8[13107200]{0:T(1024)(128)(4,1)}), s8[524288]{0:T(1024)(128)(4,1)S(1)}, s32[]{:S(2)}) async-start(s8[13107200]{0:T(1024)(128)(4,1)} %bitcast.128), calls=%async_computation.3 | async-start | bytes 1048576
  43.3 8.5 %collective-permute-start.7 = (bf16[384,2560]{1,0:T(8,128)(2,1)}, bf16[384,2560]{1,0:T(8,128)(2,1)S(1)}, u32[]{:S(2)}, u32[]{:S(2)}) collective-permute-start(bf16[384,2560]{1,0:T(8,128)(2,1)} %fusion.7), channel_id=1, source_target_pairs={{0,1},{1,0},{2,3},{3,2},{4,5},{5,4},{6,7},{7,6},{8,9},{9,8},{10,11... | collective-permute-start | bytes 5898248 | tf_op jit(solution)/shard_map/ppermute | solution.py:93

commit v11 on v10

--- a/solution.py
+++ b/solution.py
@@ -70,7 +70,9 @@
     key_arrivals = [from_x[0]] + relay_chain(keys)
     value_arrivals = [from_x[1]] + relay_chain(values)
     state = fold_block(state, keys, values, query_heads)
-    for key_rows, value_rows in zip(key_arrivals, value_arrivals):
+    for index, (key_rows, value_rows) in enumerate(zip(key_arrivals, value_arrivals)):
+        if index < 2:
+            state = lax.optimization_barrier(state)
         state = fold_block(state, key_rows, value_rows, query_heads)
     running_max, running_sum, numerator = state
     attended = (

time: 53.8 us -> 64.3 us (1.20)
  matrix products: 16.2 us -> 25.3 us
  other arithmetic: 4.57 us -> 7.63 us
  starting transfers between devices: 11.3 us -> 8.94 us
    dot_general x5, matrix products: 4.28 us -> 8.51 us  [fold_block(): jnp.einsum('qhk,khd->qhd', weights.astype(jnp.bfloat16), value_heads, pre...]
    dot_general x2, matrix products: 9.54 us -> 12.5 us  [partial_for(): jnp.dot(attended, cols, preferred_element_type=jnp.float32)]
    ppermute x5, starting transfers between devices: 5.92 us -> 3.72 us  [swap_within_four(): lax.ppermute(value, 'blk', [(source, source ^ bit) for source in range(co...]
    select_n x2, other arithmetic: 0.07 us -> 2.17 us  [relay_chain(): forward = jnp.where((position == 0) | (position == 3), from_y, from_z)]
    dot_general x5, matrix products: 2.36 us -> 4.31 us  [fold_block(): jnp.einsum('qhd,khd->qhk', query_heads, key_heads, preferred_element_type...]
    ppermute x5, waiting for transfers between devices: 10.3 us -> 11.8 us  [swap_within_four(): lax.ppermute(value, 'blk', [(source, source ^ bit) for source in range(co...]
    ppermute x2, waiting for transfers between devices: 5.59 us -> 4.45 us  [shift_groups(): return lax.ppermute(value, 'blk', pairs)]
    another operation x1, other arithmetic: 0.89 us -> 1.87 us  [on_device(): from_x = swap_within_four(jnp.stack((keys, values)), 1)]
  transfers between devices with their start and end apart: 8 -> 8, of which waited for: 6 -> 4; matrix products, arithmetic and copies ran while one was open for 29% -> 33% of each run, Pallas kernels for 0% -> 0%
where the time goes in v11:
time: 64.3 us; the launch traced here: 63.9 us
  matrix products  25.3 us (39%)
  waiting for transfers between devices  16.2 us (25%)
  starting transfers between devices  8.94 us (14%)
  other arithmetic  7.63 us (12%)
  local copies, waits for them, and re-layouts  5.54 us (9%)
    dot_general x2, matrix products, partial_for(): jnp.dot(attended, cols, preferred_element_type=jnp.float32)  12.5 us
    ppermute x5, waiting for transfers between devices, swap_within_four(): lax.ppermute(value, 'blk', [(source, source ^ bit) for source in range(co...  11.8 us
    dot_general x5, matrix products, fold_block(): jnp.einsum('qhk,khd->qhd', weights.astype(jnp.bfloat16), value_heads, pre...  8.51 us
    ppermute x2, waiting for transfers between devices, shift_groups(): return lax.ppermute(value, 'blk', pairs)  4.45 us
    dot_general x5, matrix products, fold_block(): jnp.einsum('qhd,khd->qhk', query_heads, key_heads, preferred_element_type...  4.31 us
    unnamed x7, local copies, waits for them, and re-layouts  3.79 us
    ppermute x5, starting transfers between devices, swap_within_four(): lax.ppermute(value, 'blk', [(source, source ^ bit) for source in range(co...  3.72 us
    ppermute x1, starting transfers between devices, on_device(): received.append(lax.ppermute(sent, 'mp', pairs))  2.68 us
  transfers between devices with their start and end apart: 8, of which 4 were waited for; matrix products, arithmetic and copies ran while one was open for 33% of the time, Pallas kernels for 0%

profile of v11, /device:TPU:1, one launch (start us, length us, event | category | flops | bytes accessed | tf_op | source)
XLA Modules:
  0.0 63.9 jit_solution(10802979701779801615)
XLA Ops:
  0.0 2.0 %copy.25 = bf16[128,1280]{0,1:T(8,128)(2,1)} copy(bf16[128,1280]{1,0:T(8,128)(2,1)} %param.5) | data formatting | bytes 655360 | tf_op args[1]
  2.0 2.1 %collective-permute-start.1 = (bf16[128,1280]{0,1:T(8,128)(2,1)}, bf16[128,1280]{0,1:T(8,128)(2,1)}, u32[]{:S(2)}, u32[]{:S(2)}) collective-permute-start(bf16[128,1280]{0,1:T(8,128)(2,1)} %copy.25), channel_id=1, source_target_pairs={{0,4},{2,6},{4,0},{6,2},{8,12},{10,14},{12,8},{14,10},{16,20},{18,... | collective-permute-start | bytes 983048 | tf_op jit(solution)/shard_map/ppermute | solution.py:14
  4.0 1.2 %copy.28 = bf16[128,1280]{0,1:T(8,128)(2,1)S(1)} copy(bf16[128,1280]{1,0:T(8,128)(2,1)} %param.6) | data formatting | bytes 655360 | tf_op args[2]
  5.3 1.9 %pad_maximum_fusion = bf16[2,128,1280]{1,2,0:T(8,128)(2,1)} fusion(bf16[1,128,1280]{1,2,0:T(8,128)(2,1)S(1)} %bitcast.108, bf16[1,128,1280]{1,2,0:T(8,128)(2,1)} %bitcast.5), kind=kLoop, calls=%fused_computation.53 | loop fusion | flops 327680 | bytes 1310720 | tf_op jit(solution)/shard_map/stack | solution.py:69
  7.2 1.4 %collective-permute-start = (bf16[2,128,1280]{1,2,0:T(8,128)(2,1)}, bf16[2,128,1280]{1,2,0:T(8,128)(2,1)}, u32[]{:S(2)}, u32[]{:S(2)}) collective-permute-start(bf16[2,128,1280]{1,2,0:T(8,128)(2,1)} %pad_maximum_fusion), channel_id=1, source_target_pairs={{0,2},{2,0},{4,6},{6,4},{8,10},{10,8},{12,14},{14,12},{16,18},{18,... | collective-permute-start | bytes 1966088 | tf_op jit(solution)/shard_map/ppermute | solution.py:14
  9.2 1.4 %bitcast_reduce_fusion.4 = (f32[384,10]{0,1:T(8,128)S(1)}, f32[10,128,384]{2,1,0:T(8,128)S(1)}) fusion(bf16[128,10,128]{0,2,1:T(8,128)(2,1)} %bitcast, bf16[384,10,128]{0,2,1:T(8,128)(2,1)S(1)} %bitcast.103), kind=kOutput, calls=%fused_computation.29 | convolution fusion | flops 126808320 | bytes 3292160 | tf_op jit(solution)/shard_map/qhd,khd->qhk/dot_general | solution.py:42
  11.1 2.0 %bitcast_add_fusion.4 = f32[384,10,128]{2,0,1:T(8,128)} fusion(bf16[128,10,128]{0,2,1:T(8,128)(2,1)S(1)} %bitcast.109, f32[10,128,384]{2,1,0:T(8,128)S(1)} %get-tuple-element.35, f32[384,10]{0,1:T(8,128)S(1)} %get-tuple-element.28, f32[384,10]{0,1:T(8,128)S(1)} %get-tuple-element.11), kind=kOutput, calls=%fused_computation.27 | convolution fusion | flops 127795200 | bytes 4290560 | tf_op jit(solution)/shard_map/qhk,khd->qhd/dot_general | solution.py:48
  13.1 1.3 %collective-permute-start.3 = (bf16[128,1280]{0,1:T(8,128)(2,1)}, bf16[128,1280]{0,1:T(8,128)(2,1)S(1)}, u32[]{:S(2)}, u32[]{:S(2)}) collective-permute-start(bf16[128,1280]{0,1:T(8,128)(2,1)} %collective-permute-done.1), channel_id=1, source_target_pairs={{0,8},{2,10},{4,28},{6,30},{8,16},{10,18},{12,4},{14,6},{16,24},{1... | collective-permute-start | bytes 983048 | tf_op jit(solution)/shard_map/ppermute | solution.py:25
  14.4 4.4 %collective-permute-done.2 = bf16[128,1280]{0,1:T(8,128)(2,1)} collective-permute-done((bf16[128,1280]{0,1:T(8,128)(2,1)S(1)}, bf16[128,1280]{0,1:T(8,128)(2,1)}, u32[]{:S(2)}, u32[]{:S(2)}) %collective-permute-start.2) | collective-permute-done | bytes 327712 | tf_op jit(solution)/shard_map/ppermute | solution.py:14
  18.8 1.2 %collective-permute-start.4 = (bf16[128,1280]{0,1:T(8,128)(2,1)}, bf16[128,1280]{0,1:T(8,128)(2,1)S(1)}, u32[]{:S(2)}, u32[]{:S(2)}) collective-permute-start(bf16[128,1280]{0,1:T(8,128)(2,1)} %collective-permute-done.2), channel_id=1, source_target_pairs={{0,8},{2,10},{4,28},{6,30},{8,16},{10,18},{12,4},{14,6},{16,24},{1... | collective-permute-start | bytes 983048 | tf_op jit(solution)/shard_map/ppermute | solution.py:25
  20.0 1.4 %bitcast_reduce_fusion.2 = (f32[384,10]{0,1:T(8,128)S(1)}, f32[10,128,384]{2,1,0:T(8,128)S(1)}) fusion(bf16[128,10,128]{0,2,1:T(8,128)(2,1)} %bitcast.11, bf16[384,10,128]{0,2,1:T(8,128)(2,1)S(1)} %bitcast.104), kind=kOutput, calls=%fused_computation.21 | convolution fusion | flops 126808320 | bytes 3292160 | tf_op jit(solution)/shard_map/qhd,khd->qhk/dot_general | solution.py:42
  21.5 1.3 %collective-permute-done = bf16[2,128,1280]{1,2,0:T(8,128)(2,1)} collective-permute-done((bf16[2,128,1280]{1,2,0:T(8,128)(2,1)}, bf16[2,128,1280]{1,2,0:T(8,128)(2,1)}, u32[]{:S(2)}, u32[]{:S(2)}) %collective-permute-start) | collective-permute-done | bytes 655392 | tf_op jit(solution)/shard_map/ppermute | solution.py:14
  22.8 1.1 %fusion.55 = (bf16[1,128,1280]{1,2,0:T(8,128)(2,1)S(1)}, bf16[1,128,1280]{1,2,0:T(8,128)(2,1)S(1)}) fusion(bf16[2,128,1280]{1,2,0:T(8,128)(2,1)} %collective-permute-done), kind=kLoop, calls=%fused_computation.72 | loop fusion | bytes 1310720 | tf_op jit(solution)/shard_map/slice | solution.py:71
  24.4 1.2 %broadcast_select_fusion.1 = bf16[128,1280]{0,1:T(8,128)(2,1)S(1)} fusion(bf16[128,1280]{0,1:T(8,128)(2,1)} %collective-permute-done.1, bf16[128,1280]{0,1:T(8,128)(2,1)S(1)} %collective-permute-done.3, pred[]{:T(512)S(6)} %or.4), kind=kLoop, calls=%fused_computation.55 | loop fusion | flops 163840 | bytes 983041 | tf_op jit(solution)/shard_map/jit(_where)/select_n | solution.py:32
  26.1 4.4 %collective-permute-done.4 = bf16[128,1280]{0,1:T(8,128)(2,1)S(1)} collective-permute-done((bf16[128,1280]{0,1:T(8,128)(2,1)}, bf16[128,1280]{0,1:T(8,128)(2,1)S(1)}, u32[]{:S(2)}, u32[]{:S(2)}) %collective-permute-start.4) | collective-permute-done | bytes 327712 | tf_op jit(solution)/shard_map/ppermute | solution.py:25
  30.5 1.0 %broadcast_select_fusion = bf16[128,1280]{0,1:T(8,128)(2,1)S(1)} fusion(bf16[128,1280]{0,1:T(8,128)(2,1)} %collective-permute-done.2, bf16[128,1280]{0,1:T(8,128)(2,1)S(1)} %collective-permute-done.4, pred[]{:T(512)S(6)} %or.4), kind=kLoop, calls=%fused_computation.54 | loop fusion | flops 163840 | bytes 983041 | tf_op jit(solution)/shard_map/jit(_where)/select_n | solution.py:32
  31.5 1.2 %bitcast_add_fusion.3 = f32[384,10,128]{2,0,1:T(8,128)S(1)} fusion(f32[384,10,128]{2,0,1:T(8,128)S(1)} %copy-done, bf16[128,10,128]{0,2,1:T(8,128)(2,1)S(1)} %bitcast.110, f32[10,128,384]{2,1,0:T(8,128)S(1)} %get-tuple-element.37, f32[384,10]{0,1:T(8,128)S(1)} %get-tuple-element.25, f32[384,10]{0,1:T(8,128)S(1)} %max.12), kind=kOutput, calls=%fused_computation.23 | convolution fusion | flops 128286720 | bytes 6256640 | tf_op jit(solution)/shard_map/qhk,khd->qhd/dot_general | solution.py:48
  34.2 6.1 %collective-permute-done.6 = bf16[128,1280]{0,1:T(8,128)(2,1)S(1)} collective-permute-done((bf16[128,1280]{0,1:T(8,128)(2,1)S(1)}, bf16[128,1280]{0,1:T(8,128)(2,1)S(1)}, u32[]{:S(2)}, u32[]{:S(2)}) %collective-permute-start.6) | collective-permute-done | bytes 327712 | tf_op jit(solution)/shard_map/ppermute | solution.py:14
  40.9 1.5 %fusion.32 = f32[10,384,128]{2,1,0:T(8,128)S(1)} fusion(bf16[128,10,128]{0,2,1:T(8,128)(2,1)} %bitcast.13, f32[10,128,384]{2,1,0:T(8,128)S(1)} %get-tuple-element.39, f32[384,10]{0,1:T(8,128)S(1)} %get-tuple-element.23), kind=kOutput, calls=%fused_computation.42 | convolution fusion | flops 127303680 | bytes 4275200 | tf_op jit(solution)/shard_map/qhk,khd->qhd/dot_general | solution.py:48
  43.2 3.1 %fusion.11 = bf16[384,10,128]{2,0,1:T(8,128)(2,1)S(1)} fusion(f32[10,128,384]{1,2,0:T(8,128)S(1)} %fusion.29, f32[10,384,128]{2,1,0:T(8,128)S(1)} %fusion.32, f32[384,10,128]{2,0,1:T(8,128)S(1)} %bitcast_add_fusion.3, bf16[128,10,128]{0,2,1:T(8,128)(2,1)S(1)} %bitcast.116, f32[10,128,384]{2,1,0:T(8,128)S(1)} %get-tuple-element.33, ...), kind=kOutput, calls=%fused_computation.9 | convolution fusion | flops 131235840 | bytes 9251840 | tf_op jit(solution)/shard_map/qhk,khd->qhd/dot_general | solution.py:48
  46.9 6.9 %fusion.7 = bf16[384,2560]{1,0:T(8,128)(2,1)} fusion(bf16[384,1280]{0,1:T(8,128)(2,1)S(1)} %bitcast.113, bf16[1280,5120]{1,0:T(8,128)(2,1)} %param.7, s32[]{:T(128)S(6)} %select_n.37), kind=kOutput, calls=%fused_computation.5 | convolution fusion | flops 2517565440 | bytes 9502724 | tf_op jit(solution)/shard_map/dot_general | solution.py:89
  53.8 2.7 %collective-permute-start.7 = (bf16[384,2560]{1,0:T(8,128)(2,1)}, bf16[384,2560]{1,0:T(8,128)(2,1)S(1)}, u32[]{:S(2)}, u32[]{:S(2)}) collective-permute-start(bf16[384,2560]{1,0:T(8,128)(2,1)} %fusion.7), channel_id=1, source_target_pairs={{0,1},{1,0},{2,3},{3,2},{4,5},{5,4},{6,7},{7,6},{8,9},{9,8},{10,11... | collective-permute-start | bytes 5898248 | tf_op jit(solution)/shard_map/ppermute | solution.py:95
  56.5 5.6 %fusion.4 = bf16[384,2560]{1,0:T(8,128)(2,1)S(1)} fusion(bf16[384,1280]{0,1:T(8,128)(2,1)S(1)} %bitcast.114, bf16[1280,5120]{1,0:T(8,128)(2,1)} %param.7, s32[]{:T(128)S(6)} %select_n.35), kind=kOutput, calls=%fused_computation.4 | convolution fusion | flops 2517565440 | bytes 9502724 | tf_op jit(solution)/shard_map/dot_general | solution.py:89
  62.1 1.7 %add_convert_fusion = bf16[384,2560]{1,0:T(8,128)(2,1)} fusion(bf16[384,2560]{1,0:T(8,128)(2,1)S(1)} %collective-permute-done.7, bf16[384,2560]{1,0:T(8,128)(2,1)S(1)} %fusion.4), kind=kLoop, calls=%fused_computation.6 | loop fusion | flops 3932160 | bytes 5898240 | tf_op jit(solution)/shard_map/convert_element_type | solution.py:99
  (26 shorter events, 5.4 us)
Async XLA Ops:
  0.0 8.6 %copy-start.1 = (bf16[384,1280]{1,0:T(8,128)(2,1)S(1)}, bf16[384,1280]{1,0:T(8,128)(2,1)}, u32[]{:S(2)}) copy-start(bf16[384,1280]{1,0:T(8,128)(2,1)} %param.4) | copy-start | bytes 2949124
  2.0 11.2 %collective-permute-start.1 = (bf16[128,1280]{0,1:T(8,128)(2,1)}, bf16[128,1280]{0,1:T(8,128)(2,1)}, u32[]{:S(2)}, u32[]{:S(2)}) collective-permute-start(bf16[128,1280]{0,1:T(8,128)(2,1)} %copy.25), channel_id=1, source_target_pairs={{0,4},{2,6},{4,0},{6,2},{8,12},{10,14},{12,8},{14,10},{16,20},{18,... | collective-permute-start | bytes 983048 | tf_op jit(solution)/shard_map/ppermute | solution.py:14
  5.2 13.6 %collective-permute-start.2 = (bf16[128,1280]{0,1:T(8,128)(2,1)S(1)}, bf16[128,1280]{0,1:T(8,128)(2,1)}, u32[]{:S(2)}, u32[]{:S(2)}) collective-permute-start(bf16[128,1280]{0,1:T(8,128)(2,1)S(1)} %copy.28), channel_id=1, source_target_pairs={{0,4},{2,6},{4,0},{6,2},{8,12},{10,14},{12,8},{14,10},{16,20},{18,... | collective-permute-start | bytes 983048 | tf_op jit(solution)/shard_map/ppermute | solution.py:14
  7.2 15.7 %collective-permute-start = (bf16[2,128,1280]{1,2,0:T(8,128)(2,1)}, bf16[2,128,1280]{1,2,0:T(8,128)(2,1)}, u32[]{:S(2)}, u32[]{:S(2)}) collective-permute-start(bf16[2,128,1280]{1,2,0:T(8,128)(2,1)} %pad_maximum_fusion), channel_id=1, source_target_pairs={{0,2},{2,0},{4,6},{6,4},{8,10},{10,8},{12,14},{14,12},{16,18},{18,... | collective-permute-start | bytes 1966088 | tf_op jit(solution)/shard_map/ppermute | solution.py:14
  13.1 11.3 %collective-permute-start.3 = (bf16[128,1280]{0,1:T(8,128)(2,1)}, bf16[128,1280]{0,1:T(8,128)(2,1)S(1)}, u32[]{:S(2)}, u32[]{:S(2)}) collective-permute-start(bf16[128,1280]{0,1:T(8,128)(2,1)} %collective-permute-done.1), channel_id=1, source_target_pairs={{0,8},{2,10},{4,28},{6,30},{8,16},{10,18},{12,4},{14,6},{16,24},{1... | collective-permute-start | bytes 983048 | tf_op jit(solution)/shard_map/ppermute | solution.py:25
  18.8 11.7 %collective-permute-start.4 = (bf16[128,1280]{0,1:T(8,128)(2,1)}, bf16[128,1280]{0,1:T(8,128)(2,1)S(1)}, u32[]{:S(2)}, u32[]{:S(2)}) collective-permute-start(bf16[128,1280]{0,1:T(8,128)(2,1)} %collective-permute-done.2), channel_id=1, source_target_pairs={{0,8},{2,10},{4,28},{6,30},{8,16},{10,18},{12,4},{14,6},{16,24},{1... | collective-permute-start | bytes 983048 | tf_op jit(solution)/shard_map/ppermute | solution.py:25
  24.4 7.1 %copy-start = (f32[384,10,128]{2,0,1:T(8,128)S(1)}, f32[384,10,128]{2,0,1:T(8,128)}, u32[]{:S(2)}) copy-start(f32[384,10,128]{2,0,1:T(8,128)} %bitcast_add_fusion.4) | copy-start | bytes 5898244
  25.6 7.8 %collective-permute-start.5 = (bf16[128,1280]{0,1:T(8,128)(2,1)S(1)}, bf16[128,1280]{0,1:T(8,128)(2,1)S(1)}, u32[]{:S(2)}, u32[]{:S(2)}) collective-permute-start(bf16[128,1280]{0,1:T(8,128)(2,1)S(1)} %broadcast_select_fusion.1), channel_id=1, source_target_pairs={{0,2},{2,0},{4,6},{6,4},{8,10},{10,8},{12,14},{14,12},{16,18},{18,... | collective-permute-start | bytes 983048 | tf_op jit(solution)/shard_map/ppermute | solution.py:14
  32.8 7.5 %collective-permute-start.6 = (bf16[128,1280]{0,1:T(8,128)(2,1)S(1)}, bf16[128,1280]{0,1:T(8,128)(2,1)S(1)}, u32[]{:S(2)}, u32[]{:S(2)}) collective-permute-start(bf16[128,1280]{0,1:T(8,128)(2,1)S(1)} %broadcast_select_fusion), channel_id=1, source_target_pairs={{0,2},{2,0},{4,6},{6,4},{8,10},{10,8},{12,14},{14,12},{16,18},{18,... | collective-permute-start | bytes 983048 | tf_op jit(solution)/shard_map/ppermute | solution.py:14
  53.8 8.3 %collective-permute-start.7 = (bf16[384,2560]{1,0:T(8,128)(2,1)}, bf16[384,2560]{1,0:T(8,128)(2,1)S(1)}, u32[]{:S(2)}, u32[]{:S(2)}) collective-permute-start(bf16[384,2560]{1,0:T(8,128)(2,1)} %fusion.7), channel_id=1, source_target_pairs={{0,1},{1,0},{2,3},{3,2},{4,5},{5,4},{6,7},{7,6},{8,9},{9,8},{10,11... | collective-permute-start | bytes 5898248 | tf_op jit(solution)/shard_map/ppermute | solution.py:95

commit v12 on v10

--- a/solution.py
+++ b/solution.py
@@ -25,12 +25,15 @@
     return lax.ppermute(value, "blk", pairs)
 
 
-def relay_chain(own):
+def relay_chain(own, stored=False):
+    def hold(value):
+        return with_layout_constraint(value, Layout(major_to_minor=(0, 1))) if stored else value
+
     position = lax.axis_index("blk") % 4
-    from_y = swap_within_four(own, 2)
-    from_z = shift_groups(from_y)
-    forward = jnp.where((position == 0) | (position == 3), from_y, from_z)
-    from_last = swap_within_four(forward, 1)
+    from_y = hold(swap_within_four(hold(own), 2))
+    from_z = hold(shift_groups(from_y))
+    forward = hold(jnp.where((position == 0) | (position == 3), from_y, from_z))
+    from_last = hold(swap_within_four(forward, 1))
     return [from_y, from_z, from_last]
 
 
@@ -64,10 +67,11 @@
         jnp.zeros((row_count, head_count), jnp.float32),
         jnp.zeros((row_count, head_count, HS), jnp.float32),
     )
+    key_chain = relay_chain(keys, stored=True)
     keys = with_layout_constraint(keys, Layout(major_to_minor=(1, 0)))
     values = with_layout_constraint(values, Layout(major_to_minor=(1, 0)))
     from_x = swap_within_four(jnp.stack((keys, values)), 1)
-    key_arrivals = [from_x[0]] + relay_chain(keys)
+    key_arrivals = [from_x[0]] + key_chain
     value_arrivals = [from_x[1]] + relay_chain(values)
     state = fold_block(state, keys, values, query_heads)
     for key_rows, value_rows in zip(key_arrivals, value_arrivals):

time: 53.8 us -> 75.3 us (1.40)
  matrix products: 16.2 us -> 32.6 us
  local copies, waits for them, and re-layouts: 5.41 us -> 16.9 us
  waiting for transfers between devices: 15.9 us -> 7.81 us
  other arithmetic: 4.57 us -> 8.24 us
  starting transfers between devices: 11.3 us -> 8.71 us
    dot_general x5, matrix products: 2.36 us -> 9.23 us  [fold_block(): jnp.einsum('qhd,khd->qhk', query_heads, key_heads, preferred_element_type...]
    ppermute x5, waiting for transfers between devices: 10.3 us -> 3.67 us  [swap_within_four(): lax.ppermute(value, 'blk', [(source, source ^ bit) for source in range(co...]
    dot_general x5, matrix products: 4.28 us -> 10.2 us  [fold_block(): jnp.einsum('qhk,khd->qhd', weights.astype(jnp.bfloat16), value_heads, pre...]
    another operation x0 -> x3, local copies, waits for them, and re-layouts: none -> 5.62 us  [hold(): with_layout_constraint(value, Layout(major_to_minor=(0, 1)))]
    ppermute x0 -> x3, local copies, waits for them, and re-layouts: none -> 4.96 us  [the longest x2 3.05 us: swap_within_four(): lax.ppermute(value, 'blk', [(source, source ^ bit) for source in range(co...]
    select_n x2, other arithmetic: 0.07 us -> 3.76 us  [relay_chain(): forward = hold(jnp.where((position == 0) | (position == 3), from_y, from_z))]
    dot_general x2, matrix products: 9.54 us -> 13.2 us  [partial_for(): jnp.dot(attended, cols, preferred_element_type=jnp.float32)]
    ppermute x5, starting transfers between devices: 5.92 us -> 3.68 us  [swap_within_four(): lax.ppermute(value, 'blk', [(source, source ^ bit) for source in range(co...]
  transfers between devices with their start and end apart: 8 -> 8, of which waited for: 6 -> 3; matrix products, arithmetic and copies ran while one was open for 29% -> 53% of each run, Pallas kernels for 0% -> 0%
where the time goes in v12:
time: 75.3 us; the launch traced here: 74.4 us
  matrix products  32.6 us (43%)
  local copies, waits for them, and re-layouts  16.9 us (22%)
  starting transfers between devices  8.71 us (12%)
  other arithmetic  8.24 us (11%)
  waiting for transfers between devices  7.81 us (10%)
    dot_general x2, matrix products, partial_for(): jnp.dot(attended, cols, preferred_element_type=jnp.float32)  13.2 us
    dot_general x5, matrix products, fold_block(): jnp.einsum('qhk,khd->qhd', weights.astype(jnp.bfloat16), value_heads, pre...  10.2 us
    dot_general x5, matrix products, fold_block(): jnp.einsum('qhd,khd->qhk', query_heads, key_heads, preferred_element_type...  9.23 us
    another operation x3, local copies, waits for them, and re-layouts, hold(): with_layout_constraint(value, Layout(major_to_minor=(0, 1)))  5.62 us
    unnamed x25, local copies, waits for them, and re-layouts  5.21 us
    ppermute x2, waiting for transfers between devices, shift_groups(): return lax.ppermute(value, 'blk', pairs)  4.15 us
    select_n x2, other arithmetic, relay_chain(): forward = hold(jnp.where((position == 0) | (position == 3), from_y, from_z))  3.76 us
    ppermute x5, starting transfers between devices, swap_within_four(): lax.ppermute(value, 'blk', [(source, source ^ bit) for source in range(co...  3.68 us
  transfers between devices with their start and end apart: 8, of which 3 were waited for; matrix products, arithmetic and copies ran while one was open for 53% of the time, Pallas kernels for 0%

profile of v12, /device:TPU:1, one launch (start us, length us, event | category | flops | bytes accessed | tf_op | source)
XLA Modules:
  0.0 74.4 jit_solution(16158927909023774248)
XLA Ops:
  0.0 2.1 %collective-permute-start.1 = (bf16[128,1280]{1,0:T(8,128)(2,1)}, bf16[128,1280]{1,0:T(8,128)(2,1)}, u32[]{:S(2)}, u32[]{:S(2)}) collective-permute-start(bf16[128,1280]{1,0:T(8,128)(2,1)} %param.5), channel_id=1, source_target_pairs={{0,4},{2,6},{4,0},{6,2},{8,12},{10,14},{12,8},{14,10},{16,20},{18,... | collective-permute-start | bytes 983048 | tf_op jit(solution)/shard_map/ppermute | solution.py:14
  5.4 1.4 %collective-permute-start = (bf16[2,128,1280]{1,2,0:T(8,128)(2,1)}, bf16[2,128,1280]{1,2,0:T(8,128)(2,1)}, u32[]{:S(2)}, u32[]{:S(2)}) collective-permute-start(bf16[2,128,1280]{1,2,0:T(8,128)(2,1)} %pad_maximum_fusion), channel_id=1, source_target_pairs={{0,2},{2,0},{4,6},{6,4},{8,10},{10,8},{12,14},{14,12},{16,18},{18,... | collective-permute-start | bytes 1966088 | tf_op jit(solution)/shard_map/ppermute | solution.py:14
  7.9 1.7 %fusion.38 = f32[10,384,128]{1,2,0:T(8,128)} fusion(bf16[128,10,128]{0,2,1:T(8,128)(2,1)S(1)} %bitcast.117, f32[10,128,384]{2,1,0:T(8,128)S(1)} %get-tuple-element.24, f32[384,10]{0,1:T(8,128)S(1)} %get-tuple-element.23), kind=kOutput, calls=%fused_computation.46 | convolution fusion | flops 127303680 | bytes 4275200 | tf_op jit(solution)/shard_map/qhk,khd->qhd/dot_general | solution.py:51
  11.4 1.9 %copy.35 = bf16[128,1280]{0,1:T(8,128)(2,1)} copy(bf16[128,1280]{1,0:T(8,128)(2,1)} %collective-permute-done.1) | data formatting | bytes 655360 | tf_op jit(solution)/shard_map/layout_constraint | solution.py:30
  13.3 3.5 %collective-permute-done.2 = bf16[128,1280]{1,0:T(8,128)(2,1)} collective-permute-done((bf16[128,1280]{1,0:T(8,128)(2,1)}, bf16[128,1280]{1,0:T(8,128)(2,1)}, u32[]{:S(2)}, u32[]{:S(2)}) %collective-permute-start.2) | collective-permute-done | bytes 327712 | tf_op jit(solution)/shard_map/ppermute | solution.py:14
  16.8 1.9 %copy.39 = bf16[128,1280]{0,1:T(8,128)(2,1)} copy(bf16[128,1280]{1,0:T(8,128)(2,1)} %collective-permute-done.2) | data formatting | bytes 655360 | tf_op jit(solution)/shard_map/ppermute | solution.py:14
  19.9 1.4 %bitcast_reduce_fusion.2 = (f32[384,10]{0,1:T(8,128)S(1)}, f32[10,128,384]{2,1,0:T(8,128)S(1)}) fusion(bf16[128,10,128]{0,2,1:T(8,128)(2,1)} %bitcast.124, bf16[384,10,128]{0,2,1:T(8,128)(2,1)S(1)} %bitcast.112), kind=kOutput, calls=%fused_computation.21 | convolution fusion | flops 126808320 | bytes 3292160 | tf_op jit(solution)/shard_map/qhd,khd->qhk/dot_general | solution.py:45
  21.4 1.9 %broadcast_select_fusion.1 = bf16[128,1280]{1,0:T(8,128)(2,1)} fusion(bf16[128,1280]{1,0:T(8,128)(2,1)} %collective-permute-done.1, bf16[128,1280]{1,0:T(8,128)(2,1)S(1)} %collective-permute-done.3, pred[]{:T(512)S(6)} %or.4), kind=kLoop, calls=%fused_computation.59 | loop fusion | flops 163840 | bytes 983041 | tf_op jit(solution)/shard_map/jit(_where)/select_n | solution.py:35
  24.6 4.1 %collective-permute-done.4 = bf16[128,1280]{1,0:T(8,128)(2,1)S(1)} collective-permute-done((bf16[128,1280]{1,0:T(8,128)(2,1)}, bf16[128,1280]{1,0:T(8,128)(2,1)S(1)}, u32[]{:S(2)}, u32[]{:S(2)}) %collective-permute-start.4) | collective-permute-done | bytes 327712 | tf_op jit(solution)/shard_map/ppermute | solution.py:25
  28.7 1.9 %broadcast_select_fusion = bf16[128,1280]{1,0:T(8,128)(2,1)} fusion(bf16[128,1280]{1,0:T(8,128)(2,1)} %collective-permute-done.2, bf16[128,1280]{1,0:T(8,128)(2,1)S(1)} %collective-permute-done.4, pred[]{:T(512)S(6)} %or.4), kind=kLoop, calls=%fused_computation.58 | loop fusion | flops 163840 | bytes 983041 | tf_op jit(solution)/shard_map/jit(_where)/select_n | solution.py:35
  30.6 1.8 %bitcast_reduce_fusion.3 = (f32[384,10]{0,1:T(8,128)S(1)}, f32[10,128,384]{2,1,0:T(8,128)}) fusion(bf16[128,10,128]{0,2,1:T(8,128)(2,1)S(1)} %bitcast.123, bf16[384,10,128]{0,2,1:T(8,128)(2,1)S(1)} %bitcast.113), kind=kOutput, calls=%fused_computation.26 | convolution fusion | flops 126808320 | bytes 3292160 | tf_op jit(solution)/shard_map/qhd,khd->qhk/dot_general | solution.py:45
  32.4 1.9 %copy.41 = bf16[128,1280]{0,1:T(8,128)(2,1)} copy(bf16[128,1280]{1,0:T(8,128)(2,1)} %copy-done.6) | data formatting | bytes 655360 | tf_op jit(solution)/shard_map/layout_constraint | solution.py:30
  34.2 1.9 %copy.44 = bf16[128,1280]{0,1:T(8,128)(2,1)} copy(bf16[128,1280]{1,0:T(8,128)(2,1)} %copy-done.7) | data formatting | bytes 655360 | tf_op jit(solution)/shard_map/ppermute | solution.py:25
  36.1 2.7 %bitcast_reduce_fusion.1 = (f32[384,10]{0,1:T(8,128)S(1)}, f32[10,128,384]{2,1,0:T(8,128)}) fusion(bf16[128,10,128]{0,2,1:T(8,128)(2,1)} %bitcast.125, bf16[384,10,128]{0,2,1:T(8,128)(2,1)S(1)} %bitcast.114), kind=kOutput, calls=%fused_computation.16 | convolution fusion | flops 126808320 | bytes 3292160 | tf_op jit(solution)/shard_map/qhd,khd->qhk/dot_general | solution.py:45
  38.9 1.9 %copy.46 = bf16[128,1280]{0,1:T(8,128)(2,1)} copy(bf16[128,1280]{1,0:T(8,128)(2,1)} %collective-permute-done.5) | data formatting | bytes 655360 | tf_op jit(solution)/shard_map/layout_constraint | solution.py:30
  40.7 2.9 %bitcast_reduce_fusion = (f32[384,10]{0,1:T(8,128)S(1)}, f32[10,128,384]{2,1,0:T(8,128)}) fusion(bf16[128,10,128]{0,2,1:T(8,128)(2,1)} %bitcast.126, bf16[384,10,128]{0,2,1:T(8,128)(2,1)S(1)} %bitcast.115), kind=kOutput, calls=%fused_computation.11 | convolution fusion | flops 126808320 | bytes 3292160 | tf_op jit(solution)/shard_map/qhd,khd->qhk/dot_general | solution.py:45
  43.6 1.8 %fusion.36 = f32[10,128,384]{2,1,0:T(8,128)} fusion(bf16[128,10,128]{0,2,1:T(8,128)(2,1)S(1)} %bitcast.120, f32[10,128,384]{2,1,0:T(8,128)S(1)} %copy-done, f32[384,10]{0,1:T(8,128)S(1)} %get-tuple-element.13), kind=kOutput, calls=%fused_computation.45 | convolution fusion | flops 127303680 | bytes 4275200 | tf_op jit(solution)/shard_map/qhk,khd->qhd/dot_general | solution.py:51
  46.4 1.8 %fusion.34 = f32[10,384,128]{1,2,0:T(8,128)} fusion(bf16[128,10,128]{0,2,1:T(8,128)(2,1)S(1)} %bitcast.121, f32[10,128,384]{2,1,0:T(8,128)S(1)} %get-tuple-element.22, f32[384,10]{0,1:T(8,128)S(1)} %get-tuple-element.12), kind=kOutput, calls=%fused_computation.44 | convolution fusion | flops 127303680 | bytes 4275200 | tf_op jit(solution)/shard_map/qhk,khd->qhd/dot_general | solution.py:51
  49.3 2.2 %fusion.31 = f32[10,128,384]{2,1,0:T(8,128)S(1)} fusion(bf16[128,10,128]{0,2,1:T(8,128)(2,1)S(1)} %bitcast.122, f32[10,128,384]{2,1,0:T(8,128)} %get-tuple-element.18, f32[384,10]{0,1:T(8,128)S(1)} %get-tuple-element.10), kind=kOutput, calls=%fused_computation.43 | convolution fusion | flops 127303680 | bytes 4275200 | tf_op jit(solution)/shard_map/qhk,khd->qhd/dot_general | solution.py:51
  54.2 2.7 %fusion.11 = bf16[384,10,128]{0,2,1:T(8,128)(2,1)S(1)} fusion(f32[10,128,384]{2,1,0:T(8,128)S(1)} %fusion.31, f32[10,384,128]{1,2,0:T(8,128)} %fusion.34, f32[10,128,384]{2,1,0:T(8,128)S(1)} %copy-done.4, f32[10,384,128]{1,2,0:T(8,128)S(1)} %copy-done.3, bf16[128,10,128]{0,2,1:T(8,128)(2,1)S(1)} %bitcast.127, f32[10,128,384]{2,1,0:T(8,128)S(1)} %copy-done.2, ...), kind=kOutput, calls=%fused_computation.9 | convolution fusion | flops 132710400 | bytes 11248640 | tf_op jit(solution)/shard_map/qhk,khd->qhd/dot_general | solution.py:51
  56.9 7.3 %fusion.7 = bf16[384,2560]{1,0:T(8,128)(2,1)} fusion(bf16[384,1280]{0,1:T(8,128)(2,1)S(1)} %bitcast.128, bf16[1280,5120]{1,0:T(8,128)(2,1)} %param.7, s32[]{:T(128)S(6)} %select_n.37), kind=kOutput, calls=%fused_computation.5 | convolution fusion | flops 2517565440 | bytes 9502724 | tf_op jit(solution)/shard_map/dot_general | solution.py:91
  64.2 2.6 %collective-permute-start.7 = (bf16[384,2560]{1,0:T(8,128)(2,1)}, bf16[384,2560]{1,0:T(8,128)(2,1)S(1)}, u32[]{:S(2)}, u32[]{:S(2)}) collective-permute-start(bf16[384,2560]{1,0:T(8,128)(2,1)} %fusion.7), channel_id=1, source_target_pairs={{0,1},{1,0},{2,3},{3,2},{4,5},{5,4},{6,7},{7,6},{8,9},{9,8},{10,11... | collective-permute-start | bytes 5898248 | tf_op jit(solution)/shard_map/ppermute | solution.py:97
  66.7 5.9 %fusion.4 = bf16[384,2560]{1,0:T(8,128)(2,1)S(1)} fusion(bf16[384,1280]{0,1:T(8,128)(2,1)} %bitcast.129, bf16[1280,5120]{1,0:T(8,128)(2,1)} %param.7, s32[]{:T(128)S(6)} %select_n.35), kind=kOutput, calls=%fused_computation.4 | convolution fusion | flops 2517565440 | bytes 9502724 | tf_op jit(solution)/shard_map/dot_general | solution.py:91
  72.7 1.7 %add_convert_fusion = bf16[384,2560]{1,0:T(8,128)(2,1)} fusion(bf16[384,2560]{1,0:T(8,128)(2,1)S(1)} %collective-permute-done.7, bf16[384,2560]{1,0:T(8,128)(2,1)S(1)} %fusion.4), kind=kLoop, calls=%fused_computation.6 | loop fusion | flops 3932160 | bytes 5898240 | tf_op jit(solution)/shard_map/convert_element_type | solution.py:101
  (45 shorter events, 13.6 us)
Async XLA Ops:
  0.0 6.8 %copy-start.8 = (bf16[384,1280]{1,0:T(8,128)(2,1)S(1)}, bf16[384,1280]{1,0:T(8,128)(2,1)}, u32[]{:S(2)}) copy-start(bf16[384,1280]{1,0:T(8,128)(2,1)} %param.4) | copy-start | bytes 2949124
  0.0 9.8 %collective-permute-start.1 = (bf16[128,1280]{1,0:T(8,128)(2,1)}, bf16[128,1280]{1,0:T(8,128)(2,1)}, u32[]{:S(2)}, u32[]{:S(2)}) collective-permute-start(bf16[128,1280]{1,0:T(8,128)(2,1)} %param.5), channel_id=1, source_target_pairs={{0,4},{2,6},{4,0},{6,2},{8,12},{10,14},{12,8},{14,10},{16,20},{18,... | collective-permute-start | bytes 983048 | tf_op jit(solution)/shard_map/ppermute | solution.py:14
  2.1 14.7 %collective-permute-start.2 = (bf16[128,1280]{1,0:T(8,128)(2,1)}, bf16[128,1280]{1,0:T(8,128)(2,1)}, u32[]{:S(2)}, u32[]{:S(2)}) collective-permute-start(bf16[128,1280]{1,0:T(8,128)(2,1)} %param.6), channel_id=1, source_target_pairs={{0,4},{2,6},{4,0},{6,2},{8,12},{10,14},{12,8},{14,10},{16,20},{18,... | collective-permute-start | bytes 983048 | tf_op jit(solution)/shard_map/ppermute | solution.py:14
  5.4 18.0 %collective-permute-start = (bf16[2,128,1280]{1,2,0:T(8,128)(2,1)}, bf16[2,128,1280]{1,2,0:T(8,128)(2,1)}, u32[]{:S(2)}, u32[]{:S(2)}) collective-permute-start(bf16[2,128,1280]{1,2,0:T(8,128)(2,1)} %pad_maximum_fusion), channel_id=1, source_target_pairs={{0,2},{2,0},{4,6},{6,4},{8,10},{10,8},{12,14},{14,12},{16,18},{18,... | collective-permute-start | bytes 1966088 | tf_op jit(solution)/shard_map/ppermute | solution.py:14
  9.8 11.6 %collective-permute-start.3 = (bf16[128,1280]{1,0:T(8,128)(2,1)}, bf16[128,1280]{1,0:T(8,128)(2,1)S(1)}, u32[]{:S(2)}, u32[]{:S(2)}) collective-permute-start(bf16[128,1280]{1,0:T(8,128)(2,1)} %collective-permute-done.1), channel_id=1, source_target_pairs={{0,8},{2,10},{4,28},{6,30},{8,16},{10,18},{12,4},{14,6},{16,24},{1... | collective-permute-start | bytes 983048 | tf_op jit(solution)/shard_map/ppermute | solution.py:25
  18.7 10.0 %collective-permute-start.4 = (bf16[128,1280]{1,0:T(8,128)(2,1)}, bf16[128,1280]{1,0:T(8,128)(2,1)S(1)}, u32[]{:S(2)}, u32[]{:S(2)}) collective-permute-start(bf16[128,1280]{1,0:T(8,128)(2,1)} %collective-permute-done.2), channel_id=1, source_target_pairs={{0,8},{2,10},{4,28},{6,30},{8,16},{10,18},{12,4},{14,6},{16,24},{1... | collective-permute-start | bytes 983048 | tf_op jit(solution)/shard_map/ppermute | solution.py:25
  21.4 2.1 %copy-start.6 = (bf16[128,1280]{1,0:T(8,128)(2,1)}, bf16[128,1280]{1,0:T(8,128)(2,1)S(1)}, u32[]{:S(2)}) copy-start(bf16[128,1280]{1,0:T(8,128)(2,1)S(1)} %collective-permute-done.3) | copy-start | bytes 983044
  23.3 15.6 %collective-permute-start.5 = (bf16[128,1280]{1,0:T(8,128)(2,1)}, bf16[128,1280]{1,0:T(8,128)(2,1)}, u32[]{:S(2)}, u32[]{:S(2)}) collective-permute-start(bf16[128,1280]{1,0:T(8,128)(2,1)} %broadcast_select_fusion.1), channel_id=1, source_target_pairs={{0,2},{2,0},{4,6},{6,4},{8,10},{10,8},{12,14},{14,12},{16,18},{18,... | collective-permute-start | bytes 983048 | tf_op jit(solution)/shard_map/ppermute | solution.py:14
  28.7 3.6 %copy-start.7 = (bf16[128,1280]{1,0:T(8,128)(2,1)}, bf16[128,1280]{1,0:T(8,128)(2,1)S(1)}, u32[]{:S(2)}) copy-start(bf16[128,1280]{1,0:T(8,128)(2,1)S(1)} %collective-permute-done.4) | copy-start | bytes 983044
  32.4 15.7 %collective-permute-start.6 = (bf16[128,1280]{1,0:T(8,128)(2,1)}, bf16[128,1280]{1,0:T(8,128)(2,1)}, u32[]{:S(2)}, u32[]{:S(2)}) collective-permute-start(bf16[128,1280]{1,0:T(8,128)(2,1)} %broadcast_select_fusion), channel_id=1, source_target_pairs={{0,2},{2,0},{4,6},{6,4},{8,10},{10,8},{12,14},{14,12},{16,18},{18,... | collective-permute-start | bytes 983048 | tf_op jit(solution)/shard_map/ppermute | solution.py:14
  40.7 2.9 %copy-start = (f32[10,128,384]{2,1,0:T(8,128)S(1)}, f32[10,128,384]{2,1,0:T(8,128)}, u32[]{:S(2)}) copy-start(f32[10,128,384]{2,1,0:T(8,128)} %get-tuple-element.26) | copy-start | bytes 5898244
  45.4 1.0 %copy-start.5 = (bf16[128,1280]{0,1:T(8,128)(2,1)S(1)}, bf16[128,1280]{0,1:T(8,128)(2,1)}, u32[]{:S(2)}) copy-start(bf16[128,1280]{0,1:T(8,128)(2,1)} %copy.39) | copy-start | bytes 983044
  49.3 2.2 %copy-start.1 = (f32[10,128,384]{2,1,0:T(8,128)S(1)}, f32[10,128,384]{2,1,0:T(8,128)}, u32[]{:S(2)}) copy-start(f32[10,128,384]{2,1,0:T(8,128)} %get-tuple-element.18) | copy-start | bytes 5898244
  49.3 2.7 %copy-start.2 = (f32[10,128,384]{2,1,0:T(8,128)S(1)}, f32[10,128,384]{2,1,0:T(8,128)}, u32[]{:S(2)}) copy-start(f32[10,128,384]{2,1,0:T(8,128)} %get-tuple-element.20) | copy-start | bytes 5898244
  52.0 1.5 %copy-start.3 = (f32[10,384,128]{1,2,0:T(8,128)S(1)}, f32[10,384,128]{1,2,0:T(8,128)}, u32[]{:S(2)}) copy-start(f32[10,384,128]{1,2,0:T(8,128)} %fusion.38) | copy-start | bytes 5898244
  52.0 2.1 %copy-start.4 = (f32[10,128,384]{2,1,0:T(8,128)S(1)}, f32[10,128,384]{2,1,0:T(8,128)}, u32[]{:S(2)}) copy-start(f32[10,128,384]{2,1,0:T(8,128)} %fusion.36) | copy-start | bytes 5898244
  52.0 2.2 %copy-start.9 = (bf16[128,1280]{0,1:T(8,128)(2,1)S(1)}, bf16[128,1280]{0,1:T(8,128)(2,1)}, u32[]{:S(2)}) copy-start(bf16[128,1280]{0,1:T(8,128)(2,1)} %copy.44) | copy-start | bytes 983044
  56.9 7.3 %copy-start.10 = (bf16[384,10,128]{0,2,1:T(8,128)(2,1)}, bf16[384,10,128]{0,2,1:T(8,128)(2,1)S(1)}, u32[]{:S(2)}) copy-start(bf16[384,10,128]{0,2,1:T(8,128)(2,1)S(1)} %fusion.11) | copy-start | bytes 2949124
  64.2 8.5 %collective-permute-start.7 = (bf16[384,2560]{1,0:T(8,128)(2,1)}, bf16[384,2560]{1,0:T(8,128)(2,1)S(1)}, u32[]{:S(2)}, u32[]{:S(2)}) collective-permute-start(bf16[384,2560]{1,0:T(8,128)(2,1)} %fusion.7), channel_id=1, source_target_pairs={{0,1},{1,0},{2,3},{3,2},{4,5},{5,4},{6,7},{7,6},{8,9},{9,8},{10,11... | collective-permute-start | bytes 5898248 | tf_op jit(solution)/shard_map/ppermute | solution.py:97

commit v13 on v10

--- a/solution.py
+++ b/solution.py
@@ -25,12 +25,20 @@
     return lax.ppermute(value, "blk", pairs)
 
 
+def swap_pairs(value, pairs):
+    count = lax.axis_size("blk")
+    return lax.ppermute(
+        value, "blk", [(s, s ^ 1) for s in range(count) if (s % 4) in pairs]
+    )
+
+
 def relay_chain(own):
     position = lax.axis_index("blk") % 4
     from_y = swap_within_four(own, 2)
     from_z = shift_groups(from_y)
-    forward = jnp.where((position == 0) | (position == 3), from_y, from_z)
-    from_last = swap_within_four(forward, 1)
+    last_via_y = swap_pairs(from_y, (0, 3))
+    last_via_z = swap_pairs(from_z, (1, 2))
+    from_last = jnp.where((position == 1) | (position == 2), last_via_y, last_via_z)
     return [from_y, from_z, from_last]
 
 

time: 53.8 us -> 63.5 us (1.18)
  starting transfers between devices: 11.3 us -> 16.3 us
  waiting for transfers between devices: 15.9 us -> 19.1 us
  matrix products: 16.2 us -> 18.4 us
  local copies, waits for them, and re-layouts: 5.41 us -> 4.3 us
    ppermute x0 -> x4, waiting for transfers between devices: none -> 11.1 us  [swap_pairs(): lax.ppermute(value, 'blk', [(s, s ^ 1) for s in range(count) if s % 4 in...]
    ppermute x0 -> x4, starting transfers between devices: none -> 7.2 us  [swap_pairs(): lax.ppermute(value, 'blk', [(s, s ^ 1) for s in range(count) if s % 4 in...]
    ppermute x2, waiting for transfers between devices: 5.59 us -> 1.16 us  [shift_groups(): return lax.ppermute(value, 'blk', pairs)]
    ppermute x5 -> x3, waiting for transfers between devices: 10.3 us -> 6.85 us  [swap_within_four(): lax.ppermute(value, 'blk', [(source, source ^ bit) for source in range(co...]
    ppermute x5 -> x3, starting transfers between devices: 5.92 us -> 3.63 us  [swap_within_four(): lax.ppermute(value, 'blk', [(source, source ^ bit) for source in range(co...]
    dot_general x5, matrix products: 4.28 us -> 5.44 us  [fold_block(): jnp.einsum('qhk,khd->qhd', weights.astype(jnp.bfloat16), value_heads, pre...]
    slice x1, local copies, waits for them, and re-layouts: 1.12 us -> 0.04 us  [on_device(): value_arrivals = [from_x[1]] + relay_chain(values)]
    dot_general x5, matrix products: 2.36 us -> 3.37 us  [fold_block(): jnp.einsum('qhd,khd->qhk', query_heads, key_heads, preferred_element_type...]
  transfers between devices with their start and end apart: 8 -> 10, of which waited for: 6 -> 5; matrix products, arithmetic and copies ran while one was open for 29% -> 21% of each run, Pallas kernels for 0% -> 0%
where the time goes in v13:
time: 63.5 us; the launch traced here: 62.9 us
  waiting for transfers between devices  19.1 us (30%)
  matrix products  18.4 us (29%)
  starting transfers between devices  16.3 us (26%)
  other arithmetic  4.51 us (7%)
  local copies, waits for them, and re-layouts  4.3 us (7%)
    ppermute x4, waiting for transfers between devices, swap_pairs(): lax.ppermute(value, 'blk', [(s, s ^ 1) for s in range(count) if s % 4 in...  11.1 us
    dot_general x2, matrix products, partial_for(): jnp.dot(attended, cols, preferred_element_type=jnp.float32)  9.57 us
    ppermute x4, starting transfers between devices, swap_pairs(): lax.ppermute(value, 'blk', [(s, s ^ 1) for s in range(count) if s % 4 in...  7.2 us
    ppermute x3, waiting for transfers between devices, swap_within_four(): lax.ppermute(value, 'blk', [(source, source ^ bit) for source in range(co...  6.85 us
    dot_general x5, matrix products, fold_block(): jnp.einsum('qhk,khd->qhd', weights.astype(jnp.bfloat16), value_heads, pre...  5.44 us
    unnamed x15, local copies, waits for them, and re-layouts  4.25 us
    ppermute x3, starting transfers between devices, swap_within_four(): lax.ppermute(value, 'blk', [(source, source ^ bit) for source in range(co...  3.63 us
    dot_general x5, matrix products, fold_block(): jnp.einsum('qhd,khd->qhk', query_heads, key_heads, preferred_element_type...  3.37 us
  transfers between devices with their start and end apart: 10, of which 5 were waited for; matrix products, arithmetic and copies ran while one was open for 21% of the time, Pallas kernels for 0%

profile of v13, /device:TPU:1, one launch (start us, length us, event | category | flops | bytes accessed | tf_op | source)
XLA Modules:
  0.0 62.9 jit_solution(6495538253406885681)
XLA Ops:
  0.0 1.3 %copy.24 = bf16[128,1280]{0,1:T(8,128)(2,1)S(1)} copy(bf16[128,1280]{1,0:T(8,128)(2,1)} %param.6) | data formatting | bytes 655360 | tf_op args[2]
  1.3 2.1 %collective-permute-start.2 = (bf16[128,1280]{0,1:T(8,128)(2,1)S(1)}, bf16[128,1280]{0,1:T(8,128)(2,1)}, u32[]{:S(2)}, u32[]{:S(2)}) collective-permute-start(bf16[128,1280]{0,1:T(8,128)(2,1)S(1)} %copy.24), channel_id=1, source_target_pairs={{0,4},{2,6},{4,0},{6,2},{8,12},{10,14},{12,8},{14,10},{16,20},{18,... | collective-permute-start | bytes 983048 | tf_op jit(solution)/shard_map/ppermute | solution.py:14
  3.4 1.2 %copy.21 = bf16[128,1280]{0,1:T(8,128)(2,1)S(1)} copy(bf16[128,1280]{1,0:T(8,128)(2,1)} %param.5) | data formatting | bytes 655360 | tf_op args[1]
  5.5 1.4 %collective-permute-start = (bf16[2,128,1280]{1,2,0:T(8,128)(2,1)}, bf16[2,128,1280]{1,2,0:T(8,128)(2,1)S(1)}, u32[]{:S(2)}, u32[]{:S(2)}) collective-permute-start(bf16[2,128,1280]{1,2,0:T(8,128)(2,1)} %pad_maximum_fusion), channel_id=1, source_target_pairs={{0,2},{2,0},{4,6},{6,4},{8,10},{10,8},{12,14},{14,12},{16,18},{18,... | collective-permute-start | bytes 1966088 | tf_op jit(solution)/shard_map/ppermute | solution.py:14
  8.1 1.7 %fusion.38 = f32[10,384,128]{1,2,0:T(8,128)} fusion(bf16[128,10,128]{0,2,1:T(8,128)(2,1)S(1)} %bitcast.117, f32[10,128,384]{2,1,0:T(8,128)S(1)} %get-tuple-element.24, f32[384,10]{0,1:T(8,128)S(1)} %get-tuple-element.23), kind=kOutput, calls=%fused_computation.46 | convolution fusion | flops 127303680 | bytes 4275200 | tf_op jit(solution)/shard_map/qhk,khd->qhd/dot_general | solution.py:56
  9.8 1.1 %collective-permute-done.2 = bf16[128,1280]{0,1:T(8,128)(2,1)} collective-permute-done((bf16[128,1280]{0,1:T(8,128)(2,1)S(1)}, bf16[128,1280]{0,1:T(8,128)(2,1)}, u32[]{:S(2)}, u32[]{:S(2)}) %collective-permute-start.2) | collective-permute-done | bytes 327712 | tf_op jit(solution)/shard_map/ppermute | solution.py:14
  10.9 1.2 %collective-permute-start.4 = (bf16[128,1280]{0,1:T(8,128)(2,1)}, bf16[128,1280]{0,1:T(8,128)(2,1)S(1)}, u32[]{:S(2)}, u32[]{:S(2)}) collective-permute-start(bf16[128,1280]{0,1:T(8,128)(2,1)} %collective-permute-done.2), channel_id=1, source_target_pairs={{0,8},{2,10},{4,28},{6,30},{8,16},{10,18},{12,4},{14,6},{16,24},{1... | collective-permute-start | bytes 983048 | tf_op jit(solution)/shard_map/ppermute | solution.py:25
  12.1 5.8 %collective-permute-done.1 = bf16[128,1280]{0,1:T(8,128)(2,1)} collective-permute-done((bf16[128,1280]{0,1:T(8,128)(2,1)S(1)}, bf16[128,1280]{0,1:T(8,128)(2,1)}, u32[]{:S(2)}, u32[]{:S(2)}) %collective-permute-start.1) | collective-permute-done | bytes 327712 | tf_op jit(solution)/shard_map/ppermute | solution.py:14
  17.9 1.2 %collective-permute-start.3 = (bf16[128,1280]{0,1:T(8,128)(2,1)}, bf16[128,1280]{0,1:T(8,128)(2,1)S(1)}, u32[]{:S(2)}, u32[]{:S(2)}) collective-permute-start(bf16[128,1280]{0,1:T(8,128)(2,1)} %collective-permute-done.1), channel_id=1, source_target_pairs={{0,8},{2,10},{4,28},{6,30},{8,16},{10,18},{12,4},{14,6},{16,24},{1... | collective-permute-start | bytes 983048 | tf_op jit(solution)/shard_map/ppermute | solution.py:25
  19.6 3.1 %collective-permute-start.7 = (bf16[128,1280]{0,1:T(8,128)(2,1)}, bf16[128,1280]{0,1:T(8,128)(2,1)S(1)}, u32[]{:S(2)}, u32[]{:S(2)}) collective-permute-start(bf16[128,1280]{0,1:T(8,128)(2,1)} %collective-permute-done.2), channel_id=1, source_target_pairs={{0,2},{6,4},{8,10},{14,12},{16,18},{22,20},{24,26},{30,28},{1,3},{... | collective-permute-start | bytes 983048 | tf_op jit(solution)/shard_map/ppermute | solution.py:30
  22.7 1.3 %collective-permute-start.5 = (bf16[128,1280]{0,1:T(8,128)(2,1)}, bf16[128,1280]{0,1:T(8,128)(2,1)S(1)}, u32[]{:S(2)}, u32[]{:S(2)}) collective-permute-start(bf16[128,1280]{0,1:T(8,128)(2,1)} %collective-permute-done.1), channel_id=1, source_target_pairs={{0,2},{6,4},{8,10},{14,12},{16,18},{22,20},{24,26},{30,28},{1,3},{... | collective-permute-start | bytes 983048 | tf_op jit(solution)/shard_map/ppermute | solution.py:30
  24.0 1.5 %bitcast_reduce_fusion.2 = (f32[384,10]{0,1:T(8,128)S(1)}, f32[10,128,384]{2,1,0:T(8,128)S(1)}) fusion(bf16[128,10,128]{0,2,1:T(8,128)(2,1)} %bitcast.11, bf16[384,10,128]{0,2,1:T(8,128)(2,1)S(1)} %bitcast.112), kind=kOutput, calls=%fused_computation.21 | convolution fusion | flops 126808320 | bytes 3292160 | tf_op jit(solution)/shard_map/qhd,khd->qhk/dot_general | solution.py:50
  25.5 1.3 %collective-permute-start.8 = (bf16[128,1280]{0,1:T(8,128)(2,1)S(1)}, bf16[128,1280]{0,1:T(8,128)(2,1)S(1)}, u32[]{:S(2)}, u32[]{:S(2)}) collective-permute-start(bf16[128,1280]{0,1:T(8,128)(2,1)S(1)} %collective-permute-done.4), channel_id=1, source_target_pairs={{2,0},{4,6},{10,8},{12,14},{18,16},{20,22},{26,24},{28,30},{3,1},{... | collective-permute-start | bytes 983048 | tf_op jit(solution)/shard_map/ppermute | solution.py:30
  26.8 1.2 %collective-permute-done.3 = bf16[128,1280]{0,1:T(8,128)(2,1)S(1)} collective-permute-done((bf16[128,1280]{0,1:T(8,128)(2,1)}, bf16[128,1280]{0,1:T(8,128)(2,1)S(1)}, u32[]{:S(2)}, u32[]{:S(2)}) %collective-permute-start.3) | collective-permute-done | bytes 327712 | tf_op jit(solution)/shard_map/ppermute | solution.py:25
  28.0 1.5 %collective-permute-start.6 = (bf16[128,1280]{0,1:T(8,128)(2,1)S(1)}, bf16[128,1280]{0,1:T(8,128)(2,1)S(1)}, u32[]{:S(2)}, u32[]{:S(2)}) collective-permute-start(bf16[128,1280]{0,1:T(8,128)(2,1)S(1)} %collective-permute-done.3), channel_id=1, source_target_pairs={{2,0},{4,6},{10,8},{12,14},{18,16},{20,22},{26,24},{28,30},{3,1},{... | collective-permute-start | bytes 983048 | tf_op jit(solution)/shard_map/ppermute | solution.py:30
  30.5 4.8 %collective-permute-done.5 = bf16[128,1280]{0,1:T(8,128)(2,1)S(1)} collective-permute-done((bf16[128,1280]{0,1:T(8,128)(2,1)}, bf16[128,1280]{0,1:T(8,128)(2,1)S(1)}, u32[]{:S(2)}, u32[]{:S(2)}) %collective-permute-start.5) | collective-permute-done | bytes 327712 | tf_op jit(solution)/shard_map/ppermute | solution.py:30
  35.3 6.3 %collective-permute-done.6 = bf16[128,1280]{0,1:T(8,128)(2,1)S(1)} collective-permute-done((bf16[128,1280]{0,1:T(8,128)(2,1)S(1)}, bf16[128,1280]{0,1:T(8,128)(2,1)S(1)}, u32[]{:S(2)}, u32[]{:S(2)}) %collective-permute-start.6) | collective-permute-done | bytes 327712 | tf_op jit(solution)/shard_map/ppermute | solution.py:30
  43.4 1.6 %fusion.34 = f32[10,384,128]{1,2,0:T(8,128)S(1)} fusion(bf16[128,10,128]{0,2,1:T(8,128)(2,1)} %bitcast.13, f32[10,128,384]{2,1,0:T(8,128)S(1)} %get-tuple-element.22, f32[384,10]{0,1:T(8,128)S(1)} %get-tuple-element.12), kind=kOutput, calls=%fused_computation.44 | convolution fusion | flops 127303680 | bytes 4275200 | tf_op jit(solution)/shard_map/qhk,khd->qhd/dot_general | solution.py:56
  46.2 1.1 %copy-done = f32[10,384,128]{1,2,0:T(8,128)S(1)} copy-done((f32[10,384,128]{1,2,0:T(8,128)S(1)}, f32[10,384,128]{1,2,0:T(8,128)}, u32[]{:S(2)}) %copy-start) | copy-done | bytes 1966104
  47.4 1.2 %fusion.11 = bf16[384,10,128]{0,2,1:T(8,128)(2,1)S(1)} fusion(f32[10,384,128]{1,2,0:T(8,128)S(1)} %fusion.32, f32[10,384,128]{1,2,0:T(8,128)S(1)} %fusion.34, f32[10,128,384]{2,1,0:T(8,128)S(1)} %fusion.36, f32[10,384,128]{1,2,0:T(8,128)S(1)} %copy-done, bf16[128,10,128]{0,2,1:T(8,128)(2,1)S(1)} %bitcast.125, f32[10,128,384]{2,1,0:T(8,128)S(1)} %get-tuple-element.18, ...), kind=kOutput, calls=%fused_computation.9 | convolution fusion | flops 132710400 | bytes 11248640 | tf_op jit(solution)/shard_map/qhk,khd->qhd/dot_general | solution.py:56
  48.6 4.0 %fusion.7 = bf16[384,2560]{1,0:T(8,128)(2,1)} fusion(bf16[384,1280]{0,1:T(8,128)(2,1)S(1)} %bitcast.128, bf16[1280,5120]{1,0:T(8,128)(2,1)S(1)} %bitcast.127, s32[]{:T(128)S(6)} %select_n.37), kind=kOutput, calls=%fused_computation.5 | convolution fusion | flops 2517565440 | bytes 9502724 | tf_op jit(solution)/shard_map/dot_general | solution.py:95
  52.6 3.0 %collective-permute-start.9 = (bf16[384,2560]{1,0:T(8,128)(2,1)}, bf16[384,2560]{1,0:T(8,128)(2,1)S(1)}, u32[]{:S(2)}, u32[]{:S(2)}) collective-permute-start(bf16[384,2560]{1,0:T(8,128)(2,1)} %fusion.7), channel_id=1, source_target_pairs={{0,1},{1,0},{2,3},{3,2},{4,5},{5,4},{6,7},{7,6},{8,9},{9,8},{10,11... | collective-permute-start | bytes 5898248 | tf_op jit(solution)/shard_map/ppermute | solution.py:101
  55.5 5.6 %fusion.4 = bf16[384,2560]{1,0:T(8,128)(2,1)S(1)} fusion(bf16[384,1280]{0,1:T(8,128)(2,1)S(1)} %bitcast.129, bf16[1280,5120]{1,0:T(8,128)(2,1)} %param.7, s32[]{:T(128)S(6)} %select_n.35), kind=kOutput, calls=%fused_computation.4 | convolution fusion | flops 2517565440 | bytes 9502724 | tf_op jit(solution)/shard_map/dot_general | solution.py:95
  61.2 1.7 %add_convert_fusion = bf16[384,2560]{1,0:T(8,128)(2,1)} fusion(bf16[384,2560]{1,0:T(8,128)(2,1)S(1)} %collective-permute-done.9, bf16[384,2560]{1,0:T(8,128)(2,1)S(1)} %fusion.4), kind=kLoop, calls=%fused_computation.6 | loop fusion | flops 3932160 | bytes 5898240 | tf_op jit(solution)/shard_map/convert_element_type | solution.py:105
  (35 shorter events, 6.4 us)
Async XLA Ops:
  0.0 7.0 %copy-start.1 = (bf16[384,1280]{1,0:T(8,128)(2,1)S(1)}, bf16[384,1280]{1,0:T(8,128)(2,1)}, u32[]{:S(2)}) copy-start(bf16[384,1280]{1,0:T(8,128)(2,1)} %param.4) | copy-start | bytes 2949124
  1.3 9.6 %collective-permute-start.2 = (bf16[128,1280]{0,1:T(8,128)(2,1)S(1)}, bf16[128,1280]{0,1:T(8,128)(2,1)}, u32[]{:S(2)}, u32[]{:S(2)}) collective-permute-start(bf16[128,1280]{0,1:T(8,128)(2,1)S(1)} %copy.24), channel_id=1, source_target_pairs={{0,4},{2,6},{4,0},{6,2},{8,12},{10,14},{12,8},{14,10},{16,20},{18,... | collective-permute-start | bytes 983048 | tf_op jit(solution)/shard_map/ppermute | solution.py:14
  4.6 13.4 %collective-permute-start.1 = (bf16[128,1280]{0,1:T(8,128)(2,1)S(1)}, bf16[128,1280]{0,1:T(8,128)(2,1)}, u32[]{:S(2)}, u32[]{:S(2)}) collective-permute-start(bf16[128,1280]{0,1:T(8,128)(2,1)S(1)} %copy.21), channel_id=1, source_target_pairs={{0,4},{2,6},{4,0},{6,2},{8,12},{10,14},{12,8},{14,10},{16,20},{18,... | collective-permute-start | bytes 983048 | tf_op jit(solution)/shard_map/ppermute | solution.py:14
  5.5 23.9 %collective-permute-start = (bf16[2,128,1280]{1,2,0:T(8,128)(2,1)}, bf16[2,128,1280]{1,2,0:T(8,128)(2,1)S(1)}, u32[]{:S(2)}, u32[]{:S(2)}) collective-permute-start(bf16[2,128,1280]{1,2,0:T(8,128)(2,1)} %pad_maximum_fusion), channel_id=1, source_target_pairs={{0,2},{2,0},{4,6},{6,4},{8,10},{10,8},{12,14},{14,12},{16,18},{18,... | collective-permute-start | bytes 1966088 | tf_op jit(solution)/shard_map/ppermute | solution.py:14
  10.9 14.6 %collective-permute-start.4 = (bf16[128,1280]{0,1:T(8,128)(2,1)}, bf16[128,1280]{0,1:T(8,128)(2,1)S(1)}, u32[]{:S(2)}, u32[]{:S(2)}) collective-permute-start(bf16[128,1280]{0,1:T(8,128)(2,1)} %collective-permute-done.2), channel_id=1, source_target_pairs={{0,8},{2,10},{4,28},{6,30},{8,16},{10,18},{12,4},{14,6},{16,24},{1... | collective-permute-start | bytes 983048 | tf_op jit(solution)/shard_map/ppermute | solution.py:25
  17.9 10.0 %collective-permute-start.3 = (bf16[128,1280]{0,1:T(8,128)(2,1)}, bf16[128,1280]{0,1:T(8,128)(2,1)S(1)}, u32[]{:S(2)}, u32[]{:S(2)}) collective-permute-start(bf16[128,1280]{0,1:T(8,128)(2,1)} %collective-permute-done.1), channel_id=1, source_target_pairs={{0,8},{2,10},{4,28},{6,30},{8,16},{10,18},{12,4},{14,6},{16,24},{1... | collective-permute-start | bytes 983048 | tf_op jit(solution)/shard_map/ppermute | solution.py:25
  19.6 10.9 %collective-permute-start.7 = (bf16[128,1280]{0,1:T(8,128)(2,1)}, bf16[128,1280]{0,1:T(8,128)(2,1)S(1)}, u32[]{:S(2)}, u32[]{:S(2)}) collective-permute-start(bf16[128,1280]{0,1:T(8,128)(2,1)} %collective-permute-done.2), channel_id=1, source_target_pairs={{0,2},{6,4},{8,10},{14,12},{16,18},{22,20},{24,26},{30,28},{1,3},{... | collective-permute-start | bytes 983048 | tf_op jit(solution)/shard_map/ppermute | solution.py:30
  22.7 12.6 %collective-permute-start.5 = (bf16[128,1280]{0,1:T(8,128)(2,1)}, bf16[128,1280]{0,1:T(8,128)(2,1)S(1)}, u32[]{:S(2)}, u32[]{:S(2)}) collective-permute-start(bf16[128,1280]{0,1:T(8,128)(2,1)} %collective-permute-done.1), channel_id=1, source_target_pairs={{0,2},{6,4},{8,10},{14,12},{16,18},{22,20},{24,26},{30,28},{1,3},{... | collective-permute-start | bytes 983048 | tf_op jit(solution)/shard_map/ppermute | solution.py:30
  25.5 9.8 %collective-permute-start.8 = (bf16[128,1280]{0,1:T(8,128)(2,1)S(1)}, bf16[128,1280]{0,1:T(8,128)(2,1)S(1)}, u32[]{:S(2)}, u32[]{:S(2)}) collective-permute-start(bf16[128,1280]{0,1:T(8,128)(2,1)S(1)} %collective-permute-done.4), channel_id=1, source_target_pairs={{2,0},{4,6},{10,8},{12,14},{18,16},{20,22},{26,24},{28,30},{3,1},{... | collective-permute-start | bytes 983048 | tf_op jit(solution)/shard_map/ppermute | solution.py:30
  28.0 13.6 %collective-permute-start.6 = (bf16[128,1280]{0,1:T(8,128)(2,1)S(1)}, bf16[128,1280]{0,1:T(8,128)(2,1)S(1)}, u32[]{:S(2)}, u32[]{:S(2)}) collective-permute-start(bf16[128,1280]{0,1:T(8,128)(2,1)S(1)} %collective-permute-done.3), channel_id=1, source_target_pairs={{2,0},{4,6},{10,8},{12,14},{18,16},{20,22},{26,24},{28,30},{3,1},{... | collective-permute-start | bytes 983048 | tf_op jit(solution)/shard_map/ppermute | solution.py:30
  29.5 19.1 %slice-start = ((s8[13107200]{0:T(1024)(128)(4,1)}), s8[4194304]{0:T(1024)(128)(4,1)S(1)}, s32[]{:S(2)}) async-start(s8[13107200]{0:T(1024)(128)(4,1)} %bitcast.126), calls=%async_computation | async-start | bytes 8388608
  41.7 6.9 %slice-start.1 = ((s8[13107200]{0:T(1024)(128)(4,1)}), s8[4194304]{0:T(1024)(128)(4,1)S(1)}, s32[]{:S(2)}) async-start(s8[13107200]{0:T(1024)(128)(4,1)} %bitcast.126), calls=%async_computation.1 | async-start | bytes 8388608
  43.4 5.2 %slice-start.2 = ((s8[13107200]{0:T(1024)(128)(4,1)}), s8[4194304]{0:T(1024)(128)(4,1)S(1)}, s32[]{:S(2)}) async-start(s8[13107200]{0:T(1024)(128)(4,1)} %bitcast.126), calls=%async_computation.2 | async-start | bytes 8388608
  45.8 1.5 %copy-start = (f32[10,384,128]{1,2,0:T(8,128)S(1)}, f32[10,384,128]{1,2,0:T(8,128)}, u32[]{:S(2)}) copy-start(f32[10,384,128]{1,2,0:T(8,128)} %fusion.38) | copy-start | bytes 5898244
  47.4 1.2 %slice-start.3 = ((s8[13107200]{0:T(1024)(128)(4,1)}), s8[524288]{0:T(1024)(128)(4,1)S(1)}, s32[]{:S(2)}) async-start(s8[13107200]{0:T(1024)(128)(4,1)} %bitcast.126), calls=%async_computation.3 | async-start | bytes 1048576
  52.6 8.6 %collective-permute-start.9 = (bf16[384,2560]{1,0:T(8,128)(2,1)}, bf16[384,2560]{1,0:T(8,128)(2,1)S(1)}, u32[]{:S(2)}, u32[]{:S(2)}) collective-permute-start(bf16[384,2560]{1,0:T(8,128)(2,1)} %fusion.7), channel_id=1, source_target_pairs={{0,1},{1,0},{2,3},{3,2},{4,5},{5,4},{6,7},{7,6},{8,9},{9,8},{10,11... | collective-permute-start | bytes 5898248 | tf_op jit(solution)/shard_map/ppermute | solution.py:101

commit v14 on v10

--- a/solution.py
+++ b/solution.py
@@ -69,8 +69,9 @@
     from_x = swap_within_four(jnp.stack((keys, values)), 1)
     key_arrivals = [from_x[0]] + relay_chain(keys)
     value_arrivals = [from_x[1]] + relay_chain(values)
-    state = fold_block(state, keys, values, query_heads)
-    for key_rows, value_rows in zip(key_arrivals, value_arrivals):
+    blocks = list(zip(key_arrivals, value_arrivals))
+    blocks.insert(3, (keys, values))
+    for key_rows, value_rows in blocks:
         state = fold_block(state, key_rows, value_rows, query_heads)
     running_max, running_sum, numerator = state
     attended = (

time: 53.8 us -> 56.5 us (1.050)
  the two profiles are of different devices: /device:TPU:1 before, /device:TPU:5 now
where the time goes in v14:
time: 56.5 us; the launch traced here: 56 us
  matrix products  19.1 us (34%)
  starting transfers between devices  14.6 us (26%)
  waiting for transfers between devices  11.7 us (21%)
  other arithmetic  5.62 us (10%)
  local copies, waits for them, and re-layouts  4.66 us (8%)
    ppermute x5, waiting for transfers between devices, swap_within_four(): lax.ppermute(value, 'blk', [(source, source ^ bit) for source in range(co...  11.7 us
    dot_general x2, matrix products, partial_for(): jnp.dot(attended, cols, preferred_element_type=jnp.float32)  9.58 us
    ppermute x2, starting transfers between devices, shift_groups(): return lax.ppermute(value, 'blk', pairs)  6.64 us
    ppermute x5, starting transfers between devices, swap_within_four(): lax.ppermute(value, 'blk', [(source, source ^ bit) for source in range(co...  5.31 us
    dot_general x5, matrix products, fold_block(): jnp.einsum('qhd,khd->qhk', query_heads, key_heads, preferred_element_type...  5.28 us
    dot_general x5, matrix products, fold_block(): jnp.einsum('qhk,khd->qhd', weights.astype(jnp.bfloat16), value_heads, pre...  4.27 us
    unnamed x15, local copies, waits for them, and re-layouts  3.54 us
    ppermute x1, starting transfers between devices, on_device(): received.append(lax.ppermute(sent, 'mp', pairs))  2.69 us
  transfers between devices with their start and end apart: 8, of which 4 were waited for; matrix products, arithmetic and copies ran while one was open for 32% of the time, Pallas kernels for 0%

profile of v14, /device:TPU:5, one launch (start us, length us, event | category | flops | bytes accessed | tf_op | source)
XLA Modules:
  0.0 56.0 jit_solution(9265540011780975134)
XLA Ops:
  0.0 1.3 %copy.21 = bf16[128,1280]{0,1:T(8,128)(2,1)S(1)} copy(bf16[128,1280]{1,0:T(8,128)(2,1)} %param.5) | data formatting | bytes 655360 | tf_op args[1]
  1.4 1.2 %copy.22 = bf16[128,1280]{0,1:T(8,128)(2,1)S(1)} copy(bf16[128,1280]{1,0:T(8,128)(2,1)} %param.6) | data formatting | bytes 655360 | tf_op args[2]
  2.6 1.5 %collective-permute-start.2 = (bf16[128,1280]{0,1:T(8,128)(2,1)S(1)}, bf16[128,1280]{0,1:T(8,128)(2,1)}, u32[]{:S(2)}, u32[]{:S(2)}) collective-permute-start(bf16[128,1280]{0,1:T(8,128)(2,1)S(1)} %copy.22), channel_id=1, source_target_pairs={{0,4},{2,6},{4,0},{6,2},{8,12},{10,14},{12,8},{14,10},{16,20},{18,... | collective-permute-start | bytes 983048 | tf_op jit(solution)/shard_map/ppermute | solution.py:14
  4.1 0.9 %pad_maximum_fusion = bf16[2,128,1280]{1,2,0:T(8,128)(2,1)} fusion(bf16[1,128,1280]{1,2,0:T(8,128)(2,1)S(1)} %bitcast.116, bf16[1,128,1280]{1,2,0:T(8,128)(2,1)S(1)} %bitcast.118), kind=kLoop, calls=%fused_computation.57 | loop fusion | flops 327680 | bytes 1310720 | tf_op jit(solution)/shard_map/stack | solution.py:69
  5.0 1.2 %collective-permute-start = (bf16[2,128,1280]{1,2,0:T(8,128)(2,1)}, bf16[2,128,1280]{1,2,0:T(8,128)(2,1)}, u32[]{:S(2)}, u32[]{:S(2)}) collective-permute-start(bf16[2,128,1280]{1,2,0:T(8,128)(2,1)} %pad_maximum_fusion), channel_id=1, source_target_pairs={{0,2},{2,0},{4,6},{6,4},{8,10},{10,8},{12,14},{14,12},{16,18},{18,... | collective-permute-start | bytes 1966088 | tf_op jit(solution)/shard_map/ppermute | solution.py:14
  6.8 3.2 %collective-permute-done.1 = bf16[128,1280]{0,1:T(8,128)(2,1)} collective-permute-done((bf16[128,1280]{0,1:T(8,128)(2,1)S(1)}, bf16[128,1280]{0,1:T(8,128)(2,1)}, u32[]{:S(2)}, u32[]{:S(2)}) %collective-permute-start.1) | collective-permute-done | bytes 327712 | tf_op jit(solution)/shard_map/ppermute | solution.py:14
  10.0 3.3 %collective-permute-start.3 = (bf16[128,1280]{0,1:T(8,128)(2,1)}, bf16[128,1280]{0,1:T(8,128)(2,1)}, u32[]{:S(2)}, u32[]{:S(2)}) collective-permute-start(bf16[128,1280]{0,1:T(8,128)(2,1)} %collective-permute-done.1), channel_id=1, source_target_pairs={{0,8},{2,10},{4,28},{6,30},{8,16},{10,18},{12,4},{14,6},{16,24},{1... | collective-permute-start | bytes 983048 | tf_op jit(solution)/shard_map/ppermute | solution.py:25
  13.4 1.4 %bitcast_reduce_fusion.1 = (f32[384,10]{0,1:T(8,128)S(1)}, f32[10,128,384]{2,1,0:T(8,128)S(1)}) fusion(bf16[128,10,128]{0,2,1:T(8,128)(2,1)} %bitcast.119, bf16[384,10,128]{0,2,1:T(8,128)(2,1)S(1)} %bitcast.111), kind=kOutput, calls=%fused_computation.16 | convolution fusion | flops 126808320 | bytes 3292160 | tf_op jit(solution)/shard_map/qhd,khd->qhk/dot_general | solution.py:42
  14.8 2.2 %collective-permute-done.2 = bf16[128,1280]{0,1:T(8,128)(2,1)} collective-permute-done((bf16[128,1280]{0,1:T(8,128)(2,1)S(1)}, bf16[128,1280]{0,1:T(8,128)(2,1)}, u32[]{:S(2)}, u32[]{:S(2)}) %collective-permute-start.2) | collective-permute-done | bytes 327712 | tf_op jit(solution)/shard_map/ppermute | solution.py:14
  17.1 3.3 %collective-permute-start.4 = (bf16[128,1280]{0,1:T(8,128)(2,1)}, bf16[128,1280]{0,1:T(8,128)(2,1)S(1)}, u32[]{:S(2)}, u32[]{:S(2)}) collective-permute-start(bf16[128,1280]{0,1:T(8,128)(2,1)} %collective-permute-done.2), channel_id=1, source_target_pairs={{0,8},{2,10},{4,28},{6,30},{8,16},{10,18},{12,4},{14,6},{16,24},{1... | collective-permute-start | bytes 983048 | tf_op jit(solution)/shard_map/ppermute | solution.py:25
  20.4 1.4 %bitcast_reduce_fusion.3 = (f32[384,10]{0,1:T(8,128)S(1)}, f32[10,128,384]{2,1,0:T(8,128)S(1)}) fusion(bf16[128,10,128]{0,2,1:T(8,128)(2,1)} %bitcast.7, bf16[384,10,128]{0,2,1:T(8,128)(2,1)S(1)} %bitcast.112), kind=kOutput, calls=%fused_computation.26 | convolution fusion | flops 126808320 | bytes 3292160 | tf_op jit(solution)/shard_map/qhd,khd->qhk/dot_general | solution.py:42
  21.9 1.0 %broadcast_select_fusion.1 = bf16[128,1280]{0,1:T(8,128)(2,1)S(1)} fusion(bf16[128,1280]{0,1:T(8,128)(2,1)} %collective-permute-done.1, bf16[128,1280]{0,1:T(8,128)(2,1)} %collective-permute-done.3, pred[]{:T(512)S(6)} %or.4), kind=kLoop, calls=%fused_computation.59 | loop fusion | flops 163840 | bytes 983041 | tf_op jit(solution)/shard_map/jit(_where)/select_n | solution.py:32
  22.9 1.3 %collective-permute-start.5 = (bf16[128,1280]{0,1:T(8,128)(2,1)S(1)}, bf16[128,1280]{0,1:T(8,128)(2,1)S(1)}, u32[]{:S(2)}, u32[]{:S(2)}) collective-permute-start(bf16[128,1280]{0,1:T(8,128)(2,1)S(1)} %broadcast_select_fusion.1), channel_id=1, source_target_pairs={{0,2},{2,0},{4,6},{6,4},{8,10},{10,8},{12,14},{14,12},{16,18},{18,... | collective-permute-start | bytes 983048 | tf_op jit(solution)/shard_map/ppermute | solution.py:14
  24.2 1.1 %fusion.58 = (bf16[1,128,1280]{1,2,0:T(8,128)(2,1)S(1)}, bf16[1,128,1280]{1,2,0:T(8,128)(2,1)S(1)}) fusion(bf16[2,128,1280]{1,2,0:T(8,128)(2,1)} %collective-permute-done), kind=kLoop, calls=%fused_computation.74 | loop fusion | bytes 1310720 | tf_op jit(solution)/shard_map/slice | solution.py:71
  25.8 1.4 %bitcast_reduce_fusion.2 = (f32[384,10]{0,1:T(8,128)S(1)}, f32[10,128,384]{2,1,0:T(8,128)S(1)}) fusion(bf16[128,10,128]{0,2,1:T(8,128)(2,1)} %bitcast.11, bf16[384,10,128]{0,2,1:T(8,128)(2,1)S(1)} %bitcast.114), kind=kOutput, calls=%fused_computation.21 | convolution fusion | flops 126808320 | bytes 3292160 | tf_op jit(solution)/shard_map/qhd,khd->qhk/dot_general | solution.py:42
  27.3 1.3 %collective-permute-start.6 = (bf16[128,1280]{0,1:T(8,128)(2,1)S(1)}, bf16[128,1280]{0,1:T(8,128)(2,1)S(1)}, u32[]{:S(2)}, u32[]{:S(2)}) collective-permute-start(bf16[128,1280]{0,1:T(8,128)(2,1)S(1)} %broadcast_select_fusion), channel_id=1, source_target_pairs={{0,2},{2,0},{4,6},{6,4},{8,10},{10,8},{12,14},{14,12},{16,18},{18,... | collective-permute-start | bytes 983048 | tf_op jit(solution)/shard_map/ppermute | solution.py:14
  29.4 1.0 %collective-permute-done.5 = bf16[128,1280]{0,1:T(8,128)(2,1)S(1)} collective-permute-done((bf16[128,1280]{0,1:T(8,128)(2,1)S(1)}, bf16[128,1280]{0,1:T(8,128)(2,1)S(1)}, u32[]{:S(2)}, u32[]{:S(2)}) %collective-permute-start.5) | collective-permute-done | bytes 327712 | tf_op jit(solution)/shard_map/ppermute | solution.py:14
  32.1 5.3 %collective-permute-done.6 = bf16[128,1280]{0,1:T(8,128)(2,1)S(1)} collective-permute-done((bf16[128,1280]{0,1:T(8,128)(2,1)S(1)}, bf16[128,1280]{0,1:T(8,128)(2,1)S(1)}, u32[]{:S(2)}, u32[]{:S(2)}) %collective-permute-start.6) | collective-permute-done | bytes 327712 | tf_op jit(solution)/shard_map/ppermute | solution.py:14
  37.9 1.7 %fusion.36 = f32[10,384,128]{1,2,0:T(8,128)S(1)} fusion(bf16[128,10,128]{0,2,1:T(8,128)(2,1)} %bitcast.9, f32[10,128,384]{2,1,0:T(8,128)S(1)} %get-tuple-element.26, f32[384,10]{0,1:T(8,128)S(1)} %get-tuple-element.13), kind=kOutput, calls=%fused_computation.45 | convolution fusion | flops 127303680 | bytes 4275200 | tf_op jit(solution)/shard_map/qhk,khd->qhd/dot_general | solution.py:48
  40.4 1.2 %fusion.11 = bf16[384,10,128]{0,2,1:T(8,128)(2,1)S(1)} fusion(f32[10,128,384]{2,1,0:T(8,128)S(1)} %fusion.31, f32[10,384,128]{1,2,0:T(8,128)S(1)} %fusion.33, f32[10,384,128]{1,2,0:T(8,128)S(1)} %fusion.36, f32[10,128,384]{2,1,0:T(8,128)S(1)} %fusion.38, bf16[128,10,128]{0,2,1:T(8,128)(2,1)S(1)} %bitcast.123, f32[10,128,384]{2,1,0:T(8,128)S(1)} %get-tuple-element.22, ...), kind=kOutput, calls=%fused_computation.9 | convolution fusion | flops 132710400 | bytes 11248640 | tf_op jit(solution)/shard_map/qhk,khd->qhd/dot_general | solution.py:48
  42.0 4.0 %fusion.7 = bf16[384,2560]{1,0:T(8,128)(2,1)} fusion(bf16[384,1280]{0,1:T(8,128)(2,1)S(1)} %bitcast.127, bf16[1280,5120]{1,0:T(8,128)(2,1)S(1)} %bitcast.126, s32[]{:T(128)S(6)} %select_n.37), kind=kOutput, calls=%fused_computation.5 | convolution fusion | flops 2517565440 | bytes 9502724 | tf_op jit(solution)/shard_map/dot_general | solution.py:88
  46.0 2.7 %collective-permute-start.7 = (bf16[384,2560]{1,0:T(8,128)(2,1)}, bf16[384,2560]{1,0:T(8,128)(2,1)S(1)}, u32[]{:S(2)}, u32[]{:S(2)}) collective-permute-start(bf16[384,2560]{1,0:T(8,128)(2,1)} %fusion.7), channel_id=1, source_target_pairs={{0,1},{1,0},{2,3},{3,2},{4,5},{5,4},{6,7},{7,6},{8,9},{9,8},{10,11... | collective-permute-start | bytes 5898248 | tf_op jit(solution)/shard_map/ppermute | solution.py:94
  48.7 5.6 %fusion.4 = bf16[384,2560]{1,0:T(8,128)(2,1)S(1)} fusion(bf16[384,1280]{0,1:T(8,128)(2,1)S(1)} %bitcast.128, bf16[1280,5120]{1,0:T(8,128)(2,1)} %param.7, s32[]{:T(128)S(6)} %select_n.35), kind=kOutput, calls=%fused_computation.4 | convolution fusion | flops 2517565440 | bytes 9502724 | tf_op jit(solution)/shard_map/dot_general | solution.py:88
  54.3 1.7 %add_convert_fusion = bf16[384,2560]{1,0:T(8,128)(2,1)} fusion(bf16[384,2560]{1,0:T(8,128)(2,1)S(1)} %collective-permute-done.7, bf16[384,2560]{1,0:T(8,128)(2,1)S(1)} %fusion.4), kind=kLoop, calls=%fused_computation.6 | loop fusion | flops 3932160 | bytes 5898240 | tf_op jit(solution)/shard_map/convert_element_type | solution.py:98
  (30 shorter events, 5.5 us)
Async XLA Ops:
  0.0 6.2 %copy-start.1 = (bf16[384,1280]{1,0:T(8,128)(2,1)S(1)}, bf16[384,1280]{1,0:T(8,128)(2,1)}, u32[]{:S(2)}) copy-start(bf16[384,1280]{1,0:T(8,128)(2,1)} %param.4) | copy-start | bytes 2949124
  1.3 5.5 %copy-start = (bf16[128,1280]{0,1:T(8,128)(2,1)}, bf16[128,1280]{0,1:T(8,128)(2,1)S(1)}, u32[]{:S(2)}) copy-start(bf16[128,1280]{0,1:T(8,128)(2,1)S(1)} %copy.21) | copy-start | bytes 983044
  1.3 8.8 %collective-permute-start.1 = (bf16[128,1280]{0,1:T(8,128)(2,1)S(1)}, bf16[128,1280]{0,1:T(8,128)(2,1)}, u32[]{:S(2)}, u32[]{:S(2)}) collective-permute-start(bf16[128,1280]{0,1:T(8,128)(2,1)S(1)} %copy.21), channel_id=1, source_target_pairs={{0,4},{2,6},{4,0},{6,2},{8,12},{10,14},{12,8},{14,10},{16,20},{18,... | collective-permute-start | bytes 983048 | tf_op jit(solution)/shard_map/ppermute | solution.py:14
  2.6 14.5 %collective-permute-start.2 = (bf16[128,1280]{0,1:T(8,128)(2,1)S(1)}, bf16[128,1280]{0,1:T(8,128)(2,1)}, u32[]{:S(2)}, u32[]{:S(2)}) collective-permute-start(bf16[128,1280]{0,1:T(8,128)(2,1)S(1)} %copy.22), channel_id=1, source_target_pairs={{0,4},{2,6},{4,0},{6,2},{8,12},{10,14},{12,8},{14,10},{16,20},{18,... | collective-permute-start | bytes 983048 | tf_op jit(solution)/shard_map/ppermute | solution.py:14
  5.0 19.2 %collective-permute-start = (bf16[2,128,1280]{1,2,0:T(8,128)(2,1)}, bf16[2,128,1280]{1,2,0:T(8,128)(2,1)}, u32[]{:S(2)}, u32[]{:S(2)}) collective-permute-start(bf16[2,128,1280]{1,2,0:T(8,128)(2,1)} %pad_maximum_fusion), channel_id=1, source_target_pairs={{0,2},{2,0},{4,6},{6,4},{8,10},{10,8},{12,14},{14,12},{16,18},{18,... | collective-permute-start | bytes 1966088 | tf_op jit(solution)/shard_map/ppermute | solution.py:14
  10.0 11.8 %collective-permute-start.3 = (bf16[128,1280]{0,1:T(8,128)(2,1)}, bf16[128,1280]{0,1:T(8,128)(2,1)}, u32[]{:S(2)}, u32[]{:S(2)}) collective-permute-start(bf16[128,1280]{0,1:T(8,128)(2,1)} %collective-permute-done.1), channel_id=1, source_target_pairs={{0,8},{2,10},{4,28},{6,30},{8,16},{10,18},{12,4},{14,6},{16,24},{1... | collective-permute-start | bytes 983048 | tf_op jit(solution)/shard_map/ppermute | solution.py:25
  17.1 10.1 %collective-permute-start.4 = (bf16[128,1280]{0,1:T(8,128)(2,1)}, bf16[128,1280]{0,1:T(8,128)(2,1)S(1)}, u32[]{:S(2)}, u32[]{:S(2)}) collective-permute-start(bf16[128,1280]{0,1:T(8,128)(2,1)} %collective-permute-done.2), channel_id=1, source_target_pairs={{0,8},{2,10},{4,28},{6,30},{8,16},{10,18},{12,4},{14,6},{16,24},{1... | collective-permute-start | bytes 983048 | tf_op jit(solution)/shard_map/ppermute | solution.py:25
  22.9 7.5 %collective-permute-start.5 = (bf16[128,1280]{0,1:T(8,128)(2,1)S(1)}, bf16[128,1280]{0,1:T(8,128)(2,1)S(1)}, u32[]{:S(2)}, u32[]{:S(2)}) collective-permute-start(bf16[128,1280]{0,1:T(8,128)(2,1)S(1)} %broadcast_select_fusion.1), channel_id=1, source_target_pairs={{0,2},{2,0},{4,6},{6,4},{8,10},{10,8},{12,14},{14,12},{16,18},{18,... | collective-permute-start | bytes 983048 | tf_op jit(solution)/shard_map/ppermute | solution.py:14
  27.3 10.1 %collective-permute-start.6 = (bf16[128,1280]{0,1:T(8,128)(2,1)S(1)}, bf16[128,1280]{0,1:T(8,128)(2,1)S(1)}, u32[]{:S(2)}, u32[]{:S(2)}) collective-permute-start(bf16[128,1280]{0,1:T(8,128)(2,1)S(1)} %broadcast_select_fusion), channel_id=1, source_target_pairs={{0,2},{2,0},{4,6},{6,4},{8,10},{10,8},{12,14},{14,12},{16,18},{18,... | collective-permute-start | bytes 983048 | tf_op jit(solution)/shard_map/ppermute | solution.py:14
  31.6 9.9 %slice-start = ((s8[13107200]{0:T(1024)(128)(4,1)}), s8[4194304]{0:T(1024)(128)(4,1)S(1)}, s32[]{:S(2)}) async-start(s8[13107200]{0:T(1024)(128)(4,1)} %bitcast.125), calls=%async_computation | async-start | bytes 8388608
  37.4 4.2 %slice-start.1 = ((s8[13107200]{0:T(1024)(128)(4,1)}), s8[4194304]{0:T(1024)(128)(4,1)S(1)}, s32[]{:S(2)}) async-start(s8[13107200]{0:T(1024)(128)(4,1)} %bitcast.125), calls=%async_computation.1 | async-start | bytes 8388608
  39.6 2.2 %slice-start.2 = ((s8[13107200]{0:T(1024)(128)(4,1)}), s8[4194304]{0:T(1024)(128)(4,1)S(1)}, s32[]{:S(2)}) async-start(s8[13107200]{0:T(1024)(128)(4,1)} %bitcast.125), calls=%async_computation.2 | async-start | bytes 8388608
  40.4 1.6 %slice-start.3 = ((s8[13107200]{0:T(1024)(128)(4,1)}), s8[524288]{0:T(1024)(128)(4,1)S(1)}, s32[]{:S(2)}) async-start(s8[13107200]{0:T(1024)(128)(4,1)} %bitcast.125), calls=%async_computation.3 | async-start | bytes 1048576
  46.0 8.3 %collective-permute-start.7 = (bf16[384,2560]{1,0:T(8,128)(2,1)}, bf16[384,2560]{1,0:T(8,128)(2,1)S(1)}, u32[]{:S(2)}, u32[]{:S(2)}) collective-permute-start(bf16[384,2560]{1,0:T(8,128)(2,1)} %fusion.7), channel_id=1, source_target_pairs={{0,1},{1,0},{2,3},{3,2},{4,5},{5,4},{6,7},{7,6},{8,9},{9,8},{10,11... | collective-permute-start | bytes 5898248 | tf_op jit(solution)/shard_map/ppermute | solution.py:94

commit v15 on v10

--- a/solution.py
+++ b/solution.py
@@ -66,9 +66,10 @@
     )
     keys = with_layout_constraint(keys, Layout(major_to_minor=(1, 0)))
     values = with_layout_constraint(values, Layout(major_to_minor=(1, 0)))
-    from_x = swap_within_four(jnp.stack((keys, values)), 1)
-    key_arrivals = [from_x[0]] + relay_chain(keys)
-    value_arrivals = [from_x[1]] + relay_chain(values)
+    width = keys.shape[1]
+    from_x = swap_within_four(jnp.concatenate((keys, values), axis=1), 1)
+    key_arrivals = [from_x[:, :width]] + relay_chain(keys)
+    value_arrivals = [from_x[:, width:]] + relay_chain(values)
     state = fold_block(state, keys, values, query_heads)
     for key_rows, value_rows in zip(key_arrivals, value_arrivals):
         state = fold_block(state, key_rows, value_rows, query_heads)

time: 53.8 us -> 54.1 us (level)
    another operation x1 -> x0, other arithmetic: 0.89 us -> none  [on_device(): from_x = swap_within_four(jnp.stack((keys, values)), 1)]
    concatenate x0 -> x1, other arithmetic: none -> 0.88 us  [on_device(): from_x = swap_within_four(jnp.concatenate((keys, values), axis=1), 1)]
    unnamed x15 -> x17, local copies, waits for them, and re-layouts: 4.29 us -> 4.23 us
  transfers between devices with their start and end apart: 8 -> 8, of which waited for: 6 -> 6; matrix products, arithmetic and copies ran while one was open for 29% -> 30% of each run, Pallas kernels for 0% -> 0%
where the time goes in v15:
time: 54.1 us; the launch traced here: 53.9 us
  matrix products  16.6 us (31%)
  waiting for transfers between devices  15.9 us (29%)
  starting transfers between devices  11.3 us (21%)
  local copies, waits for them, and re-layouts  5.35 us (10%)
  other arithmetic  4.56 us (8%)
    ppermute x5, waiting for transfers between devices, swap_within_four(): lax.ppermute(value, 'blk', [(source, source ^ bit) for source in range(co...  10.3 us
    dot_general x2, matrix products, partial_for(): jnp.dot(attended, cols, preferred_element_type=jnp.float32)  9.87 us
    ppermute x5, starting transfers between devices, swap_within_four(): lax.ppermute(value, 'blk', [(source, source ^ bit) for source in range(co...  5.92 us
    ppermute x2, waiting for transfers between devices, shift_groups(): return lax.ppermute(value, 'blk', pairs)  5.61 us
    dot_general x5, matrix products, fold_block(): jnp.einsum('qhk,khd->qhd', weights.astype(jnp.bfloat16), value_heads, pre...  4.34 us
    unnamed x17, local copies, waits for them, and re-layouts  4.23 us
    ppermute x1, starting transfers between devices, on_device(): received.append(lax.ppermute(sent, 'mp', pairs))  2.91 us
    ppermute x2, starting transfers between devices, shift_groups(): return lax.ppermute(value, 'blk', pairs)  2.48 us
  transfers between devices with their start and end apart: 8, of which 6 were waited for; matrix products, arithmetic and copies ran while one was open for 30% of the time, Pallas kernels for 0%

profile of v15, /device:TPU:1, one launch (start us, length us, event | category | flops | bytes accessed | tf_op | source)
XLA Modules:
  0.0 53.9 jit_solution(8805126492191083196)
XLA Ops:
  0.0 1.3 %copy.21 = bf16[128,1280]{0,1:T(8,128)(2,1)S(1)} copy(bf16[128,1280]{1,0:T(8,128)(2,1)} %param.5) | data formatting | bytes 655360 | tf_op args[1]
  1.3 2.1 %collective-permute-start.1 = (bf16[128,1280]{0,1:T(8,128)(2,1)S(1)}, bf16[128,1280]{0,1:T(8,128)(2,1)S(1)}, u32[]{:S(2)}, u32[]{:S(2)}) collective-permute-start(bf16[128,1280]{0,1:T(8,128)(2,1)S(1)} %copy.21), channel_id=1, source_target_pairs={{0,4},{2,6},{4,0},{6,2},{8,12},{10,14},{12,8},{14,10},{16,20},{18,... | collective-permute-start | bytes 983048 | tf_op jit(solution)/shard_map/ppermute | solution.py:14
  3.4 1.2 %copy.24 = bf16[128,1280]{0,1:T(8,128)(2,1)S(1)} copy(bf16[128,1280]{1,0:T(8,128)(2,1)} %param.6) | data formatting | bytes 655360 | tf_op args[2]
  4.7 0.9 %pad_maximum_fusion = bf16[128,2560]{0,1:T(8,128)(2,1)} fusion(bf16[128,1280]{0,1:T(8,128)(2,1)S(1)} %copy.24, bf16[128,1280]{0,1:T(8,128)(2,1)S(1)} %copy.21), kind=kLoop, calls=%fused_computation.57 | loop fusion | flops 1310720 | bytes 1310720 | tf_op jit(solution)/shard_map/concatenate | solution.py:70
  5.5 1.4 %collective-permute-start = (bf16[128,2560]{0,1:T(8,128)(2,1)}, bf16[128,2560]{0,1:T(8,128)(2,1)}, u32[]{:S(2)}, u32[]{:S(2)}) collective-permute-start(bf16[128,2560]{0,1:T(8,128)(2,1)} %pad_maximum_fusion), channel_id=1, source_target_pairs={{0,2},{2,0},{4,6},{6,4},{8,10},{10,8},{12,14},{14,12},{16,18},{18,... | collective-permute-start | bytes 1966088 | tf_op jit(solution)/shard_map/ppermute | solution.py:14
  7.0 0.6 %copy.22 = bf16[384,1280]{0,1:T(8,128)(2,1)S(1)} copy(bf16[384,1280]{1,0:T(8,128)(2,1)S(1)} %copy-done.1) | data formatting | bytes 1966080 | tf_op args[0]
  8.1 1.7 %fusion.38 = f32[10,384,128]{1,2,0:T(8,128)} fusion(bf16[128,10,128]{0,2,1:T(8,128)(2,1)S(1)} %bitcast.114, f32[10,128,384]{2,1,0:T(8,128)S(1)} %get-tuple-element.24, f32[384,10]{0,1:T(8,128)S(1)} %get-tuple-element.23), kind=kOutput, calls=%fused_computation.46 | convolution fusion | flops 127303680 | bytes 4275200 | tf_op jit(solution)/shard_map/qhk,khd->qhd/dot_general | solution.py:48
  9.8 1.1 %collective-permute-done.1 = bf16[128,1280]{0,1:T(8,128)(2,1)S(1)} collective-permute-done((bf16[128,1280]{0,1:T(8,128)(2,1)S(1)}, bf16[128,1280]{0,1:T(8,128)(2,1)S(1)}, u32[]{:S(2)}, u32[]{:S(2)}) %collective-permute-start.1) | collective-permute-done | bytes 327712 | tf_op jit(solution)/shard_map/ppermute | solution.py:14
  10.9 1.2 %collective-permute-start.3 = (bf16[128,1280]{0,1:T(8,128)(2,1)S(1)}, bf16[128,1280]{0,1:T(8,128)(2,1)S(1)}, u32[]{:S(2)}, u32[]{:S(2)}) collective-permute-start(bf16[128,1280]{0,1:T(8,128)(2,1)S(1)} %collective-permute-done.1), channel_id=1, source_target_pairs={{0,8},{2,10},{4,28},{6,30},{8,16},{10,18},{12,4},{14,6},{16,24},{1... | collective-permute-start | bytes 983048 | tf_op jit(solution)/shard_map/ppermute | solution.py:25
  12.5 5.4 %collective-permute-done.2 = bf16[128,1280]{0,1:T(8,128)(2,1)S(1)} collective-permute-done((bf16[128,1280]{0,1:T(8,128)(2,1)S(1)}, bf16[128,1280]{0,1:T(8,128)(2,1)S(1)}, u32[]{:S(2)}, u32[]{:S(2)}) %collective-permute-start.2) | collective-permute-done | bytes 327712 | tf_op jit(solution)/shard_map/ppermute | solution.py:14
  17.9 1.2 %collective-permute-start.4 = (bf16[128,1280]{0,1:T(8,128)(2,1)S(1)}, bf16[128,1280]{0,1:T(8,128)(2,1)S(1)}, u32[]{:S(2)}, u32[]{:S(2)}) collective-permute-start(bf16[128,1280]{0,1:T(8,128)(2,1)S(1)} %collective-permute-done.2), channel_id=1, source_target_pairs={{0,8},{2,10},{4,28},{6,30},{8,16},{10,18},{12,4},{14,6},{16,24},{1... | collective-permute-start | bytes 983048 | tf_op jit(solution)/shard_map/ppermute | solution.py:25
  19.7 1.2 %collective-permute-start.5 = (bf16[128,1280]{0,1:T(8,128)(2,1)S(1)}, bf16[128,1280]{0,1:T(8,128)(2,1)S(1)}, u32[]{:S(2)}, u32[]{:S(2)}) collective-permute-start(bf16[128,1280]{0,1:T(8,128)(2,1)S(1)} %broadcast_select_fusion.1), channel_id=1, source_target_pairs={{0,2},{2,0},{4,6},{6,4},{8,10},{10,8},{12,14},{14,12},{16,18},{18,... | collective-permute-start | bytes 983048 | tf_op jit(solution)/shard_map/ppermute | solution.py:14
  21.2 1.1 %fusion.58 = (bf16[128,1280]{0,1:T(8,128)(2,1)S(1)}, bf16[128,1280]{0,1:T(8,128)(2,1)S(1)}) fusion(bf16[128,2560]{0,1:T(8,128)(2,1)} %collective-permute-done), kind=kLoop, calls=%fused_computation.74 | loop fusion | bytes 1310720 | tf_op jit(solution)/shard_map/slice | solution.py:72
  22.3 5.6 %collective-permute-done.4 = bf16[128,1280]{0,1:T(8,128)(2,1)S(1)} collective-permute-done((bf16[128,1280]{0,1:T(8,128)(2,1)S(1)}, bf16[128,1280]{0,1:T(8,128)(2,1)S(1)}, u32[]{:S(2)}, u32[]{:S(2)}) %collective-permute-start.4) | collective-permute-done | bytes 327712 | tf_op jit(solution)/shard_map/ppermute | solution.py:25
  28.4 1.1 %collective-permute-start.6 = (bf16[128,1280]{0,1:T(8,128)(2,1)S(1)}, bf16[128,1280]{0,1:T(8,128)(2,1)S(1)}, u32[]{:S(2)}, u32[]{:S(2)}) collective-permute-start(bf16[128,1280]{0,1:T(8,128)(2,1)S(1)} %broadcast_select_fusion), channel_id=1, source_target_pairs={{0,2},{2,0},{4,6},{6,4},{8,10},{10,8},{12,14},{14,12},{16,18},{18,... | collective-permute-start | bytes 983048 | tf_op jit(solution)/shard_map/ppermute | solution.py:14
  30.9 0.7 %fusion.23 = (f32[384,10]{0,1:T(8,128)S(1)}, f32[384,10]{0,1:T(8,128)S(1)}) fusion(f32[10,128,384]{2,1,0:T(8,128)S(1)} %get-tuple-element.26, f32[384,10]{0,1:T(8,128)S(1)} %get-tuple-element.13, f32[384,10]{0,1:T(8,128)S(1)} %get-tuple-element.12, f32[10,128,384]{2,1,0:T(8,128)S(1)} %get-tuple-element.22), kind=kLoop, calls=%fused_computation.35 | loop fusion | flops 2941440 | bytes 3993600 | tf_op jit(solution)/shard_map/reduce_sum | solution.py:47
  32.2 3.6 %collective-permute-done.6 = bf16[128,1280]{0,1:T(8,128)(2,1)S(1)} collective-permute-done((bf16[128,1280]{0,1:T(8,128)(2,1)S(1)}, bf16[128,1280]{0,1:T(8,128)(2,1)S(1)}, u32[]{:S(2)}, u32[]{:S(2)}) %collective-permute-start.6) | collective-permute-done | bytes 327712 | tf_op jit(solution)/shard_map/ppermute | solution.py:14
  36.2 0.7 %fusion.27 = (f32[384,10]{0,1:T(8,128)S(1)}, f32[384,10]{0,1:T(8,128)S(1)}) fusion(f32[10,128,384]{2,1,0:T(8,128)S(1)} %get-tuple-element.20, f32[384,10]{0,1:T(8,128)S(1)} %get-tuple-element.11, f32[384,10]{0,1:T(8,128)S(1)} %get-tuple-element.10, f32[10,128,384]{2,1,0:T(8,128)S(1)} %get-tuple-element.18), kind=kLoop, calls=%fused_computation.39 | loop fusion | flops 2941440 | bytes 3993600 | tf_op jit(solution)/shard_map/reduce_sum | solution.py:47
  37.0 0.7 %copy-done = f32[10,384,128]{1,2,0:T(8,128)S(1)} copy-done((f32[10,384,128]{1,2,0:T(8,128)S(1)}, f32[10,384,128]{1,2,0:T(8,128)}, u32[]{:S(2)}) %copy-start) | copy-done | bytes 1966104
  37.7 1.2 %fusion.11 = bf16[384,10,128]{0,2,1:T(8,128)(2,1)S(1)} fusion(f32[10,128,384]{2,1,0:T(8,128)S(1)} %fusion.31, f32[10,384,128]{1,2,0:T(8,128)S(1)} %fusion.34, f32[10,128,384]{2,1,0:T(8,128)S(1)} %fusion.36, f32[10,384,128]{1,2,0:T(8,128)S(1)} %copy-done, bf16[128,10,128]{0,2,1:T(8,128)(2,1)S(1)} %bitcast.122, f32[10,128,384]{2,1,0:T(8,128)S(1)} %get-tuple-element.20, ...), kind=kOutput, calls=%fused_computation.9 | convolution fusion | flops 132710400 | bytes 11248640 | tf_op jit(solution)/shard_map/qhk,khd->qhd/dot_general | solution.py:48
  39.3 4.0 %fusion.7 = bf16[384,2560]{1,0:T(8,128)(2,1)} fusion(bf16[384,1280]{0,1:T(8,128)(2,1)S(1)} %bitcast.126, bf16[1280,5120]{1,0:T(8,128)(2,1)S(1)} %bitcast.125, s32[]{:T(128)S(6)} %select_n.37), kind=kOutput, calls=%fused_computation.5 | convolution fusion | flops 2517565440 | bytes 9502724 | tf_op jit(solution)/shard_map/dot_general | solution.py:88
  43.3 2.9 %collective-permute-start.7 = (bf16[384,2560]{1,0:T(8,128)(2,1)}, bf16[384,2560]{1,0:T(8,128)(2,1)S(1)}, u32[]{:S(2)}, u32[]{:S(2)}) collective-permute-start(bf16[384,2560]{1,0:T(8,128)(2,1)} %fusion.7), channel_id=1, source_target_pairs={{0,1},{1,0},{2,3},{3,2},{4,5},{5,4},{6,7},{7,6},{8,9},{9,8},{10,11... | collective-permute-start | bytes 5898248 | tf_op jit(solution)/shard_map/ppermute | solution.py:94
  46.2 5.9 %fusion.4 = bf16[384,2560]{1,0:T(8,128)(2,1)S(1)} fusion(bf16[384,1280]{0,1:T(8,128)(2,1)} %bitcast.127, bf16[1280,5120]{1,0:T(8,128)(2,1)} %param.7, s32[]{:T(128)S(6)} %select_n.35), kind=kOutput, calls=%fused_computation.4 | convolution fusion | flops 2517565440 | bytes 9502724 | tf_op jit(solution)/shard_map/dot_general | solution.py:88
  52.1 1.7 %add_convert_fusion = bf16[384,2560]{1,0:T(8,128)(2,1)} fusion(bf16[384,2560]{1,0:T(8,128)(2,1)S(1)} %collective-permute-done.7, bf16[384,2560]{1,0:T(8,128)(2,1)S(1)} %fusion.4), kind=kLoop, calls=%fused_computation.6 | loop fusion | flops 3932160 | bytes 5898240 | tf_op jit(solution)/shard_map/convert_element_type | solution.py:98
  (32 shorter events, 5.0 us)
Async XLA Ops:
  0.0 7.0 %copy-start.1 = (bf16[384,1280]{1,0:T(8,128)(2,1)S(1)}, bf16[384,1280]{1,0:T(8,128)(2,1)}, u32[]{:S(2)}) copy-start(bf16[384,1280]{1,0:T(8,128)(2,1)} %param.4) | copy-start | bytes 2949124
  1.3 9.6 %collective-permute-start.1 = (bf16[128,1280]{0,1:T(8,128)(2,1)S(1)}, bf16[128,1280]{0,1:T(8,128)(2,1)S(1)}, u32[]{:S(2)}, u32[]{:S(2)}) collective-permute-start(bf16[128,1280]{0,1:T(8,128)(2,1)S(1)} %copy.21), channel_id=1, source_target_pairs={{0,4},{2,6},{4,0},{6,2},{8,12},{10,14},{12,8},{14,10},{16,20},{18,... | collective-permute-start | bytes 983048 | tf_op jit(solution)/shard_map/ppermute | solution.py:14
  4.6 13.4 %collective-permute-start.2 = (bf16[128,1280]{0,1:T(8,128)(2,1)S(1)}, bf16[128,1280]{0,1:T(8,128)(2,1)S(1)}, u32[]{:S(2)}, u32[]{:S(2)}) collective-permute-start(bf16[128,1280]{0,1:T(8,128)(2,1)S(1)} %copy.24), channel_id=1, source_target_pairs={{0,4},{2,6},{4,0},{6,2},{8,12},{10,14},{12,8},{14,10},{16,20},{18,... | collective-permute-start | bytes 983048 | tf_op jit(solution)/shard_map/ppermute | solution.py:14
  5.5 15.7 %collective-permute-start = (bf16[128,2560]{0,1:T(8,128)(2,1)}, bf16[128,2560]{0,1:T(8,128)(2,1)}, u32[]{:S(2)}, u32[]{:S(2)}) collective-permute-start(bf16[128,2560]{0,1:T(8,128)(2,1)} %pad_maximum_fusion), channel_id=1, source_target_pairs={{0,2},{2,0},{4,6},{6,4},{8,10},{10,8},{12,14},{14,12},{16,18},{18,... | collective-permute-start | bytes 1966088 | tf_op jit(solution)/shard_map/ppermute | solution.py:14
  10.9 8.8 %collective-permute-start.3 = (bf16[128,1280]{0,1:T(8,128)(2,1)S(1)}, bf16[128,1280]{0,1:T(8,128)(2,1)S(1)}, u32[]{:S(2)}, u32[]{:S(2)}) collective-permute-start(bf16[128,1280]{0,1:T(8,128)(2,1)S(1)} %collective-permute-done.1), channel_id=1, source_target_pairs={{0,8},{2,10},{4,28},{6,30},{8,16},{10,18},{12,4},{14,6},{16,24},{1... | collective-permute-start | bytes 983048 | tf_op jit(solution)/shard_map/ppermute | solution.py:25
  17.9 9.9 %collective-permute-start.4 = (bf16[128,1280]{0,1:T(8,128)(2,1)S(1)}, bf16[128,1280]{0,1:T(8,128)(2,1)S(1)}, u32[]{:S(2)}, u32[]{:S(2)}) collective-permute-start(bf16[128,1280]{0,1:T(8,128)(2,1)S(1)} %collective-permute-done.2), channel_id=1, source_target_pairs={{0,8},{2,10},{4,28},{6,30},{8,16},{10,18},{12,4},{14,6},{16,24},{1... | collective-permute-start | bytes 983048 | tf_op jit(solution)/shard_map/ppermute | solution.py:25
  19.7 10.2 %collective-permute-start.5 = (bf16[128,1280]{0,1:T(8,128)(2,1)S(1)}, bf16[128,1280]{0,1:T(8,128)(2,1)S(1)}, u32[]{:S(2)}, u32[]{:S(2)}) collective-permute-start(bf16[128,1280]{0,1:T(8,128)(2,1)S(1)} %broadcast_select_fusion.1), channel_id=1, source_target_pairs={{0,2},{2,0},{4,6},{6,4},{8,10},{10,8},{12,14},{14,12},{16,18},{18,... | collective-permute-start | bytes 983048 | tf_op jit(solution)/shard_map/ppermute | solution.py:14
  28.4 7.3 %collective-permute-start.6 = (bf16[128,1280]{0,1:T(8,128)(2,1)S(1)}, bf16[128,1280]{0,1:T(8,128)(2,1)S(1)}, u32[]{:S(2)}, u32[]{:S(2)}) collective-permute-start(bf16[128,1280]{0,1:T(8,128)(2,1)S(1)} %broadcast_select_fusion), channel_id=1, source_target_pairs={{0,2},{2,0},{4,6},{6,4},{8,10},{10,8},{12,14},{14,12},{16,18},{18,... | collective-permute-start | bytes 983048 | tf_op jit(solution)/shard_map/ppermute | solution.py:14
  30.4 8.5 %slice-start = ((s8[13107200]{0:T(1024)(128)(4,1)}), s8[4194304]{0:T(1024)(128)(4,1)S(1)}, s32[]{:S(2)}) async-start(s8[13107200]{0:T(1024)(128)(4,1)} %bitcast.124), calls=%async_computation | async-start | bytes 8388608
  31.7 7.3 %slice-start.1 = ((s8[13107200]{0:T(1024)(128)(4,1)}), s8[4194304]{0:T(1024)(128)(4,1)S(1)}, s32[]{:S(2)}) async-start(s8[13107200]{0:T(1024)(128)(4,1)} %bitcast.124), calls=%async_computation.1 | async-start | bytes 8388608
  36.2 1.5 %copy-start = (f32[10,384,128]{1,2,0:T(8,128)S(1)}, f32[10,384,128]{1,2,0:T(8,128)}, u32[]{:S(2)}) copy-start(f32[10,384,128]{1,2,0:T(8,128)} %fusion.38) | copy-start | bytes 5898244
  36.2 2.8 %slice-start.2 = ((s8[13107200]{0:T(1024)(128)(4,1)}), s8[4194304]{0:T(1024)(128)(4,1)S(1)}, s32[]{:S(2)}) async-start(s8[13107200]{0:T(1024)(128)(4,1)} %bitcast.124), calls=%async_computation.2 | async-start | bytes 8388608
  37.7 1.6 %slice-start.3 = ((s8[13107200]{0:T(1024)(128)(4,1)}), s8[524288]{0:T(1024)(128)(4,1)S(1)}, s32[]{:S(2)}) async-start(s8[13107200]{0:T(1024)(128)(4,1)} %bitcast.124), calls=%async_computation.3 | async-start | bytes 1048576
  38.9 4.4 %copy-start.2 = (bf16[384,10,128]{0,2,1:T(8,128)(2,1)}, bf16[384,10,128]{0,2,1:T(8,128)(2,1)S(1)}, u32[]{:S(2)}) copy-start(bf16[384,10,128]{0,2,1:T(8,128)(2,1)S(1)} %fusion.11) | copy-start | bytes 2949124
  43.3 8.8 %collective-permute-start.7 = (bf16[384,2560]{1,0:T(8,128)(2,1)}, bf16[384,2560]{1,0:T(8,128)(2,1)S(1)}, u32[]{:S(2)}, u32[]{:S(2)}) collective-permute-start(bf16[384,2560]{1,0:T(8,128)(2,1)} %fusion.7), channel_id=1, source_target_pairs={{0,1},{1,0},{2,3},{3,2},{4,5},{5,4},{6,7},{7,6},{8,9},{9,8},{10,11... | collective-permute-start | bytes 5898248 | tf_op jit(solution)/shard_map/ppermute | solution.py:94

commit v16 on v10

--- a/solution.py
+++ b/solution.py
@@ -59,22 +59,39 @@
     row_count = queries.shape[0]
     head_count = queries.shape[1] // HS
     query_heads = queries.reshape(row_count, head_count, HS)
-    state = (
-        jnp.full((row_count, head_count), -jnp.inf, jnp.float32),
-        jnp.zeros((row_count, head_count), jnp.float32),
-        jnp.zeros((row_count, head_count, HS), jnp.float32),
-    )
     keys = with_layout_constraint(keys, Layout(major_to_minor=(1, 0)))
     values = with_layout_constraint(values, Layout(major_to_minor=(1, 0)))
     from_x = swap_within_four(jnp.stack((keys, values)), 1)
-    key_arrivals = [from_x[0]] + relay_chain(keys)
-    value_arrivals = [from_x[1]] + relay_chain(values)
-    state = fold_block(state, keys, values, query_heads)
-    for key_rows, value_rows in zip(key_arrivals, value_arrivals):
-        state = fold_block(state, key_rows, value_rows, query_heads)
-    running_max, running_sum, numerator = state
+    key_blocks = [keys, from_x[0]] + relay_chain(keys)
+    value_blocks = [values, from_x[1]] + relay_chain(values)
+    scores = [
+        jnp.einsum(
+            "qhd,khd->qhk",
+            query_heads,
+            k.reshape(k.shape[0], head_count, HS),
+            preferred_element_type=jnp.float32,
+        )
+        * (1.0 / math.sqrt(HS))
+        for k in key_blocks
+    ]
+    row_max = scores[0].max(axis=-1)
+    for s in scores[1:]:
+        row_max = jnp.maximum(row_max, s.max(axis=-1))
+    total = None
+    numerator = None
+    for s, v in zip(scores, value_blocks):
+        weights = jnp.exp(s - row_max[:, :, None])
+        part = weights.sum(axis=-1)
+        total = part if total is None else total + part
+        product = jnp.einsum(
+            "qhk,khd->qhd",
+            weights.astype(jnp.bfloat16),
+            v.reshape(v.shape[0], head_count, HS),
+            preferred_element_type=jnp.float32,
+        )
+        numerator = product if numerator is None else numerator + product
     attended = (
-        (numerator / running_sum[:, :, None])
+        (numerator / total[:, :, None])
         .reshape(row_count, head_count * HS)
         .astype(jnp.bfloat16)
     )

time: 53.8 us -> 55.4 us (1.030)
  waiting for transfers between devices: 15.9 us -> 12.5 us
  matrix products: 16.2 us -> 18.5 us
  other arithmetic: 4.57 us -> 6.46 us
  local copies, waits for them, and re-layouts: 5.41 us -> 6.42 us
  starting transfers between devices: 11.3 us -> 10.5 us
    dot_general x10, matrix products: 6.64 us -> 8.97 us  [the longest x5 5.28 us: on_device(): jnp.einsum('qhd,khd->qhk', query_heads, k.reshape(k.shape[0], head_count,...]
    select_n x2, other arithmetic: 0.07 us -> 2.04 us  [relay_chain(): forward = jnp.where((position == 0) | (position == 3), from_y, from_z)]
    ppermute x2, waiting for transfers between devices: 5.59 us -> 3.91 us  [shift_groups(): return lax.ppermute(value, 'blk', pairs)]
    ppermute x5, waiting for transfers between devices: 10.3 us -> 8.59 us  [swap_within_four(): lax.ppermute(value, 'blk', [(source, source ^ bit) for source in range(co...]
    unnamed x15, local copies, waits for them, and re-layouts: 4.29 us -> 5.31 us
    ppermute x5, starting transfers between devices: 5.92 us -> 4.99 us  [swap_within_four(): lax.ppermute(value, 'blk', [(source, source ^ bit) for source in range(co...]
    reduce_sum x3 -> x1, other arithmetic: 1.81 us -> 1.77 us  [on_device(): part = weights.sum(axis=-1)]
  transfers between devices with their start and end apart: 8 -> 8, of which waited for: 6 -> 4; matrix products, arithmetic and copies ran while one was open for 29% -> 38% of each run, Pallas kernels for 0% -> 0%
where the time goes in v16:
time: 55.4 us; the launch traced here: 54.6 us
  matrix products  18.5 us (33%)
  waiting for transfers between devices  12.5 us (23%)
  starting transfers between devices  10.5 us (19%)
  other arithmetic  6.46 us (12%)
  local copies, waits for them, and re-layouts  6.42 us (12%)
    dot_general x2, matrix products, partial_for(): jnp.dot(attended, cols, preferred_element_type=jnp.float32)  9.54 us
    ppermute x5, waiting for transfers between devices, swap_within_four(): lax.ppermute(value, 'blk', [(source, source ^ bit) for source in range(co...  8.59 us
    unnamed x15, local copies, waits for them, and re-layouts  5.31 us
    dot_general x5, matrix products, on_device(): jnp.einsum('qhd,khd->qhk', query_heads, k.reshape(k.shape[0], head_count,...  5.28 us
    ppermute x5, starting transfers between devices, swap_within_four(): lax.ppermute(value, 'blk', [(source, source ^ bit) for source in range(co...  4.99 us
    ppermute x2, waiting for transfers between devices, shift_groups(): return lax.ppermute(value, 'blk', pairs)  3.91 us
    dot_general x5, matrix products, on_device(): jnp.einsum('qhk,khd->qhd', weights.astype(jnp.bfloat16), v.reshape(v.shap...  3.69 us
    ppermute x1, starting transfers between devices, on_device(): received.append(lax.ppermute(sent, 'mp', pairs))  2.99 us
  transfers between devices with their start and end apart: 8, of which 4 were waited for; matrix products, arithmetic and copies ran while one was open for 38% of the time, Pallas kernels for 0%

profile of v16, /device:TPU:1, one launch (start us, length us, event | category | flops | bytes accessed | tf_op | source)
XLA Modules:
  0.0 54.6 jit_solution(13550292002536562616)
XLA Ops:
  0.0 1.3 %copy.21 = bf16[128,1280]{0,1:T(8,128)(2,1)S(1)} copy(bf16[128,1280]{1,0:T(8,128)(2,1)} %param.5) | data formatting | bytes 655360 | tf_op args[1]
  1.3 2.1 %collective-permute-start.1 = (bf16[128,1280]{0,1:T(8,128)(2,1)S(1)}, bf16[128,1280]{0,1:T(8,128)(2,1)}, u32[]{:S(2)}, u32[]{:S(2)}) collective-permute-start(bf16[128,1280]{0,1:T(8,128)(2,1)S(1)} %copy.21), channel_id=1, source_target_pairs={{0,4},{2,6},{4,0},{6,2},{8,12},{10,14},{12,8},{14,10},{16,20},{18,... | collective-permute-start | bytes 983048 | tf_op jit(solution)/shard_map/ppermute | solution.py:14
  3.4 1.2 %copy.24 = bf16[128,1280]{0,1:T(8,128)(2,1)S(1)} copy(bf16[128,1280]{1,0:T(8,128)(2,1)} %param.6) | data formatting | bytes 655360 | tf_op args[2]
  5.6 1.4 %collective-permute-start = (bf16[2,128,1280]{1,2,0:T(8,128)(2,1)}, bf16[2,128,1280]{1,2,0:T(8,128)(2,1)}, u32[]{:S(2)}, u32[]{:S(2)}) collective-permute-start(bf16[2,128,1280]{1,2,0:T(8,128)(2,1)} %pad_maximum_fusion), channel_id=1, source_target_pairs={{0,2},{2,0},{4,6},{6,4},{8,10},{10,8},{12,14},{14,12},{16,18},{18,... | collective-permute-start | bytes 1966088 | tf_op jit(solution)/shard_map/ppermute | solution.py:14
  7.6 3.3 %collective-permute-done.1 = bf16[128,1280]{0,1:T(8,128)(2,1)} collective-permute-done((bf16[128,1280]{0,1:T(8,128)(2,1)S(1)}, bf16[128,1280]{0,1:T(8,128)(2,1)}, u32[]{:S(2)}, u32[]{:S(2)}) %collective-permute-start.1) | collective-permute-done | bytes 327712 | tf_op jit(solution)/shard_map/ppermute | solution.py:14
  10.9 1.2 %collective-permute-start.2 = (bf16[128,1280]{0,1:T(8,128)(2,1)}, bf16[128,1280]{0,1:T(8,128)(2,1)}, u32[]{:S(2)}, u32[]{:S(2)}) collective-permute-start(bf16[128,1280]{0,1:T(8,128)(2,1)} %collective-permute-done.1), channel_id=1, source_target_pairs={{0,8},{2,10},{4,28},{6,30},{8,16},{10,18},{12,4},{14,6},{16,24},{1... | collective-permute-start | bytes 983048 | tf_op jit(solution)/shard_map/ppermute | solution.py:25
  12.2 1.4 %bitcast_reduce_fusion.4 = (f32[384,10]{0,1:T(8,128)S(1)}, f32[10,128,384]{2,1,0:T(8,128)S(1)}) fusion(bf16[128,10,128]{0,2,1:T(8,128)(2,1)} %bitcast.109, bf16[384,10,128]{0,2,1:T(8,128)(2,1)S(1)} %bitcast.101), kind=kOutput, calls=%fused_computation.26 | convolution fusion | flops 126808320 | bytes 3292160 | tf_op jit(solution)/shard_map/qhd,khd->qhk/dot_general | solution.py:68
  13.6 4.3 %collective-permute-done.4 = bf16[128,1280]{0,1:T(8,128)(2,1)} collective-permute-done((bf16[128,1280]{0,1:T(8,128)(2,1)S(1)}, bf16[128,1280]{0,1:T(8,128)(2,1)}, u32[]{:S(2)}, u32[]{:S(2)}) %collective-permute-start.4) | collective-permute-done | bytes 327712 | tf_op jit(solution)/shard_map/ppermute | solution.py:14
  17.9 1.2 %collective-permute-start.5 = (bf16[128,1280]{0,1:T(8,128)(2,1)}, bf16[128,1280]{0,1:T(8,128)(2,1)S(1)}, u32[]{:S(2)}, u32[]{:S(2)}) collective-permute-start(bf16[128,1280]{0,1:T(8,128)(2,1)} %collective-permute-done.4), channel_id=1, source_target_pairs={{0,8},{2,10},{4,28},{6,30},{8,16},{10,18},{12,4},{14,6},{16,24},{1... | collective-permute-start | bytes 983048 | tf_op jit(solution)/shard_map/ppermute | solution.py:25
  19.2 1.4 %bitcast_reduce_fusion.2 = (f32[384,10]{0,1:T(8,128)S(1)}, f32[10,128,384]{2,1,0:T(8,128)S(1)}) fusion(bf16[128,10,128]{0,2,1:T(8,128)(2,1)} %bitcast.7, bf16[384,10,128]{0,2,1:T(8,128)(2,1)S(1)} %bitcast.102), kind=kOutput, calls=%fused_computation.20 | convolution fusion | flops 126808320 | bytes 3292160 | tf_op jit(solution)/shard_map/qhd,khd->qhk/dot_general | solution.py:68
  20.6 1.0 %broadcast_select_fusion.1 = bf16[128,1280]{0,1:T(8,128)(2,1)S(1)} fusion(bf16[128,1280]{0,1:T(8,128)(2,1)} %collective-permute-done.1, bf16[128,1280]{0,1:T(8,128)(2,1)} %collective-permute-done.2, pred[]{:T(512)S(6)} %or.4), kind=kLoop, calls=%fused_computation.54 | loop fusion | flops 163840 | bytes 983041 | tf_op jit(solution)/shard_map/jit(_where)/select_n | solution.py:32
  21.7 1.3 %collective-permute-start.3 = (bf16[128,1280]{0,1:T(8,128)(2,1)S(1)}, bf16[128,1280]{0,1:T(8,128)(2,1)S(1)}, u32[]{:S(2)}, u32[]{:S(2)}) collective-permute-start(bf16[128,1280]{0,1:T(8,128)(2,1)S(1)} %broadcast_select_fusion.1), channel_id=1, source_target_pairs={{0,2},{2,0},{4,6},{6,4},{8,10},{10,8},{12,14},{14,12},{16,18},{18,... | collective-permute-start | bytes 983048 | tf_op jit(solution)/shard_map/ppermute | solution.py:14
  23.0 1.1 %fusion.53 = (bf16[1,128,1280]{1,2,0:T(8,128)(2,1)S(1)}, bf16[1,128,1280]{1,2,0:T(8,128)(2,1)S(1)}) fusion(bf16[2,128,1280]{1,2,0:T(8,128)(2,1)} %collective-permute-done), kind=kLoop, calls=%fused_computation.64 | loop fusion | bytes 1310720 | tf_op jit(solution)/shard_map/slice | solution.py:66
  24.1 3.9 %collective-permute-done.5 = bf16[128,1280]{0,1:T(8,128)(2,1)S(1)} collective-permute-done((bf16[128,1280]{0,1:T(8,128)(2,1)}, bf16[128,1280]{0,1:T(8,128)(2,1)S(1)}, u32[]{:S(2)}, u32[]{:S(2)}) %collective-permute-start.5) | collective-permute-done | bytes 327712 | tf_op jit(solution)/shard_map/ppermute | solution.py:25
  28.0 1.0 %broadcast_select_fusion = bf16[128,1280]{0,1:T(8,128)(2,1)S(1)} fusion(bf16[128,1280]{0,1:T(8,128)(2,1)} %collective-permute-done.4, bf16[128,1280]{0,1:T(8,128)(2,1)S(1)} %collective-permute-done.5, pred[]{:T(512)S(6)} %or.4), kind=kLoop, calls=%fused_computation.53 | loop fusion | flops 163840 | bytes 983041 | tf_op jit(solution)/shard_map/jit(_where)/select_n | solution.py:32
  29.6 1.4 %bitcast_reduce_fusion.1 = (f32[384,10]{0,1:T(8,128)S(1)}, f32[10,128,384]{2,1,0:T(8,128)S(1)}) fusion(bf16[128,10,128]{0,2,1:T(8,128)(2,1)} %bitcast.9, bf16[384,10,128]{0,2,1:T(8,128)(2,1)S(1)} %bitcast.104), kind=kOutput, calls=%fused_computation.17 | convolution fusion | flops 126808320 | bytes 3292160 | tf_op jit(solution)/shard_map/qhd,khd->qhk/dot_general | solution.py:68
  32.5 1.8 %fusion.19 = (f32[384,10]{0,1:T(8,128)S(1)}, f32[384,10]{0,1:T(8,128)S(1)}, f32[384,10]{0,1:T(8,128)S(1)}, f32[384,10]{0,1:T(8,128)S(1)}, f32[384,10]{0,1:T(8,128)S(1)}) fusion(f32[10,128,384]{2,1,0:T(8,128)S(1)} %get-tuple-element.21, f32[384,10]{0,1:T(8,128)S(1)} %maximum_maximum_fusion, f32[10,128,384]{2,1,0:T(8,128)S(1)} %get-tuple-element.19, ...), kind=kLoop, calls=%fused_computation.30 | loop fusion | flops 7353600 | bytes 9922560 | tf_op jit(solution)/shard_map/reduce_sum | solution.py:84
  34.3 1.4 %fusion.30 = f32[10,384,128]{1,2,0:T(8,128)S(1)} fusion(bf16[128,10,128]{0,2,1:T(8,128)(2,1)} %bitcast.17, f32[10,128,384]{2,1,0:T(8,128)S(1)} %get-tuple-element.17, f32[384,10]{0,1:T(8,128)S(1)} %maximum_maximum_fusion), kind=kOutput, calls=%fused_computation.39 | convolution fusion | flops 127303680 | bytes 4275200 | tf_op jit(solution)/shard_map/qhk,khd->qhd/dot_general | solution.py:86
  35.7 1.0 %collective-permute-done.6 = bf16[128,1280]{0,1:T(8,128)(2,1)S(1)} collective-permute-done((bf16[128,1280]{0,1:T(8,128)(2,1)S(1)}, bf16[128,1280]{0,1:T(8,128)(2,1)S(1)}, u32[]{:S(2)}, u32[]{:S(2)}) %collective-permute-start.6) | collective-permute-done | bytes 327712 | tf_op jit(solution)/shard_map/ppermute | solution.py:14
  38.9 1.4 %slice-done.3 = s8[4194304]{0:T(1024)(128)(4,1)S(1)} async-done(((s8[13107200]{0:T(1024)(128)(4,1)}), s8[4194304]{0:T(1024)(128)(4,1)S(1)}, s32[]{:S(2)}) %slice-start.3) | async-done | bytes 4194328
  40.3 3.9 %fusion.7 = bf16[384,2560]{1,0:T(8,128)(2,1)} fusion(bf16[384,1280]{0,1:T(8,128)(2,1)S(1)} %bitcast.113, bf16[1280,5120]{1,0:T(8,128)(2,1)S(1)} %bitcast.118, s32[]{:T(128)S(6)} %select_n.37), kind=kOutput, calls=%fused_computation.5 | convolution fusion | flops 2517565440 | bytes 9502724 | tf_op jit(solution)/shard_map/dot_general | solution.py:104
  44.2 3.0 %collective-permute-start.7 = (bf16[384,2560]{1,0:T(8,128)(2,1)}, bf16[384,2560]{1,0:T(8,128)(2,1)S(1)}, u32[]{:S(2)}, u32[]{:S(2)}) collective-permute-start(bf16[384,2560]{1,0:T(8,128)(2,1)} %fusion.7), channel_id=1, source_target_pairs={{0,1},{1,0},{2,3},{3,2},{4,5},{5,4},{6,7},{7,6},{8,9},{9,8},{10,11... | collective-permute-start | bytes 5898248 | tf_op jit(solution)/shard_map/ppermute | solution.py:110
  47.2 5.6 %fusion.4 = bf16[384,2560]{1,0:T(8,128)(2,1)S(1)} fusion(bf16[384,1280]{0,1:T(8,128)(2,1)S(1)} %bitcast.114, bf16[1280,5120]{1,0:T(8,128)(2,1)} %param.7, s32[]{:T(128)S(6)} %select_n.35), kind=kOutput, calls=%fused_computation.4 | convolution fusion | flops 2517565440 | bytes 9502724 | tf_op jit(solution)/shard_map/dot_general | solution.py:104
  52.8 1.7 %add_convert_fusion = bf16[384,2560]{1,0:T(8,128)(2,1)} fusion(bf16[384,2560]{1,0:T(8,128)(2,1)S(1)} %collective-permute-done.7, bf16[384,2560]{1,0:T(8,128)(2,1)S(1)} %fusion.4), kind=kLoop, calls=%fused_computation.6 | loop fusion | flops 3932160 | bytes 5898240 | tf_op jit(solution)/shard_map/convert_element_type | solution.py:114
  (28 shorter events, 5.8 us)
Async XLA Ops:
  0.0 7.0 %copy-start.1 = (bf16[384,1280]{1,0:T(8,128)(2,1)S(1)}, bf16[384,1280]{1,0:T(8,128)(2,1)}, u32[]{:S(2)}) copy-start(bf16[384,1280]{1,0:T(8,128)(2,1)} %param.4) | copy-start | bytes 2949124
  1.3 6.4 %copy-start = (bf16[128,1280]{0,1:T(8,128)(2,1)}, bf16[128,1280]{0,1:T(8,128)(2,1)S(1)}, u32[]{:S(2)}) copy-start(bf16[128,1280]{0,1:T(8,128)(2,1)S(1)} %copy.21) | copy-start | bytes 983044
  1.3 9.6 %collective-permute-start.1 = (bf16[128,1280]{0,1:T(8,128)(2,1)S(1)}, bf16[128,1280]{0,1:T(8,128)(2,1)}, u32[]{:S(2)}, u32[]{:S(2)}) collective-permute-start(bf16[128,1280]{0,1:T(8,128)(2,1)S(1)} %copy.21), channel_id=1, source_target_pairs={{0,4},{2,6},{4,0},{6,2},{8,12},{10,14},{12,8},{14,10},{16,20},{18,... | collective-permute-start | bytes 983048 | tf_op jit(solution)/shard_map/ppermute | solution.py:14
  4.6 13.4 %collective-permute-start.4 = (bf16[128,1280]{0,1:T(8,128)(2,1)S(1)}, bf16[128,1280]{0,1:T(8,128)(2,1)}, u32[]{:S(2)}, u32[]{:S(2)}) collective-permute-start(bf16[128,1280]{0,1:T(8,128)(2,1)S(1)} %copy.24), channel_id=1, source_target_pairs={{0,4},{2,6},{4,0},{6,2},{8,12},{10,14},{12,8},{14,10},{16,20},{18,... | collective-permute-start | bytes 983048 | tf_op jit(solution)/shard_map/ppermute | solution.py:14
  5.6 17.3 %collective-permute-start = (bf16[2,128,1280]{1,2,0:T(8,128)(2,1)}, bf16[2,128,1280]{1,2,0:T(8,128)(2,1)}, u32[]{:S(2)}, u32[]{:S(2)}) collective-permute-start(bf16[2,128,1280]{1,2,0:T(8,128)(2,1)} %pad_maximum_fusion), channel_id=1, source_target_pairs={{0,2},{2,0},{4,6},{6,4},{8,10},{10,8},{12,14},{14,12},{16,18},{18,... | collective-permute-start | bytes 1966088 | tf_op jit(solution)/shard_map/ppermute | solution.py:14
  10.9 9.7 %collective-permute-start.2 = (bf16[128,1280]{0,1:T(8,128)(2,1)}, bf16[128,1280]{0,1:T(8,128)(2,1)}, u32[]{:S(2)}, u32[]{:S(2)}) collective-permute-start(bf16[128,1280]{0,1:T(8,128)(2,1)} %collective-permute-done.1), channel_id=1, source_target_pairs={{0,8},{2,10},{4,28},{6,30},{8,16},{10,18},{12,4},{14,6},{16,24},{1... | collective-permute-start | bytes 983048 | tf_op jit(solution)/shard_map/ppermute | solution.py:25
  17.9 10.0 %collective-permute-start.5 = (bf16[128,1280]{0,1:T(8,128)(2,1)}, bf16[128,1280]{0,1:T(8,128)(2,1)S(1)}, u32[]{:S(2)}, u32[]{:S(2)}) collective-permute-start(bf16[128,1280]{0,1:T(8,128)(2,1)} %collective-permute-done.4), channel_id=1, source_target_pairs={{0,8},{2,10},{4,28},{6,30},{8,16},{10,18},{12,4},{14,6},{16,24},{1... | collective-permute-start | bytes 983048 | tf_op jit(solution)/shard_map/ppermute | solution.py:25
  21.7 9.4 %collective-permute-start.3 = (bf16[128,1280]{0,1:T(8,128)(2,1)S(1)}, bf16[128,1280]{0,1:T(8,128)(2,1)S(1)}, u32[]{:S(2)}, u32[]{:S(2)}) collective-permute-start(bf16[128,1280]{0,1:T(8,128)(2,1)S(1)} %broadcast_select_fusion.1), channel_id=1, source_target_pairs={{0,2},{2,0},{4,6},{6,4},{8,10},{10,8},{12,14},{14,12},{16,18},{18,... | collective-permute-start | bytes 983048 | tf_op jit(solution)/shard_map/ppermute | solution.py:14
  29.5 7.2 %collective-permute-start.6 = (bf16[128,1280]{0,1:T(8,128)(2,1)S(1)}, bf16[128,1280]{0,1:T(8,128)(2,1)S(1)}, u32[]{:S(2)}, u32[]{:S(2)}) collective-permute-start(bf16[128,1280]{0,1:T(8,128)(2,1)S(1)} %broadcast_select_fusion), channel_id=1, source_target_pairs={{0,2},{2,0},{4,6},{6,4},{8,10},{10,8},{12,14},{14,12},{16,18},{18,... | collective-permute-start | bytes 983048 | tf_op jit(solution)/shard_map/ppermute | solution.py:14
  32.5 5.6 %slice-start = ((s8[13107200]{0:T(1024)(128)(4,1)}), s8[524288]{0:T(1024)(128)(4,1)S(1)}, s32[]{:S(2)}) async-start(s8[13107200]{0:T(1024)(128)(4,1)} %bitcast.117), calls=%async_computation | async-start | bytes 1048576
  32.5 5.6 %slice-start.1 = ((s8[13107200]{0:T(1024)(128)(4,1)}), s8[4194304]{0:T(1024)(128)(4,1)S(1)}, s32[]{:S(2)}) async-start(s8[13107200]{0:T(1024)(128)(4,1)} %bitcast.117), calls=%async_computation.1 | async-start | bytes 8388608
  36.7 2.2 %slice-start.2 = ((s8[13107200]{0:T(1024)(128)(4,1)}), s8[4194304]{0:T(1024)(128)(4,1)S(1)}, s32[]{:S(2)}) async-start(s8[13107200]{0:T(1024)(128)(4,1)} %bitcast.117), calls=%async_computation.2 | async-start | bytes 8388608
  37.2 3.1 %slice-start.3 = ((s8[13107200]{0:T(1024)(128)(4,1)}), s8[4194304]{0:T(1024)(128)(4,1)S(1)}, s32[]{:S(2)}) async-start(s8[13107200]{0:T(1024)(128)(4,1)} %bitcast.117), calls=%async_computation.3 | async-start | bytes 8388608
  44.2 8.6 %collective-permute-start.7 = (bf16[384,2560]{1,0:T(8,128)(2,1)}, bf16[384,2560]{1,0:T(8,128)(2,1)S(1)}, u32[]{:S(2)}, u32[]{:S(2)}) collective-permute-start(bf16[384,2560]{1,0:T(8,128)(2,1)} %fusion.7), channel_id=1, source_target_pairs={{0,1},{1,0},{2,3},{3,2},{4,5},{5,4},{6,7},{7,6},{8,9},{9,8},{10,11... | collective-permute-start | bytes 5898248 | tf_op jit(solution)/shard_map/ppermute | solution.py:110

commit v17 on v10

--- a/solution.py
+++ b/solution.py
@@ -86,11 +86,16 @@
         cols = lax.dynamic_slice_in_dim(out_weight, owner * width, width, axis=1)
         return jnp.dot(attended, cols, preferred_element_type=jnp.float32).astype(jnp.bfloat16)
 
+    def half_for(owner, half):
+        step = width // 2
+        cols = lax.dynamic_slice_in_dim(out_weight, owner * width + half * step, step, axis=1)
+        return jnp.dot(attended, cols, preferred_element_type=jnp.float32).astype(jnp.bfloat16)
+
     received = []
     for offset in range(1, groups):
-        sent = partial_for((me + offset) % groups)
         pairs = [(source, (source + offset) % groups) for source in range(groups)]
-        received.append(lax.ppermute(sent, "mp", pairs))
+        halves = [lax.ppermute(half_for((me + offset) % groups, h), "mp", pairs) for h in (0, 1)]
+        received.append(jnp.concatenate(halves, axis=1))
     summed = lax.optimization_barrier(partial_for(me)).astype(jnp.float32)
     for part in received:
         summed = summed + part.astype(jnp.float32)

time: 53.8 us -> 54.6 us (1.015)
    dot_general x0 -> x2, matrix products: none -> 3.96 us  [half_for(): jnp.dot(attended, cols, preferred_element_type=jnp.float32)]
    dot_general x2 -> x1, matrix products: 9.54 us -> 5.92 us  [partial_for(): jnp.dot(attended, cols, preferred_element_type=jnp.float32)]
    ppermute x1 -> x2, starting transfers between devices: 2.89 us -> 2.98 us  [on_device(): lax.ppermute(half_for((me + offset) % groups, h), 'mp', pairs)]
    unnamed x15 -> x17, local copies, waits for them, and re-layouts: 4.29 us -> 4.28 us
  transfers between devices with their start and end apart: 8 -> 9, of which waited for: 6 -> 6; matrix products, arithmetic and copies ran while one was open for 29% -> 34% of each run, Pallas kernels for 0% -> 0%
where the time goes in v17:
time: 54.6 us; the launch traced here: 54 us
  matrix products  16.5 us (30%)
  waiting for transfers between devices  15.8 us (29%)
  starting transfers between devices  11.4 us (21%)
  local copies, waits for them, and re-layouts  5.4 us (10%)
  other arithmetic  4.61 us (8%)
    ppermute x5, waiting for transfers between devices, swap_within_four(): lax.ppermute(value, 'blk', [(source, source ^ bit) for source in range(co...  10.3 us
    ppermute x5, starting transfers between devices, swap_within_four(): lax.ppermute(value, 'blk', [(source, source ^ bit) for source in range(co...  5.92 us
    dot_general x1, matrix products, partial_for(): jnp.dot(attended, cols, preferred_element_type=jnp.float32)  5.92 us
    ppermute x2, waiting for transfers between devices, shift_groups(): return lax.ppermute(value, 'blk', pairs)  5.58 us
    unnamed x17, local copies, waits for them, and re-layouts  4.28 us
    dot_general x5, matrix products, fold_block(): jnp.einsum('qhk,khd->qhd', weights.astype(jnp.bfloat16), value_heads, pre...  4.28 us
    dot_general x2, matrix products, half_for(): jnp.dot(attended, cols, preferred_element_type=jnp.float32)  3.96 us
    ppermute x2, starting transfers between devices, on_device(): lax.ppermute(half_for((me + offset) % groups, h), 'mp', pairs)  2.98 us
  transfers between devices with their start and end apart: 9, of which 6 were waited for; matrix products, arithmetic and copies ran while one was open for 34% of the time, Pallas kernels for 0%

profile of v17, /device:TPU:1, one launch (start us, length us, event | category | flops | bytes accessed | tf_op | source)
XLA Modules:
  0.0 54.0 jit_solution(6837374589292877619)
XLA Ops:
  0.0 1.3 %copy.21 = bf16[128,1280]{0,1:T(8,128)(2,1)S(1)} copy(bf16[128,1280]{1,0:T(8,128)(2,1)} %param.5) | data formatting | bytes 655360 | tf_op args[1]
  1.3 2.1 %collective-permute-start.1 = (bf16[128,1280]{0,1:T(8,128)(2,1)S(1)}, bf16[128,1280]{0,1:T(8,128)(2,1)S(1)}, u32[]{:S(2)}, u32[]{:S(2)}) collective-permute-start(bf16[128,1280]{0,1:T(8,128)(2,1)S(1)} %copy.21), channel_id=1, source_target_pairs={{0,4},{2,6},{4,0},{6,2},{8,12},{10,14},{12,8},{14,10},{16,20},{18,... | collective-permute-start | bytes 983048 | tf_op jit(solution)/shard_map/ppermute | solution.py:14
  3.4 1.2 %copy.24 = bf16[128,1280]{0,1:T(8,128)(2,1)S(1)} copy(bf16[128,1280]{1,0:T(8,128)(2,1)} %param.6) | data formatting | bytes 655360 | tf_op args[2]
  4.7 0.9 %pad_maximum_fusion = bf16[2,128,1280]{1,2,0:T(8,128)(2,1)} fusion(bf16[1,128,1280]{1,2,0:T(8,128)(2,1)S(1)} %bitcast.117, bf16[1,128,1280]{1,2,0:T(8,128)(2,1)S(1)} %bitcast.119), kind=kLoop, calls=%fused_computation.60 | loop fusion | flops 327680 | bytes 1310720 | tf_op jit(solution)/shard_map/stack | solution.py:69
  5.6 1.4 %collective-permute-start = (bf16[2,128,1280]{1,2,0:T(8,128)(2,1)}, bf16[2,128,1280]{1,2,0:T(8,128)(2,1)}, u32[]{:S(2)}, u32[]{:S(2)}) collective-permute-start(bf16[2,128,1280]{1,2,0:T(8,128)(2,1)} %pad_maximum_fusion), channel_id=1, source_target_pairs={{0,2},{2,0},{4,6},{6,4},{8,10},{10,8},{12,14},{14,12},{16,18},{18,... | collective-permute-start | bytes 1966088 | tf_op jit(solution)/shard_map/ppermute | solution.py:14
  8.1 1.7 %fusion.43 = f32[10,384,128]{1,2,0:T(8,128)} fusion(bf16[128,10,128]{0,2,1:T(8,128)(2,1)S(1)} %bitcast.118, f32[10,128,384]{2,1,0:T(8,128)S(1)} %get-tuple-element.24, f32[384,10]{0,1:T(8,128)S(1)} %get-tuple-element.23), kind=kOutput, calls=%fused_computation.49 | convolution fusion | flops 127303680 | bytes 4275200 | tf_op jit(solution)/shard_map/qhk,khd->qhd/dot_general | solution.py:48
  9.9 1.1 %collective-permute-done.1 = bf16[128,1280]{0,1:T(8,128)(2,1)S(1)} collective-permute-done((bf16[128,1280]{0,1:T(8,128)(2,1)S(1)}, bf16[128,1280]{0,1:T(8,128)(2,1)S(1)}, u32[]{:S(2)}, u32[]{:S(2)}) %collective-permute-start.1) | collective-permute-done | bytes 327712 | tf_op jit(solution)/shard_map/ppermute | solution.py:14
  10.9 1.2 %collective-permute-start.3 = (bf16[128,1280]{0,1:T(8,128)(2,1)S(1)}, bf16[128,1280]{0,1:T(8,128)(2,1)S(1)}, u32[]{:S(2)}, u32[]{:S(2)}) collective-permute-start(bf16[128,1280]{0,1:T(8,128)(2,1)S(1)} %collective-permute-done.1), channel_id=1, source_target_pairs={{0,8},{2,10},{4,28},{6,30},{8,16},{10,18},{12,4},{14,6},{16,24},{1... | collective-permute-start | bytes 983048 | tf_op jit(solution)/shard_map/ppermute | solution.py:25
  12.5 5.4 %collective-permute-done.2 = bf16[128,1280]{0,1:T(8,128)(2,1)S(1)} collective-permute-done((bf16[128,1280]{0,1:T(8,128)(2,1)S(1)}, bf16[128,1280]{0,1:T(8,128)(2,1)S(1)}, u32[]{:S(2)}, u32[]{:S(2)}) %collective-permute-start.2) | collective-permute-done | bytes 327712 | tf_op jit(solution)/shard_map/ppermute | solution.py:14
  17.9 1.2 %collective-permute-start.4 = (bf16[128,1280]{0,1:T(8,128)(2,1)S(1)}, bf16[128,1280]{0,1:T(8,128)(2,1)S(1)}, u32[]{:S(2)}, u32[]{:S(2)}) collective-permute-start(bf16[128,1280]{0,1:T(8,128)(2,1)S(1)} %collective-permute-done.2), channel_id=1, source_target_pairs={{0,8},{2,10},{4,28},{6,30},{8,16},{10,18},{12,4},{14,6},{16,24},{1... | collective-permute-start | bytes 983048 | tf_op jit(solution)/shard_map/ppermute | solution.py:25
  19.7 1.2 %collective-permute-start.5 = (bf16[128,1280]{0,1:T(8,128)(2,1)S(1)}, bf16[128,1280]{0,1:T(8,128)(2,1)S(1)}, u32[]{:S(2)}, u32[]{:S(2)}) collective-permute-start(bf16[128,1280]{0,1:T(8,128)(2,1)S(1)} %broadcast_select_fusion.1), channel_id=1, source_target_pairs={{0,2},{2,0},{4,6},{6,4},{8,10},{10,8},{12,14},{14,12},{16,18},{18,... | collective-permute-start | bytes 983048 | tf_op jit(solution)/shard_map/ppermute | solution.py:14
  21.2 1.1 %fusion.64 = (bf16[1,128,1280]{1,2,0:T(8,128)(2,1)S(1)}, bf16[1,128,1280]{1,2,0:T(8,128)(2,1)S(1)}) fusion(bf16[2,128,1280]{1,2,0:T(8,128)(2,1)} %collective-permute-done), kind=kLoop, calls=%fused_computation.78 | loop fusion | bytes 1310720 | tf_op jit(solution)/shard_map/slice | solution.py:71
  22.3 5.5 %collective-permute-done.4 = bf16[128,1280]{0,1:T(8,128)(2,1)S(1)} collective-permute-done((bf16[128,1280]{0,1:T(8,128)(2,1)S(1)}, bf16[128,1280]{0,1:T(8,128)(2,1)S(1)}, u32[]{:S(2)}, u32[]{:S(2)}) %collective-permute-start.4) | collective-permute-done | bytes 327712 | tf_op jit(solution)/shard_map/ppermute | solution.py:25
  28.4 1.1 %collective-permute-start.6 = (bf16[128,1280]{0,1:T(8,128)(2,1)S(1)}, bf16[128,1280]{0,1:T(8,128)(2,1)S(1)}, u32[]{:S(2)}, u32[]{:S(2)}) collective-permute-start(bf16[128,1280]{0,1:T(8,128)(2,1)S(1)} %broadcast_select_fusion), channel_id=1, source_target_pairs={{0,2},{2,0},{4,6},{6,4},{8,10},{10,8},{12,14},{14,12},{16,18},{18,... | collective-permute-start | bytes 983048 | tf_op jit(solution)/shard_map/ppermute | solution.py:14
  30.9 0.7 %fusion.28 = (f32[384,10]{0,1:T(8,128)S(1)}, f32[384,10]{0,1:T(8,128)S(1)}) fusion(f32[10,128,384]{2,1,0:T(8,128)S(1)} %get-tuple-element.26, f32[384,10]{0,1:T(8,128)S(1)} %get-tuple-element.13, f32[384,10]{0,1:T(8,128)S(1)} %get-tuple-element.12, f32[10,128,384]{2,1,0:T(8,128)S(1)} %get-tuple-element.22), kind=kLoop, calls=%fused_computation.38 | loop fusion | flops 2941440 | bytes 3993600 | tf_op jit(solution)/shard_map/reduce_sum | solution.py:47
  32.1 3.6 %collective-permute-done.6 = bf16[128,1280]{0,1:T(8,128)(2,1)S(1)} collective-permute-done((bf16[128,1280]{0,1:T(8,128)(2,1)S(1)}, bf16[128,1280]{0,1:T(8,128)(2,1)S(1)}, u32[]{:S(2)}, u32[]{:S(2)}) %collective-permute-start.6) | collective-permute-done | bytes 327712 | tf_op jit(solution)/shard_map/ppermute | solution.py:14
  36.2 0.7 %fusion.32 = (f32[384,10]{0,1:T(8,128)S(1)}, f32[384,10]{0,1:T(8,128)S(1)}) fusion(f32[10,128,384]{2,1,0:T(8,128)S(1)} %get-tuple-element.20, f32[384,10]{0,1:T(8,128)S(1)} %get-tuple-element.11, f32[384,10]{0,1:T(8,128)S(1)} %get-tuple-element.10, f32[10,128,384]{2,1,0:T(8,128)S(1)} %get-tuple-element.18), kind=kLoop, calls=%fused_computation.42 | loop fusion | flops 2941440 | bytes 3993600 | tf_op jit(solution)/shard_map/reduce_sum | solution.py:47
  37.0 0.7 %copy-done = f32[10,384,128]{1,2,0:T(8,128)S(1)} copy-done((f32[10,384,128]{1,2,0:T(8,128)S(1)}, f32[10,384,128]{1,2,0:T(8,128)}, u32[]{:S(2)}) %copy-start) | copy-done | bytes 1966104
  37.7 1.1 %fusion.16 = bf16[384,10,128]{0,2,1:T(8,128)(2,1)S(1)} fusion(f32[10,128,384]{2,1,0:T(8,128)S(1)} %fusion.36, f32[10,384,128]{1,2,0:T(8,128)S(1)} %fusion.39, f32[10,128,384]{2,1,0:T(8,128)S(1)} %fusion.41, f32[10,384,128]{1,2,0:T(8,128)S(1)} %copy-done, bf16[128,10,128]{0,2,1:T(8,128)(2,1)S(1)} %bitcast.127, f32[10,128,384]{2,1,0:T(8,128)S(1)} %get-tuple-element.20, ...), kind=kOutput, calls=%fused_computation.12 | convolution fusion | flops 132710400 | bytes 11248640 | tf_op jit(solution)/shard_map/qhk,khd->qhd/dot_general | solution.py:48
  39.3 1.5 %fusion.12 = bf16[384,1280]{1,0:T(8,128)(2,1)S(1)} fusion(bf16[384,1280]{0,1:T(8,128)(2,1)S(1)} %bitcast.131, bf16[1280,5120]{1,0:T(8,128)(2,1)S(1)} %bitcast.130, s32[]{:T(128)S(6)} %select_n.43), kind=kOutput, calls=%fused_computation.9 | convolution fusion | flops 1258782720 | bytes 5242884 | tf_op jit(solution)/shard_map/dot_general | solution.py:92
  40.8 2.9 %collective-permute-start.8 = (bf16[384,1280]{1,0:T(8,128)(2,1)S(1)}, bf16[384,1280]{1,0:T(8,128)(2,1)S(1)}, u32[]{:S(2)}, u32[]{:S(2)}) collective-permute-start(bf16[384,1280]{1,0:T(8,128)(2,1)S(1)} %fusion.12), channel_id=1, source_target_pairs={{0,1},{1,0},{2,3},{3,2},{4,5},{5,4},{6,7},{7,6},{8,9},{9,8},{10,11... | collective-permute-start | bytes 2949128 | tf_op jit(solution)/shard_map/ppermute | solution.py:97
  43.8 2.5 %fusion.9 = bf16[384,1280]{1,0:T(8,128)(2,1)} fusion(bf16[384,1280]{0,1:T(8,128)(2,1)S(1)} %bitcast.132, bf16[1280,5120]{1,0:T(8,128)(2,1)S(1)} %bitcast.130, s32[]{:T(128)S(6)} %select_n.42), kind=kOutput, calls=%fused_computation.8 | convolution fusion | flops 1258782720 | bytes 5242884 | tf_op jit(solution)/shard_map/dot_general | solution.py:92
  46.3 5.9 %fusion.2 = bf16[384,2560]{1,0:T(8,128)(2,1)S(1)} fusion(bf16[384,1280]{0,1:T(8,128)(2,1)} %bitcast.133, bf16[1280,5120]{1,0:T(8,128)(2,1)} %param.7, s32[]{:T(128)S(6)} %select_n.40), kind=kOutput, calls=%fused_computation.2 | convolution fusion | flops 2517565440 | bytes 9502724 | tf_op jit(solution)/shard_map/dot_general | solution.py:87
  52.2 1.8 %add_convert_fusion = bf16[384,2560]{1,0:T(8,128)(2,1)} fusion(bf16[384,2560]{1,0:T(8,128)(2,1)S(1)} %fusion.2, bf16[384,1280]{1,0:T(8,128)(2,1)S(1)} %collective-permute-done.8, bf16[384,1280]{1,0:T(8,128)(2,1)S(1)} %collective-permute-done.7), kind=kLoop, calls=%fused_computation.3 | loop fusion | flops 6881280 | bytes 5898240 | tf_op jit(solution)/shard_map/convert_element_type | solution.py:102
  (35 shorter events, 5.8 us)
Async XLA Ops:
  0.0 7.0 %copy-start.1 = (bf16[384,1280]{1,0:T(8,128)(2,1)S(1)}, bf16[384,1280]{1,0:T(8,128)(2,1)}, u32[]{:S(2)}) copy-start(bf16[384,1280]{1,0:T(8,128)(2,1)} %param.4) | copy-start | bytes 2949124
  1.3 9.6 %collective-permute-start.1 = (bf16[128,1280]{0,1:T(8,128)(2,1)S(1)}, bf16[128,1280]{0,1:T(8,128)(2,1)S(1)}, u32[]{:S(2)}, u32[]{:S(2)}) collective-permute-start(bf16[128,1280]{0,1:T(8,128)(2,1)S(1)} %copy.21), channel_id=1, source_target_pairs={{0,4},{2,6},{4,0},{6,2},{8,12},{10,14},{12,8},{14,10},{16,20},{18,... | collective-permute-start | bytes 983048 | tf_op jit(solution)/shard_map/ppermute | solution.py:14
  4.6 13.4 %collective-permute-start.2 = (bf16[128,1280]{0,1:T(8,128)(2,1)S(1)}, bf16[128,1280]{0,1:T(8,128)(2,1)S(1)}, u32[]{:S(2)}, u32[]{:S(2)}) collective-permute-start(bf16[128,1280]{0,1:T(8,128)(2,1)S(1)} %copy.24), channel_id=1, source_target_pairs={{0,4},{2,6},{4,0},{6,2},{8,12},{10,14},{12,8},{14,10},{16,20},{18,... | collective-permute-start | bytes 983048 | tf_op jit(solution)/shard_map/ppermute | solution.py:14
  5.6 15.7 %collective-permute-start = (bf16[2,128,1280]{1,2,0:T(8,128)(2,1)}, bf16[2,128,1280]{1,2,0:T(8,128)(2,1)}, u32[]{:S(2)}, u32[]{:S(2)}) collective-permute-start(bf16[2,128,1280]{1,2,0:T(8,128)(2,1)} %pad_maximum_fusion), channel_id=1, source_target_pairs={{0,2},{2,0},{4,6},{6,4},{8,10},{10,8},{12,14},{14,12},{16,18},{18,... | collective-permute-start | bytes 1966088 | tf_op jit(solution)/shard_map/ppermute | solution.py:14
  10.9 8.8 %collective-permute-start.3 = (bf16[128,1280]{0,1:T(8,128)(2,1)S(1)}, bf16[128,1280]{0,1:T(8,128)(2,1)S(1)}, u32[]{:S(2)}, u32[]{:S(2)}) collective-permute-start(bf16[128,1280]{0,1:T(8,128)(2,1)S(1)} %collective-permute-done.1), channel_id=1, source_target_pairs={{0,8},{2,10},{4,28},{6,30},{8,16},{10,18},{12,4},{14,6},{16,24},{1... | collective-permute-start | bytes 983048 | tf_op jit(solution)/shard_map/ppermute | solution.py:25
  17.9 9.9 %collective-permute-start.4 = (bf16[128,1280]{0,1:T(8,128)(2,1)S(1)}, bf16[128,1280]{0,1:T(8,128)(2,1)S(1)}, u32[]{:S(2)}, u32[]{:S(2)}) collective-permute-start(bf16[128,1280]{0,1:T(8,128)(2,1)S(1)} %collective-permute-done.2), channel_id=1, source_target_pairs={{0,8},{2,10},{4,28},{6,30},{8,16},{10,18},{12,4},{14,6},{16,24},{1... | collective-permute-start | bytes 983048 | tf_op jit(solution)/shard_map/ppermute | solution.py:25
  19.7 10.2 %collective-permute-start.5 = (bf16[128,1280]{0,1:T(8,128)(2,1)S(1)}, bf16[128,1280]{0,1:T(8,128)(2,1)S(1)}, u32[]{:S(2)}, u32[]{:S(2)}) collective-permute-start(bf16[128,1280]{0,1:T(8,128)(2,1)S(1)} %broadcast_select_fusion.1), channel_id=1, source_target_pairs={{0,2},{2,0},{4,6},{6,4},{8,10},{10,8},{12,14},{14,12},{16,18},{18,... | collective-permute-start | bytes 983048 | tf_op jit(solution)/shard_map/ppermute | solution.py:14
  28.4 7.3 %collective-permute-start.6 = (bf16[128,1280]{0,1:T(8,128)(2,1)S(1)}, bf16[128,1280]{0,1:T(8,128)(2,1)S(1)}, u32[]{:S(2)}, u32[]{:S(2)}) collective-permute-start(bf16[128,1280]{0,1:T(8,128)(2,1)S(1)} %broadcast_select_fusion), channel_id=1, source_target_pairs={{0,2},{2,0},{4,6},{6,4},{8,10},{10,8},{12,14},{14,12},{16,18},{18,... | collective-permute-start | bytes 983048 | tf_op jit(solution)/shard_map/ppermute | solution.py:14
  30.4 8.5 %slice-start = ((s8[13107200]{0:T(1024)(128)(4,1)}), s8[4194304]{0:T(1024)(128)(4,1)S(1)}, s32[]{:S(2)}) async-start(s8[13107200]{0:T(1024)(128)(4,1)} %bitcast.129), calls=%async_computation | async-start | bytes 8388608
  31.7 7.2 %slice-start.1 = ((s8[13107200]{0:T(1024)(128)(4,1)}), s8[4194304]{0:T(1024)(128)(4,1)S(1)}, s32[]{:S(2)}) async-start(s8[13107200]{0:T(1024)(128)(4,1)} %bitcast.129), calls=%async_computation.1 | async-start | bytes 8388608
  36.2 1.5 %copy-start = (f32[10,384,128]{1,2,0:T(8,128)S(1)}, f32[10,384,128]{1,2,0:T(8,128)}, u32[]{:S(2)}) copy-start(f32[10,384,128]{1,2,0:T(8,128)} %fusion.43) | copy-start | bytes 5898244
  36.2 2.8 %slice-start.2 = ((s8[13107200]{0:T(1024)(128)(4,1)}), s8[4194304]{0:T(1024)(128)(4,1)S(1)}, s32[]{:S(2)}) async-start(s8[13107200]{0:T(1024)(128)(4,1)} %bitcast.129), calls=%async_computation.2 | async-start | bytes 8388608
  37.7 1.6 %slice-start.3 = ((s8[13107200]{0:T(1024)(128)(4,1)}), s8[524288]{0:T(1024)(128)(4,1)S(1)}, s32[]{:S(2)}) async-start(s8[13107200]{0:T(1024)(128)(4,1)} %bitcast.129), calls=%async_computation.3 | async-start | bytes 1048576
  38.9 4.9 %copy-start.2 = (bf16[384,10,128]{0,2,1:T(8,128)(2,1)}, bf16[384,10,128]{0,2,1:T(8,128)(2,1)S(1)}, u32[]{:S(2)}) copy-start(bf16[384,10,128]{0,2,1:T(8,128)(2,1)S(1)} %fusion.16) | copy-start | bytes 2949124
  40.8 11.4 %collective-permute-start.8 = (bf16[384,1280]{1,0:T(8,128)(2,1)S(1)}, bf16[384,1280]{1,0:T(8,128)(2,1)S(1)}, u32[]{:S(2)}, u32[]{:S(2)}) collective-permute-start(bf16[384,1280]{1,0:T(8,128)(2,1)S(1)} %fusion.12), channel_id=1, source_target_pairs={{0,1},{1,0},{2,3},{3,2},{4,5},{5,4},{6,7},{7,6},{8,9},{9,8},{10,11... | collective-permute-start | bytes 2949128 | tf_op jit(solution)/shard_map/ppermute | solution.py:97
  46.2 6.0 %collective-permute-start.7 = (bf16[384,1280]{1,0:T(8,128)(2,1)}, bf16[384,1280]{1,0:T(8,128)(2,1)S(1)}, u32[]{:S(2)}, u32[]{:S(2)}) collective-permute-start(bf16[384,1280]{1,0:T(8,128)(2,1)} %fusion.9), channel_id=1, source_target_pairs={{0,1},{1,0},{2,3},{3,2},{4,5},{5,4},{6,7},{7,6},{8,9},{9,8},{10,11... | collective-permute-start | bytes 2949128 | tf_op jit(solution)/shard_map/ppermute | solution.py:97

commit v18 on v17

--- a/solution.py
+++ b/solution.py
@@ -66,9 +66,10 @@
     )
     keys = with_layout_constraint(keys, Layout(major_to_minor=(1, 0)))
     values = with_layout_constraint(values, Layout(major_to_minor=(1, 0)))
-    from_x = swap_within_four(jnp.stack((keys, values)), 1)
-    key_arrivals = [from_x[0]] + relay_chain(keys)
-    value_arrivals = [from_x[1]] + relay_chain(values)
+    width = keys.shape[1]
+    from_x = swap_within_four(jnp.concatenate((keys, values), axis=1), 1)
+    key_arrivals = [from_x[:, :width]] + relay_chain(keys)
+    value_arrivals = [from_x[:, width:]] + relay_chain(values)
     state = fold_block(state, keys, values, query_heads)
     for key_rows, value_rows in zip(key_arrivals, value_arrivals):
         state = fold_block(state, key_rows, value_rows, query_heads)

time: 54.6 us -> 54.6 us (level)
    another operation x1 -> x0, other arithmetic: 0.91 us -> none  [on_device(): from_x = swap_within_four(jnp.stack((keys, values)), 1)]
    concatenate x0 -> x1, other arithmetic: none -> 0.89 us  [on_device(): from_x = swap_within_four(jnp.concatenate((keys, values), axis=1), 1)]
where the time goes in v18:
time: 54.6 us; the launch traced here: 54 us
  matrix products  16.5 us (30%)
  waiting for transfers between devices  15.9 us (29%)
  starting transfers between devices  11.4 us (21%)
  local copies, waits for them, and re-layouts  5.4 us (10%)
  other arithmetic  4.6 us (8%)
    ppermute x5, waiting for transfers between devices, swap_within_four(): lax.ppermute(value, 'blk', [(source, source ^ bit) for source in range(co...  10.3 us
    ppermute x5, starting transfers between devices, swap_within_four(): lax.ppermute(value, 'blk', [(source, source ^ bit) for source in range(co...  5.92 us
    dot_general x1, matrix products, partial_for(): jnp.dot(attended, cols, preferred_element_type=jnp.float32)  5.92 us
    ppermute x2, waiting for transfers between devices, shift_groups(): return lax.ppermute(value, 'blk', pairs)  5.6 us
    unnamed x17, local copies, waits for them, and re-layouts  4.28 us
    dot_general x5, matrix products, fold_block(): jnp.einsum('qhk,khd->qhd', weights.astype(jnp.bfloat16), value_heads, pre...  4.28 us
    dot_general x2, matrix products, half_for(): jnp.dot(attended, cols, preferred_element_type=jnp.float32)  3.96 us
    ppermute x2, starting transfers between devices, on_device(): lax.ppermute(half_for((me + offset) % groups, h), 'mp', pairs)  2.98 us
  transfers between devices with their start and end apart: 9, of which 6 were waited for; matrix products, arithmetic and copies ran while one was open for 34% of the time, Pallas kernels for 0%

profile of v18, /device:TPU:1, one launch (start us, length us, event | category | flops | bytes accessed | tf_op | source)
XLA Modules:
  0.0 54.0 jit_solution(18330120809621792929)
XLA Ops:
  0.0 1.3 %copy.21 = bf16[128,1280]{0,1:T(8,128)(2,1)S(1)} copy(bf16[128,1280]{1,0:T(8,128)(2,1)} %param.5) | data formatting | bytes 655360 | tf_op args[1]
  1.3 2.1 %collective-permute-start.1 = (bf16[128,1280]{0,1:T(8,128)(2,1)S(1)}, bf16[128,1280]{0,1:T(8,128)(2,1)S(1)}, u32[]{:S(2)}, u32[]{:S(2)}) collective-permute-start(bf16[128,1280]{0,1:T(8,128)(2,1)S(1)} %copy.21), channel_id=1, source_target_pairs={{0,4},{2,6},{4,0},{6,2},{8,12},{10,14},{12,8},{14,10},{16,20},{18,... | collective-permute-start | bytes 983048 | tf_op jit(solution)/shard_map/ppermute | solution.py:14
  3.4 1.2 %copy.24 = bf16[128,1280]{0,1:T(8,128)(2,1)S(1)} copy(bf16[128,1280]{1,0:T(8,128)(2,1)} %param.6) | data formatting | bytes 655360 | tf_op args[2]
  4.7 0.9 %pad_maximum_fusion = bf16[128,2560]{0,1:T(8,128)(2,1)} fusion(bf16[128,1280]{0,1:T(8,128)(2,1)S(1)} %copy.24, bf16[128,1280]{0,1:T(8,128)(2,1)S(1)} %copy.21), kind=kLoop, calls=%fused_computation.60 | loop fusion | flops 1310720 | bytes 1310720 | tf_op jit(solution)/shard_map/concatenate | solution.py:70
  5.5 1.4 %collective-permute-start = (bf16[128,2560]{0,1:T(8,128)(2,1)}, bf16[128,2560]{0,1:T(8,128)(2,1)}, u32[]{:S(2)}, u32[]{:S(2)}) collective-permute-start(bf16[128,2560]{0,1:T(8,128)(2,1)} %pad_maximum_fusion), channel_id=1, source_target_pairs={{0,2},{2,0},{4,6},{6,4},{8,10},{10,8},{12,14},{14,12},{16,18},{18,... | collective-permute-start | bytes 1966088 | tf_op jit(solution)/shard_map/ppermute | solution.py:14
  8.1 1.7 %fusion.43 = f32[10,384,128]{1,2,0:T(8,128)} fusion(bf16[128,10,128]{0,2,1:T(8,128)(2,1)S(1)} %bitcast.115, f32[10,128,384]{2,1,0:T(8,128)S(1)} %get-tuple-element.24, f32[384,10]{0,1:T(8,128)S(1)} %get-tuple-element.23), kind=kOutput, calls=%fused_computation.49 | convolution fusion | flops 127303680 | bytes 4275200 | tf_op jit(solution)/shard_map/qhk,khd->qhd/dot_general | solution.py:48
  9.8 1.1 %collective-permute-done.1 = bf16[128,1280]{0,1:T(8,128)(2,1)S(1)} collective-permute-done((bf16[128,1280]{0,1:T(8,128)(2,1)S(1)}, bf16[128,1280]{0,1:T(8,128)(2,1)S(1)}, u32[]{:S(2)}, u32[]{:S(2)}) %collective-permute-start.1) | collective-permute-done | bytes 327712 | tf_op jit(solution)/shard_map/ppermute | solution.py:14
  10.9 1.2 %collective-permute-start.3 = (bf16[128,1280]{0,1:T(8,128)(2,1)S(1)}, bf16[128,1280]{0,1:T(8,128)(2,1)S(1)}, u32[]{:S(2)}, u32[]{:S(2)}) collective-permute-start(bf16[128,1280]{0,1:T(8,128)(2,1)S(1)} %collective-permute-done.1), channel_id=1, source_target_pairs={{0,8},{2,10},{4,28},{6,30},{8,16},{10,18},{12,4},{14,6},{16,24},{1... | collective-permute-start | bytes 983048 | tf_op jit(solution)/shard_map/ppermute | solution.py:25
  12.5 5.4 %collective-permute-done.2 = bf16[128,1280]{0,1:T(8,128)(2,1)S(1)} collective-permute-done((bf16[128,1280]{0,1:T(8,128)(2,1)S(1)}, bf16[128,1280]{0,1:T(8,128)(2,1)S(1)}, u32[]{:S(2)}, u32[]{:S(2)}) %collective-permute-start.2) | collective-permute-done | bytes 327712 | tf_op jit(solution)/shard_map/ppermute | solution.py:14
  17.9 1.2 %collective-permute-start.4 = (bf16[128,1280]{0,1:T(8,128)(2,1)S(1)}, bf16[128,1280]{0,1:T(8,128)(2,1)S(1)}, u32[]{:S(2)}, u32[]{:S(2)}) collective-permute-start(bf16[128,1280]{0,1:T(8,128)(2,1)S(1)} %collective-permute-done.2), channel_id=1, source_target_pairs={{0,8},{2,10},{4,28},{6,30},{8,16},{10,18},{12,4},{14,6},{16,24},{1... | collective-permute-start | bytes 983048 | tf_op jit(solution)/shard_map/ppermute | solution.py:25
  19.7 1.2 %collective-permute-start.5 = (bf16[128,1280]{0,1:T(8,128)(2,1)S(1)}, bf16[128,1280]{0,1:T(8,128)(2,1)S(1)}, u32[]{:S(2)}, u32[]{:S(2)}) collective-permute-start(bf16[128,1280]{0,1:T(8,128)(2,1)S(1)} %broadcast_select_fusion.1), channel_id=1, source_target_pairs={{0,2},{2,0},{4,6},{6,4},{8,10},{10,8},{12,14},{14,12},{16,18},{18,... | collective-permute-start | bytes 983048 | tf_op jit(solution)/shard_map/ppermute | solution.py:14
  21.2 1.1 %fusion.64 = (bf16[128,1280]{0,1:T(8,128)(2,1)S(1)}, bf16[128,1280]{0,1:T(8,128)(2,1)S(1)}) fusion(bf16[128,2560]{0,1:T(8,128)(2,1)} %collective-permute-done), kind=kLoop, calls=%fused_computation.78 | loop fusion | bytes 1310720 | tf_op jit(solution)/shard_map/slice | solution.py:72
  22.3 5.5 %collective-permute-done.4 = bf16[128,1280]{0,1:T(8,128)(2,1)S(1)} collective-permute-done((bf16[128,1280]{0,1:T(8,128)(2,1)S(1)}, bf16[128,1280]{0,1:T(8,128)(2,1)S(1)}, u32[]{:S(2)}, u32[]{:S(2)}) %collective-permute-start.4) | collective-permute-done | bytes 327712 | tf_op jit(solution)/shard_map/ppermute | solution.py:25
  28.4 1.1 %collective-permute-start.6 = (bf16[128,1280]{0,1:T(8,128)(2,1)S(1)}, bf16[128,1280]{0,1:T(8,128)(2,1)S(1)}, u32[]{:S(2)}, u32[]{:S(2)}) collective-permute-start(bf16[128,1280]{0,1:T(8,128)(2,1)S(1)} %broadcast_select_fusion), channel_id=1, source_target_pairs={{0,2},{2,0},{4,6},{6,4},{8,10},{10,8},{12,14},{14,12},{16,18},{18,... | collective-permute-start | bytes 983048 | tf_op jit(solution)/shard_map/ppermute | solution.py:14
  30.9 0.7 %fusion.28 = (f32[384,10]{0,1:T(8,128)S(1)}, f32[384,10]{0,1:T(8,128)S(1)}) fusion(f32[10,128,384]{2,1,0:T(8,128)S(1)} %get-tuple-element.26, f32[384,10]{0,1:T(8,128)S(1)} %get-tuple-element.13, f32[384,10]{0,1:T(8,128)S(1)} %get-tuple-element.12, f32[10,128,384]{2,1,0:T(8,128)S(1)} %get-tuple-element.22), kind=kLoop, calls=%fused_computation.38 | loop fusion | flops 2941440 | bytes 3993600 | tf_op jit(solution)/shard_map/reduce_sum | solution.py:47
  32.1 3.6 %collective-permute-done.6 = bf16[128,1280]{0,1:T(8,128)(2,1)S(1)} collective-permute-done((bf16[128,1280]{0,1:T(8,128)(2,1)S(1)}, bf16[128,1280]{0,1:T(8,128)(2,1)S(1)}, u32[]{:S(2)}, u32[]{:S(2)}) %collective-permute-start.6) | collective-permute-done | bytes 327712 | tf_op jit(solution)/shard_map/ppermute | solution.py:14
  36.2 0.7 %fusion.32 = (f32[384,10]{0,1:T(8,128)S(1)}, f32[384,10]{0,1:T(8,128)S(1)}) fusion(f32[10,128,384]{2,1,0:T(8,128)S(1)} %get-tuple-element.20, f32[384,10]{0,1:T(8,128)S(1)} %get-tuple-element.11, f32[384,10]{0,1:T(8,128)S(1)} %get-tuple-element.10, f32[10,128,384]{2,1,0:T(8,128)S(1)} %get-tuple-element.18), kind=kLoop, calls=%fused_computation.42 | loop fusion | flops 2941440 | bytes 3993600 | tf_op jit(solution)/shard_map/reduce_sum | solution.py:47
  37.0 0.7 %copy-done = f32[10,384,128]{1,2,0:T(8,128)S(1)} copy-done((f32[10,384,128]{1,2,0:T(8,128)S(1)}, f32[10,384,128]{1,2,0:T(8,128)}, u32[]{:S(2)}) %copy-start) | copy-done | bytes 1966104
  37.7 1.1 %fusion.16 = bf16[384,10,128]{0,2,1:T(8,128)(2,1)S(1)} fusion(f32[10,128,384]{2,1,0:T(8,128)S(1)} %fusion.36, f32[10,384,128]{1,2,0:T(8,128)S(1)} %fusion.39, f32[10,128,384]{2,1,0:T(8,128)S(1)} %fusion.41, f32[10,384,128]{1,2,0:T(8,128)S(1)} %copy-done, bf16[128,10,128]{0,2,1:T(8,128)(2,1)S(1)} %bitcast.123, f32[10,128,384]{2,1,0:T(8,128)S(1)} %get-tuple-element.20, ...), kind=kOutput, calls=%fused_computation.12 | convolution fusion | flops 132710400 | bytes 11248640 | tf_op jit(solution)/shard_map/qhk,khd->qhd/dot_general | solution.py:48
  39.3 1.5 %fusion.12 = bf16[384,1280]{1,0:T(8,128)(2,1)S(1)} fusion(bf16[384,1280]{0,1:T(8,128)(2,1)S(1)} %bitcast.127, bf16[1280,5120]{1,0:T(8,128)(2,1)S(1)} %bitcast.126, s32[]{:T(128)S(6)} %select_n.43), kind=kOutput, calls=%fused_computation.9 | convolution fusion | flops 1258782720 | bytes 5242884 | tf_op jit(solution)/shard_map/dot_general | solution.py:93
  40.8 2.9 %collective-permute-start.8 = (bf16[384,1280]{1,0:T(8,128)(2,1)S(1)}, bf16[384,1280]{1,0:T(8,128)(2,1)S(1)}, u32[]{:S(2)}, u32[]{:S(2)}) collective-permute-start(bf16[384,1280]{1,0:T(8,128)(2,1)S(1)} %fusion.12), channel_id=1, source_target_pairs={{0,1},{1,0},{2,3},{3,2},{4,5},{5,4},{6,7},{7,6},{8,9},{9,8},{10,11... | collective-permute-start | bytes 2949128 | tf_op jit(solution)/shard_map/ppermute | solution.py:98
  43.8 2.5 %fusion.9 = bf16[384,1280]{1,0:T(8,128)(2,1)} fusion(bf16[384,1280]{0,1:T(8,128)(2,1)S(1)} %bitcast.128, bf16[1280,5120]{1,0:T(8,128)(2,1)S(1)} %bitcast.126, s32[]{:T(128)S(6)} %select_n.42), kind=kOutput, calls=%fused_computation.8 | convolution fusion | flops 1258782720 | bytes 5242884 | tf_op jit(solution)/shard_map/dot_general | solution.py:93
  46.3 5.9 %fusion.2 = bf16[384,2560]{1,0:T(8,128)(2,1)S(1)} fusion(bf16[384,1280]{0,1:T(8,128)(2,1)} %bitcast.129, bf16[1280,5120]{1,0:T(8,128)(2,1)} %param.7, s32[]{:T(128)S(6)} %select_n.40), kind=kOutput, calls=%fused_computation.2 | convolution fusion | flops 2517565440 | bytes 9502724 | tf_op jit(solution)/shard_map/dot_general | solution.py:88
  52.2 1.8 %add_convert_fusion = bf16[384,2560]{1,0:T(8,128)(2,1)} fusion(bf16[384,2560]{1,0:T(8,128)(2,1)S(1)} %fusion.2, bf16[384,1280]{1,0:T(8,128)(2,1)S(1)} %collective-permute-done.8, bf16[384,1280]{1,0:T(8,128)(2,1)S(1)} %collective-permute-done.7), kind=kLoop, calls=%fused_computation.3 | loop fusion | flops 6881280 | bytes 5898240 | tf_op jit(solution)/shard_map/convert_element_type | solution.py:103
  (35 shorter events, 5.7 us)
Async XLA Ops:
  0.0 7.0 %copy-start.1 = (bf16[384,1280]{1,0:T(8,128)(2,1)S(1)}, bf16[384,1280]{1,0:T(8,128)(2,1)}, u32[]{:S(2)}) copy-start(bf16[384,1280]{1,0:T(8,128)(2,1)} %param.4) | copy-start | bytes 2949124
  1.3 9.6 %collective-permute-start.1 = (bf16[128,1280]{0,1:T(8,128)(2,1)S(1)}, bf16[128,1280]{0,1:T(8,128)(2,1)S(1)}, u32[]{:S(2)}, u32[]{:S(2)}) collective-permute-start(bf16[128,1280]{0,1:T(8,128)(2,1)S(1)} %copy.21), channel_id=1, source_target_pairs={{0,4},{2,6},{4,0},{6,2},{8,12},{10,14},{12,8},{14,10},{16,20},{18,... | collective-permute-start | bytes 983048 | tf_op jit(solution)/shard_map/ppermute | solution.py:14
  4.6 13.4 %collective-permute-start.2 = (bf16[128,1280]{0,1:T(8,128)(2,1)S(1)}, bf16[128,1280]{0,1:T(8,128)(2,1)S(1)}, u32[]{:S(2)}, u32[]{:S(2)}) collective-permute-start(bf16[128,1280]{0,1:T(8,128)(2,1)S(1)} %copy.24), channel_id=1, source_target_pairs={{0,4},{2,6},{4,0},{6,2},{8,12},{10,14},{12,8},{14,10},{16,20},{18,... | collective-permute-start | bytes 983048 | tf_op jit(solution)/shard_map/ppermute | solution.py:14
  5.5 15.7 %collective-permute-start = (bf16[128,2560]{0,1:T(8,128)(2,1)}, bf16[128,2560]{0,1:T(8,128)(2,1)}, u32[]{:S(2)}, u32[]{:S(2)}) collective-permute-start(bf16[128,2560]{0,1:T(8,128)(2,1)} %pad_maximum_fusion), channel_id=1, source_target_pairs={{0,2},{2,0},{4,6},{6,4},{8,10},{10,8},{12,14},{14,12},{16,18},{18,... | collective-permute-start | bytes 1966088 | tf_op jit(solution)/shard_map/ppermute | solution.py:14
  10.9 8.8 %collective-permute-start.3 = (bf16[128,1280]{0,1:T(8,128)(2,1)S(1)}, bf16[128,1280]{0,1:T(8,128)(2,1)S(1)}, u32[]{:S(2)}, u32[]{:S(2)}) collective-permute-start(bf16[128,1280]{0,1:T(8,128)(2,1)S(1)} %collective-permute-done.1), channel_id=1, source_target_pairs={{0,8},{2,10},{4,28},{6,30},{8,16},{10,18},{12,4},{14,6},{16,24},{1... | collective-permute-start | bytes 983048 | tf_op jit(solution)/shard_map/ppermute | solution.py:25
  17.9 9.9 %collective-permute-start.4 = (bf16[128,1280]{0,1:T(8,128)(2,1)S(1)}, bf16[128,1280]{0,1:T(8,128)(2,1)S(1)}, u32[]{:S(2)}, u32[]{:S(2)}) collective-permute-start(bf16[128,1280]{0,1:T(8,128)(2,1)S(1)} %collective-permute-done.2), channel_id=1, source_target_pairs={{0,8},{2,10},{4,28},{6,30},{8,16},{10,18},{12,4},{14,6},{16,24},{1... | collective-permute-start | bytes 983048 | tf_op jit(solution)/shard_map/ppermute | solution.py:25
  19.7 10.2 %collective-permute-start.5 = (bf16[128,1280]{0,1:T(8,128)(2,1)S(1)}, bf16[128,1280]{0,1:T(8,128)(2,1)S(1)}, u32[]{:S(2)}, u32[]{:S(2)}) collective-permute-start(bf16[128,1280]{0,1:T(8,128)(2,1)S(1)} %broadcast_select_fusion.1), channel_id=1, source_target_pairs={{0,2},{2,0},{4,6},{6,4},{8,10},{10,8},{12,14},{14,12},{16,18},{18,... | collective-permute-start | bytes 983048 | tf_op jit(solution)/shard_map/ppermute | solution.py:14
  28.4 7.3 %collective-permute-start.6 = (bf16[128,1280]{0,1:T(8,128)(2,1)S(1)}, bf16[128,1280]{0,1:T(8,128)(2,1)S(1)}, u32[]{:S(2)}, u32[]{:S(2)}) collective-permute-start(bf16[128,1280]{0,1:T(8,128)(2,1)S(1)} %broadcast_select_fusion), channel_id=1, source_target_pairs={{0,2},{2,0},{4,6},{6,4},{8,10},{10,8},{12,14},{14,12},{16,18},{18,... | collective-permute-start | bytes 983048 | tf_op jit(solution)/shard_map/ppermute | solution.py:14
  30.4 8.5 %slice-start = ((s8[13107200]{0:T(1024)(128)(4,1)}), s8[4194304]{0:T(1024)(128)(4,1)S(1)}, s32[]{:S(2)}) async-start(s8[13107200]{0:T(1024)(128)(4,1)} %bitcast.125), calls=%async_computation | async-start | bytes 8388608
  31.7 7.2 %slice-start.1 = ((s8[13107200]{0:T(1024)(128)(4,1)}), s8[4194304]{0:T(1024)(128)(4,1)S(1)}, s32[]{:S(2)}) async-start(s8[13107200]{0:T(1024)(128)(4,1)} %bitcast.125), calls=%async_computation.1 | async-start | bytes 8388608
  36.2 1.5 %copy-start = (f32[10,384,128]{1,2,0:T(8,128)S(1)}, f32[10,384,128]{1,2,0:T(8,128)}, u32[]{:S(2)}) copy-start(f32[10,384,128]{1,2,0:T(8,128)} %fusion.43) | copy-start | bytes 5898244
  36.2 2.8 %slice-start.2 = ((s8[13107200]{0:T(1024)(128)(4,1)}), s8[4194304]{0:T(1024)(128)(4,1)S(1)}, s32[]{:S(2)}) async-start(s8[13107200]{0:T(1024)(128)(4,1)} %bitcast.125), calls=%async_computation.2 | async-start | bytes 8388608
  37.7 1.6 %slice-start.3 = ((s8[13107200]{0:T(1024)(128)(4,1)}), s8[524288]{0:T(1024)(128)(4,1)S(1)}, s32[]{:S(2)}) async-start(s8[13107200]{0:T(1024)(128)(4,1)} %bitcast.125), calls=%async_computation.3 | async-start | bytes 1048576
  38.9 4.9 %copy-start.2 = (bf16[384,10,128]{0,2,1:T(8,128)(2,1)}, bf16[384,10,128]{0,2,1:T(8,128)(2,1)S(1)}, u32[]{:S(2)}) copy-start(bf16[384,10,128]{0,2,1:T(8,128)(2,1)S(1)} %fusion.16) | copy-start | bytes 2949124
  40.8 11.4 %collective-permute-start.8 = (bf16[384,1280]{1,0:T(8,128)(2,1)S(1)}, bf16[384,1280]{1,0:T(8,128)(2,1)S(1)}, u32[]{:S(2)}, u32[]{:S(2)}) collective-permute-start(bf16[384,1280]{1,0:T(8,128)(2,1)S(1)} %fusion.12), channel_id=1, source_target_pairs={{0,1},{1,0},{2,3},{3,2},{4,5},{5,4},{6,7},{7,6},{8,9},{9,8},{10,11... | collective-permute-start | bytes 2949128 | tf_op jit(solution)/shard_map/ppermute | solution.py:98
  46.2 6.0 %collective-permute-start.7 = (bf16[384,1280]{1,0:T(8,128)(2,1)}, bf16[384,1280]{1,0:T(8,128)(2,1)S(1)}, u32[]{:S(2)}, u32[]{:S(2)}) collective-permute-start(bf16[384,1280]{1,0:T(8,128)(2,1)} %fusion.9), channel_id=1, source_target_pairs={{0,1},{1,0},{2,3},{3,2},{4,5},{5,4},{6,7},{7,6},{8,9},{9,8},{10,11... | collective-permute-start | bytes 2949128 | tf_op jit(solution)/shard_map/ppermute | solution.py:98
